TPU v7x, 512 devices: a whole 4x8x8 slice. The times are simulated.
512 devices in a mesh: region: 4 (over z_lo), gx: 16 (over y, z_hi), gy: 8 (over x, core).
Axes of the slice: x: 4, y: 8, z: 8 (z_hi: 2, z_lo: 4; z = z_hi * 4 + z_lo), core: 2. Of those that a mesh axis runs over, the one named last changes fastest.
Arguments:
- spins: float32 [3, 8, 512, 1024], P(None, 'region', 'gx', 'gy'), may hold values from -1 to 1, as said below
- uniforms: float32 [2, 8, 512, 1024], P(None, 'region', 'gx', 'gy'), may hold values from 0 to 1
- trials: float32 [2, 3, 8, 512, 1024], P(None, None, 'region', 'gx', 'gy'), may hold values from -1 to 1
- exch_kernel: float32 [3, 3, 3], replicated, may hold values from -0.5 to 1
- film_m: float32 [3, 8192, 2048], P(None, ('region', 'gx'), 'gy'), may hold values from -1 to 1, as said below
- film_anis: float32 [8192, 2048], P(('region', 'gx'), 'gy'), may hold values from 0.2 to 2
Outputs:
- spins_out: float32 [3, 8, 512, 1024], P(None, 'region', 'gx', 'gy')
- film_out: float32 [3, 8192, 2048], P(None, ('region', 'gx'), 'gy')
Inputs may be any that keep to these rules, and one draw needn't show every extreme that they name: `spins`: the three components of each site form a unit vector. `film_m`: the three components of each cell form a unit vector.
All inputs are finite; a program needn't handle non-finite values.
Results may differ from a plain program's by a relative error of at most 0.0001.
Values sent between devices are 32-bit elements; how exact they have to be, the bound alone decides.
No kernel may reach another device: no remote copies, remote signals or barrier semaphores. Data moves between devices by JAX's collectives and lax.ppermute only.
A program may use at most 64 MiB of HBM per device.

v0:
```python
import jax
import jax.numpy as jnp
from jax import lax
from jax.sharding import Mesh
from jax.sharding import PartitionSpec as P

K = 8
SWEEPS = 2
REGION_GX = ("region", "gx_0", "gx_1")
GY = ("gy_0", "gy_1")
GX = ("gx_0", "gx_1")


coupling_down = 1.0
anisotropy = 0.5
inverse_temp = 2.0
softness = 0.05
step_cone = 0.4
coupling_up = 2.0
damping = 0.1
time_step = 0.05


def with_halo(array, sides, width):
    edges = {}
    for axis, dim in sides:
        count, length = (lax.axis_size(axis), array.shape[dim])
        up = [(i, (i + 1) % count) for i in range(count - 1)]
        last = lax.slice_in_dim(array, length - width, length, axis=dim)
        leading = lax.slice_in_dim(array, 0, width, axis=dim)
        edges[dim] = (
            lax.ppermute(last, axis, up),
            lax.ppermute(leading, axis, [(b, a) for a, b in up]),
        )
    done = []
    for _, dim in sides:
        low, high = edges[dim]
        around = [(width, width) if d in done else (0, 0) for d in range(array.ndim)]
        array = jnp.concatenate([jnp.pad(low, around), array, jnp.pad(high, around)], axis=dim)
        done.append(dim)
    return array


def split_up(array, dim, count):
    shape = array.shape
    parts = array.reshape(*shape[:dim], count, shape[dim] // count, *shape[dim + 1 :])
    return jnp.moveaxis(parts, dim, 0)


def summed_on_arrival(array, axis, dim):
    parts = split_up(array, dim, lax.axis_size(axis))
    arrived = lax.all_to_all(parts, axis, split_axis=0, concat_axis=0, tiled=True)
    return arrived.sum(axis=0)


def summed_rows(array, axes, dim):
    far, near = axes
    own = summed_on_arrival(split_up(array, dim, lax.axis_size(far)), near, dim + 1)
    return jnp.sum(lax.all_to_all(own, far, 0, 0, tiled=True), axis=0)


def picked(array, axis, root):
    return lax.dynamic_index_in_dim(lax.all_gather(array, axis), root, 0, keepdims=False)


def copy_for_each(array, axis):
    count = lax.axis_size(axis)
    return lax.all_to_all(
        jnp.broadcast_to(array[None], (count, *array.shape)), axis, 0, 0, tiled=True
    )


def laid_out(parts, dim):
    shape = list(parts.shape[1:])
    shape[dim] *= parts.shape[0]
    return jnp.moveaxis(parts, 0, dim).reshape(shape)


def whole_of(array, axes, dim):
    far, near = axes
    parts = copy_for_each(copy_for_each(array, far), near)
    return laid_out(parts.swapaxes(0, 1).reshape(-1, *array.shape), dim)


def normalized(vector):
    return vector / jnp.sqrt(jnp.sum(vector * vector, axis=0, keepdims=True))


def apply_kernel(matrix, vector):
    return jnp.stack(
        [
            matrix[component, 0] * vector[0]
            + matrix[component, 1] * vector[1]
            + matrix[component, 2] * vector[2]
            for component in range(3)
        ]
    )


def apply_transposed(matrix, vector):
    return jnp.stack(
        [
            matrix[0, component] * vector[0]
            + matrix[1, component] * vector[1]
            + matrix[2, component] * vector[2]
            for component in range(3)
        ]
    )


def local_field(padded, exch_kernel):
    forward = (padded[:, 2:, 1:-1, 1:-1], padded[:, 1:-1, 2:, 1:-1], padded[:, 1:-1, 1:-1, 2:])
    backward = (padded[:, :-2, 1:-1, 1:-1], padded[:, 1:-1, :-2, 1:-1], padded[:, 1:-1, 1:-1, :-2])
    summed = apply_kernel(exch_kernel[0], forward[0]) + apply_transposed(
        exch_kernel[0], backward[0]
    )
    for direction in (1, 2):
        summed = summed + apply_kernel(exch_kernel[direction], forward[direction])
        summed = summed + apply_transposed(exch_kernel[direction], backward[direction])
    return summed


def metropolis(spins, padded, exch_kernel, film_near, trial_move, uniform_draw, colour_mask):
    field_sum = local_field(padded, exch_kernel) + coupling_down * film_near
    proposal = normalized(spins + step_cone * trial_move)
    change = -jnp.sum((proposal - spins) * field_sum, axis=0) - anisotropy * (
        proposal[2] * proposal[2] - spins[2] * spins[2]
    )
    accept = jnp.exp(jnp.minimum(-inverse_temp * change, 0.0))
    weight = jax.nn.sigmoid((accept - uniform_draw) / softness)
    blended = normalized((1.0 - weight) * spins + weight * proposal)
    return jnp.where(colour_mask[None], blended, spins)


def cross_product(left, right):
    return jnp.stack(
        [
            left[1] * right[2] - left[2] * right[1],
            left[2] * right[0] - left[0] * right[2],
            left[0] * right[1] - left[1] * right[0],
        ]
    )


def film_rate(magnet, padded, film_anis, interface):
    laplace_sum = (
        padded[:, 2:, 1:-1]
        + padded[:, :-2, 1:-1]
        + padded[:, 1:-1, 2:]
        + padded[:, 1:-1, :-2]
        - 4.0 * magnet
    )
    field_sum = laplace_sum + coupling_up * interface
    field_sum = jnp.stack([field_sum[0], field_sum[1], field_sum[2] + film_anis * magnet[2]])
    precession = cross_product(magnet, field_sum)
    relaxation = cross_product(magnet, precession)
    return -(precession + damping * relaxation) / (1.0 + damping * damping)


def film_halo(magnet):
    return with_halo(magnet, ((REGION_GX, 1), (GY, 2)), 1)


def body(spins, uniforms, trials, exch_kernel, film_m, film_anis):
    layers_dev = spins.shape[1]
    rows_x = spins.shape[2]
    rows_y = spins.shape[3]
    piece_x = rows_x // K
    piece_y = rows_y // K
    gx_count = lax.axis_size(GX)
    gy_count = lax.axis_size(GY)
    tile_count = gx_count * gy_count
    region_pos = lax.axis_index("region")
    gx_pos = lax.axis_index(GX)
    gy_pos = lax.axis_index(GY)
    first_tile = (region_pos == 0) & (gx_pos == 0) & (gy_pos == 0)
    film_block = film_m[:, : piece_x * gx_count, : piece_y * gy_count]
    stack_spins, unif_all, trial_all = (spins, uniforms, trials)
    layer_pos = region_pos * layers_dev + jnp.arange(layers_dev, dtype=jnp.int32)
    pieces = (
        film_block.reshape(3, gx_count, piece_x, gy_count, piece_y)
        .transpose(1, 3, 0, 2, 4)
        .reshape(tile_count, 3, piece_x, piece_y)
    )
    pieces = jnp.where(first_tile, pieces, 0.0)
    placed = summed_rows(pieces, (("gx_0", "gx_1", "gy_0"), "gy_1"), 0)[0]
    own_cells = picked(placed, "region", 0)
    film_cells = jnp.repeat(jnp.repeat(own_cells, K, axis=1), K, axis=2)
    film_near = jnp.broadcast_to(film_cells[:, None], (3, stack_spins.shape[1], rows_x, rows_y))
    x_global = gx_pos * rows_x + jnp.arange(rows_x, dtype=jnp.int32)
    y_global = gy_pos * rows_y + jnp.arange(rows_y, dtype=jnp.int32)
    parity = (layer_pos[:, None, None] + x_global[None, :, None] + y_global[None, None, :]) % 2
    for sweep_index in range(SWEEPS):
        for colour in (0, 1):
            padded = with_halo(stack_spins, (("region", 1), (GX, 2), (GY, 3)), 1)
            stack_spins = metropolis(
                stack_spins,
                padded,
                exch_kernel,
                film_near,
                trial_all[sweep_index],
                unif_all[sweep_index],
                parity == colour,
            )
    averages = stack_spins[:, 0].reshape(3, piece_x, K, piece_y, K).mean(axis=(2, 4))
    gathered = whole_of(averages[None], (("gx_0", "gx_1", "gy_0"), "gy_1"), 0)
    assembled = (
        gathered.reshape(gx_count, gy_count, 3, piece_x, piece_y)
        .transpose(2, 0, 3, 1, 4)
        .reshape(3, gx_count * piece_x, gy_count * piece_y)
    )
    padded_block = jnp.pad(
        assembled,
        (
            (0, 0),
            (0, film_m.shape[1] - assembled.shape[1]),
            (0, film_m.shape[2] - assembled.shape[2]),
        ),
    )
    interface = jnp.where(first_tile, padded_block, 0.0)
    rate_start = film_rate(film_m, film_halo(film_m), film_anis, interface)
    predicted = film_m + time_step * rate_start
    rate_trial = film_rate(predicted, film_halo(predicted), film_anis, interface)
    corrected = film_m + 0.5 * time_step * (rate_start + rate_trial)
    return (stack_spins, normalized(corrected))


def solution(mesh):
    finer = Mesh(
        mesh.devices.reshape(mesh.shape["region"], 8, 2, 4, 2),
        ("region", "gx_0", "gx_1", "gy_0", "gy_1"),
    )
    in_specs = (
        P(None, "region", GX, GY),
        P(None, "region", GX, GY),
        P(None, None, "region", GX, GY),
        P(),
        P(None, REGION_GX, GY),
        P(REGION_GX, GY),
    )
    out_specs = (P(None, "region", GX, GY), P(None, REGION_GX, GY))
    return jax.shard_map(body, mesh=finer, in_specs=in_specs, out_specs=out_specs, check_vma=False)
```

profile of v0, /device:TPU:1, one launch (start us, length us, event | category | flops | bytes accessed | tf_op | source)
XLA Modules:
  0.0 337.0 jit_solution(14933307176130261837)
XLA Ops:
  1.5 4.8 %collective-permute-start.1 = (f32[3,1,32,128]{3,2,1,0:T(8,128)S(1)}, f32[3,1,32,128]{3,2,1,0:T(8,128)S(1)}, u32[]{:S(2)}, u32[]{:S(2)}) collective-permute-start(f32[3,1,32,128]{3,2,1,0:T(8,128)S(1)} %get-tuple-element.208), channel_id=1, source_target_pairs={{0,128},{128,256},{256,384},{1,129},{129,257},{257,385},{2,130},{1... | collective-permute-start | bytes 147464 | tf_op jit(solution)/shard_map/ppermute | solution.py:32
  7.7 9.7 %collective-permute-start.3 = (f32[3,2,1,128]{3,2,1,0:T(1,128)S(1)}, f32[3,2,1,128]{3,2,1,0:T(1,128)S(1)}, u32[]{:S(2)}, u32[]{:S(2)}) collective-permute-start(f32[3,2,1,128]{3,2,1,0:T(1,128)S(1)} %get-tuple-element.204), channel_id=1, source_target_pairs={{0,8},{8,16},{16,24},{24,32},{32,40},{40,48},{48,56},{56,64},{64,7... | collective-permute-start | bytes 9224 | tf_op jit(solution)/shard_map/ppermute | solution.py:32
  18.8 4.2 %collective-permute-start.5 = (f32[3,2,32,1]{3,2,1,0:T(8,128)S(1)}, f32[3,2,32,1]{3,2,1,0:T(8,128)S(1)}, u32[]{:S(2)}, u32[]{:S(2)}) collective-permute-start(f32[3,2,32,1]{3,2,1,0:T(8,128)S(1)} %get-tuple-element.200), channel_id=1, source_target_pairs={{0,1},{1,2},{2,3},{3,4},{4,5},{5,6},{6,7},{8,9},{9,10},{10,11},{11... | collective-permute-start | bytes 2312 | tf_op jit(solution)/shard_map/ppermute | solution.py:32
  24.0 3.5 %all_to_all.20 = f32[2,1,12288]{2,1,0:T(1,128)S(1)} all-to-all(f32[2,1,12288]{2,1,0:T(1,128)S(1)} %reshape.178), channel_id=1, replica_groups=mesh['region'=4,'gx_0'=8,'gx_1'=2,'gy_0'=4,'gy_1'=2] {'gy_1'}, dimensions={0} | all-to-all | bytes 196608 | tf_op jit(solution)/shard_map/all_to_all | solution.py:52
  30.4 16.1 %all-to-all-start.1 = ((f32[64,1,192]{2,1,0:T(1,128)}), f32[64,1,192]{2,1,0:T(1,128)S(1)}, u32[]{:S(2)}, u32[]{:S(2)}) async-start(f32[64,1,192]{2,1,0:T(1,128)} %reshape.180), calls=%async_computation.1 | async-start | bytes 131072 | tf_op jit(solution)/shard_map/all_to_all | solution.py:59
  50.8 3.2 multiply_add_fusion.67
  54.0 3.7 %multiply_add_fusion.69 = (f32[1,2,32,128]{3,2,1,0:T(8,128)S(1)}, f32[1,2,32,128]{3,2,1,0:T(8,128)S(1)}) fusion(f32[1,2,32,128]{3,2,1,0:T(8,128)S(1)} %get-tuple-element.133, f32[1,2,32,128]{3,2,1,0:T(8,128)S(1)} %get-tuple-element.134, f32[1,2,32,128]{3,2,1,0:T(8,128)S(1)} %get-tuple-element.135, f32[]{:T(128)} %bitcast.17, f32[]{:T(128)} %bitcast.16, ...), kind=kLoop, calls=%fused_computation.346 | loop fusion | flops 81920 | bytes 163864 | tf_op jit(solution)/shard_map/add | solution.py:92
  57.7 3.8 %multiply_add_fusion.66 = (f32[1,2,32,128]{3,2,1,0:T(8,128)S(1)}, f32[1,2,32,128]{3,2,1,0:T(8,128)S(1)}) fusion(f32[1,2,32,128]{3,2,1,0:T(8,128)S(1)} %get-tuple-element.87, f32[1,2,32,128]{3,2,1,0:T(8,128)S(1)} %get-tuple-element.86, f32[1,2,32,128]{3,2,1,0:T(8,128)S(1)} %get-tuple-element.85, f32[]{:T(128)} %bitcast.19, f32[]{:T(128)} %bitcast.16, ...), kind=kLoop, calls=%fused_computation.343 | loop fusion | flops 81920 | bytes 163864 | tf_op jit(solution)/shard_map/add | solution.py:103
  61.6 5.6 %multiply_add_fusion.76 = (f32[1,2,32,128]{3,2,1,0:T(8,128)S(1)}, f32[1,2,32,128]{3,2,1,0:T(8,128)S(1)}, f32[1,2,32,128]{3,2,1,0:T(8,128)S(1)}) fusion(f32[3,3,32,128]{3,2,1,0:T(8,128)S(1)} %get-tuple-element.211, f32[]{:T(128)} %bitcast.4, f32[]{:T(128)} %bitcast.3, f32[]{:T(128)} %bitcast.2, f32[]{:T(128)} %bitcast.7, f32[]{:T(128)} %bitcast.6, ...), kind=kLoop, calls=%fused_computation.353 | loop fusion | flops 122880 | bytes 196644 | tf_op jit(solution)/shard_map/add | solution.py:92
  67.2 5.6 %multiply_add_fusion.73 = (f32[1,2,32,128]{3,2,1,0:T(8,128)S(1)}, f32[1,2,32,128]{3,2,1,0:T(8,128)S(1)}, f32[1,2,32,128]{3,2,1,0:T(8,128)S(1)}) fusion(f32[3,3,32,128]{3,2,1,0:T(8,128)S(1)} %get-tuple-element.198, f32[]{:T(128)} %bitcast.8, f32[]{:T(128)} %bitcast.5, f32[]{:T(128)} %bitcast.2, f32[]{:T(128)} %bitcast.9, f32[]{:T(128)} %bitcast.6, ...), kind=kLoop, calls=%fused_computation.350 | loop fusion | flops 122880 | bytes 196644 | tf_op jit(solution)/shard_map/add | solution.py:103
  73.2 5.7 %multiply_add_fusion.64 = (f32[1,2,32,128]{3,2,1,0:T(8,128)S(1)}, f32[1,2,32,128]{3,2,1,0:T(8,128)S(1)}, f32[1,2,32,128]{3,2,1,0:T(8,128)S(1)}) fusion(f32[3,4,34,129]{3,2,1,0:T(8,128)S(1)} %get-tuple-element.131, f32[]{:T(128)} %bitcast.24, f32[]{:T(128)} %bitcast.23, f32[]{:T(128)} %bitcast.22, f32[]{:T(128)} %bitcast.27, f32[]{:T(128)} %bitcast.26, ...), kind=kLoop, calls=%fused_computation.341 | loop fusion | flops 122880 | bytes 196644 | tf_op jit(solution)/shard_map/add | solution.py:92
  78.9 5.6 %multiply_add_fusion.61 = (f32[1,2,32,128]{3,2,1,0:T(8,128)S(1)}, f32[1,2,32,128]{3,2,1,0:T(8,128)S(1)}, f32[1,2,32,128]{3,2,1,0:T(8,128)S(1)}) fusion(f32[3,4,34,129]{3,2,1,0:T(8,128)S(1)} %get-tuple-element.130, f32[]{:T(128)} %bitcast.28, f32[]{:T(128)} %bitcast.25, f32[]{:T(128)} %bitcast.22, f32[]{:T(128)} %bitcast.29, f32[]{:T(128)} %bitcast.26, ...), kind=kLoop, calls=%fused_computation.338 | loop fusion | flops 122880 | bytes 196644 | tf_op jit(solution)/shard_map/add | solution.py:103
  85.6 11.6 %all-gather = f32[12,4,16]{2,1,0:T(4,128)S(1)} all-gather(f32[3,4,16]{2,1,0:T(4,128)S(1)} %reduce_sum.151), channel_id=2, replica_groups=mesh['region'=4,'gx_0'=8,'gx_1'=2,'gy_0'=4,'gy_1'=2] {'region'}, dimensions={0}, use_global_device_ids=true | all-gather | bytes 3840 | tf_op jit(solution)/shard_map/all_gather | solution.py:63
  104.0 7.9 %collective-permute-start.9 = (f32[3,2,1,128]{3,2,1,0:T(1,128)S(1)}, f32[3,2,1,128]{3,2,1,0:T(1,128)S(1)}, u32[]{:S(2)}, u32[]{:S(2)}) collective-permute-start(f32[3,2,1,128]{3,2,1,0:T(1,128)S(1)} %get-tuple-element.182), channel_id=1, source_target_pairs={{0,8},{8,16},{16,24},{24,32},{32,40},{40,48},{48,56},{56,64},{64,7... | collective-permute-start | bytes 9224 | tf_op jit(solution)/shard_map/ppermute | solution.py:32
  112.0 6.8 %collective-permute-start.11 = (f32[3,2,32,1]{3,2,1,0:T(8,128)S(1)}, f32[3,2,32,1]{3,2,1,0:T(8,128)S(1)}, u32[]{:S(2)}, u32[]{:S(2)}) collective-permute-start(f32[3,2,32,1]{3,2,1,0:T(8,128)S(1)} %get-tuple-element.178), channel_id=1, source_target_pairs={{0,1},{1,2},{2,3},{3,4},{4,5},{5,6},{6,7},{8,9},{9,10},{10,11},{11... | collective-permute-start | bytes 2312 | tf_op jit(solution)/shard_map/ppermute | solution.py:32
  120.9 3.9 %collective-permute-done.10 = f32[3,2,32,1]{3,2,1,0:T(8,128)S(1)} collective-permute-done((f32[3,2,32,1]{3,2,1,0:T(8,128)S(1)}, f32[3,2,32,1]{3,2,1,0:T(8,128)S(1)}, u32[]{:S(2)}, u32[]{:S(2)}) %collective-permute-start.10) | collective-permute-done | bytes 800 | tf_op jit(solution)/shard_map/ppermute | solution.py:33
  125.1 5.7 %multiply_add_fusion.46 = (f32[1,2,32,128]{3,2,1,0:T(8,128)S(1)}, f32[1,2,32,128]{3,2,1,0:T(8,128)S(1)}, f32[1,2,32,128]{3,2,1,0:T(8,128)S(1)}) fusion(f32[3,4,34,129]{3,2,1,0:T(8,128)S(1)} %get-tuple-element.129, f32[]{:T(128)} %bitcast.24, f32[]{:T(128)} %bitcast.23, f32[]{:T(128)} %bitcast.22, f32[]{:T(128)} %bitcast.27, f32[]{:T(128)} %bitcast.26, ...), kind=kLoop, calls=%fused_computation.322 | loop fusion | flops 122880 | bytes 196644 | tf_op jit(solution)/shard_map/add | solution.py:92
  130.8 5.6 %multiply_add_fusion.43 = (f32[1,2,32,128]{3,2,1,0:T(8,128)S(1)}, f32[1,2,32,128]{3,2,1,0:T(8,128)S(1)}, f32[1,2,32,128]{3,2,1,0:T(8,128)S(1)}) fusion(f32[3,4,34,129]{3,2,1,0:T(8,128)S(1)} %get-tuple-element.128, f32[]{:T(128)} %bitcast.28, f32[]{:T(128)} %bitcast.25, f32[]{:T(128)} %bitcast.22, f32[]{:T(128)} %bitcast.29, f32[]{:T(128)} %bitcast.26, ...), kind=kLoop, calls=%fused_computation.319 | loop fusion | flops 122880 | bytes 196644 | tf_op jit(solution)/shard_map/add | solution.py:103
  136.4 3.2 multiply_add_fusion.55
  139.6 3.8 %multiply_add_fusion.57 = (f32[1,2,32,128]{3,2,1,0:T(8,128)S(1)}, f32[1,2,32,128]{3,2,1,0:T(8,128)S(1)}) fusion(f32[1,2,32,128]{3,2,1,0:T(8,128)S(1)} %get-tuple-element.189, f32[1,2,32,128]{3,2,1,0:T(8,128)S(1)} %get-tuple-element.190, f32[1,2,32,128]{3,2,1,0:T(8,128)S(1)} %get-tuple-element.191, f32[]{:T(128)} %bitcast.7, f32[]{:T(128)} %bitcast.6, ...), kind=kLoop, calls=%fused_computation.333 | loop fusion | flops 81920 | bytes 163864 | tf_op jit(solution)/shard_map/add | solution.py:92
  143.4 3.7 %multiply_add_fusion.54 = (f32[1,2,32,128]{3,2,1,0:T(8,128)S(1)}, f32[1,2,32,128]{3,2,1,0:T(8,128)S(1)}) fusion(f32[1,2,32,128]{3,2,1,0:T(8,128)S(1)} %get-tuple-element.73, f32[1,2,32,128]{3,2,1,0:T(8,128)S(1)} %get-tuple-element.72, f32[1,2,32,128]{3,2,1,0:T(8,128)S(1)} %get-tuple-element.71, f32[]{:T(128)} %bitcast.9, f32[]{:T(128)} %bitcast.6, ...), kind=kLoop, calls=%fused_computation.330 | loop fusion | flops 81920 | bytes 163864 | tf_op jit(solution)/shard_map/add | solution.py:103
  149.1 3.7 %multiply_add_fusion.51 = (f32[1,2,32,128]{3,2,1,0:T(8,128)S(1)}, f32[1,2,32,128]{3,2,1,0:T(8,128)S(1)}) fusion(f32[1,2,32,128]{3,2,1,0:T(8,128)S(1)} %get-tuple-element.69, f32[1,2,32,128]{3,2,1,0:T(8,128)S(1)} %get-tuple-element.68, f32[1,2,32,128]{3,2,1,0:T(8,128)S(1)} %get-tuple-element.67, f32[]{:T(128)} %bitcast.17, f32[]{:T(128)} %bitcast.16, ...), kind=kLoop, calls=%fused_computation.327 | loop fusion | flops 81920 | bytes 163864 | tf_op jit(solution)/shard_map/add | solution.py:92
  154.6 3.8 %multiply_add_fusion.48 = (f32[1,2,32,128]{3,2,1,0:T(8,128)S(1)}, f32[1,2,32,128]{3,2,1,0:T(8,128)S(1)}) fusion(f32[1,2,32,128]{3,2,1,0:T(8,128)S(1)} %get-tuple-element.65, f32[1,2,32,128]{3,2,1,0:T(8,128)S(1)} %get-tuple-element.64, f32[1,2,32,128]{3,2,1,0:T(8,128)S(1)} %get-tuple-element.63, f32[]{:T(128)} %bitcast.19, f32[]{:T(128)} %bitcast.16, ...), kind=kLoop, calls=%fused_computation.324 | loop fusion | flops 81920 | bytes 163864 | tf_op jit(solution)/shard_map/add | solution.py:103
  158.7 4.3 %collective-permute-start.13 = (f32[3,1,32,128]{3,2,1,0:T(8,128)S(1)}, f32[3,1,32,128]{3,2,1,0:T(8,128)S(1)}, u32[]{:S(2)}, u32[]{:S(2)}) collective-permute-start(f32[3,1,32,128]{3,2,1,0:T(8,128)S(1)} %get-tuple-element.174), channel_id=1, source_target_pairs={{0,128},{128,256},{256,384},{1,129},{129,257},{257,385},{2,130},{1... | collective-permute-start | bytes 147464 | tf_op jit(solution)/shard_map/ppermute | solution.py:32
  165.6 8.5 %collective-permute-start.15 = (f32[3,2,1,128]{3,2,1,0:T(1,128)S(1)}, f32[3,2,1,128]{3,2,1,0:T(1,128)S(1)}, u32[]{:S(2)}, u32[]{:S(2)}) collective-permute-start(f32[3,2,1,128]{3,2,1,0:T(1,128)S(1)} %get-tuple-element.164), channel_id=1, source_target_pairs={{0,8},{8,16},{16,24},{24,32},{32,40},{40,48},{48,56},{56,64},{64,7... | collective-permute-start | bytes 9224 | tf_op jit(solution)/shard_map/ppermute | solution.py:32
  178.6 3.9 %collective-permute-done.16 = f32[3,2,32,1]{3,2,1,0:T(8,128)S(1)} collective-permute-done((f32[3,2,32,1]{3,2,1,0:T(8,128)S(1)}, f32[3,2,32,1]{3,2,1,0:T(8,128)S(1)}, u32[]{:S(2)}, u32[]{:S(2)}) %collective-permute-start.16) | collective-permute-done | bytes 800 | tf_op jit(solution)/shard_map/ppermute | solution.py:33
  182.8 5.7 %multiply_add_fusion.28 = (f32[1,2,32,128]{3,2,1,0:T(8,128)S(1)}, f32[1,2,32,128]{3,2,1,0:T(8,128)S(1)}, f32[1,2,32,128]{3,2,1,0:T(8,128)S(1)}) fusion(f32[3,4,34,129]{3,2,1,0:T(8,128)S(1)} %get-tuple-element.127, f32[]{:T(128)} %bitcast.24, f32[]{:T(128)} %bitcast.23, f32[]{:T(128)} %bitcast.22, f32[]{:T(128)} %bitcast.27, f32[]{:T(128)} %bitcast.26, ...), kind=kLoop, calls=%fused_computation.303 | loop fusion | flops 122880 | bytes 196644 | tf_op jit(solution)/shard_map/add | solution.py:92
  188.5 5.6 %multiply_add_fusion.25 = (f32[1,2,32,128]{3,2,1,0:T(8,128)S(1)}, f32[1,2,32,128]{3,2,1,0:T(8,128)S(1)}, f32[1,2,32,128]{3,2,1,0:T(8,128)S(1)}) fusion(f32[3,4,34,129]{3,2,1,0:T(8,128)S(1)} %get-tuple-element.126, f32[]{:T(128)} %bitcast.28, f32[]{:T(128)} %bitcast.25, f32[]{:T(128)} %bitcast.22, f32[]{:T(128)} %bitcast.29, f32[]{:T(128)} %bitcast.26, ...), kind=kLoop, calls=%fused_computation.300 | loop fusion | flops 122880 | bytes 196644 | tf_op jit(solution)/shard_map/add | solution.py:103
  194.2 3.2 multiply_add_fusion.37
  197.4 3.8 %multiply_add_fusion.39 = (f32[1,2,32,128]{3,2,1,0:T(8,128)S(1)}, f32[1,2,32,128]{3,2,1,0:T(8,128)S(1)}) fusion(f32[1,2,32,128]{3,2,1,0:T(8,128)S(1)} %get-tuple-element.171, f32[1,2,32,128]{3,2,1,0:T(8,128)S(1)} %get-tuple-element.172, f32[1,2,32,128]{3,2,1,0:T(8,128)S(1)} %get-tuple-element.173, f32[]{:T(128)} %bitcast.7, f32[]{:T(128)} %bitcast.6, ...), kind=kLoop, calls=%fused_computation.314 | loop fusion | flops 81920 | bytes 163864 | tf_op jit(solution)/shard_map/add | solution.py:92
  201.2 3.7 %multiply_add_fusion.36 = (f32[1,2,32,128]{3,2,1,0:T(8,128)S(1)}, f32[1,2,32,128]{3,2,1,0:T(8,128)S(1)}) fusion(f32[1,2,32,128]{3,2,1,0:T(8,128)S(1)} %get-tuple-element.51, f32[1,2,32,128]{3,2,1,0:T(8,128)S(1)} %get-tuple-element.50, f32[1,2,32,128]{3,2,1,0:T(8,128)S(1)} %get-tuple-element.49, f32[]{:T(128)} %bitcast.9, f32[]{:T(128)} %bitcast.6, ...), kind=kLoop, calls=%fused_computation.311 | loop fusion | flops 81920 | bytes 163864 | tf_op jit(solution)/shard_map/add | solution.py:103
  206.8 3.7 %multiply_add_fusion.33 = (f32[1,2,32,128]{3,2,1,0:T(8,128)S(1)}, f32[1,2,32,128]{3,2,1,0:T(8,128)S(1)}) fusion(f32[1,2,32,128]{3,2,1,0:T(8,128)S(1)} %get-tuple-element.47, f32[1,2,32,128]{3,2,1,0:T(8,128)S(1)} %get-tuple-element.46, f32[1,2,32,128]{3,2,1,0:T(8,128)S(1)} %get-tuple-element.45, f32[]{:T(128)} %bitcast.17, f32[]{:T(128)} %bitcast.16, ...), kind=kLoop, calls=%fused_computation.308 | loop fusion | flops 81920 | bytes 163864 | tf_op jit(solution)/shard_map/add | solution.py:92
  212.4 3.8 %multiply_add_fusion.30 = (f32[1,2,32,128]{3,2,1,0:T(8,128)S(1)}, f32[1,2,32,128]{3,2,1,0:T(8,128)S(1)}) fusion(f32[1,2,32,128]{3,2,1,0:T(8,128)S(1)} %get-tuple-element.43, f32[1,2,32,128]{3,2,1,0:T(8,128)S(1)} %get-tuple-element.42, f32[1,2,32,128]{3,2,1,0:T(8,128)S(1)} %get-tuple-element.41, f32[]{:T(128)} %bitcast.19, f32[]{:T(128)} %bitcast.16, ...), kind=kLoop, calls=%fused_computation.305 | loop fusion | flops 81920 | bytes 163864 | tf_op jit(solution)/shard_map/add | solution.py:103
  217.9 4.3 %collective-permute-start.19 = (f32[3,1,32,128]{3,2,1,0:T(8,128)S(1)}, f32[3,1,32,128]{3,2,1,0:T(8,128)S(1)}, u32[]{:S(2)}, u32[]{:S(2)}) collective-permute-start(f32[3,1,32,128]{3,2,1,0:T(8,128)S(1)} %get-tuple-element.156), channel_id=1, source_target_pairs={{0,128},{128,256},{256,384},{1,129},{129,257},{257,385},{2,130},{1... | collective-permute-start | bytes 147464 | tf_op jit(solution)/shard_map/ppermute | solution.py:32
  223.4 9.1 %collective-permute-start.21 = (f32[3,2,1,128]{3,2,1,0:T(1,128)S(1)}, f32[3,2,1,128]{3,2,1,0:T(1,128)S(1)}, u32[]{:S(2)}, u32[]{:S(2)}) collective-permute-start(f32[3,2,1,128]{3,2,1,0:T(1,128)S(1)} %get-tuple-element.146), channel_id=1, source_target_pairs={{0,8},{8,16},{16,24},{24,32},{32,40},{40,48},{48,56},{56,64},{64,7... | collective-permute-start | bytes 9224 | tf_op jit(solution)/shard_map/ppermute | solution.py:32
  237.0 3.6 %collective-permute-start.27 = (f32[3,128,1]{2,1,0:T(8,128)S(1)}, f32[3,128,1]{2,1,0:T(8,128)S(1)}, u32[]{:S(2)}, u32[]{:S(2)}) collective-permute-start(f32[3,128,1]{2,1,0:T(8,128)S(1)} %get-tuple-element.121), channel_id=1, source_target_pairs={{0,1},{1,2},{2,3},{3,4},{4,5},{5,6},{6,7},{8,9},{9,10},{10,11},{11... | collective-permute-start | bytes 4616 | tf_op jit(solution)/shard_map/ppermute | solution.py:32
  241.1 5.7 %multiply_add_fusion.10 = (f32[1,2,32,128]{3,2,1,0:T(8,128)S(1)}, f32[1,2,32,128]{3,2,1,0:T(8,128)S(1)}, f32[1,2,32,128]{3,2,1,0:T(8,128)S(1)}) fusion(f32[3,4,34,129]{3,2,1,0:T(8,128)S(1)} %get-tuple-element.125, f32[]{:T(128)} %bitcast.24, f32[]{:T(128)} %bitcast.23, f32[]{:T(128)} %bitcast.22, f32[]{:T(128)} %bitcast.27, f32[]{:T(128)} %bitcast.26, ...), kind=kLoop, calls=%fused_computation.284 | loop fusion | flops 122880 | bytes 196644 | tf_op jit(solution)/shard_map/add | solution.py:92
  246.8 5.6 %multiply_add_fusion.7 = (f32[1,2,32,128]{3,2,1,0:T(8,128)S(1)}, f32[1,2,32,128]{3,2,1,0:T(8,128)S(1)}, f32[1,2,32,128]{3,2,1,0:T(8,128)S(1)}) fusion(f32[3,4,34,129]{3,2,1,0:T(8,128)S(1)} %get-tuple-element.124, f32[]{:T(128)} %bitcast.28, f32[]{:T(128)} %bitcast.25, f32[]{:T(128)} %bitcast.22, f32[]{:T(128)} %bitcast.29, f32[]{:T(128)} %bitcast.26, ...), kind=kLoop, calls=%fused_computation.281 | loop fusion | flops 122880 | bytes 196644 | tf_op jit(solution)/shard_map/add | solution.py:103
  252.5 3.2 multiply_add_fusion.19
  255.7 3.8 %multiply_add_fusion.21 = (f32[1,2,32,128]{3,2,1,0:T(8,128)S(1)}, f32[1,2,32,128]{3,2,1,0:T(8,128)S(1)}) fusion(f32[1,2,32,128]{3,2,1,0:T(8,128)S(1)} %get-tuple-element.153, f32[1,2,32,128]{3,2,1,0:T(8,128)S(1)} %get-tuple-element.154, f32[1,2,32,128]{3,2,1,0:T(8,128)S(1)} %get-tuple-element.155, f32[]{:T(128)} %bitcast.7, f32[]{:T(128)} %bitcast.6, ...), kind=kLoop, calls=%fused_computation.295 | loop fusion | flops 81920 | bytes 163864 | tf_op jit(solution)/shard_map/add | solution.py:92
  259.5 3.7 %multiply_add_fusion.18 = (f32[1,2,32,128]{3,2,1,0:T(8,128)S(1)}, f32[1,2,32,128]{3,2,1,0:T(8,128)S(1)}) fusion(f32[1,2,32,128]{3,2,1,0:T(8,128)S(1)} %get-tuple-element.29, f32[1,2,32,128]{3,2,1,0:T(8,128)S(1)} %get-tuple-element.28, f32[1,2,32,128]{3,2,1,0:T(8,128)S(1)} %get-tuple-element.27, f32[]{:T(128)} %bitcast.9, f32[]{:T(128)} %bitcast.6, ...), kind=kLoop, calls=%fused_computation.292 | loop fusion | flops 81920 | bytes 163864 | tf_op jit(solution)/shard_map/add | solution.py:103
  265.1 3.7 %multiply_add_fusion.15 = (f32[1,2,32,128]{3,2,1,0:T(8,128)S(1)}, f32[1,2,32,128]{3,2,1,0:T(8,128)S(1)}) fusion(f32[1,2,32,128]{3,2,1,0:T(8,128)S(1)} %get-tuple-element.25, f32[1,2,32,128]{3,2,1,0:T(8,128)S(1)} %get-tuple-element.24, f32[1,2,32,128]{3,2,1,0:T(8,128)S(1)} %get-tuple-element.23, f32[]{:T(128)} %bitcast.17, f32[]{:T(128)} %bitcast.16, ...), kind=kLoop, calls=%fused_computation.289 | loop fusion | flops 81920 | bytes 163864 | tf_op jit(solution)/shard_map/add | solution.py:92
  270.7 3.8 %multiply_add_fusion.12 = (f32[1,2,32,128]{3,2,1,0:T(8,128)S(1)}, f32[1,2,32,128]{3,2,1,0:T(8,128)S(1)}) fusion(f32[1,2,32,128]{3,2,1,0:T(8,128)S(1)} %get-tuple-element.21, f32[1,2,32,128]{3,2,1,0:T(8,128)S(1)} %get-tuple-element.20, f32[1,2,32,128]{3,2,1,0:T(8,128)S(1)} %get-tuple-element.19, f32[]{:T(128)} %bitcast.19, f32[]{:T(128)} %bitcast.16, ...), kind=kLoop, calls=%fused_computation.286 | loop fusion | flops 81920 | bytes 163864 | tf_op jit(solution)/shard_map/add | solution.py:103
  276.5 17.4 %all-to-all-start.2 = ((f32[64,1,192]{2,1,0:T(1,128)}), f32[64,1,192]{2,1,0:T(1,128)S(1)}, u32[]{:S(2)}, u32[]{:S(2)}) async-start(f32[64,1,192]{2,1,0:T(1,128)} %reshape.182), calls=%async_computation.2 | async-start | bytes 131072 | tf_op jit(solution)/shard_map/all_to_all | solution.py:68
  295.3 7.9 %collective-permute-start.25 = (f32[3,1,256]{2,1,0:T(1,128)S(1)}, f32[3,1,256]{2,1,0:T(1,128)S(1)}, u32[]{:S(2)}, u32[]{:S(2)}) collective-permute-start(f32[3,1,256]{2,1,0:T(1,128)S(1)} %get-tuple-element.122), channel_id=1, source_target_pairs={{0,8},{8,16},{16,24},{24,32},{32,40},{40,48},{48,56},{56,64},{64,7... | collective-permute-start | bytes 9224 | tf_op jit(solution)/shard_map/ppermute | solution.py:32
  308.9 3.8 %all_to_all.21 = f32[2,1,12288]{2,1,0:T(1,128)S(1)} all-to-all(f32[2,1,12288]{2,1,0:T(1,128)S(1)} %reshape.184), channel_id=1, replica_groups=mesh['region'=4,'gx_0'=8,'gx_1'=2,'gy_0'=4,'gy_1'=2] {'gy_1'}, dimensions={0} | all-to-all | bytes 196608 | tf_op jit(solution)/shard_map/all_to_all | solution.py:68
  317.4 7.9 %collective-permute-start.29 = (f32[3,1,256]{2,1,0:T(1,128)S(1)}, f32[3,1,256]{2,1,0:T(1,128)S(1)}, u32[]{:S(2)}, u32[]{:S(2)}) collective-permute-start(f32[3,1,256]{2,1,0:T(1,128)S(1)} %get-tuple-element.118), channel_id=1, source_target_pairs={{0,8},{8,16},{16,24},{24,32},{32,40},{40,48},{48,56},{56,64},{64,7... | collective-permute-start | bytes 9224 | tf_op jit(solution)/shard_map/ppermute | solution.py:32
  331.0 4.4 %collective-permute-done.30 = f32[3,128,1]{2,1,0:T(8,128)S(1)} collective-permute-done((f32[3,128,1]{2,1,0:T(8,128)S(1)}, f32[3,128,1]{2,1,0:T(8,128)S(1)}, u32[]{:S(2)}, u32[]{:S(2)}) %collective-permute-start.30) | collective-permute-done | bytes 1568 | tf_op jit(solution)/shard_map/ppermute | solution.py:33
  (185 shorter events, 69.3 us)
Async XLA Ops:
  0.6 7.0 %copy-start.1 = (f32[3,2,32,128]{3,2,1,0:T(8,128)S(1)}, f32[3,2,32,128]{3,2,1,0:T(8,128)}, u32[]{:S(2)}) copy-start(f32[3,2,32,128]{3,2,1,0:T(8,128)} %param.6) | copy-start | bytes 294916
  0.6 22.4 %copy-start = (f32[3,128,256]{2,1,0:T(8,128)S(1)}, f32[3,128,256]{2,1,0:T(8,128)}, u32[]{:S(2)}) copy-start(f32[3,128,256]{2,1,0:T(8,128)} %param.10) | copy-start | bytes 1179652
  1.5 49.2 %collective-permute-start.1 = (f32[3,1,32,128]{3,2,1,0:T(8,128)S(1)}, f32[3,1,32,128]{3,2,1,0:T(8,128)S(1)}, u32[]{:S(2)}, u32[]{:S(2)}) collective-permute-start(f32[3,1,32,128]{3,2,1,0:T(8,128)S(1)} %get-tuple-element.208), channel_id=1, source_target_pairs={{0,128},{128,256},{256,384},{1,129},{129,257},{257,385},{2,130},{1... | collective-permute-start | bytes 147464 | tf_op jit(solution)/shard_map/ppermute | solution.py:32
  6.4 44.4 %collective-permute-start = (f32[3,1,32,128]{3,2,1,0:T(8,128)S(1)}, f32[3,1,32,128]{3,2,1,0:T(8,128)S(1)}, u32[]{:S(2)}, u32[]{:S(2)}) collective-permute-start(f32[3,1,32,128]{3,2,1,0:T(8,128)S(1)} %get-tuple-element.209), channel_id=1, source_target_pairs={{128,0},{256,128},{384,256},{129,1},{257,129},{385,257},{130,2},{2... | collective-permute-start | bytes 147464 | tf_op jit(solution)/shard_map/ppermute | solution.py:33
  7.7 40.5 %collective-permute-start.3 = (f32[3,2,1,128]{3,2,1,0:T(1,128)S(1)}, f32[3,2,1,128]{3,2,1,0:T(1,128)S(1)}, u32[]{:S(2)}, u32[]{:S(2)}) collective-permute-start(f32[3,2,1,128]{3,2,1,0:T(1,128)S(1)} %get-tuple-element.204), channel_id=1, source_target_pairs={{0,8},{8,16},{16,24},{24,32},{32,40},{40,48},{48,56},{56,64},{64,7... | collective-permute-start | bytes 9224 | tf_op jit(solution)/shard_map/ppermute | solution.py:32
  17.4 33.3 %collective-permute-start.2 = (f32[3,2,1,128]{3,2,1,0:T(1,128)S(1)}, f32[3,2,1,128]{3,2,1,0:T(1,128)S(1)}, u32[]{:S(2)}, u32[]{:S(2)}) collective-permute-start(f32[3,2,1,128]{3,2,1,0:T(1,128)S(1)} %get-tuple-element.205), channel_id=1, source_target_pairs={{8,0},{16,8},{24,16},{32,24},{40,32},{48,40},{56,48},{64,56},{72,6... | collective-permute-start | bytes 9224 | tf_op jit(solution)/shard_map/ppermute | solution.py:33
  18.8 54.1 %collective-permute-start.5 = (f32[3,2,32,1]{3,2,1,0:T(8,128)S(1)}, f32[3,2,32,1]{3,2,1,0:T(8,128)S(1)}, u32[]{:S(2)}, u32[]{:S(2)}) collective-permute-start(f32[3,2,32,1]{3,2,1,0:T(8,128)S(1)} %get-tuple-element.200), channel_id=1, source_target_pairs={{0,1},{1,2},{2,3},{3,4},{4,5},{5,6},{6,7},{8,9},{9,10},{10,11},{11... | collective-permute-start | bytes 2312 | tf_op jit(solution)/shard_map/ppermute | solution.py:32
  29.4 17.1 %copy-start.6 = (f32[3,3,3]{2,1,0:T(4,128)S(1)}, f32[3,3,3]{2,1,0:T(4,128)}, u32[]{:S(2)}) copy-start(f32[3,3,3]{2,1,0:T(4,128)} %param.9) | copy-start | bytes 328
  30.4 20.4 %copy-start.2 = (f32[2,3,2,32,128]{4,3,2,1,0:T(8,128)S(1)}, f32[2,3,2,32,128]{4,3,2,1,0:T(8,128)}, u32[]{:S(2)}) copy-start(f32[2,3,2,32,128]{4,3,2,1,0:T(8,128)} %param.8) | copy-start | bytes 589828
  30.4 54.2 %all-to-all-start.1 = ((f32[64,1,192]{2,1,0:T(1,128)}), f32[64,1,192]{2,1,0:T(1,128)S(1)}, u32[]{:S(2)}, u32[]{:S(2)}) async-start(f32[64,1,192]{2,1,0:T(1,128)} %reshape.180), calls=%async_computation.1 | async-start | bytes 131072 | tf_op jit(solution)/shard_map/all_to_all | solution.py:59
  48.1 24.8 %collective-permute-start.4 = (f32[3,2,32,1]{3,2,1,0:T(8,128)S(1)}, f32[3,2,32,1]{3,2,1,0:T(8,128)S(1)}, u32[]{:S(2)}, u32[]{:S(2)}) collective-permute-start(f32[3,2,32,1]{3,2,1,0:T(8,128)S(1)} %get-tuple-element.201), channel_id=1, source_target_pairs={{1,0},{2,1},{3,2},{4,3},{5,4},{6,5},{7,6},{9,8},{10,9},{11,10},{12... | collective-permute-start | bytes 2312 | tf_op jit(solution)/shard_map/ppermute | solution.py:33
  97.4 0.9 copy-start.4
  98.5 26.3 %collective-permute-start.7 = (f32[3,1,32,128]{3,2,1,0:T(8,128)S(1)}, f32[3,1,32,128]{3,2,1,0:T(8,128)S(1)}, u32[]{:S(2)}, u32[]{:S(2)}) collective-permute-start(f32[3,1,32,128]{3,2,1,0:T(8,128)S(1)} %get-tuple-element.192), channel_id=1, source_target_pairs={{0,128},{128,256},{256,384},{1,129},{129,257},{257,385},{2,130},{1... | collective-permute-start | bytes 147464 | tf_op jit(solution)/shard_map/ppermute | solution.py:32
  101.4 23.4 %collective-permute-start.6 = (f32[3,1,32,128]{3,2,1,0:T(8,128)S(1)}, f32[3,1,32,128]{3,2,1,0:T(8,128)S(1)}, u32[]{:S(2)}, u32[]{:S(2)}) collective-permute-start(f32[3,1,32,128]{3,2,1,0:T(8,128)S(1)} %get-tuple-element.193), channel_id=1, source_target_pairs={{128,0},{256,128},{384,256},{129,1},{257,129},{385,257},{130,2},{2... | collective-permute-start | bytes 147464 | tf_op jit(solution)/shard_map/ppermute | solution.py:33
  102.7 16.1 %collective-permute-start.8 = (f32[3,2,1,128]{3,2,1,0:T(1,128)S(1)}, f32[3,2,1,128]{3,2,1,0:T(1,128)S(1)}, u32[]{:S(2)}, u32[]{:S(2)}) collective-permute-start(f32[3,2,1,128]{3,2,1,0:T(1,128)S(1)} %get-tuple-element.183), channel_id=1, source_target_pairs={{8,0},{16,8},{24,16},{32,24},{40,32},{48,40},{56,48},{64,56},{72,6... | collective-permute-start | bytes 9224 | tf_op jit(solution)/shard_map/ppermute | solution.py:33
  104.0 16.8 %collective-permute-start.9 = (f32[3,2,1,128]{3,2,1,0:T(1,128)S(1)}, f32[3,2,1,128]{3,2,1,0:T(1,128)S(1)}, u32[]{:S(2)}, u32[]{:S(2)}) collective-permute-start(f32[3,2,1,128]{3,2,1,0:T(1,128)S(1)} %get-tuple-element.182), channel_id=1, source_target_pairs={{0,8},{8,16},{16,24},{24,32},{32,40},{40,48},{48,56},{56,64},{64,7... | collective-permute-start | bytes 9224 | tf_op jit(solution)/shard_map/ppermute | solution.py:32
  112.0 8.8 %collective-permute-start.11 = (f32[3,2,32,1]{3,2,1,0:T(8,128)S(1)}, f32[3,2,32,1]{3,2,1,0:T(8,128)S(1)}, u32[]{:S(2)}, u32[]{:S(2)}) collective-permute-start(f32[3,2,32,1]{3,2,1,0:T(8,128)S(1)} %get-tuple-element.178), channel_id=1, source_target_pairs={{0,1},{1,2},{2,3},{3,4},{4,5},{5,6},{6,7},{8,9},{9,10},{10,11},{11... | collective-permute-start | bytes 2312 | tf_op jit(solution)/shard_map/ppermute | solution.py:32
  118.9 5.9 %collective-permute-start.10 = (f32[3,2,32,1]{3,2,1,0:T(8,128)S(1)}, f32[3,2,32,1]{3,2,1,0:T(8,128)S(1)}, u32[]{:S(2)}, u32[]{:S(2)}) collective-permute-start(f32[3,2,32,1]{3,2,1,0:T(8,128)S(1)} %get-tuple-element.179), channel_id=1, source_target_pairs={{1,0},{2,1},{3,2},{4,3},{5,4},{6,5},{7,6},{9,8},{10,9},{11,10},{12... | collective-permute-start | bytes 2312 | tf_op jit(solution)/shard_map/ppermute | solution.py:33
  158.7 23.8 %collective-permute-start.13 = (f32[3,1,32,128]{3,2,1,0:T(8,128)S(1)}, f32[3,1,32,128]{3,2,1,0:T(8,128)S(1)}, u32[]{:S(2)}, u32[]{:S(2)}) collective-permute-start(f32[3,1,32,128]{3,2,1,0:T(8,128)S(1)} %get-tuple-element.174), channel_id=1, source_target_pairs={{0,128},{128,256},{256,384},{1,129},{129,257},{257,385},{2,130},{1... | collective-permute-start | bytes 147464 | tf_op jit(solution)/shard_map/ppermute | solution.py:32
  163.0 19.6 %collective-permute-start.12 = (f32[3,1,32,128]{3,2,1,0:T(8,128)S(1)}, f32[3,1,32,128]{3,2,1,0:T(8,128)S(1)}, u32[]{:S(2)}, u32[]{:S(2)}) collective-permute-start(f32[3,1,32,128]{3,2,1,0:T(8,128)S(1)} %get-tuple-element.175), channel_id=1, source_target_pairs={{128,0},{256,128},{384,256},{129,1},{257,129},{385,257},{130,2},{2... | collective-permute-start | bytes 147464 | tf_op jit(solution)/shard_map/ppermute | solution.py:33
  164.3 12.3 %collective-permute-start.14 = (f32[3,2,1,128]{3,2,1,0:T(1,128)S(1)}, f32[3,2,1,128]{3,2,1,0:T(1,128)S(1)}, u32[]{:S(2)}, u32[]{:S(2)}) collective-permute-start(f32[3,2,1,128]{3,2,1,0:T(1,128)S(1)} %get-tuple-element.165), channel_id=1, source_target_pairs={{8,0},{16,8},{24,16},{32,24},{40,32},{48,40},{56,48},{64,56},{72,6... | collective-permute-start | bytes 9224 | tf_op jit(solution)/shard_map/ppermute | solution.py:33
  165.6 13.0 %collective-permute-start.15 = (f32[3,2,1,128]{3,2,1,0:T(1,128)S(1)}, f32[3,2,1,128]{3,2,1,0:T(1,128)S(1)}, u32[]{:S(2)}, u32[]{:S(2)}) collective-permute-start(f32[3,2,1,128]{3,2,1,0:T(1,128)S(1)} %get-tuple-element.164), channel_id=1, source_target_pairs={{0,8},{8,16},{16,24},{24,32},{32,40},{40,48},{48,56},{56,64},{64,7... | collective-permute-start | bytes 9224 | tf_op jit(solution)/shard_map/ppermute | solution.py:32
  174.2 4.4 %collective-permute-start.17 = (f32[3,2,32,1]{3,2,1,0:T(8,128)S(1)}, f32[3,2,32,1]{3,2,1,0:T(8,128)S(1)}, u32[]{:S(2)}, u32[]{:S(2)}) collective-permute-start(f32[3,2,32,1]{3,2,1,0:T(8,128)S(1)} %get-tuple-element.160), channel_id=1, source_target_pairs={{0,1},{1,2},{2,3},{3,4},{4,5},{5,6},{6,7},{8,9},{9,10},{10,11},{11... | collective-permute-start | bytes 2312 | tf_op jit(solution)/shard_map/ppermute | solution.py:32
  176.6 5.9 %collective-permute-start.16 = (f32[3,2,32,1]{3,2,1,0:T(8,128)S(1)}, f32[3,2,32,1]{3,2,1,0:T(8,128)S(1)}, u32[]{:S(2)}, u32[]{:S(2)}) collective-permute-start(f32[3,2,32,1]{3,2,1,0:T(8,128)S(1)} %get-tuple-element.161), channel_id=1, source_target_pairs={{1,0},{2,1},{3,2},{4,3},{5,4},{6,5},{7,6},{9,8},{10,9},{11,10},{12... | collective-permute-start | bytes 2312 | tf_op jit(solution)/shard_map/ppermute | solution.py:33
  216.5 18.4 %collective-permute-start.20 = (f32[3,2,1,128]{3,2,1,0:T(1,128)S(1)}, f32[3,2,1,128]{3,2,1,0:T(1,128)S(1)}, u32[]{:S(2)}, u32[]{:S(2)}) collective-permute-start(f32[3,2,1,128]{3,2,1,0:T(1,128)S(1)} %get-tuple-element.147), channel_id=1, source_target_pairs={{8,0},{16,8},{24,16},{32,24},{40,32},{48,40},{56,48},{64,56},{72,6... | collective-permute-start | bytes 9224 | tf_op jit(solution)/shard_map/ppermute | solution.py:33
  217.9 23.0 %collective-permute-start.19 = (f32[3,1,32,128]{3,2,1,0:T(8,128)S(1)}, f32[3,1,32,128]{3,2,1,0:T(8,128)S(1)}, u32[]{:S(2)}, u32[]{:S(2)}) collective-permute-start(f32[3,1,32,128]{3,2,1,0:T(8,128)S(1)} %get-tuple-element.156), channel_id=1, source_target_pairs={{0,128},{128,256},{256,384},{1,129},{129,257},{257,385},{2,130},{1... | collective-permute-start | bytes 147464 | tf_op jit(solution)/shard_map/ppermute | solution.py:32
  222.1 18.7 %collective-permute-start.18 = (f32[3,1,32,128]{3,2,1,0:T(8,128)S(1)}, f32[3,1,32,128]{3,2,1,0:T(8,128)S(1)}, u32[]{:S(2)}, u32[]{:S(2)}) collective-permute-start(f32[3,1,32,128]{3,2,1,0:T(8,128)S(1)} %get-tuple-element.157), channel_id=1, source_target_pairs={{128,0},{256,128},{384,256},{129,1},{257,129},{385,257},{130,2},{2... | collective-permute-start | bytes 147464 | tf_op jit(solution)/shard_map/ppermute | solution.py:33
  223.4 13.6 %collective-permute-start.21 = (f32[3,2,1,128]{3,2,1,0:T(1,128)S(1)}, f32[3,2,1,128]{3,2,1,0:T(1,128)S(1)}, u32[]{:S(2)}, u32[]{:S(2)}) collective-permute-start(f32[3,2,1,128]{3,2,1,0:T(1,128)S(1)} %get-tuple-element.146), channel_id=1, source_target_pairs={{0,8},{8,16},{16,24},{24,32},{32,40},{40,48},{48,56},{56,64},{64,7... | collective-permute-start | bytes 9224 | tf_op jit(solution)/shard_map/ppermute | solution.py:32
  232.5 8.2 %collective-permute-start.23 = (f32[3,2,32,1]{3,2,1,0:T(8,128)S(1)}, f32[3,2,32,1]{3,2,1,0:T(8,128)S(1)}, u32[]{:S(2)}, u32[]{:S(2)}) collective-permute-start(f32[3,2,32,1]{3,2,1,0:T(8,128)S(1)} %get-tuple-element.142), channel_id=1, source_target_pairs={{0,1},{1,2},{2,3},{3,4},{4,5},{5,6},{6,7},{8,9},{9,10},{10,11},{11... | collective-permute-start | bytes 2312 | tf_op jit(solution)/shard_map/ppermute | solution.py:32
  234.9 5.9 %collective-permute-start.22 = (f32[3,2,32,1]{3,2,1,0:T(8,128)S(1)}, f32[3,2,32,1]{3,2,1,0:T(8,128)S(1)}, u32[]{:S(2)}, u32[]{:S(2)}) collective-permute-start(f32[3,2,32,1]{3,2,1,0:T(8,128)S(1)} %get-tuple-element.143), channel_id=1, source_target_pairs={{1,0},{2,1},{3,2},{4,3},{5,4},{6,5},{7,6},{9,8},{10,9},{11,10},{12... | collective-permute-start | bytes 2312 | tf_op jit(solution)/shard_map/ppermute | solution.py:33
  237.0 77.5 %collective-permute-start.27 = (f32[3,128,1]{2,1,0:T(8,128)S(1)}, f32[3,128,1]{2,1,0:T(8,128)S(1)}, u32[]{:S(2)}, u32[]{:S(2)}) collective-permute-start(f32[3,128,1]{2,1,0:T(8,128)S(1)} %get-tuple-element.121), channel_id=1, source_target_pairs={{0,1},{1,2},{2,3},{3,4},{4,5},{5,6},{6,7},{8,9},{9,10},{10,11},{11... | collective-permute-start | bytes 4616 | tf_op jit(solution)/shard_map/ppermute | solution.py:32
  274.7 0.6 copy-start.5
  276.5 31.1 %all-to-all-start.2 = ((f32[64,1,192]{2,1,0:T(1,128)}), f32[64,1,192]{2,1,0:T(1,128)S(1)}, u32[]{:S(2)}, u32[]{:S(2)}) async-start(f32[64,1,192]{2,1,0:T(1,128)} %reshape.182), calls=%async_computation.2 | async-start | bytes 131072 | tf_op jit(solution)/shard_map/all_to_all | solution.py:68
  294.0 20.6 %collective-permute-start.24 = (f32[3,1,256]{2,1,0:T(1,128)S(1)}, f32[3,1,256]{2,1,0:T(1,128)S(1)}, u32[]{:S(2)}, u32[]{:S(2)}) collective-permute-start(f32[3,1,256]{2,1,0:T(1,128)S(1)} %get-tuple-element.123), channel_id=1, source_target_pairs={{8,0},{16,8},{24,16},{32,24},{40,32},{48,40},{56,48},{64,56},{72,6... | collective-permute-start | bytes 9224 | tf_op jit(solution)/shard_map/ppermute | solution.py:33
  295.3 19.3 %collective-permute-start.25 = (f32[3,1,256]{2,1,0:T(1,128)S(1)}, f32[3,1,256]{2,1,0:T(1,128)S(1)}, u32[]{:S(2)}, u32[]{:S(2)}) collective-permute-start(f32[3,1,256]{2,1,0:T(1,128)S(1)} %get-tuple-element.122), channel_id=1, source_target_pairs={{0,8},{8,16},{16,24},{24,32},{32,40},{40,48},{48,56},{56,64},{64,7... | collective-permute-start | bytes 9224 | tf_op jit(solution)/shard_map/ppermute | solution.py:32
  303.2 11.4 %collective-permute-start.26 = (f32[3,128,1]{2,1,0:T(8,128)S(1)}, f32[3,128,1]{2,1,0:T(8,128)S(1)}, u32[]{:S(2)}, u32[]{:S(2)}) collective-permute-start(f32[3,128,1]{2,1,0:T(8,128)S(1)} %get-tuple-element.120), channel_id=1, source_target_pairs={{1,0},{2,1},{3,2},{4,3},{5,4},{6,5},{7,6},{9,8},{10,9},{11,10},{12... | collective-permute-start | bytes 4616 | tf_op jit(solution)/shard_map/ppermute | solution.py:33
  314.9 0.9 copy-start.3
  316.1 19.3 %collective-permute-start.28 = (f32[3,1,256]{2,1,0:T(1,128)S(1)}, f32[3,1,256]{2,1,0:T(1,128)S(1)}, u32[]{:S(2)}, u32[]{:S(2)}) collective-permute-start(f32[3,1,256]{2,1,0:T(1,128)S(1)} %get-tuple-element.119), channel_id=1, source_target_pairs={{8,0},{16,8},{24,16},{32,24},{40,32},{48,40},{56,48},{64,56},{72,6... | collective-permute-start | bytes 9224 | tf_op jit(solution)/shard_map/ppermute | solution.py:33
  317.4 18.0 %collective-permute-start.29 = (f32[3,1,256]{2,1,0:T(1,128)S(1)}, f32[3,1,256]{2,1,0:T(1,128)S(1)}, u32[]{:S(2)}, u32[]{:S(2)}) collective-permute-start(f32[3,1,256]{2,1,0:T(1,128)S(1)} %get-tuple-element.118), channel_id=1, source_target_pairs={{0,8},{8,16},{16,24},{24,32},{32,40},{40,48},{48,56},{56,64},{64,7... | collective-permute-start | bytes 9224 | tf_op jit(solution)/shard_map/ppermute | solution.py:32
  325.5 5.6 %collective-permute-start.31 = (f32[3,128,1]{2,1,0:T(8,128)S(1)}, f32[3,128,1]{2,1,0:T(8,128)S(1)}, u32[]{:S(2)}, u32[]{:S(2)}) collective-permute-start(f32[3,128,1]{2,1,0:T(8,128)S(1)} %get-tuple-element.117), channel_id=1, source_target_pairs={{0,1},{1,2},{2,3},{3,4},{4,5},{5,6},{6,7},{8,9},{9,10},{10,11},{11... | collective-permute-start | bytes 4616 | tf_op jit(solution)/shard_map/ppermute | solution.py:32
  328.4 7.0 %collective-permute-start.30 = (f32[3,128,1]{2,1,0:T(8,128)S(1)}, f32[3,128,1]{2,1,0:T(8,128)S(1)}, u32[]{:S(2)}, u32[]{:S(2)}) collective-permute-start(f32[3,128,1]{2,1,0:T(8,128)S(1)} %get-tuple-element.116), channel_id=1, source_target_pairs={{1,0},{2,1},{3,2},{4,3},{5,4},{6,5},{7,6},{9,8},{10,9},{11,10},{12... | collective-permute-start | bytes 4616 | tf_op jit(solution)/shard_map/ppermute | solution.py:33
where the time goes:
time: 340 us; the launch traced here: 337 us
  starting transfers between devices  149 us (44%)
  other arithmetic  141 us (41%)
  blocking collectives  18.8 us (6%)
  waiting for transfers between devices  15.5 us (5%)
  local copies, waits for them, and re-layouts  11.3 us (3%)
    ppermute x16, starting transfers between devices, with_halo(): lax.ppermute(last, axis, up)  89.7 us
    add x19, other arithmetic, apply_transposed(): matrix[0, component] * vector[0] + matrix[1, component] * vector[1]  72.8 us
    add x15, other arithmetic, apply_kernel(): matrix[component, 0] * vector[0] + matrix[component, 1] * vector[1]  60.5 us
    ppermute x16, starting transfers between devices, with_halo(): lax.ppermute(leading, axis, [(b, a) for a, b in up])  25.3 us
    all_to_all x1, starting transfers between devices, copy_for_each(): lax.all_to_all(jnp.broadcast_to(array[None], (count, *array.shape)), axis...  17.4 us
    all_to_all x1, starting transfers between devices, summed_rows(): return jnp.sum(lax.all_to_all(own, far, 0, 0, tiled=True), axis=0)  16.1 us
    ppermute x16, waiting for transfers between devices, with_halo(): lax.ppermute(leading, axis, [(b, a) for a, b in up])  12.4 us
    all_gather x1, blocking collectives, picked(): lax.all_gather(array, axis)  11.6 us
  transfers between devices with their start and end apart: 34, of which 6 were waited for; matrix products, arithmetic and copies ran while one was open for 23% of the time, Pallas kernels for 0%

commit v1 on v0

--- a/solution.py
+++ b/solution.py
@@ -1,8 +1,12 @@
+import functools
+
 import jax
 import jax.numpy as jnp
 from jax import lax
 from jax.sharding import Mesh
 from jax.sharding import PartitionSpec as P
+from jax.experimental import pallas as pl
+from jax.experimental.pallas import tpu as pltpu
 
 K = 8
 SWEEPS = 2
@@ -132,6 +136,89 @@
     return jnp.where(colour_mask[None], blended, spins)
 
 
+def sweep_kernel(colour, sweep, k_ref, s_ref, lo_ref, hi_ref, xlo_ref, xhi_ref, ylo_ref, yhi_ref,
+                 film_ref, trial_ref, unif_ref,
+                 out_ref, olo_ref, ohi_ref, oxlo_ref, oxhi_ref, oylo_ref, oyhi_ref):
+    layers, rows_x, rows_y = s_ref.shape[1:]
+    row = lax.broadcasted_iota(jnp.int32, (rows_x, rows_y), 0)
+    col = lax.broadcasted_iota(jnp.int32, (rows_x, rows_y), 1)
+    kk = [[[k_ref[d * 9 + a * 3 + b] for b in range(3)] for a in range(3)] for d in range(3)]
+    for l in range(layers):
+        s = [s_ref[c, l] for c in range(3)]
+        below = [lo_ref[c, 0] if l == 0 else s_ref[c, l - 1] for c in range(3)]
+        above = [hi_ref[c, 0] if l == layers - 1 else s_ref[c, l + 1] for c in range(3)]
+        xp = [jnp.where(row == rows_x - 1, xhi_ref[c, l], pltpu.roll(s[c], rows_x - 1, 0)) for c in range(3)]
+        xm = [jnp.where(row == 0, xlo_ref[c, l], pltpu.roll(s[c], 1, 0)) for c in range(3)]
+        yp = [jnp.where(col == rows_y - 1, yhi_ref[c, l], pltpu.roll(s[c], rows_y - 1, 1)) for c in range(3)]
+        ym = [jnp.where(col == 0, ylo_ref[c, l], pltpu.roll(s[c], 1, 1)) for c in range(3)]
+        fwd = (above, xp, yp)
+        bwd = (below, xm, ym)
+        field = []
+        for c in range(3):
+            total = film_ref[c] * coupling_down
+            for d in range(3):
+                m = kk[d]
+                total = total + (m[c][0] * fwd[d][0] + m[c][1] * fwd[d][1] + m[c][2] * fwd[d][2])
+                total = total + (m[0][c] * bwd[d][0] + m[1][c] * bwd[d][1] + m[2][c] * bwd[d][2])
+            field.append(total)
+        raw = [s[c] + step_cone * trial_ref[sweep, c, l] for c in range(3)]
+        norm = jnp.sqrt(raw[0] * raw[0] + raw[1] * raw[1] + raw[2] * raw[2])
+        prop = [raw[c] / norm for c in range(3)]
+        dot = (prop[0] - s[0]) * field[0] + (prop[1] - s[1]) * field[1] + (prop[2] - s[2]) * field[2]
+        change = -dot - anisotropy * (prop[2] * prop[2] - s[2] * s[2])
+        accept = jnp.exp(jnp.minimum(-inverse_temp * change, 0.0))
+        weight = 1.0 / (1.0 + jnp.exp(-((accept - unif_ref[sweep, l]) / softness)))
+        mix = [(1.0 - weight) * s[c] + weight * prop[c] for c in range(3)]
+        mnorm = jnp.sqrt(mix[0] * mix[0] + mix[1] * mix[1] + mix[2] * mix[2])
+        chosen = ((row + col + l) % 2) == colour
+        for c in range(3):
+            new = jnp.where(chosen, mix[c] / mnorm, s[c])
+            out_ref[c, l] = new
+            if l == 0:
+                olo_ref[c, 0] = new
+            if l == layers - 1:
+                ohi_ref[c, 0] = new
+            oxlo_ref[c, l] = new[0:1, :]
+            oxhi_ref[c, l] = new[rows_x - 1:rows_x, :]
+            oylo_ref[c, l] = new[:, 0:1]
+            oyhi_ref[c, l] = new[:, rows_y - 1:rows_y]
+
+
+def half_sweep(spins, halos, exch_flat, film_cells, trials, uniforms, sweep, colour):
+    comps, layers, rows_x, rows_y = spins.shape
+    vmem = pl.BlockSpec(memory_space=pltpu.VMEM)
+    smem = pl.BlockSpec(memory_space=pltpu.SMEM)
+    dt = spins.dtype
+    out_shape = (
+        jax.ShapeDtypeStruct(spins.shape, dt),
+        jax.ShapeDtypeStruct((comps, 1, rows_x, rows_y), dt),
+        jax.ShapeDtypeStruct((comps, 1, rows_x, rows_y), dt),
+        jax.ShapeDtypeStruct((comps, layers, 1, rows_y), dt),
+        jax.ShapeDtypeStruct((comps, layers, 1, rows_y), dt),
+        jax.ShapeDtypeStruct((comps, layers, rows_x, 1), dt),
+        jax.ShapeDtypeStruct((comps, layers, rows_x, 1), dt),
+    )
+    sites = layers * rows_x * rows_y
+    return pl.pallas_call(
+        functools.partial(sweep_kernel, colour, sweep),
+        out_shape=out_shape,
+        in_specs=[smem] + [vmem] * 10,
+        out_specs=tuple([vmem] * 7),
+        cost_estimate=pl.CostEstimate(flops=200 * sites, transcendentals=4 * sites, bytes_accessed=4 * 14 * sites),
+    )(exch_flat, spins, *halos, film_cells, trials, uniforms)
+
+
+def spin_halos(faces):
+    lo, hi, xlo, xhi, ylo, yhi = faces
+    out = []
+    for axis, low_src, high_src in (("region", hi, lo), (GX, xhi, xlo), (GY, yhi, ylo)):
+        count = lax.axis_size(axis)
+        up = [(i, i + 1) for i in range(count - 1)]
+        out.append(lax.ppermute(low_src, axis, up))
+        out.append(lax.ppermute(high_src, axis, [(b, a) for a, b in up]))
+    return out
+
+
 def cross_product(left, right):
     return jnp.stack(
         [
@@ -176,7 +263,7 @@
     first_tile = (region_pos == 0) & (gx_pos == 0) & (gy_pos == 0)
     film_block = film_m[:, : piece_x * gx_count, : piece_y * gy_count]
     stack_spins, unif_all, trial_all = (spins, uniforms, trials)
-    layer_pos = region_pos * layers_dev + jnp.arange(layers_dev, dtype=jnp.int32)
+    assert layers_dev % 2 == 0 and rows_x % 2 == 0 and rows_y % 2 == 0
     pieces = (
         film_block.reshape(3, gx_count, piece_x, gy_count, piece_y)
         .transpose(1, 3, 0, 2, 4)
@@ -186,21 +273,20 @@
     placed = summed_rows(pieces, (("gx_0", "gx_1", "gy_0"), "gy_1"), 0)[0]
     own_cells = picked(placed, "region", 0)
     film_cells = jnp.repeat(jnp.repeat(own_cells, K, axis=1), K, axis=2)
-    film_near = jnp.broadcast_to(film_cells[:, None], (3, stack_spins.shape[1], rows_x, rows_y))
-    x_global = gx_pos * rows_x + jnp.arange(rows_x, dtype=jnp.int32)
-    y_global = gy_pos * rows_y + jnp.arange(rows_y, dtype=jnp.int32)
-    parity = (layer_pos[:, None, None] + x_global[None, :, None] + y_global[None, None, :]) % 2
+    exch_flat = exch_kernel.reshape(-1)
+    faces = (
+        stack_spins[:, :1],
+        stack_spins[:, -1:],
+        stack_spins[:, :, :1],
+        stack_spins[:, :, -1:],
+        stack_spins[:, :, :, :1],
+        stack_spins[:, :, :, -1:],
+    )
     for sweep_index in range(SWEEPS):
         for colour in (0, 1):
-            padded = with_halo(stack_spins, (("region", 1), (GX, 2), (GY, 3)), 1)
-            stack_spins = metropolis(
-                stack_spins,
-                padded,
-                exch_kernel,
-                film_near,
-                trial_all[sweep_index],
-                unif_all[sweep_index],
-                parity == colour,
+            halos = spin_halos(faces)
+            stack_spins, *faces = half_sweep(
+                stack_spins, halos, exch_flat, film_cells, trial_all, unif_all, sweep_index, colour
             )
     averages = stack_spins[:, 0].reshape(3, piece_x, K, piece_y, K).mean(axis=(2, 4))
     gathered = whole_of(averages[None], (("gx_0", "gx_1", "gy_0"), "gy_1"), 0)

time: 340 us -> 227 us (0.67)
  other arithmetic: 141 us -> 6.71 us
  waiting for transfers between devices: 15.5 us -> 33 us
  starting transfers between devices: 149 us -> 140 us
  Pallas kernels: 0 us -> 8.75 us
    add x38 -> x0, other arithmetic: 133 us -> none  [the longest x19 72.8 us: apply_transposed(): matrix[0, component] * vector[0] + matrix[1, component] * vector[1]]
    ppermute x0 -> x24, starting transfers between devices: none -> 79.7 us  [the longest x12 56 us: spin_halos(): out.append(lax.ppermute(low_src, axis, up))]
    ppermute x16 -> x4, starting transfers between devices: 89.7 us -> 20.7 us  [with_halo(): lax.ppermute(last, axis, up)]
    ppermute x0 -> x24, waiting for transfers between devices: none -> 18.3 us  [the longest x12 14.4 us: spin_halos(): out.append(lax.ppermute(high_src, axis, [(b, a) for a, b in up]))]
    ppermute x16 -> x4, starting transfers between devices: 25.3 us -> 7.74 us  [with_halo(): lax.ppermute(leading, axis, [(b, a) for a, b in up])]
    all_to_all x1, waiting for transfers between devices: 0.01 us -> 8.82 us  [summed_rows(): return jnp.sum(lax.all_to_all(own, far, 0, 0, tiled=True), axis=0)]
    pallas_call x0 -> x4, Pallas kernels: none -> 8.75 us  [half_sweep(): pl.pallas_call(functools.partial(sweep_kernel, colour, sweep), out_shape=...]
    ppermute x16 -> x4, waiting for transfers between devices: 12.4 us -> 4.4 us  [with_halo(): lax.ppermute(leading, axis, [(b, a) for a, b in up])]
  transfers between devices with their start and end apart: 34 -> 34, of which waited for: 6 -> 10; matrix products, arithmetic and copies ran while one was open for 23% -> 6% of each run, Pallas kernels for 0% -> 1%
where the time goes in v1:
time: 227 us; the launch traced here: 226 us
  starting transfers between devices  140 us (62%)
  waiting for transfers between devices  33 us (15%)
  blocking collectives  21.5 us (9%)
  local copies, waits for them, and re-layouts  13.7 us (6%)
  Pallas kernels  8.75 us (4%)
  other arithmetic  6.71 us (3%)
    ppermute x12, starting transfers between devices, spin_halos(): out.append(lax.ppermute(low_src, axis, up))  56 us
    ppermute x12, starting transfers between devices, spin_halos(): out.append(lax.ppermute(high_src, axis, [(b, a) for a, b in up]))  23.7 us
    ppermute x4, starting transfers between devices, with_halo(): lax.ppermute(last, axis, up)  20.7 us
    all_to_all x1, starting transfers between devices, summed_rows(): return jnp.sum(lax.all_to_all(own, far, 0, 0, tiled=True), axis=0)  16.3 us
    all_to_all x1, starting transfers between devices, copy_for_each(): lax.all_to_all(jnp.broadcast_to(array[None], (count, *array.shape)), axis...  15.9 us
    ppermute x12, waiting for transfers between devices, spin_halos(): out.append(lax.ppermute(high_src, axis, [(b, a) for a, b in up]))  14.4 us
    all_gather x1, blocking collectives, picked(): lax.all_gather(array, axis)  11.5 us
    all_to_all x1, waiting for transfers between devices, summed_rows(): return jnp.sum(lax.all_to_all(own, far, 0, 0, tiled=True), axis=0)  8.82 us
  transfers between devices with their start and end apart: 34, of which 10 were waited for; matrix products, arithmetic and copies ran while one was open for 6% of the time, Pallas kernels for 1%

profile of v1, /device:TPU:1, one launch (start us, length us, event | category | flops | bytes accessed | tf_op | source)
XLA Modules:
  0.0 225.5 jit_solution(14861536269193222193)
XLA Ops:
  1.5 4.8 %collective-permute-start = (f32[3,1,32,128]{3,2,1,0:T(8,128)S(1)}, f32[3,1,32,128]{3,2,1,0:T(8,128)S(1)}, u32[]{:S(2)}, u32[]{:S(2)}) collective-permute-start(f32[3,1,32,128]{3,2,1,0:T(8,128)S(1)} %get-tuple-element.71), channel_id=1, source_target_pairs={{0,128},{128,256},{256,384},{1,129},{129,257},{257,385},{2,130},{1... | collective-permute-start | bytes 147464 | tf_op jit(solution)/shard_map/ppermute | solution.py:217
  6.3 1.3 collective-permute-start.1
  7.7 9.7 %collective-permute-start.2 = (f32[3,2,1,128]{3,2,1,0:T(1,128)S(1)}, f32[3,2,1,128]{3,2,1,0:T(1,128)S(1)}, u32[]{:S(2)}, u32[]{:S(2)}) collective-permute-start(f32[3,2,1,128]{3,2,1,0:T(1,128)S(1)} %get-tuple-element.69), channel_id=1, source_target_pairs={{0,8},{8,16},{16,24},{24,32},{32,40},{40,48},{48,56},{56,64},{64,7... | collective-permute-start | bytes 9224 | tf_op jit(solution)/shard_map/ppermute | solution.py:217
  17.4 1.3 collective-permute-start.3
  20.5 4.7 %all_to_all.20 = f32[2,1,12288]{2,1,0:T(1,128)S(1)} all-to-all(f32[2,1,12288]{2,1,0:T(1,128)S(1)} %reshape.55), channel_id=1, replica_groups=mesh['region'=4,'gx_0'=8,'gx_1'=2,'gy_0'=4,'gy_1'=2] {'gy_1'}, dimensions={0} | all-to-all | bytes 196608 | tf_op jit(solution)/shard_map/all_to_all | solution.py:56
  28.2 16.3 %all-to-all-start.1 = ((f32[64,1,192]{2,1,0:T(1,128)}), f32[64,1,192]{2,1,0:T(1,128)S(1)}, u32[]{:S(2)}, u32[]{:S(2)}) async-start(f32[64,1,192]{2,1,0:T(1,128)} %reshape.57), calls=%async_computation.1 | async-start | bytes 131072 | tf_op jit(solution)/shard_map/all_to_all | solution.py:63
  44.6 3.7 %collective-permute-start.4 = (f32[3,2,32,1]{3,2,1,0:T(8,128)S(1)}, f32[3,2,32,1]{3,2,1,0:T(8,128)S(1)}, u32[]{:S(2)}, u32[]{:S(2)}) collective-permute-start(f32[3,2,32,1]{3,2,1,0:T(8,128)S(1)} %get-tuple-element.67), channel_id=1, source_target_pairs={{0,1},{1,2},{2,3},{3,4},{4,5},{5,6},{6,7},{8,9},{9,10},{10,11},{11... | collective-permute-start | bytes 2312 | tf_op jit(solution)/shard_map/ppermute | solution.py:217
  49.0 8.8 %all-to-all-done.1 = f32[64,1,192]{2,1,0:T(1,128)S(1)} async-done(((f32[64,1,192]{2,1,0:T(1,128)}), f32[64,1,192]{2,1,0:T(1,128)S(1)}, u32[]{:S(2)}, u32[]{:S(2)}) %all-to-all-start.1) | async-done | bytes 49184 | tf_op jit(solution)/shard_map/all_to_all | solution.py:63
  59.0 11.5 %all-gather = f32[12,4,16]{2,1,0:T(4,128)S(1)} all-gather(f32[3,4,16]{2,1,0:T(4,128)S(1)} %reduce_sum.42), channel_id=2, replica_groups=mesh['region'=4,'gx_0'=8,'gx_1'=2,'gy_0'=4,'gy_1'=2] {'region'}, dimensions={0}, use_global_device_ids=true | all-gather | bytes 3840 | tf_op jit(solution)/shard_map/all_gather | solution.py:67
  70.6 6.6 %collective-permute-start.5 = (f32[3,2,32,1]{3,2,1,0:T(8,128)S(1)}, f32[3,2,32,1]{3,2,1,0:T(8,128)S(1)}, u32[]{:S(2)}, u32[]{:S(2)}) collective-permute-start(f32[3,2,32,1]{3,2,1,0:T(8,128)S(1)} %get-tuple-element.66), channel_id=1, source_target_pairs={{1,0},{2,1},{3,2},{4,3},{5,4},{6,5},{7,6},{9,8},{10,9},{11,10},{12... | collective-permute-start | bytes 2312 | tf_op jit(solution)/shard_map/ppermute | solution.py:218
  77.9 1.7 collective-permute-done.5.yhi_ref
  80.9 2.2 shard_map.77
  83.1 3.1 %collective-permute-start.6 = (f32[3,1,32,128]{3,2,1,0:T(8,128)}, f32[3,1,32,128]{3,2,1,0:T(8,128)S(1)}, u32[]{:S(2)}, u32[]{:S(2)}) collective-permute-start(f32[3,1,32,128]{3,2,1,0:T(8,128)} %get-tuple-element.25), channel_id=1, source_target_pairs={{0,128},{128,256},{256,384},{1,129},{129,257},{257,385},{2,130},{1... | collective-permute-start | bytes 147464 | tf_op jit(solution)/shard_map/ppermute | solution.py:217
  86.2 1.3 collective-permute-start.7
  87.5 2.5 %collective-permute-start.8 = (f32[3,2,1,128]{3,2,1,0:T(1,128)S(1)}, f32[3,2,1,128]{3,2,1,0:T(1,128)S(1)}, u32[]{:S(2)}, u32[]{:S(2)}) collective-permute-start(f32[3,2,1,128]{3,2,1,0:T(1,128)S(1)} %copy-done.31), channel_id=1, source_target_pairs={{0,8},{8,16},{16,24},{24,32},{32,40},{40,48},{48,56},{56,64},{64,7... | collective-permute-start | bytes 9224 | tf_op jit(solution)/shard_map/ppermute | solution.py:217
  90.0 1.3 collective-permute-start.9
  91.3 2.4 %collective-permute-start.10 = (f32[3,2,32,1]{3,2,1,0:T(8,128)}, f32[3,2,32,1]{3,2,1,0:T(8,128)S(1)}, u32[]{:S(2)}, u32[]{:S(2)}) collective-permute-start(f32[3,2,32,1]{3,2,1,0:T(8,128)} %get-tuple-element.29), channel_id=1, source_target_pairs={{0,1},{1,2},{2,3},{3,4},{4,5},{5,6},{6,7},{8,9},{9,10},{10,11},{11... | collective-permute-start | bytes 2312 | tf_op jit(solution)/shard_map/ppermute | solution.py:217
  93.7 1.9 collective-permute-done.10.ylo_ref
  95.6 1.9 collective-permute-start.11
  97.5 4.8 %collective-permute-done.11.yhi_ref = f32[3,2,32,1]{3,2,1,0:T(8,128)S(1)} collective-permute-done((f32[3,2,32,1]{3,2,1,0:T(8,128)}, f32[3,2,32,1]{3,2,1,0:T(8,128)S(1)}, u32[]{:S(2)}, u32[]{:S(2)}) %collective-permute-start.11) | collective-permute-done | bytes 800 | tf_op jit(solution)/shard_map/ppermute | solution.py:218
  103.0 2.2 shard_map.78
  105.2 4.4 %collective-permute-start.12 = (f32[3,1,32,128]{3,2,1,0:T(8,128)}, f32[3,1,32,128]{3,2,1,0:T(8,128)S(1)}, u32[]{:S(2)}, u32[]{:S(2)}) collective-permute-start(f32[3,1,32,128]{3,2,1,0:T(8,128)} %get-tuple-element.32), channel_id=1, source_target_pairs={{0,128},{128,256},{256,384},{1,129},{129,257},{257,385},{2,130},{1... | collective-permute-start | bytes 147464 | tf_op jit(solution)/shard_map/ppermute | solution.py:217
  109.6 1.3 collective-permute-start.13
  110.9 8.2 %collective-permute-start.14 = (f32[3,2,1,128]{3,2,1,0:T(1,128)}, f32[3,2,1,128]{3,2,1,0:T(1,128)S(1)}, u32[]{:S(2)}, u32[]{:S(2)}) collective-permute-start(f32[3,2,1,128]{3,2,1,0:T(1,128)} %get-tuple-element.34), channel_id=1, source_target_pairs={{0,8},{8,16},{16,24},{24,32},{32,40},{40,48},{48,56},{56,64},{64,7... | collective-permute-start | bytes 9224 | tf_op jit(solution)/shard_map/ppermute | solution.py:217
  119.0 1.3 collective-permute-start.15
  120.3 2.5 %collective-permute-start.16 = (f32[3,2,32,1]{3,2,1,0:T(8,128)}, f32[3,2,32,1]{3,2,1,0:T(8,128)S(1)}, u32[]{:S(2)}, u32[]{:S(2)}) collective-permute-start(f32[3,2,32,1]{3,2,1,0:T(8,128)} %get-tuple-element.36), channel_id=1, source_target_pairs={{0,1},{1,2},{2,3},{3,4},{4,5},{5,6},{6,7},{8,9},{9,10},{10,11},{11... | collective-permute-start | bytes 2312 | tf_op jit(solution)/shard_map/ppermute | solution.py:217
  122.8 1.9 collective-permute-done.16.ylo_ref
  124.8 1.9 collective-permute-start.17
  126.7 4.8 %collective-permute-done.17.yhi_ref = f32[3,2,32,1]{3,2,1,0:T(8,128)S(1)} collective-permute-done((f32[3,2,32,1]{3,2,1,0:T(8,128)}, f32[3,2,32,1]{3,2,1,0:T(8,128)S(1)}, u32[]{:S(2)}, u32[]{:S(2)}) %collective-permute-start.17) | collective-permute-done | bytes 800 | tf_op jit(solution)/shard_map/ppermute | solution.py:218
  132.1 2.2 shard_map.79
  134.3 2.0 collective-permute-start.22
  136.4 4.3 %collective-permute-start.18 = (f32[3,1,32,128]{3,2,1,0:T(8,128)}, f32[3,1,32,128]{3,2,1,0:T(8,128)S(1)}, u32[]{:S(2)}, u32[]{:S(2)}) collective-permute-start(f32[3,1,32,128]{3,2,1,0:T(8,128)} %get-tuple-element.39), channel_id=1, source_target_pairs={{0,128},{128,256},{256,384},{1,129},{129,257},{257,385},{2,130},{1... | collective-permute-start | bytes 147464 | tf_op jit(solution)/shard_map/ppermute | solution.py:217
  140.7 1.3 collective-permute-start.19
  142.0 8.4 %collective-permute-start.20 = (f32[3,2,1,128]{3,2,1,0:T(1,128)S(1)}, f32[3,2,1,128]{3,2,1,0:T(1,128)S(1)}, u32[]{:S(2)}, u32[]{:S(2)}) collective-permute-start(f32[3,2,1,128]{3,2,1,0:T(1,128)S(1)} %copy-done.29), channel_id=1, source_target_pairs={{0,8},{8,16},{16,24},{24,32},{32,40},{40,48},{48,56},{56,64},{64,7... | collective-permute-start | bytes 9224 | tf_op jit(solution)/shard_map/ppermute | solution.py:217
  150.5 1.3 collective-permute-start.21
  151.8 3.0 %collective-permute-start.23 = (f32[3,2,32,1]{3,2,1,0:T(8,128)}, f32[3,2,32,1]{3,2,1,0:T(8,128)S(1)}, u32[]{:S(2)}, u32[]{:S(2)}) collective-permute-start(f32[3,2,32,1]{3,2,1,0:T(8,128)} %get-tuple-element.44), channel_id=1, source_target_pairs={{1,0},{2,1},{3,2},{4,3},{5,4},{6,5},{7,6},{9,8},{10,9},{11,10},{12... | collective-permute-start | bytes 2312 | tf_op jit(solution)/shard_map/ppermute | solution.py:218
  154.9 3.0 %collective-permute-done.23.yhi_ref = f32[3,2,32,1]{3,2,1,0:T(8,128)S(1)} collective-permute-done((f32[3,2,32,1]{3,2,1,0:T(8,128)}, f32[3,2,32,1]{3,2,1,0:T(8,128)S(1)}, u32[]{:S(2)}, u32[]{:S(2)}) %collective-permute-start.23) | collective-permute-done | bytes 800 | tf_op jit(solution)/shard_map/ppermute | solution.py:218
  157.9 1.9 collective-permute-start.27
  160.5 2.2 shard_map.80
  165.1 15.9 %all-to-all-start.2 = ((f32[64,1,192]{2,1,0:T(1,128)}), f32[64,1,192]{2,1,0:T(1,128)S(1)}, u32[]{:S(2)}, u32[]{:S(2)}) async-start(f32[64,1,192]{2,1,0:T(1,128)} %reshape.59), calls=%async_computation.2 | async-start | bytes 131072 | tf_op jit(solution)/shard_map/all_to_all | solution.py:72
  181.1 1.3 collective-permute-start.24
  182.4 7.9 %collective-permute-start.25 = (f32[3,1,256]{2,1,0:T(1,128)S(1)}, f32[3,1,256]{2,1,0:T(1,128)S(1)}, u32[]{:S(2)}, u32[]{:S(2)}) collective-permute-start(f32[3,1,256]{2,1,0:T(1,128)S(1)} %get-tuple-element.64), channel_id=1, source_target_pairs={{0,8},{8,16},{16,24},{24,32},{32,40},{40,48},{48,56},{56,64},{64,7... | collective-permute-start | bytes 9224 | tf_op jit(solution)/shard_map/ppermute | solution.py:36
  190.3 3.2 %collective-permute-start.26 = (f32[3,128,1]{2,1,0:T(8,128)S(1)}, f32[3,128,1]{2,1,0:T(8,128)S(1)}, u32[]{:S(2)}, u32[]{:S(2)}) collective-permute-start(f32[3,128,1]{2,1,0:T(8,128)S(1)} %get-tuple-element.62), channel_id=1, source_target_pairs={{1,0},{2,1},{3,2},{4,3},{5,4},{6,5},{7,6},{9,8},{10,9},{11,10},{12... | collective-permute-start | bytes 4616 | tf_op jit(solution)/shard_map/ppermute | solution.py:37
  195.7 5.4 %all_to_all.21 = f32[2,1,12288]{2,1,0:T(1,128)S(1)} all-to-all(f32[2,1,12288]{2,1,0:T(1,128)S(1)} %reshape.61), channel_id=1, replica_groups=mesh['region'=4,'gx_0'=8,'gx_1'=2,'gy_0'=4,'gy_1'=2] {'gy_1'}, dimensions={0} | all-to-all | bytes 196608 | tf_op jit(solution)/shard_map/all_to_all | solution.py:72
  206.0 7.9 %collective-permute-start.29 = (f32[3,1,256]{2,1,0:T(1,128)S(1)}, f32[3,1,256]{2,1,0:T(1,128)S(1)}, u32[]{:S(2)}, u32[]{:S(2)}) collective-permute-start(f32[3,1,256]{2,1,0:T(1,128)S(1)} %get-tuple-element.60), channel_id=1, source_target_pairs={{0,8},{8,16},{16,24},{24,32},{32,40},{40,48},{48,56},{56,64},{64,7... | collective-permute-start | bytes 9224 | tf_op jit(solution)/shard_map/ppermute | solution.py:36
  214.0 3.0 %collective-permute-start.31 = (f32[3,128,1]{2,1,0:T(8,128)S(1)}, f32[3,128,1]{2,1,0:T(8,128)S(1)}, u32[]{:S(2)}, u32[]{:S(2)}) collective-permute-start(f32[3,128,1]{2,1,0:T(8,128)S(1)} %get-tuple-element.59), channel_id=1, source_target_pairs={{0,1},{1,2},{2,3},{3,4},{4,5},{5,6},{6,7},{8,9},{9,10},{10,11},{11... | collective-permute-start | bytes 4616 | tf_op jit(solution)/shard_map/ppermute | solution.py:36
  217.0 1.9 collective-permute-start.30
  219.6 4.4 %collective-permute-done.30 = f32[3,128,1]{2,1,0:T(8,128)S(1)} collective-permute-done((f32[3,128,1]{2,1,0:T(8,128)S(1)}, f32[3,128,1]{2,1,0:T(8,128)S(1)}, u32[]{:S(2)}, u32[]{:S(2)}) %collective-permute-start.30) | collective-permute-done | bytes 1568 | tf_op jit(solution)/shard_map/ppermute | solution.py:37
  (150 shorter events, 23.3 us)
Async XLA Ops:
  0.6 7.0 %copy-start.2 = (f32[3,2,32,128]{3,2,1,0:T(8,128)S(1)}, f32[3,2,32,128]{3,2,1,0:T(8,128)}, u32[]{:S(2)}) copy-start(f32[3,2,32,128]{3,2,1,0:T(8,128)} %s_ref.1) | copy-start | bytes 294916
  1.5 78.1 %collective-permute-start = (f32[3,1,32,128]{3,2,1,0:T(8,128)S(1)}, f32[3,1,32,128]{3,2,1,0:T(8,128)S(1)}, u32[]{:S(2)}, u32[]{:S(2)}) collective-permute-start(f32[3,1,32,128]{3,2,1,0:T(8,128)S(1)} %get-tuple-element.71), channel_id=1, source_target_pairs={{0,128},{128,256},{256,384},{1,129},{129,257},{257,385},{2,130},{1... | collective-permute-start | bytes 147464 | tf_op jit(solution)/shard_map/ppermute | solution.py:217
  6.3 73.3 %collective-permute-start.1 = (f32[3,1,32,128]{3,2,1,0:T(8,128)S(1)}, f32[3,1,32,128]{3,2,1,0:T(8,128)S(1)}, u32[]{:S(2)}, u32[]{:S(2)}) collective-permute-start(f32[3,1,32,128]{3,2,1,0:T(8,128)S(1)} %get-tuple-element.70), channel_id=1, source_target_pairs={{128,0},{256,128},{384,256},{129,1},{257,129},{385,257},{130,2},{2... | collective-permute-start | bytes 147464 | tf_op jit(solution)/shard_map/ppermute | solution.py:218
  7.7 72.0 %collective-permute-start.2 = (f32[3,2,1,128]{3,2,1,0:T(1,128)S(1)}, f32[3,2,1,128]{3,2,1,0:T(1,128)S(1)}, u32[]{:S(2)}, u32[]{:S(2)}) collective-permute-start(f32[3,2,1,128]{3,2,1,0:T(1,128)S(1)} %get-tuple-element.69), channel_id=1, source_target_pairs={{0,8},{8,16},{16,24},{24,32},{32,40},{40,48},{48,56},{56,64},{64,7... | collective-permute-start | bytes 9224 | tf_op jit(solution)/shard_map/ppermute | solution.py:217
  17.4 62.2 %collective-permute-start.3 = (f32[3,2,1,128]{3,2,1,0:T(1,128)S(1)}, f32[3,2,1,128]{3,2,1,0:T(1,128)S(1)}, u32[]{:S(2)}, u32[]{:S(2)}) collective-permute-start(f32[3,2,1,128]{3,2,1,0:T(1,128)S(1)} %get-tuple-element.68), channel_id=1, source_target_pairs={{8,0},{16,8},{24,16},{32,24},{40,32},{48,40},{56,48},{64,56},{72,6... | collective-permute-start | bytes 9224 | tf_op jit(solution)/shard_map/ppermute | solution.py:218
  28.2 29.6 %all-to-all-start.1 = ((f32[64,1,192]{2,1,0:T(1,128)}), f32[64,1,192]{2,1,0:T(1,128)S(1)}, u32[]{:S(2)}, u32[]{:S(2)}) async-start(f32[64,1,192]{2,1,0:T(1,128)} %reshape.57), calls=%async_computation.1 | async-start | bytes 131072 | tf_op jit(solution)/shard_map/all_to_all | solution.py:63
  44.5 3.8 %copy-start.19 = (f32[3,3,3]{2,1,0:T(4,128)S(1)}, f32[3,3,3]{2,1,0:T(4,128)}, u32[]{:S(2)}) copy-start(f32[3,3,3]{2,1,0:T(4,128)} %param.9) | copy-start | bytes 328
  44.6 25.9 %collective-permute-start.4 = (f32[3,2,32,1]{3,2,1,0:T(8,128)S(1)}, f32[3,2,32,1]{3,2,1,0:T(8,128)S(1)}, u32[]{:S(2)}, u32[]{:S(2)}) collective-permute-start(f32[3,2,32,1]{3,2,1,0:T(8,128)S(1)} %get-tuple-element.67), channel_id=1, source_target_pairs={{0,1},{1,2},{2,3},{3,4},{4,5},{5,6},{6,7},{8,9},{9,10},{10,11},{11... | collective-permute-start | bytes 2312 | tf_op jit(solution)/shard_map/ppermute | solution.py:217
  70.6 6.6 %copy-start.3 = (f32[3,2,32,1]{3,2,1,0:T(8,128)}, f32[3,2,32,1]{3,2,1,0:T(8,128)S(1)}, u32[]{:S(2)}) copy-start(f32[3,2,32,1]{3,2,1,0:T(8,128)S(1)} %collective-permute-done.4.ylo_ref) | copy-start | bytes 2308
  70.6 9.1 %collective-permute-start.5 = (f32[3,2,32,1]{3,2,1,0:T(8,128)S(1)}, f32[3,2,32,1]{3,2,1,0:T(8,128)S(1)}, u32[]{:S(2)}, u32[]{:S(2)}) collective-permute-start(f32[3,2,32,1]{3,2,1,0:T(8,128)S(1)} %get-tuple-element.66), channel_id=1, source_target_pairs={{1,0},{2,1},{3,2},{4,3},{5,4},{6,5},{7,6},{9,8},{10,9},{11,10},{12... | collective-permute-start | bytes 2312 | tf_op jit(solution)/shard_map/ppermute | solution.py:218
  83.1 4.4 %copy-start.31 = (f32[3,2,1,128]{3,2,1,0:T(1,128)S(1)}, f32[3,2,1,128]{3,2,1,0:T(1,128)}, u32[]{:S(2)}) copy-start(f32[3,2,1,128]{3,2,1,0:T(1,128)} %get-tuple-element.27) | copy-start | bytes 9220
  83.1 6.9 %copy-start.30 = (f32[3,2,1,128]{3,2,1,0:T(1,128)S(1)}, f32[3,2,1,128]{3,2,1,0:T(1,128)}, u32[]{:S(2)}) copy-start(f32[3,2,1,128]{3,2,1,0:T(1,128)} %get-tuple-element.28) | copy-start | bytes 9220
  83.1 19.2 %collective-permute-start.6 = (f32[3,1,32,128]{3,2,1,0:T(8,128)}, f32[3,1,32,128]{3,2,1,0:T(8,128)S(1)}, u32[]{:S(2)}, u32[]{:S(2)}) collective-permute-start(f32[3,1,32,128]{3,2,1,0:T(8,128)} %get-tuple-element.25), channel_id=1, source_target_pairs={{0,128},{128,256},{256,384},{1,129},{129,257},{257,385},{2,130},{1... | collective-permute-start | bytes 147464 | tf_op jit(solution)/shard_map/ppermute | solution.py:217
  86.2 16.2 %collective-permute-start.7 = (f32[3,1,32,128]{3,2,1,0:T(8,128)}, f32[3,1,32,128]{3,2,1,0:T(8,128)S(1)}, u32[]{:S(2)}, u32[]{:S(2)}) collective-permute-start(f32[3,1,32,128]{3,2,1,0:T(8,128)} %get-tuple-element.26), channel_id=1, source_target_pairs={{128,0},{256,128},{384,256},{129,1},{257,129},{385,257},{130,2},{2... | collective-permute-start | bytes 147464 | tf_op jit(solution)/shard_map/ppermute | solution.py:218
  87.5 14.8 %collective-permute-start.8 = (f32[3,2,1,128]{3,2,1,0:T(1,128)S(1)}, f32[3,2,1,128]{3,2,1,0:T(1,128)S(1)}, u32[]{:S(2)}, u32[]{:S(2)}) collective-permute-start(f32[3,2,1,128]{3,2,1,0:T(1,128)S(1)} %copy-done.31), channel_id=1, source_target_pairs={{0,8},{8,16},{16,24},{24,32},{32,40},{40,48},{48,56},{56,64},{64,7... | collective-permute-start | bytes 9224 | tf_op jit(solution)/shard_map/ppermute | solution.py:217
  90.0 12.3 %collective-permute-start.9 = (f32[3,2,1,128]{3,2,1,0:T(1,128)S(1)}, f32[3,2,1,128]{3,2,1,0:T(1,128)S(1)}, u32[]{:S(2)}, u32[]{:S(2)}) collective-permute-start(f32[3,2,1,128]{3,2,1,0:T(1,128)S(1)} %copy-done.30), channel_id=1, source_target_pairs={{8,0},{16,8},{24,16},{32,24},{40,32},{48,40},{56,48},{64,56},{72,6... | collective-permute-start | bytes 9224 | tf_op jit(solution)/shard_map/ppermute | solution.py:218
  91.3 4.3 %collective-permute-start.10 = (f32[3,2,32,1]{3,2,1,0:T(8,128)}, f32[3,2,32,1]{3,2,1,0:T(8,128)S(1)}, u32[]{:S(2)}, u32[]{:S(2)}) collective-permute-start(f32[3,2,32,1]{3,2,1,0:T(8,128)} %get-tuple-element.29), channel_id=1, source_target_pairs={{0,1},{1,2},{2,3},{3,4},{4,5},{5,6},{6,7},{8,9},{9,10},{10,11},{11... | collective-permute-start | bytes 2312 | tf_op jit(solution)/shard_map/ppermute | solution.py:217
  95.6 6.8 %copy-start.6 = (f32[3,2,32,1]{3,2,1,0:T(8,128)}, f32[3,2,32,1]{3,2,1,0:T(8,128)S(1)}, u32[]{:S(2)}) copy-start(f32[3,2,32,1]{3,2,1,0:T(8,128)S(1)} %collective-permute-done.10.ylo_ref) | copy-start | bytes 2308
  95.6 6.7 %collective-permute-start.11 = (f32[3,2,32,1]{3,2,1,0:T(8,128)}, f32[3,2,32,1]{3,2,1,0:T(8,128)S(1)}, u32[]{:S(2)}, u32[]{:S(2)}) collective-permute-start(f32[3,2,32,1]{3,2,1,0:T(8,128)} %get-tuple-element.30), channel_id=1, source_target_pairs={{1,0},{2,1},{3,2},{4,3},{5,4},{6,5},{7,6},{9,8},{10,9},{11,10},{12... | collective-permute-start | bytes 2312 | tf_op jit(solution)/shard_map/ppermute | solution.py:218
  102.3 0.6 copy-start.9
  105.2 49.6 %copy-start = (f32[3,128,256]{2,1,0:T(8,128)S(1)}, f32[3,128,256]{2,1,0:T(8,128)}, u32[]{:S(2)}) copy-start(f32[3,128,256]{2,1,0:T(8,128)} %param.10) | copy-start | bytes 1179652
  105.2 26.3 %collective-permute-start.12 = (f32[3,1,32,128]{3,2,1,0:T(8,128)}, f32[3,1,32,128]{3,2,1,0:T(8,128)S(1)}, u32[]{:S(2)}, u32[]{:S(2)}) collective-permute-start(f32[3,1,32,128]{3,2,1,0:T(8,128)} %get-tuple-element.32), channel_id=1, source_target_pairs={{0,128},{128,256},{256,384},{1,129},{129,257},{257,385},{2,130},{1... | collective-permute-start | bytes 147464 | tf_op jit(solution)/shard_map/ppermute | solution.py:217
  109.6 22.0 %collective-permute-start.13 = (f32[3,1,32,128]{3,2,1,0:T(8,128)}, f32[3,1,32,128]{3,2,1,0:T(8,128)S(1)}, u32[]{:S(2)}, u32[]{:S(2)}) collective-permute-start(f32[3,1,32,128]{3,2,1,0:T(8,128)} %get-tuple-element.33), channel_id=1, source_target_pairs={{128,0},{256,128},{384,256},{129,1},{257,129},{385,257},{130,2},{2... | collective-permute-start | bytes 147464 | tf_op jit(solution)/shard_map/ppermute | solution.py:218
  110.9 20.6 %collective-permute-start.14 = (f32[3,2,1,128]{3,2,1,0:T(1,128)}, f32[3,2,1,128]{3,2,1,0:T(1,128)S(1)}, u32[]{:S(2)}, u32[]{:S(2)}) collective-permute-start(f32[3,2,1,128]{3,2,1,0:T(1,128)} %get-tuple-element.34), channel_id=1, source_target_pairs={{0,8},{8,16},{16,24},{24,32},{32,40},{40,48},{48,56},{56,64},{64,7... | collective-permute-start | bytes 9224 | tf_op jit(solution)/shard_map/ppermute | solution.py:217
  119.0 12.4 %collective-permute-start.15 = (f32[3,2,1,128]{3,2,1,0:T(1,128)}, f32[3,2,1,128]{3,2,1,0:T(1,128)S(1)}, u32[]{:S(2)}, u32[]{:S(2)}) collective-permute-start(f32[3,2,1,128]{3,2,1,0:T(1,128)} %get-tuple-element.35), channel_id=1, source_target_pairs={{8,0},{16,8},{24,16},{32,24},{40,32},{48,40},{56,48},{64,56},{72,6... | collective-permute-start | bytes 9224 | tf_op jit(solution)/shard_map/ppermute | solution.py:218
  120.3 4.4 %collective-permute-start.16 = (f32[3,2,32,1]{3,2,1,0:T(8,128)}, f32[3,2,32,1]{3,2,1,0:T(8,128)S(1)}, u32[]{:S(2)}, u32[]{:S(2)}) collective-permute-start(f32[3,2,32,1]{3,2,1,0:T(8,128)} %get-tuple-element.36), channel_id=1, source_target_pairs={{0,1},{1,2},{2,3},{3,4},{4,5},{5,6},{6,7},{8,9},{9,10},{10,11},{11... | collective-permute-start | bytes 2312 | tf_op jit(solution)/shard_map/ppermute | solution.py:217
  124.8 6.8 %copy-start.7 = (f32[3,2,32,1]{3,2,1,0:T(8,128)}, f32[3,2,32,1]{3,2,1,0:T(8,128)S(1)}, u32[]{:S(2)}) copy-start(f32[3,2,32,1]{3,2,1,0:T(8,128)S(1)} %collective-permute-done.16.ylo_ref) | copy-start | bytes 2308
  124.8 6.7 %collective-permute-start.17 = (f32[3,2,32,1]{3,2,1,0:T(8,128)}, f32[3,2,32,1]{3,2,1,0:T(8,128)S(1)}, u32[]{:S(2)}, u32[]{:S(2)}) collective-permute-start(f32[3,2,32,1]{3,2,1,0:T(8,128)} %get-tuple-element.37), channel_id=1, source_target_pairs={{1,0},{2,1},{3,2},{4,3},{5,4},{6,5},{7,6},{9,8},{10,9},{11,10},{12... | collective-permute-start | bytes 2312 | tf_op jit(solution)/shard_map/ppermute | solution.py:218
  134.3 7.6 %copy-start.29 = (f32[3,2,1,128]{3,2,1,0:T(1,128)S(1)}, f32[3,2,1,128]{3,2,1,0:T(1,128)}, u32[]{:S(2)}) copy-start(f32[3,2,1,128]{3,2,1,0:T(1,128)} %get-tuple-element.41) | copy-start | bytes 9220
  134.3 17.4 %collective-permute-start.22 = (f32[3,2,32,1]{3,2,1,0:T(8,128)}, f32[3,2,32,1]{3,2,1,0:T(8,128)S(1)}, u32[]{:S(2)}, u32[]{:S(2)}) collective-permute-start(f32[3,2,32,1]{3,2,1,0:T(8,128)} %get-tuple-element.43), channel_id=1, source_target_pairs={{0,1},{1,2},{2,3},{3,4},{4,5},{5,6},{6,7},{8,9},{9,10},{10,11},{11... | collective-permute-start | bytes 2312 | tf_op jit(solution)/shard_map/ppermute | solution.py:217
  136.4 14.0 %copy-start.28 = (f32[3,2,1,128]{3,2,1,0:T(1,128)S(1)}, f32[3,2,1,128]{3,2,1,0:T(1,128)}, u32[]{:S(2)}) copy-start(f32[3,2,1,128]{3,2,1,0:T(1,128)} %get-tuple-element.42) | copy-start | bytes 9220
  136.4 23.5 %collective-permute-start.18 = (f32[3,1,32,128]{3,2,1,0:T(8,128)}, f32[3,1,32,128]{3,2,1,0:T(8,128)S(1)}, u32[]{:S(2)}, u32[]{:S(2)}) collective-permute-start(f32[3,1,32,128]{3,2,1,0:T(8,128)} %get-tuple-element.39), channel_id=1, source_target_pairs={{0,128},{128,256},{256,384},{1,129},{129,257},{257,385},{2,130},{1... | collective-permute-start | bytes 147464 | tf_op jit(solution)/shard_map/ppermute | solution.py:217
  140.7 19.2 %collective-permute-start.19 = (f32[3,1,32,128]{3,2,1,0:T(8,128)}, f32[3,1,32,128]{3,2,1,0:T(8,128)S(1)}, u32[]{:S(2)}, u32[]{:S(2)}) collective-permute-start(f32[3,1,32,128]{3,2,1,0:T(8,128)} %get-tuple-element.40), channel_id=1, source_target_pairs={{128,0},{256,128},{384,256},{129,1},{257,129},{385,257},{130,2},{2... | collective-permute-start | bytes 147464 | tf_op jit(solution)/shard_map/ppermute | solution.py:218
  142.0 17.9 %collective-permute-start.20 = (f32[3,2,1,128]{3,2,1,0:T(1,128)S(1)}, f32[3,2,1,128]{3,2,1,0:T(1,128)S(1)}, u32[]{:S(2)}, u32[]{:S(2)}) collective-permute-start(f32[3,2,1,128]{3,2,1,0:T(1,128)S(1)} %copy-done.29), channel_id=1, source_target_pairs={{0,8},{8,16},{16,24},{24,32},{32,40},{40,48},{48,56},{56,64},{64,7... | collective-permute-start | bytes 9224 | tf_op jit(solution)/shard_map/ppermute | solution.py:217
  150.5 9.4 %collective-permute-start.21 = (f32[3,2,1,128]{3,2,1,0:T(1,128)S(1)}, f32[3,2,1,128]{3,2,1,0:T(1,128)S(1)}, u32[]{:S(2)}, u32[]{:S(2)}) collective-permute-start(f32[3,2,1,128]{3,2,1,0:T(1,128)S(1)} %copy-done.28), channel_id=1, source_target_pairs={{8,0},{16,8},{24,16},{32,24},{40,32},{48,40},{56,48},{64,56},{72,6... | collective-permute-start | bytes 9224 | tf_op jit(solution)/shard_map/ppermute | solution.py:218
  151.8 3.1 %copy-start.4 = (f32[3,2,32,1]{3,2,1,0:T(8,128)}, f32[3,2,32,1]{3,2,1,0:T(8,128)S(1)}, u32[]{:S(2)}) copy-start(f32[3,2,32,1]{3,2,1,0:T(8,128)S(1)} %collective-permute-done.22.ylo_ref) | copy-start | bytes 2308
  151.8 6.1 %collective-permute-start.23 = (f32[3,2,32,1]{3,2,1,0:T(8,128)}, f32[3,2,32,1]{3,2,1,0:T(8,128)S(1)}, u32[]{:S(2)}, u32[]{:S(2)}) collective-permute-start(f32[3,2,32,1]{3,2,1,0:T(8,128)} %get-tuple-element.44), channel_id=1, source_target_pairs={{1,0},{2,1},{3,2},{4,3},{5,4},{6,5},{7,6},{9,8},{10,9},{11,10},{12... | collective-permute-start | bytes 2312 | tf_op jit(solution)/shard_map/ppermute | solution.py:218
  157.9 2.0 copy-start.5
  157.9 45.1 %collective-permute-start.27 = (f32[3,128,1]{2,1,0:T(8,128)S(1)}, f32[3,128,1]{2,1,0:T(8,128)S(1)}, u32[]{:S(2)}, u32[]{:S(2)}) collective-permute-start(f32[3,128,1]{2,1,0:T(8,128)S(1)} %get-tuple-element.63), channel_id=1, source_target_pairs={{0,1},{1,2},{2,3},{3,4},{4,5},{5,6},{6,7},{8,9},{9,10},{10,11},{11... | collective-permute-start | bytes 4616 | tf_op jit(solution)/shard_map/ppermute | solution.py:36
  165.1 29.2 %all-to-all-start.2 = ((f32[64,1,192]{2,1,0:T(1,128)}), f32[64,1,192]{2,1,0:T(1,128)S(1)}, u32[]{:S(2)}, u32[]{:S(2)}) async-start(f32[64,1,192]{2,1,0:T(1,128)} %reshape.59), calls=%async_computation.2 | async-start | bytes 131072 | tf_op jit(solution)/shard_map/all_to_all | solution.py:72
  181.1 22.0 %collective-permute-start.24 = (f32[3,1,256]{2,1,0:T(1,128)S(1)}, f32[3,1,256]{2,1,0:T(1,128)S(1)}, u32[]{:S(2)}, u32[]{:S(2)}) collective-permute-start(f32[3,1,256]{2,1,0:T(1,128)S(1)} %get-tuple-element.65), channel_id=1, source_target_pairs={{8,0},{16,8},{24,16},{32,24},{40,32},{48,40},{56,48},{64,56},{72,6... | collective-permute-start | bytes 9224 | tf_op jit(solution)/shard_map/ppermute | solution.py:37
  182.4 20.8 %collective-permute-start.25 = (f32[3,1,256]{2,1,0:T(1,128)S(1)}, f32[3,1,256]{2,1,0:T(1,128)S(1)}, u32[]{:S(2)}, u32[]{:S(2)}) collective-permute-start(f32[3,1,256]{2,1,0:T(1,128)S(1)} %get-tuple-element.64), channel_id=1, source_target_pairs={{0,8},{8,16},{16,24},{24,32},{32,40},{40,48},{48,56},{56,64},{64,7... | collective-permute-start | bytes 9224 | tf_op jit(solution)/shard_map/ppermute | solution.py:36
  190.3 12.8 %collective-permute-start.26 = (f32[3,128,1]{2,1,0:T(8,128)S(1)}, f32[3,128,1]{2,1,0:T(8,128)S(1)}, u32[]{:S(2)}, u32[]{:S(2)}) collective-permute-start(f32[3,128,1]{2,1,0:T(8,128)S(1)} %get-tuple-element.62), channel_id=1, source_target_pairs={{1,0},{2,1},{3,2},{4,3},{5,4},{6,5},{7,6},{9,8},{10,9},{11,10},{12... | collective-permute-start | bytes 4616 | tf_op jit(solution)/shard_map/ppermute | solution.py:37
  203.5 0.9 copy-start.1
  204.7 19.3 %collective-permute-start.28 = (f32[3,1,256]{2,1,0:T(1,128)S(1)}, f32[3,1,256]{2,1,0:T(1,128)S(1)}, u32[]{:S(2)}, u32[]{:S(2)}) collective-permute-start(f32[3,1,256]{2,1,0:T(1,128)S(1)} %get-tuple-element.61), channel_id=1, source_target_pairs={{8,0},{16,8},{24,16},{32,24},{40,32},{48,40},{56,48},{64,56},{72,6... | collective-permute-start | bytes 9224 | tf_op jit(solution)/shard_map/ppermute | solution.py:37
  206.0 18.0 %collective-permute-start.29 = (f32[3,1,256]{2,1,0:T(1,128)S(1)}, f32[3,1,256]{2,1,0:T(1,128)S(1)}, u32[]{:S(2)}, u32[]{:S(2)}) collective-permute-start(f32[3,1,256]{2,1,0:T(1,128)S(1)} %get-tuple-element.60), channel_id=1, source_target_pairs={{0,8},{8,16},{16,24},{24,32},{32,40},{40,48},{48,56},{56,64},{64,7... | collective-permute-start | bytes 9224 | tf_op jit(solution)/shard_map/ppermute | solution.py:36
  214.0 5.6 %collective-permute-start.31 = (f32[3,128,1]{2,1,0:T(8,128)S(1)}, f32[3,128,1]{2,1,0:T(8,128)S(1)}, u32[]{:S(2)}, u32[]{:S(2)}) collective-permute-start(f32[3,128,1]{2,1,0:T(8,128)S(1)} %get-tuple-element.59), channel_id=1, source_target_pairs={{0,1},{1,2},{2,3},{3,4},{4,5},{5,6},{6,7},{8,9},{9,10},{10,11},{11... | collective-permute-start | bytes 4616 | tf_op jit(solution)/shard_map/ppermute | solution.py:36
  217.0 7.0 %collective-permute-start.30 = (f32[3,128,1]{2,1,0:T(8,128)S(1)}, f32[3,128,1]{2,1,0:T(8,128)S(1)}, u32[]{:S(2)}, u32[]{:S(2)}) collective-permute-start(f32[3,128,1]{2,1,0:T(8,128)S(1)} %get-tuple-element.58), channel_id=1, source_target_pairs={{1,0},{2,1},{3,2},{4,3},{5,4},{6,5},{7,6},{9,8},{10,9},{11,10},{12... | collective-permute-start | bytes 4616 | tf_op jit(solution)/shard_map/ppermute | solution.py:37
  (18 other events, 11.2 us)

commit v2 on v1

--- a/solution.py
+++ b/solution.py
@@ -136,21 +136,23 @@
     return jnp.where(colour_mask[None], blended, spins)
 
 
-def sweep_kernel(colour, sweep, k_ref, s_ref, lo_ref, hi_ref, xlo_ref, xhi_ref, ylo_ref, yhi_ref,
-                 film_ref, trial_ref, unif_ref,
-                 out_ref, olo_ref, ohi_ref, oxlo_ref, oxhi_ref, oylo_ref, oyhi_ref):
+def sweep_kernel(step_ref, k_ref, s_ref, lo_ref, hi_ref, film_ref, valid_ref, trial_ref, unif_ref,
+                 out_ref, olo_ref, ohi_ref):
     layers, rows_x, rows_y = s_ref.shape[1:]
     row = lax.broadcasted_iota(jnp.int32, (rows_x, rows_y), 0)
     col = lax.broadcasted_iota(jnp.int32, (rows_x, rows_y), 1)
+    live = valid_ref[...] > 0.5
+    sweep = step_ref[0]
+    colour = step_ref[1]
     kk = [[[k_ref[d * 9 + a * 3 + b] for b in range(3)] for a in range(3)] for d in range(3)]
     for l in range(layers):
         s = [s_ref[c, l] for c in range(3)]
         below = [lo_ref[c, 0] if l == 0 else s_ref[c, l - 1] for c in range(3)]
         above = [hi_ref[c, 0] if l == layers - 1 else s_ref[c, l + 1] for c in range(3)]
-        xp = [jnp.where(row == rows_x - 1, xhi_ref[c, l], pltpu.roll(s[c], rows_x - 1, 0)) for c in range(3)]
-        xm = [jnp.where(row == 0, xlo_ref[c, l], pltpu.roll(s[c], 1, 0)) for c in range(3)]
-        yp = [jnp.where(col == rows_y - 1, yhi_ref[c, l], pltpu.roll(s[c], rows_y - 1, 1)) for c in range(3)]
-        ym = [jnp.where(col == 0, ylo_ref[c, l], pltpu.roll(s[c], 1, 1)) for c in range(3)]
+        xp = [pltpu.roll(s[c], rows_x - 1, 0) for c in range(3)]
+        xm = [pltpu.roll(s[c], 1, 0) for c in range(3)]
+        yp = [pltpu.roll(s[c], rows_y - 1, 1) for c in range(3)]
+        ym = [pltpu.roll(s[c], 1, 1) for c in range(3)]
         fwd = (above, xp, yp)
         bwd = (below, xm, ym)
         field = []
@@ -170,7 +172,7 @@
         weight = 1.0 / (1.0 + jnp.exp(-((accept - unif_ref[sweep, l]) / softness)))
         mix = [(1.0 - weight) * s[c] + weight * prop[c] for c in range(3)]
         mnorm = jnp.sqrt(mix[0] * mix[0] + mix[1] * mix[1] + mix[2] * mix[2])
-        chosen = ((row + col + l) % 2) == colour
+        chosen = (((row + col + l) % 2) == colour) & live
         for c in range(3):
             new = jnp.where(chosen, mix[c] / mnorm, s[c])
             out_ref[c, l] = new
@@ -178,45 +180,55 @@
                 olo_ref[c, 0] = new
             if l == layers - 1:
                 ohi_ref[c, 0] = new
-            oxlo_ref[c, l] = new[0:1, :]
-            oxhi_ref[c, l] = new[rows_x - 1:rows_x, :]
-            oylo_ref[c, l] = new[:, 0:1]
-            oyhi_ref[c, l] = new[:, rows_y - 1:rows_y]
-
-
-def half_sweep(spins, halos, exch_flat, film_cells, trials, uniforms, sweep, colour):
+
+
+def half_sweep(spins, lo, hi, exch_flat, film_e, valid, trials, uniforms, sweep, colour):
     comps, layers, rows_x, rows_y = spins.shape
     vmem = pl.BlockSpec(memory_space=pltpu.VMEM)
     smem = pl.BlockSpec(memory_space=pltpu.SMEM)
     dt = spins.dtype
-    out_shape = (
-        jax.ShapeDtypeStruct(spins.shape, dt),
-        jax.ShapeDtypeStruct((comps, 1, rows_x, rows_y), dt),
-        jax.ShapeDtypeStruct((comps, 1, rows_x, rows_y), dt),
-        jax.ShapeDtypeStruct((comps, layers, 1, rows_y), dt),
-        jax.ShapeDtypeStruct((comps, layers, 1, rows_y), dt),
-        jax.ShapeDtypeStruct((comps, layers, rows_x, 1), dt),
-        jax.ShapeDtypeStruct((comps, layers, rows_x, 1), dt),
-    )
+    face = jax.ShapeDtypeStruct((comps, 1, rows_x, rows_y), dt)
+    out_shape = (jax.ShapeDtypeStruct(spins.shape, dt), face, face)
     sites = layers * rows_x * rows_y
     return pl.pallas_call(
-        functools.partial(sweep_kernel, colour, sweep),
+        sweep_kernel,
         out_shape=out_shape,
-        in_specs=[smem] + [vmem] * 10,
-        out_specs=tuple([vmem] * 7),
+        in_specs=[smem, smem] + [vmem] * 7,
+        out_specs=tuple([vmem] * 3),
         cost_estimate=pl.CostEstimate(flops=200 * sites, transcendentals=4 * sites, bytes_accessed=4 * 14 * sites),
-    )(exch_flat, spins, *halos, film_cells, trials, uniforms)
-
-
-def spin_halos(faces):
-    lo, hi, xlo, xhi, ylo, yhi = faces
-    out = []
-    for axis, low_src, high_src in (("region", hi, lo), (GX, xhi, xlo), (GY, yhi, ylo)):
-        count = lax.axis_size(axis)
-        up = [(i, i + 1) for i in range(count - 1)]
-        out.append(lax.ppermute(low_src, axis, up))
-        out.append(lax.ppermute(high_src, axis, [(b, a) for a, b in up]))
-    return out
+    )(jnp.array([sweep, colour], jnp.int32), exch_flat, spins, lo, hi, film_e, valid, trials, uniforms)
+
+
+def shift_in(array, axis, from_lower):
+    count = lax.axis_size(axis)
+    up = [(i, i + 1) for i in range(count - 1)]
+    return lax.ppermute(array, axis, up if from_lower else [(b, a) for a, b in up])
+
+
+def extended(array, width, wide):
+    rows, cols = array.shape[-2:]
+    below = shift_in(array[..., rows - width :, :], GX, True)
+    above = shift_in(array[..., :width, :], GX, False)
+    array = jnp.concatenate([array, above, below], axis=-2)
+    left = shift_in(jnp.swapaxes(array[..., cols - width :], -1, -2), GY, True)
+    right = shift_in(jnp.swapaxes(array[..., :width], -1, -2), GY, False)
+    gap = jnp.zeros(array.shape[:-1] + (wide - cols - 2 * width,), array.dtype)
+    return jnp.concatenate(
+        [array, jnp.swapaxes(right, -1, -2), gap, jnp.swapaxes(left, -1, -2)], axis=-1
+    )
+
+
+def cells_for_sites(patch, rows_x, rows_y, width, wide):
+    inner = jnp.repeat(patch[:, 1:-1], K, axis=1)
+    rows = jnp.concatenate(
+        [inner, jnp.repeat(patch[:, -1:], width, axis=1), jnp.repeat(patch[:, :1], width, axis=1)], axis=1
+    )
+    inner = jnp.repeat(rows[:, :, 1:-1], K, axis=2)
+    gap = jnp.zeros(rows.shape[:2] + (wide - rows_y - 2 * width,), rows.dtype)
+    return jnp.concatenate(
+        [inner, jnp.repeat(rows[:, :, -1:], width, axis=2), gap, jnp.repeat(rows[:, :, :1], width, axis=2)],
+        axis=2,
+    )
 
 
 def cross_product(left, right):
@@ -264,30 +276,50 @@
     film_block = film_m[:, : piece_x * gx_count, : piece_y * gy_count]
     stack_spins, unif_all, trial_all = (spins, uniforms, trials)
     assert layers_dev % 2 == 0 and rows_x % 2 == 0 and rows_y % 2 == 0
-    pieces = (
-        film_block.reshape(3, gx_count, piece_x, gy_count, piece_y)
-        .transpose(1, 3, 0, 2, 4)
-        .reshape(tile_count, 3, piece_x, piece_y)
-    )
+    width = 2 * SWEEPS
+    ext_x = rows_x + 2 * width
+    wide = -(-(rows_y + 2 * width) // 128) * 128
+    assert ext_x % 2 == 0 and wide % 2 == 0 and width <= K and width <= rows_x and width <= rows_y
+    ring = jnp.pad(film_block, ((0, 0), (1, 1 + piece_x), (1, 1 + piece_y)))
+    by_rows = jnp.stack(
+        [ring[:, k : k + piece_x * gx_count].reshape(3, gx_count, piece_x, -1)[:, :, 0] for k in range(piece_x + 2)]
+    )
+    by_cols = jnp.stack(
+        [by_rows[..., q : q + piece_y * gy_count].reshape(*by_rows.shape[:3], gy_count, piece_y)[..., 0] for q in range(piece_y + 2)]
+    )
+    pieces = by_cols.transpose(3, 4, 2, 1, 0).reshape(tile_count, 3, piece_x + 2, piece_y + 2)
     pieces = jnp.where(first_tile, pieces, 0.0)
     placed = summed_rows(pieces, (("gx_0", "gx_1", "gy_0"), "gy_1"), 0)[0]
-    own_cells = picked(placed, "region", 0)
-    film_cells = jnp.repeat(jnp.repeat(own_cells, K, axis=1), K, axis=2)
+    own_patch = picked(placed, "region", 0)
+    film_e = cells_for_sites(own_patch, rows_x, rows_y, width, wide)
     exch_flat = exch_kernel.reshape(-1)
-    faces = (
-        stack_spins[:, :1],
-        stack_spins[:, -1:],
-        stack_spins[:, :, :1],
-        stack_spins[:, :, -1:],
-        stack_spins[:, :, :, :1],
-        stack_spins[:, :, :, -1:],
-    )
+    channels = jnp.concatenate(
+        [stack_spins, trial_all.reshape(-1, layers_dev, rows_x, rows_y), unif_all], axis=0
+    )
+    channels = extended(channels, width, wide)
+    spins_e = channels[:3]
+    trials_e = channels[3 : 3 + 3 * SWEEPS].reshape(SWEEPS, 3, layers_dev, ext_x, wide)
+    unif_e = channels[3 + 3 * SWEEPS :]
+    local_x = jnp.arange(ext_x, dtype=jnp.int32)
+    local_x = jnp.where(local_x < rows_x + width, local_x, local_x - ext_x)
+    local_y = jnp.arange(wide, dtype=jnp.int32)
+    real_y = (local_y < rows_y + width) | (local_y >= wide - width)
+    local_y = jnp.where(local_y < rows_y + width, local_y, local_y - wide)
+    global_x = gx_pos * rows_x + local_x
+    global_y = gy_pos * rows_y + local_y
+    valid_x = (global_x >= 0) & (global_x < rows_x * gx_count)
+    valid_y = real_y & (global_y >= 0) & (global_y < rows_y * gy_count)
+    valid = (valid_x[:, None] & valid_y[None, :]).astype(jnp.float32)
+    lo = spins_e[:, :1]
+    hi = spins_e[:, -1:]
     for sweep_index in range(SWEEPS):
         for colour in (0, 1):
-            halos = spin_halos(faces)
-            stack_spins, *faces = half_sweep(
-                stack_spins, halos, exch_flat, film_cells, trial_all, unif_all, sweep_index, colour
+            below = shift_in(hi, "region", True)
+            above = shift_in(lo, "region", False)
+            spins_e, lo, hi = half_sweep(
+                spins_e, below, above, exch_flat, film_e, valid, trials_e, unif_e, sweep_index, colour
             )
+    stack_spins = spins_e[:, :, :rows_x, :rows_y]
     averages = stack_spins[:, 0].reshape(3, piece_x, K, piece_y, K).mean(axis=(2, 4))
     gathered = whole_of(averages[None], (("gx_0", "gx_1", "gy_0"), "gy_1"), 0)
     assembled = (

time: 227 us -> 239 us (1.053)
  local copies, waits for them, and re-layouts: 13.7 us -> 63.2 us
  starting transfers between devices: 140 us -> 99.5 us
  waiting for transfers between devices: 33 us -> 22.4 us
  other arithmetic: 6.71 us -> 12.7 us
  blocking collectives: 21.5 us -> 26.6 us
    ppermute x24 -> x12, starting transfers between devices: 79.7 us -> 32.1 us  [shift_in(): lax.ppermute(array, axis, up if from_lower else [(b, a) for a, b in up])]
    unnamed x74 -> x106, local copies, waits for them, and re-layouts: 7.17 us -> 29.8 us
    reshape x4 -> x31, local copies, waits for them, and re-layouts: 0.82 us -> 16.1 us  [the longest x18 15.5 us: body(): by_rows[..., q:q + piece_y * gy_count]]
    slice x3 -> x21, local copies, waits for them, and re-layouts: 0.96 us -> 9.86 us  [the longest x3 4.25 us: body(): by_rows[..., q:q + piece_y * gy_count]]
    all_to_all x1, waiting for transfers between devices: 8.82 us -> 0.01 us  [summed_rows(): return jnp.sum(lax.all_to_all(own, far, 0, 0, tiled=True), axis=0)]
    all_to_all x1, blocking collectives: 4.68 us -> 10.3 us  [summed_on_arrival(): lax.all_to_all(parts, axis, split_axis=0, concat_axis=0, tiled=True)]
    ppermute x4, starting transfers between devices: 20.7 us -> 26.3 us  [with_halo(): lax.ppermute(last, axis, up)]
    ppermute x4, waiting for transfers between devices: 4.4 us -> 0.01 us  [with_halo(): lax.ppermute(leading, axis, [(b, a) for a, b in up])]
  transfers between devices with their start and end apart: 34 -> 22, of which waited for: 10 -> 9; matrix products, arithmetic and copies ran while one was open for 6% -> 7% of each run, Pallas kernels for 1% -> 1%
where the time goes in v2:
time: 239 us; the launch traced here: 237 us
  starting transfers between devices  99.5 us (42%)
  local copies, waits for them, and re-layouts  63.2 us (26%)
  blocking collectives  26.6 us (11%)
  waiting for transfers between devices  22.4 us (9%)
  other arithmetic  12.7 us (5%)
  Pallas kernels  10.9 us (5%)
    ppermute x12, starting transfers between devices, shift_in(): lax.ppermute(array, axis, up if from_lower else [(b, a) for a, b in up])  32.1 us
    unnamed x106, local copies, waits for them, and re-layouts  29.8 us
    ppermute x4, starting transfers between devices, with_halo(): lax.ppermute(last, axis, up)  26.3 us
    all_to_all x1, starting transfers between devices, copy_for_each(): lax.all_to_all(jnp.broadcast_to(array[None], (count, *array.shape)), axis...  18.6 us
    ppermute x12, waiting for transfers between devices, shift_in(): lax.ppermute(array, axis, up if from_lower else [(b, a) for a, b in up])  17.3 us
    reshape x18, local copies, waits for them, and re-layouts, body(): by_rows[..., q:q + piece_y * gy_count]  15.5 us
    all_to_all x1, starting transfers between devices, summed_rows(): return jnp.sum(lax.all_to_all(own, far, 0, 0, tiled=True), axis=0)  13.4 us
    pallas_call x4, Pallas kernels, half_sweep(): pl.pallas_call(sweep_kernel, out_shape=out_shape, in_specs=[smem, smem] +...  10.9 us
  transfers between devices with their start and end apart: 22, of which 9 were waited for; matrix products, arithmetic and copies ran while one was open for 7% of the time, Pallas kernels for 1%

profile of v2, /device:TPU:1, one launch (start us, length us, event | category | flops | bytes accessed | tf_op | source)
XLA Modules:
  0.0 237.2 jit_solution(6565397806437746114)
XLA Ops:
  2.6 1.8 fusion.53
  7.0 1.6 copy.137
  9.8 1.5 copy.138
  12.6 1.5 copy.139
  15.4 1.5 copy.140
  18.2 1.5 copy.141
  21.0 1.6 copy.142
  23.8 1.5 copy.143
  26.6 1.5 copy.144
  29.4 1.5 copy.145
  32.2 1.6 copy.146
  34.1 1.5 copy.147
  40.1 1.5 copy.151
  42.0 1.5 copy.152
  43.9 1.5 copy.118
  48.8 1.5 reduce.6
  50.5 10.3 %all_to_all.20 = f32[2,1,20736]{2,1,0:T(1,128)S(1)} all-to-all(f32[2,1,20736]{2,1,0:T(1,128)S(1)} %reshape.205), channel_id=1, replica_groups=mesh['region'=4,'gx_0'=8,'gx_1'=2,'gy_0'=4,'gy_1'=2] {'gy_1'}, dimensions={0} | all-to-all | bytes 331776 | tf_op jit(solution)/shard_map/all_to_all | solution.py:56
  64.0 2.2 reduce.8
  67.3 13.4 %all-to-all-start.1 = ((f32[64,1,324]{2,1,0:T(1,128)}), f32[64,1,324]{2,1,0:T(1,128)S(1)}, u32[]{:S(2)}, u32[]{:S(2)}) async-start(f32[64,1,324]{2,1,0:T(1,128)} %reshape.207), calls=%async_computation.1 | async-start | bytes 196608 | tf_op jit(solution)/shard_map/all_to_all | solution.py:63
  80.7 1.3 collective-permute-start
  82.0 8.1 %collective-permute-start.1 = (f32[11,2,4,128]{3,2,1,0:T(4,128)S(1)}, f32[11,2,4,128]{3,2,1,0:T(4,128)S(1)}, u32[]{:S(2)}, u32[]{:S(2)}) collective-permute-start(f32[11,2,4,128]{3,2,1,0:T(4,128)S(1)} %get-tuple-element.49), channel_id=1, source_target_pairs={{0,8},{8,16},{16,24},{24,32},{32,40},{40,48},{48,56},{56,64},{64,7... | collective-permute-start | bytes 135176 | tf_op jit(solution)/shard_map/ppermute | solution.py:205
  90.2 2.3 collective-permute-done.1
  92.7 2.6 %collective-permute-start.2 = (f32[11,2,4,40]{2,3,1,0:T(8,128)S(1)}, f32[11,2,4,40]{2,3,1,0:T(8,128)S(1)}, u32[]{:S(2)}, u32[]{:S(2)}) collective-permute-start(f32[11,2,4,40]{2,3,1,0:T(8,128)S(1)} %get-tuple-element.38), channel_id=1, source_target_pairs={{1,0},{2,1},{3,2},{4,3},{5,4},{6,5},{7,6},{9,8},{10,9},{11,10},{12... | collective-permute-start | bytes 42248 | tf_op jit(solution)/shard_map/ppermute | solution.py:205
  95.3 2.9 %collective-permute-start.3 = (f32[11,2,4,40]{2,3,1,0:T(8,128)S(1)}, f32[11,2,4,40]{2,3,1,0:T(8,128)S(1)}, u32[]{:S(2)}, u32[]{:S(2)}) collective-permute-start(f32[11,2,4,40]{2,3,1,0:T(8,128)S(1)} %get-tuple-element.39), channel_id=1, source_target_pairs={{0,1},{1,2},{2,3},{3,4},{4,5},{5,6},{6,7},{8,9},{9,10},{10,11},{11... | collective-permute-start | bytes 42248 | tf_op jit(solution)/shard_map/ppermute | solution.py:205
  99.7 2.7 %collective-permute-done.2 = f32[11,2,4,40]{2,3,1,0:T(8,128)S(1)} collective-permute-done((f32[11,2,4,40]{2,3,1,0:T(8,128)S(1)}, f32[11,2,4,40]{2,3,1,0:T(8,128)S(1)}, u32[]{:S(2)}, u32[]{:S(2)}) %collective-permute-start.2) | collective-permute-done | bytes 14112 | tf_op jit(solution)/shard_map/ppermute | solution.py:205
  106.1 3.8 %collective-permute-start.4 = (f32[3,1,40,256]{3,2,1,0:T(8,128)S(1)}, f32[3,1,40,256]{3,2,1,0:T(8,128)S(1)}, u32[]{:S(2)}, u32[]{:S(2)}) collective-permute-start(f32[3,1,40,256]{3,2,1,0:T(8,128)S(1)} %get-tuple-element.37), channel_id=1, source_target_pairs={{0,128},{128,256},{256,384},{1,129},{129,257},{257,385},{2,130},{1... | collective-permute-start | bytes 368648 | tf_op jit(solution)/shard_map/ppermute | solution.py:205
  113.2 10.9 %all-gather = f32[12,6,18]{2,1,0:T(8,128)S(1)} all-gather(f32[3,6,18]{2,1,0:T(8,128)S(1)} %bitcast_reduce_fusion), channel_id=2, replica_groups=mesh['region'=4,'gx_0'=8,'gx_1'=2,'gy_0'=4,'gy_1'=2] {'region'}, dimensions={0}, use_global_device_ids=true | all-gather | bytes 6480 | tf_op jit(solution)/shard_map/all_gather | solution.py:67
  126.2 2.7 %shard_map.113 = (f32[3,2,40,256]{3,2,1,0:T(8,128)}, f32[3,1,40,256]{3,2,1,0:T(8,128)}, f32[3,1,40,256]{3,2,1,0:T(8,128)}) custom-call(s32[2]{0:T(128)} %call_exported.0.step_ref, f32[27]{0:T(128)} %reshape.166.k_ref, f32[3,2,40,256]{3,2,1,0:T(8,128)} %slice.426.s_ref, f32[3,1,40,256]{3,2,1,0:T(8,128)} %copy-done.19, f32[3,1,40,256]{3,2,1,0:T(8,128)} %copy-done.20, ...), custom_call_target="tpu_custom_call" | custom-call | flops 4096000 | bytes 1146880 | tf_op jit(solution)/shard_map/pallas_call | solution.py:193
  128.9 2.6 %collective-permute-start.6 = (f32[3,1,40,256]{3,2,1,0:T(8,128)}, f32[3,1,40,256]{3,2,1,0:T(8,128)S(1)}, u32[]{:S(2)}, u32[]{:S(2)}) collective-permute-start(f32[3,1,40,256]{3,2,1,0:T(8,128)} %get-tuple-element.13), channel_id=1, source_target_pairs={{0,128},{128,256},{256,384},{1,129},{129,257},{257,385},{2,130},{1... | collective-permute-start | bytes 368648 | tf_op jit(solution)/shard_map/ppermute | solution.py:205
  132.8 1.5 collective-permute-done.6.lo_ref
  134.3 4.0 %collective-permute-done.7.hi_ref = f32[3,1,40,256]{3,2,1,0:T(8,128)S(1)} collective-permute-done((f32[3,1,40,256]{3,2,1,0:T(8,128)}, f32[3,1,40,256]{3,2,1,0:T(8,128)S(1)}, u32[]{:S(2)}, u32[]{:S(2)}) %collective-permute-start.7) | collective-permute-done | bytes 122912 | tf_op jit(solution)/shard_map/ppermute | solution.py:205
  139.0 2.7 %shard_map.114 = (f32[3,2,40,256]{3,2,1,0:T(8,128)}, f32[3,1,40,256]{3,2,1,0:T(8,128)}, f32[3,1,40,256]{3,2,1,0:T(8,128)}) custom-call(s32[2]{0:T(128)} %call_exported.1.step_ref, f32[27]{0:T(128)} %reshape.166.k_ref, f32[3,2,40,256]{3,2,1,0:T(8,128)} %get-tuple-element.12.s_ref, f32[3,1,40,256]{3,2,1,0:T(8,128)} %copy-done.23, ...), custom_call_target="tpu_custom_call" | custom-call | flops 4096000 | bytes 1146880 | tf_op jit(solution)/shard_map/pallas_call | solution.py:193
  141.7 2.5 %collective-permute-start.8 = (f32[3,1,40,256]{3,2,1,0:T(8,128)}, f32[3,1,40,256]{3,2,1,0:T(8,128)S(1)}, u32[]{:S(2)}, u32[]{:S(2)}) collective-permute-start(f32[3,1,40,256]{3,2,1,0:T(8,128)} %get-tuple-element.16), channel_id=1, source_target_pairs={{0,128},{128,256},{256,384},{1,129},{129,257},{257,385},{2,130},{1... | collective-permute-start | bytes 368648 | tf_op jit(solution)/shard_map/ppermute | solution.py:205
  145.6 1.6 collective-permute-done.8.lo_ref
  147.2 4.0 %collective-permute-done.9.hi_ref = f32[3,1,40,256]{3,2,1,0:T(8,128)S(1)} collective-permute-done((f32[3,1,40,256]{3,2,1,0:T(8,128)}, f32[3,1,40,256]{3,2,1,0:T(8,128)S(1)}, u32[]{:S(2)}, u32[]{:S(2)}) %collective-permute-start.9) | collective-permute-done | bytes 122912 | tf_op jit(solution)/shard_map/ppermute | solution.py:205
  151.8 2.7 %shard_map.115 = (f32[3,2,40,256]{3,2,1,0:T(8,128)}, f32[3,1,40,256]{3,2,1,0:T(8,128)}, f32[3,1,40,256]{3,2,1,0:T(8,128)}) custom-call(s32[2]{0:T(128)} %constant.82.clone.step_ref, f32[27]{0:T(128)} %reshape.166.k_ref, f32[3,2,40,256]{3,2,1,0:T(8,128)} %get-tuple-element.15.s_ref, f32[3,1,40,256]{3,2,1,0:T(8,128)} %copy-done.24, ...), custom_call_target="tpu_custom_call" | custom-call | flops 4096000 | bytes 1146880 | tf_op jit(solution)/shard_map/pallas_call | solution.py:193
  154.6 3.1 %collective-permute-start.10 = (f32[3,1,40,256]{3,2,1,0:T(8,128)}, f32[3,1,40,256]{3,2,1,0:T(8,128)S(1)}, u32[]{:S(2)}, u32[]{:S(2)}) collective-permute-start(f32[3,1,40,256]{3,2,1,0:T(8,128)} %get-tuple-element.19), channel_id=1, source_target_pairs={{0,128},{128,256},{256,384},{1,129},{129,257},{257,385},{2,130},{1... | collective-permute-start | bytes 368648 | tf_op jit(solution)/shard_map/ppermute | solution.py:205
  159.1 3.7 %collective-permute-start.14 = (f32[3,128,1]{2,1,0:T(8,128)S(1)}, f32[3,128,1]{2,1,0:T(8,128)S(1)}, u32[]{:S(2)}, u32[]{:S(2)}) collective-permute-start(f32[3,128,1]{2,1,0:T(8,128)S(1)} %get-tuple-element.44), channel_id=1, source_target_pairs={{1,0},{2,1},{3,2},{4,3},{5,4},{6,5},{7,6},{9,8},{10,9},{11,10},{12... | collective-permute-start | bytes 4616 | tf_op jit(solution)/shard_map/ppermute | solution.py:37
  162.7 7.7 %collective-permute-start.15 = (f32[3,128,1]{2,1,0:T(8,128)S(1)}, f32[3,128,1]{2,1,0:T(8,128)S(1)}, u32[]{:S(2)}, u32[]{:S(2)}) collective-permute-start(f32[3,128,1]{2,1,0:T(8,128)S(1)} %get-tuple-element.45), channel_id=1, source_target_pairs={{0,1},{1,2},{2,3},{3,4},{4,5},{5,6},{6,7},{8,9},{9,10},{10,11},{11... | collective-permute-start | bytes 4616 | tf_op jit(solution)/shard_map/ppermute | solution.py:36
  171.2 2.7 %shard_map.116 = (f32[3,2,40,256]{3,2,1,0:T(8,128)}, f32[3,1,40,256]{3,2,1,0:T(8,128)}, f32[3,1,40,256]{3,2,1,0:T(8,128)}) custom-call(s32[2]{0:T(128)} %call_exported.2.step_ref, f32[27]{0:T(128)} %reshape.166.k_ref, f32[3,2,40,256]{3,2,1,0:T(8,128)} %get-tuple-element.18.s_ref, f32[3,1,40,256]{3,2,1,0:T(8,128)} %copy-done.21, ...), custom_call_target="tpu_custom_call" | custom-call | flops 4096000 | bytes 1146880 | tf_op jit(solution)/shard_map/pallas_call | solution.py:193
  176.3 18.6 %all-to-all-start.2 = ((f32[64,1,192]{2,1,0:T(1,128)}), f32[64,1,192]{2,1,0:T(1,128)S(1)}, u32[]{:S(2)}, u32[]{:S(2)}) async-start(f32[64,1,192]{2,1,0:T(1,128)} %reshape.209), calls=%async_computation.2 | async-start | bytes 131072 | tf_op jit(solution)/shard_map/all_to_all | solution.py:72
  196.3 7.9 %collective-permute-start.13 = (f32[3,1,256]{2,1,0:T(1,128)S(1)}, f32[3,1,256]{2,1,0:T(1,128)S(1)}, u32[]{:S(2)}, u32[]{:S(2)}) collective-permute-start(f32[3,1,256]{2,1,0:T(1,128)S(1)} %get-tuple-element.46), channel_id=1, source_target_pairs={{0,8},{8,16},{16,24},{24,32},{32,40},{40,48},{48,56},{56,64},{64,7... | collective-permute-start | bytes 9224 | tf_op jit(solution)/shard_map/ppermute | solution.py:36
  204.2 4.1 %all-to-all-done.2 = f32[64,1,192]{2,1,0:T(1,128)S(1)} async-done(((f32[64,1,192]{2,1,0:T(1,128)}), f32[64,1,192]{2,1,0:T(1,128)S(1)}, u32[]{:S(2)}, u32[]{:S(2)}) %all-to-all-start.2) | async-done | bytes 49184 | tf_op jit(solution)/shard_map/all_to_all | solution.py:72
  209.7 5.5 %all_to_all.21 = f32[2,1,12288]{2,1,0:T(1,128)S(1)} all-to-all(f32[2,1,12288]{2,1,0:T(1,128)S(1)} %reshape.211), channel_id=1, replica_groups=mesh['region'=4,'gx_0'=8,'gx_1'=2,'gy_0'=4,'gy_1'=2] {'gy_1'}, dimensions={0} | all-to-all | bytes 196608 | tf_op jit(solution)/shard_map/all_to_all | solution.py:72
  219.4 7.9 %collective-permute-start.17 = (f32[3,1,256]{2,1,0:T(1,128)S(1)}, f32[3,1,256]{2,1,0:T(1,128)S(1)}, u32[]{:S(2)}, u32[]{:S(2)}) collective-permute-start(f32[3,1,256]{2,1,0:T(1,128)S(1)} %get-tuple-element.42), channel_id=1, source_target_pairs={{0,8},{8,16},{16,24},{24,32},{32,40},{40,48},{48,56},{56,64},{64,7... | collective-permute-start | bytes 9224 | tf_op jit(solution)/shard_map/ppermute | solution.py:36
  227.4 2.8 %collective-permute-start.18 = (f32[3,128,1]{2,1,0:T(8,128)S(1)}, f32[3,128,1]{2,1,0:T(8,128)S(1)}, u32[]{:S(2)}, u32[]{:S(2)}) collective-permute-start(f32[3,128,1]{2,1,0:T(8,128)S(1)} %get-tuple-element.40), channel_id=1, source_target_pairs={{1,0},{2,1},{3,2},{4,3},{5,4},{6,5},{7,6},{9,8},{10,9},{11,10},{12... | collective-permute-start | bytes 4616 | tf_op jit(solution)/shard_map/ppermute | solution.py:37
  230.3 2.7 %collective-permute-start.19 = (f32[3,128,1]{2,1,0:T(8,128)S(1)}, f32[3,128,1]{2,1,0:T(8,128)S(1)}, u32[]{:S(2)}, u32[]{:S(2)}) collective-permute-start(f32[3,128,1]{2,1,0:T(8,128)S(1)} %get-tuple-element.41), channel_id=1, source_target_pairs={{0,1},{1,2},{2,3},{3,4},{4,5},{5,6},{6,7},{8,9},{9,10},{10,11},{11... | collective-permute-start | bytes 4616 | tf_op jit(solution)/shard_map/ppermute | solution.py:36
  233.0 1.5 slice.390
  (218 shorter events, 57.2 us)
Async XLA Ops:
  43.5 2.0 copy-start.5
  43.5 2.0 copy-start.6
  43.5 2.0 copy-start.7
  43.5 2.1 copy-start.8
  43.5 2.1 copy-start.9
  43.9 1.7 copy-start.10
  43.9 1.8 copy-start.11
  43.9 1.8 copy-start.12
  43.9 1.8 copy-start.13
  43.9 1.8 copy-start.14
  43.9 1.8 copy-start.15
  45.5 0.9 copy-start.16
  45.5 0.9 copy-start.17
  45.5 1.0 copy-start.18
  64.0 16.7 %copy-start.2 = (f32[2,3,2,32,128]{4,3,2,1,0:T(8,128)S(1)}, f32[2,3,2,32,128]{4,3,2,1,0:T(8,128)}, u32[]{:S(2)}) copy-start(f32[2,3,2,32,128]{4,3,2,1,0:T(8,128)} %param.12) | copy-start | bytes 589828
  64.0 16.7 %copy-start.3 = (f32[3,2,32,128]{3,2,1,0:T(8,128)S(1)}, f32[3,2,32,128]{3,2,1,0:T(8,128)}, u32[]{:S(2)}) copy-start(f32[3,2,32,128]{3,2,1,0:T(8,128)} %param.10) | copy-start | bytes 294916
  64.0 16.7 %copy-start.4 = (f32[2,2,32,128]{3,2,1,0:T(8,128)S(1)}, f32[2,2,32,128]{3,2,1,0:T(8,128)}, u32[]{:S(2)}) copy-start(f32[2,2,32,128]{3,2,1,0:T(8,128)} %param.11) | copy-start | bytes 196612
  67.3 43.8 %all-to-all-start.1 = ((f32[64,1,324]{2,1,0:T(1,128)}), f32[64,1,324]{2,1,0:T(1,128)S(1)}, u32[]{:S(2)}, u32[]{:S(2)}) async-start(f32[64,1,324]{2,1,0:T(1,128)} %reshape.207), calls=%async_computation.1 | async-start | bytes 196608 | tf_op jit(solution)/shard_map/all_to_all | solution.py:63
  80.7 9.5 %collective-permute-start = (f32[11,2,4,128]{3,2,1,0:T(4,128)S(1)}, f32[11,2,4,128]{3,2,1,0:T(4,128)S(1)}, u32[]{:S(2)}, u32[]{:S(2)}) collective-permute-start(f32[11,2,4,128]{3,2,1,0:T(4,128)S(1)} %get-tuple-element.48), channel_id=1, source_target_pairs={{8,0},{16,8},{24,16},{32,24},{40,32},{48,40},{56,48},{64,56},{72,6... | collective-permute-start | bytes 135176 | tf_op jit(solution)/shard_map/ppermute | solution.py:205
  82.0 10.4 %collective-permute-start.1 = (f32[11,2,4,128]{3,2,1,0:T(4,128)S(1)}, f32[11,2,4,128]{3,2,1,0:T(4,128)S(1)}, u32[]{:S(2)}, u32[]{:S(2)}) collective-permute-start(f32[11,2,4,128]{3,2,1,0:T(4,128)S(1)} %get-tuple-element.49), channel_id=1, source_target_pairs={{0,8},{8,16},{16,24},{24,32},{32,40},{40,48},{48,56},{56,64},{64,7... | collective-permute-start | bytes 135176 | tf_op jit(solution)/shard_map/ppermute | solution.py:205
  90.2 8.8 %copy-start.27 = (f32[3,3,3]{2,1,0:T(4,128)S(1)}, f32[3,3,3]{2,1,0:T(4,128)}, u32[]{:S(2)}) copy-start(f32[3,3,3]{2,1,0:T(4,128)} %param.13) | copy-start | bytes 328
  92.7 9.7 %collective-permute-start.2 = (f32[11,2,4,40]{2,3,1,0:T(8,128)S(1)}, f32[11,2,4,40]{2,3,1,0:T(8,128)S(1)}, u32[]{:S(2)}, u32[]{:S(2)}) collective-permute-start(f32[11,2,4,40]{2,3,1,0:T(8,128)S(1)} %get-tuple-element.38), channel_id=1, source_target_pairs={{1,0},{2,1},{3,2},{4,3},{5,4},{6,5},{7,6},{9,8},{10,9},{11,10},{12... | collective-permute-start | bytes 42248 | tf_op jit(solution)/shard_map/ppermute | solution.py:205
  95.3 8.3 %collective-permute-start.3 = (f32[11,2,4,40]{2,3,1,0:T(8,128)S(1)}, f32[11,2,4,40]{2,3,1,0:T(8,128)S(1)}, u32[]{:S(2)}, u32[]{:S(2)}) collective-permute-start(f32[11,2,4,40]{2,3,1,0:T(8,128)S(1)} %get-tuple-element.39), channel_id=1, source_target_pairs={{0,1},{1,2},{2,3},{3,4},{4,5},{5,6},{6,7},{8,9},{9,10},{10,11},{11... | collective-permute-start | bytes 42248 | tf_op jit(solution)/shard_map/ppermute | solution.py:205
  106.1 19.4 %collective-permute-start.4 = (f32[3,1,40,256]{3,2,1,0:T(8,128)S(1)}, f32[3,1,40,256]{3,2,1,0:T(8,128)S(1)}, u32[]{:S(2)}, u32[]{:S(2)}) collective-permute-start(f32[3,1,40,256]{3,2,1,0:T(8,128)S(1)} %get-tuple-element.37), channel_id=1, source_target_pairs={{0,128},{128,256},{256,384},{1,129},{129,257},{257,385},{2,130},{1... | collective-permute-start | bytes 368648 | tf_op jit(solution)/shard_map/ppermute | solution.py:205
  109.8 15.7 %collective-permute-start.5 = (f32[3,1,40,256]{3,2,1,0:T(8,128)S(1)}, f32[3,1,40,256]{3,2,1,0:T(8,128)S(1)}, u32[]{:S(2)}, u32[]{:S(2)}) collective-permute-start(f32[3,1,40,256]{3,2,1,0:T(8,128)S(1)} %get-tuple-element.36), channel_id=1, source_target_pairs={{128,0},{256,128},{384,256},{129,1},{257,129},{385,257},{130,2},{2... | collective-permute-start | bytes 368648 | tf_op jit(solution)/shard_map/ppermute | solution.py:205
  125.5 0.7 copy-start.20
  128.9 30.0 %copy-start = (f32[3,128,256]{2,1,0:T(8,128)S(1)}, f32[3,128,256]{2,1,0:T(8,128)}, u32[]{:S(2)}) copy-start(f32[3,128,256]{2,1,0:T(8,128)} %param.14) | copy-start | bytes 1179652
  128.9 5.4 %collective-permute-start.6 = (f32[3,1,40,256]{3,2,1,0:T(8,128)}, f32[3,1,40,256]{3,2,1,0:T(8,128)S(1)}, u32[]{:S(2)}, u32[]{:S(2)}) collective-permute-start(f32[3,1,40,256]{3,2,1,0:T(8,128)} %get-tuple-element.13), channel_id=1, source_target_pairs={{0,128},{128,256},{256,384},{1,129},{129,257},{257,385},{2,130},{1... | collective-permute-start | bytes 368648 | tf_op jit(solution)/shard_map/ppermute | solution.py:205
  131.5 6.8 %collective-permute-start.7 = (f32[3,1,40,256]{3,2,1,0:T(8,128)}, f32[3,1,40,256]{3,2,1,0:T(8,128)S(1)}, u32[]{:S(2)}, u32[]{:S(2)}) collective-permute-start(f32[3,1,40,256]{3,2,1,0:T(8,128)} %get-tuple-element.14), channel_id=1, source_target_pairs={{128,0},{256,128},{384,256},{129,1},{257,129},{385,257},{130,2},{2... | collective-permute-start | bytes 368648 | tf_op jit(solution)/shard_map/ppermute | solution.py:205
  134.3 4.5 %copy-start.23 = (f32[3,1,40,256]{3,2,1,0:T(8,128)}, f32[3,1,40,256]{3,2,1,0:T(8,128)S(1)}, u32[]{:S(2)}) copy-start(f32[3,1,40,256]{3,2,1,0:T(8,128)S(1)} %collective-permute-done.6.lo_ref) | copy-start | bytes 368644
  138.3 0.7 copy-start.25
  141.7 5.5 %collective-permute-start.8 = (f32[3,1,40,256]{3,2,1,0:T(8,128)}, f32[3,1,40,256]{3,2,1,0:T(8,128)S(1)}, u32[]{:S(2)}, u32[]{:S(2)}) collective-permute-start(f32[3,1,40,256]{3,2,1,0:T(8,128)} %get-tuple-element.16), channel_id=1, source_target_pairs={{0,128},{128,256},{256,384},{1,129},{129,257},{257,385},{2,130},{1... | collective-permute-start | bytes 368648 | tf_op jit(solution)/shard_map/ppermute | solution.py:205
  144.3 6.9 %collective-permute-start.9 = (f32[3,1,40,256]{3,2,1,0:T(8,128)}, f32[3,1,40,256]{3,2,1,0:T(8,128)S(1)}, u32[]{:S(2)}, u32[]{:S(2)}) collective-permute-start(f32[3,1,40,256]{3,2,1,0:T(8,128)} %get-tuple-element.17), channel_id=1, source_target_pairs={{128,0},{256,128},{384,256},{129,1},{257,129},{385,257},{130,2},{2... | collective-permute-start | bytes 368648 | tf_op jit(solution)/shard_map/ppermute | solution.py:205
  147.2 4.0 %copy-start.24 = (f32[3,1,40,256]{3,2,1,0:T(8,128)}, f32[3,1,40,256]{3,2,1,0:T(8,128)S(1)}, u32[]{:S(2)}) copy-start(f32[3,1,40,256]{3,2,1,0:T(8,128)S(1)} %collective-permute-done.8.lo_ref) | copy-start | bytes 368644
  154.6 15.9 %collective-permute-start.10 = (f32[3,1,40,256]{3,2,1,0:T(8,128)}, f32[3,1,40,256]{3,2,1,0:T(8,128)S(1)}, u32[]{:S(2)}, u32[]{:S(2)}) collective-permute-start(f32[3,1,40,256]{3,2,1,0:T(8,128)} %get-tuple-element.19), channel_id=1, source_target_pairs={{0,128},{128,256},{256,384},{1,129},{129,257},{257,385},{2,130},{1... | collective-permute-start | bytes 368648 | tf_op jit(solution)/shard_map/ppermute | solution.py:205
  157.6 12.9 %collective-permute-start.11 = (f32[3,1,40,256]{3,2,1,0:T(8,128)}, f32[3,1,40,256]{3,2,1,0:T(8,128)S(1)}, u32[]{:S(2)}, u32[]{:S(2)}) collective-permute-start(f32[3,1,40,256]{3,2,1,0:T(8,128)} %get-tuple-element.20), channel_id=1, source_target_pairs={{128,0},{256,128},{384,256},{129,1},{257,129},{385,257},{130,2},{2... | collective-permute-start | bytes 368648 | tf_op jit(solution)/shard_map/ppermute | solution.py:205
  159.1 58.1 %collective-permute-start.14 = (f32[3,128,1]{2,1,0:T(8,128)S(1)}, f32[3,128,1]{2,1,0:T(8,128)S(1)}, u32[]{:S(2)}, u32[]{:S(2)}) collective-permute-start(f32[3,128,1]{2,1,0:T(8,128)S(1)} %get-tuple-element.44), channel_id=1, source_target_pairs={{1,0},{2,1},{3,2},{4,3},{5,4},{6,5},{7,6},{9,8},{10,9},{11,10},{12... | collective-permute-start | bytes 4616 | tf_op jit(solution)/shard_map/ppermute | solution.py:37
  162.7 54.5 %collective-permute-start.15 = (f32[3,128,1]{2,1,0:T(8,128)S(1)}, f32[3,128,1]{2,1,0:T(8,128)S(1)}, u32[]{:S(2)}, u32[]{:S(2)}) collective-permute-start(f32[3,128,1]{2,1,0:T(8,128)S(1)} %get-tuple-element.45), channel_id=1, source_target_pairs={{0,1},{1,2},{2,3},{3,4},{4,5},{5,6},{6,7},{8,9},{9,10},{10,11},{11... | collective-permute-start | bytes 4616 | tf_op jit(solution)/shard_map/ppermute | solution.py:36
  170.5 0.7 copy-start.21
  170.5 0.7 copy-start.22
  176.3 32.0 %all-to-all-start.2 = ((f32[64,1,192]{2,1,0:T(1,128)}), f32[64,1,192]{2,1,0:T(1,128)S(1)}, u32[]{:S(2)}, u32[]{:S(2)}) async-start(f32[64,1,192]{2,1,0:T(1,128)} %reshape.209), calls=%async_computation.2 | async-start | bytes 131072 | tf_op jit(solution)/shard_map/all_to_all | solution.py:72
  195.0 22.2 %collective-permute-start.12 = (f32[3,1,256]{2,1,0:T(1,128)S(1)}, f32[3,1,256]{2,1,0:T(1,128)S(1)}, u32[]{:S(2)}, u32[]{:S(2)}) collective-permute-start(f32[3,1,256]{2,1,0:T(1,128)S(1)} %get-tuple-element.47), channel_id=1, source_target_pairs={{8,0},{16,8},{24,16},{32,24},{40,32},{48,40},{56,48},{64,56},{72,6... | collective-permute-start | bytes 9224 | tf_op jit(solution)/shard_map/ppermute | solution.py:37
  196.3 20.9 %collective-permute-start.13 = (f32[3,1,256]{2,1,0:T(1,128)S(1)}, f32[3,1,256]{2,1,0:T(1,128)S(1)}, u32[]{:S(2)}, u32[]{:S(2)}) collective-permute-start(f32[3,1,256]{2,1,0:T(1,128)S(1)} %get-tuple-element.46), channel_id=1, source_target_pairs={{0,8},{8,16},{16,24},{24,32},{32,40},{40,48},{48,56},{56,64},{64,7... | collective-permute-start | bytes 9224 | tf_op jit(solution)/shard_map/ppermute | solution.py:36
  216.9 0.9 copy-start.1
  218.1 17.5 %collective-permute-start.16 = (f32[3,1,256]{2,1,0:T(1,128)S(1)}, f32[3,1,256]{2,1,0:T(1,128)S(1)}, u32[]{:S(2)}, u32[]{:S(2)}) collective-permute-start(f32[3,1,256]{2,1,0:T(1,128)S(1)} %get-tuple-element.43), channel_id=1, source_target_pairs={{8,0},{16,8},{24,16},{32,24},{40,32},{48,40},{56,48},{64,56},{72,6... | collective-permute-start | bytes 9224 | tf_op jit(solution)/shard_map/ppermute | solution.py:37
  219.4 16.2 %collective-permute-start.17 = (f32[3,1,256]{2,1,0:T(1,128)S(1)}, f32[3,1,256]{2,1,0:T(1,128)S(1)}, u32[]{:S(2)}, u32[]{:S(2)}) collective-permute-start(f32[3,1,256]{2,1,0:T(1,128)S(1)} %get-tuple-element.42), channel_id=1, source_target_pairs={{0,8},{8,16},{16,24},{24,32},{32,40},{40,48},{48,56},{56,64},{64,7... | collective-permute-start | bytes 9224 | tf_op jit(solution)/shard_map/ppermute | solution.py:36
  227.4 7.1 %collective-permute-start.18 = (f32[3,128,1]{2,1,0:T(8,128)S(1)}, f32[3,128,1]{2,1,0:T(8,128)S(1)}, u32[]{:S(2)}, u32[]{:S(2)}) collective-permute-start(f32[3,128,1]{2,1,0:T(8,128)S(1)} %get-tuple-element.40), channel_id=1, source_target_pairs={{1,0},{2,1},{3,2},{4,3},{5,4},{6,5},{7,6},{9,8},{10,9},{11,10},{12... | collective-permute-start | bytes 4616 | tf_op jit(solution)/shard_map/ppermute | solution.py:37
  230.3 5.3 %collective-permute-start.19 = (f32[3,128,1]{2,1,0:T(8,128)S(1)}, f32[3,128,1]{2,1,0:T(8,128)S(1)}, u32[]{:S(2)}, u32[]{:S(2)}) collective-permute-start(f32[3,128,1]{2,1,0:T(8,128)S(1)} %get-tuple-element.41), channel_id=1, source_target_pairs={{0,1},{1,2},{2,3},{3,4},{4,5},{5,6},{6,7},{8,9},{9,10},{10,11},{11... | collective-permute-start | bytes 4616 | tf_op jit(solution)/shard_map/ppermute | solution.py:36
  (2 other events, 1.3 us)

commit v3 on v2

--- a/solution.py
+++ b/solution.py
@@ -280,14 +280,26 @@
     ext_x = rows_x + 2 * width
     wide = -(-(rows_y + 2 * width) // 128) * 128
     assert ext_x % 2 == 0 and wide % 2 == 0 and width <= K and width <= rows_x and width <= rows_y
-    ring = jnp.pad(film_block, ((0, 0), (1, 1 + piece_x), (1, 1 + piece_y)))
-    by_rows = jnp.stack(
-        [ring[:, k : k + piece_x * gx_count].reshape(3, gx_count, piece_x, -1)[:, :, 0] for k in range(piece_x + 2)]
-    )
-    by_cols = jnp.stack(
-        [by_rows[..., q : q + piece_y * gy_count].reshape(*by_rows.shape[:3], gy_count, piece_y)[..., 0] for q in range(piece_y + 2)]
-    )
-    pieces = by_cols.transpose(3, 4, 2, 1, 0).reshape(tile_count, 3, piece_x + 2, piece_y + 2)
+    tiles = film_block.reshape(3, gx_count, piece_x, gy_count, piece_y).transpose(1, 3, 0, 2, 4)
+    zero_row = jnp.zeros_like(tiles[:1, :, :, :1])
+    tiles = jnp.concatenate(
+        [
+            jnp.concatenate([zero_row, tiles[:-1, :, :, -1:]], axis=0),
+            tiles,
+            jnp.concatenate([tiles[1:, :, :, :1], zero_row], axis=0),
+        ],
+        axis=3,
+    )
+    zero_col = jnp.zeros_like(tiles[:, :1, :, :, :1])
+    tiles = jnp.concatenate(
+        [
+            jnp.concatenate([zero_col, tiles[:, :-1, :, :, -1:]], axis=1),
+            tiles,
+            jnp.concatenate([tiles[:, 1:, :, :, :1], zero_col], axis=1),
+        ],
+        axis=4,
+    )
+    pieces = tiles.reshape(tile_count, 3, piece_x + 2, piece_y + 2)
     pieces = jnp.where(first_tile, pieces, 0.0)
     placed = summed_rows(pieces, (("gx_0", "gx_1", "gy_0"), "gy_1"), 0)[0]
     own_patch = picked(placed, "region", 0)

time: 239 us -> 196 us (0.82)
  local copies, waits for them, and re-layouts: 63.2 us -> 19.8 us
    unnamed x106 -> x40, local copies, waits for them, and re-layouts: 29.8 us -> 6.26 us
    reshape x24 -> x2, local copies, waits for them, and re-layouts: 15.8 us -> 0.32 us  [body(): film_block.reshape(3, gx_count, piece_x, gy_count, piece_y)]
    slice x10 -> x2, local copies, waits for them, and re-layouts: 4.83 us -> 1.49 us  [the longest x1 1.46 us: body(): tiles[:, :-1, :, :, -1:]]
  transfers between devices with their start and end apart: 22 -> 22, of which waited for: 9 -> 10; matrix products, arithmetic and copies ran while one was open for 7% -> 8% of each run, Pallas kernels for 1% -> 1%
where the time goes in v3:
time: 196 us; the launch traced here: 195 us
  starting transfers between devices  99.1 us (51%)
  blocking collectives  26.8 us (14%)
  waiting for transfers between devices  22.6 us (12%)
  local copies, waits for them, and re-layouts  19.8 us (10%)
  other arithmetic  14.2 us (7%)
  Pallas kernels  10.9 us (6%)
    ppermute x12, starting transfers between devices, shift_in(): lax.ppermute(array, axis, up if from_lower else [(b, a) for a, b in up])  31.8 us
    ppermute x4, starting transfers between devices, with_halo(): lax.ppermute(last, axis, up)  26.2 us
    all_to_all x1, starting transfers between devices, copy_for_each(): lax.all_to_all(jnp.broadcast_to(array[None], (count, *array.shape)), axis...  18.6 us
    ppermute x12, waiting for transfers between devices, shift_in(): lax.ppermute(array, axis, up if from_lower else [(b, a) for a, b in up])  17.5 us
    all_to_all x1, starting transfers between devices, summed_rows(): return jnp.sum(lax.all_to_all(own, far, 0, 0, tiled=True), axis=0)  13.4 us
    all_gather x1, blocking collectives, picked(): lax.all_gather(array, axis)  11 us
    pallas_call x4, Pallas kernels, half_sweep(): pl.pallas_call(sweep_kernel, out_shape=out_shape, in_specs=[smem, smem] +...  10.9 us
    all_to_all x1, blocking collectives, summed_on_arrival(): lax.all_to_all(parts, axis, split_axis=0, concat_axis=0, tiled=True)  10.3 us
  transfers between devices with their start and end apart: 22, of which 10 were waited for; matrix products, arithmetic and copies ran while one was open for 8% of the time, Pallas kernels for 1%

profile of v3, /device:TPU:1, one launch (start us, length us, event | category | flops | bytes accessed | tf_op | source)
XLA Modules:
  0.0 195.0 jit_solution(1081157016338875575)
XLA Ops:
  0.6 0.9 slice.197
  2.1 1.5 fusion.49
  3.5 1.9 fusion
  6.7 1.4 reduce.6
  8.4 10.3 %all_to_all.20 = f32[2,1,20736]{2,1,0:T(1,128)S(1)} all-to-all(f32[2,1,20736]{2,1,0:T(1,128)S(1)} %reshape.113), channel_id=1, replica_groups=mesh['region'=4,'gx_0'=8,'gx_1'=2,'gy_0'=4,'gy_1'=2] {'gy_1'}, dimensions={0} | all-to-all | bytes 331776 | tf_op jit(solution)/shard_map/all_to_all | solution.py:56
  18.7 1.1 reduce.7
  21.8 2.1 %reduce.8 = f32[64,3,6,18]{3,2,1,0:T(8,128)S(1)} reduce(f32[64,3,6,1,18]{4,3,2,1,0:T(1,128)S(1)} %bitcast.220, f32[]{:T(128)} %broadcast.188), dimensions={3}, to_apply=%bitcast.210.reduce_sub_computation | reduce | bytes 165892
  24.0 1.1 reshape.115
  25.0 13.4 %all-to-all-start.1 = ((f32[64,1,324]{2,1,0:T(1,128)}), f32[64,1,324]{2,1,0:T(1,128)S(1)}, u32[]{:S(2)}, u32[]{:S(2)}) async-start(f32[64,1,324]{2,1,0:T(1,128)} %reshape.115), calls=%async_computation.1 | async-start | bytes 196608 | tf_op jit(solution)/shard_map/all_to_all | solution.py:63
  38.5 1.3 collective-permute-start
  39.8 7.9 %collective-permute-start.1 = (f32[11,2,4,128]{3,2,1,0:T(4,128)S(1)}, f32[11,2,4,128]{3,2,1,0:T(4,128)S(1)}, u32[]{:S(2)}, u32[]{:S(2)}) collective-permute-start(f32[11,2,4,128]{3,2,1,0:T(4,128)S(1)} %get-tuple-element.53), channel_id=1, source_target_pairs={{0,8},{8,16},{16,24},{24,32},{32,40},{40,48},{48,56},{56,64},{64,7... | collective-permute-start | bytes 135176 | tf_op jit(solution)/shard_map/ppermute | solution.py:205
  47.8 2.4 %collective-permute-done.1 = f32[11,2,4,128]{3,2,1,0:T(4,128)S(1)} collective-permute-done((f32[11,2,4,128]{3,2,1,0:T(4,128)S(1)}, f32[11,2,4,128]{3,2,1,0:T(4,128)S(1)}, u32[]{:S(2)}, u32[]{:S(2)}) %collective-permute-start.1) | collective-permute-done | bytes 45088 | tf_op jit(solution)/shard_map/ppermute | solution.py:205
  50.4 2.6 %collective-permute-start.2 = (f32[11,2,4,40]{2,3,1,0:T(8,128)S(1)}, f32[11,2,4,40]{2,3,1,0:T(8,128)S(1)}, u32[]{:S(2)}, u32[]{:S(2)}) collective-permute-start(f32[11,2,4,40]{2,3,1,0:T(8,128)S(1)} %get-tuple-element.42), channel_id=1, source_target_pairs={{1,0},{2,1},{3,2},{4,3},{5,4},{6,5},{7,6},{9,8},{10,9},{11,10},{12... | collective-permute-start | bytes 42248 | tf_op jit(solution)/shard_map/ppermute | solution.py:205
  53.1 2.9 %collective-permute-start.3 = (f32[11,2,4,40]{2,3,1,0:T(8,128)S(1)}, f32[11,2,4,40]{2,3,1,0:T(8,128)S(1)}, u32[]{:S(2)}, u32[]{:S(2)}) collective-permute-start(f32[11,2,4,40]{2,3,1,0:T(8,128)S(1)} %get-tuple-element.43), channel_id=1, source_target_pairs={{0,1},{1,2},{2,3},{3,4},{4,5},{5,6},{6,7},{8,9},{9,10},{10,11},{11... | collective-permute-start | bytes 42248 | tf_op jit(solution)/shard_map/ppermute | solution.py:205
  57.5 2.7 %collective-permute-done.2 = f32[11,2,4,40]{2,3,1,0:T(8,128)S(1)} collective-permute-done((f32[11,2,4,40]{2,3,1,0:T(8,128)S(1)}, f32[11,2,4,40]{2,3,1,0:T(8,128)S(1)}, u32[]{:S(2)}, u32[]{:S(2)}) %collective-permute-start.2) | collective-permute-done | bytes 14112 | tf_op jit(solution)/shard_map/ppermute | solution.py:205
  60.2 1.2 collective-permute-done.3
  63.8 3.8 %collective-permute-start.4 = (f32[3,1,40,256]{3,2,1,0:T(8,128)S(1)}, f32[3,1,40,256]{3,2,1,0:T(8,128)S(1)}, u32[]{:S(2)}, u32[]{:S(2)}) collective-permute-start(f32[3,1,40,256]{3,2,1,0:T(8,128)S(1)} %get-tuple-element.39), channel_id=1, source_target_pairs={{0,128},{128,256},{256,384},{1,129},{129,257},{257,385},{2,130},{1... | collective-permute-start | bytes 368648 | tf_op jit(solution)/shard_map/ppermute | solution.py:205
  67.5 1.3 collective-permute-start.5
  70.8 11.0 %all-gather = f32[12,6,18]{2,1,0:T(8,128)S(1)} all-gather(f32[3,6,18]{2,1,0:T(8,128)S(1)} %bitcast_reduce_fusion), channel_id=2, replica_groups=mesh['region'=4,'gx_0'=8,'gx_1'=2,'gy_0'=4,'gy_1'=2] {'region'}, dimensions={0}, use_global_device_ids=true | all-gather | bytes 6480 | tf_op jit(solution)/shard_map/all_gather | solution.py:67
  84.0 2.7 %shard_map.113 = (f32[3,2,40,256]{3,2,1,0:T(8,128)}, f32[3,1,40,256]{3,2,1,0:T(8,128)}, f32[3,1,40,256]{3,2,1,0:T(8,128)}) custom-call(s32[2]{0:T(128)} %call_exported.0.step_ref, f32[27]{0:T(128)} %reshape.97.k_ref, f32[3,2,40,256]{3,2,1,0:T(8,128)} %slice.250.s_ref, f32[3,1,40,256]{3,2,1,0:T(8,128)} %copy-done.5, f32[3,1,40,256]{3,2,1,0:T(8,128)} %copy-done.6, ...), custom_call_target="tpu_custom_call" | custom-call | flops 4096000 | bytes 1146880 | tf_op jit(solution)/shard_map/pallas_call | solution.py:193
  86.8 2.5 %collective-permute-start.6 = (f32[3,1,40,256]{3,2,1,0:T(8,128)}, f32[3,1,40,256]{3,2,1,0:T(8,128)S(1)}, u32[]{:S(2)}, u32[]{:S(2)}) collective-permute-start(f32[3,1,40,256]{3,2,1,0:T(8,128)} %get-tuple-element.13), channel_id=1, source_target_pairs={{0,128},{128,256},{256,384},{1,129},{129,257},{257,385},{2,130},{1... | collective-permute-start | bytes 368648 | tf_op jit(solution)/shard_map/ppermute | solution.py:205
  89.2 1.3 collective-permute-start.7
  90.5 1.5 collective-permute-done.6.lo_ref
  92.1 4.0 %collective-permute-done.7.hi_ref = f32[3,1,40,256]{3,2,1,0:T(8,128)S(1)} collective-permute-done((f32[3,1,40,256]{3,2,1,0:T(8,128)}, f32[3,1,40,256]{3,2,1,0:T(8,128)S(1)}, u32[]{:S(2)}, u32[]{:S(2)}) %collective-permute-start.7) | collective-permute-done | bytes 122912 | tf_op jit(solution)/shard_map/ppermute | solution.py:205
  96.7 2.7 %shard_map.114 = (f32[3,2,40,256]{3,2,1,0:T(8,128)}, f32[3,1,40,256]{3,2,1,0:T(8,128)}, f32[3,1,40,256]{3,2,1,0:T(8,128)}) custom-call(s32[2]{0:T(128)} %call_exported.1.step_ref, f32[27]{0:T(128)} %reshape.97.k_ref, f32[3,2,40,256]{3,2,1,0:T(8,128)} %get-tuple-element.12.s_ref, f32[3,1,40,256]{3,2,1,0:T(8,128)} %copy-done.9, f32[3,1,40,256]{3,2,1,0:T(8,128)} %copy-done.11, ...), custom_call_target="tpu_custom_call" | custom-call | flops 4096000 | bytes 1146880 | tf_op jit(solution)/shard_map/pallas_call | solution.py:193
  99.5 2.6 %collective-permute-start.8 = (f32[3,1,40,256]{3,2,1,0:T(8,128)}, f32[3,1,40,256]{3,2,1,0:T(8,128)S(1)}, u32[]{:S(2)}, u32[]{:S(2)}) collective-permute-start(f32[3,1,40,256]{3,2,1,0:T(8,128)} %get-tuple-element.16), channel_id=1, source_target_pairs={{0,128},{128,256},{256,384},{1,129},{129,257},{257,385},{2,130},{1... | collective-permute-start | bytes 368648 | tf_op jit(solution)/shard_map/ppermute | solution.py:205
  102.0 1.3 collective-permute-start.9
  103.3 1.6 collective-permute-done.8.lo_ref
  104.9 4.0 %collective-permute-done.9.hi_ref = f32[3,1,40,256]{3,2,1,0:T(8,128)S(1)} collective-permute-done((f32[3,1,40,256]{3,2,1,0:T(8,128)}, f32[3,1,40,256]{3,2,1,0:T(8,128)S(1)}, u32[]{:S(2)}, u32[]{:S(2)}) %collective-permute-start.9) | collective-permute-done | bytes 122912 | tf_op jit(solution)/shard_map/ppermute | solution.py:205
  109.6 2.7 %shard_map.115 = (f32[3,2,40,256]{3,2,1,0:T(8,128)}, f32[3,1,40,256]{3,2,1,0:T(8,128)}, f32[3,1,40,256]{3,2,1,0:T(8,128)}) custom-call(s32[2]{0:T(128)} %constant.84.clone.step_ref, f32[27]{0:T(128)} %reshape.97.k_ref, f32[3,2,40,256]{3,2,1,0:T(8,128)} %get-tuple-element.15.s_ref, f32[3,1,40,256]{3,2,1,0:T(8,128)} %copy-done.10, ...), custom_call_target="tpu_custom_call" | custom-call | flops 4096000 | bytes 1146880 | tf_op jit(solution)/shard_map/pallas_call | solution.py:193
  112.3 3.1 %collective-permute-start.10 = (f32[3,1,40,256]{3,2,1,0:T(8,128)}, f32[3,1,40,256]{3,2,1,0:T(8,128)S(1)}, u32[]{:S(2)}, u32[]{:S(2)}) collective-permute-start(f32[3,1,40,256]{3,2,1,0:T(8,128)} %get-tuple-element.19), channel_id=1, source_target_pairs={{0,128},{128,256},{256,384},{1,129},{129,257},{257,385},{2,130},{1... | collective-permute-start | bytes 368648 | tf_op jit(solution)/shard_map/ppermute | solution.py:205
  115.4 1.3 collective-permute-start.11
  116.8 3.7 %collective-permute-start.14 = (f32[3,128,1]{2,1,0:T(8,128)S(1)}, f32[3,128,1]{2,1,0:T(8,128)S(1)}, u32[]{:S(2)}, u32[]{:S(2)}) collective-permute-start(f32[3,128,1]{2,1,0:T(8,128)S(1)} %get-tuple-element.48), channel_id=1, source_target_pairs={{1,0},{2,1},{3,2},{4,3},{5,4},{6,5},{7,6},{9,8},{10,9},{11,10},{12... | collective-permute-start | bytes 4616 | tf_op jit(solution)/shard_map/ppermute | solution.py:37
  120.5 7.7 %collective-permute-start.15 = (f32[3,128,1]{2,1,0:T(8,128)S(1)}, f32[3,128,1]{2,1,0:T(8,128)S(1)}, u32[]{:S(2)}, u32[]{:S(2)}) collective-permute-start(f32[3,128,1]{2,1,0:T(8,128)S(1)} %get-tuple-element.49), channel_id=1, source_target_pairs={{0,1},{1,2},{2,3},{3,4},{4,5},{5,6},{6,7},{8,9},{9,10},{10,11},{11... | collective-permute-start | bytes 4616 | tf_op jit(solution)/shard_map/ppermute | solution.py:36
  128.9 2.7 %shard_map.116 = (f32[3,2,40,256]{3,2,1,0:T(8,128)}, f32[3,1,40,256]{3,2,1,0:T(8,128)}, f32[3,1,40,256]{3,2,1,0:T(8,128)}) custom-call(s32[2]{0:T(128)} %call_exported.2.step_ref, f32[27]{0:T(128)} %reshape.97.k_ref, f32[3,2,40,256]{3,2,1,0:T(8,128)} %get-tuple-element.18.s_ref, f32[3,1,40,256]{3,2,1,0:T(8,128)} %copy-done.7, f32[3,1,40,256]{3,2,1,0:T(8,128)} %copy-done.8, ...), custom_call_target="tpu_custom_call" | custom-call | flops 4096000 | bytes 1146880 | tf_op jit(solution)/shard_map/pallas_call | solution.py:193
  133.0 1.0 reshape.117
  134.0 18.6 %all-to-all-start.2 = ((f32[64,1,192]{2,1,0:T(1,128)}), f32[64,1,192]{2,1,0:T(1,128)S(1)}, u32[]{:S(2)}, u32[]{:S(2)}) async-start(f32[64,1,192]{2,1,0:T(1,128)} %reshape.117), calls=%async_computation.2 | async-start | bytes 131072 | tf_op jit(solution)/shard_map/all_to_all | solution.py:72
  152.6 1.3 collective-permute-start.12
  153.9 7.9 %collective-permute-start.13 = (f32[3,1,256]{2,1,0:T(1,128)S(1)}, f32[3,1,256]{2,1,0:T(1,128)S(1)}, u32[]{:S(2)}, u32[]{:S(2)}) collective-permute-start(f32[3,1,256]{2,1,0:T(1,128)S(1)} %get-tuple-element.50), channel_id=1, source_target_pairs={{0,8},{8,16},{16,24},{24,32},{32,40},{40,48},{48,56},{56,64},{64,7... | collective-permute-start | bytes 9224 | tf_op jit(solution)/shard_map/ppermute | solution.py:36
  161.8 4.1 %all-to-all-done.2 = f32[64,1,192]{2,1,0:T(1,128)S(1)} async-done(((f32[64,1,192]{2,1,0:T(1,128)}), f32[64,1,192]{2,1,0:T(1,128)S(1)}, u32[]{:S(2)}, u32[]{:S(2)}) %all-to-all-start.2) | async-done | bytes 49184 | tf_op jit(solution)/shard_map/all_to_all | solution.py:72
  167.3 5.5 %all_to_all.21 = f32[2,1,12288]{2,1,0:T(1,128)S(1)} all-to-all(f32[2,1,12288]{2,1,0:T(1,128)S(1)} %reshape.119), channel_id=1, replica_groups=mesh['region'=4,'gx_0'=8,'gx_1'=2,'gy_0'=4,'gy_1'=2] {'gy_1'}, dimensions={0} | all-to-all | bytes 196608 | tf_op jit(solution)/shard_map/all_to_all | solution.py:72
  172.8 0.9 reduce.11
  175.9 1.3 collective-permute-start.16
  177.2 7.9 %collective-permute-start.17 = (f32[3,1,256]{2,1,0:T(1,128)S(1)}, f32[3,1,256]{2,1,0:T(1,128)S(1)}, u32[]{:S(2)}, u32[]{:S(2)}) collective-permute-start(f32[3,1,256]{2,1,0:T(1,128)S(1)} %get-tuple-element.46), channel_id=1, source_target_pairs={{0,8},{8,16},{16,24},{24,32},{32,40},{40,48},{48,56},{56,64},{64,7... | collective-permute-start | bytes 9224 | tf_op jit(solution)/shard_map/ppermute | solution.py:36
  185.2 2.8 %collective-permute-start.18 = (f32[3,128,1]{2,1,0:T(8,128)S(1)}, f32[3,128,1]{2,1,0:T(8,128)S(1)}, u32[]{:S(2)}, u32[]{:S(2)}) collective-permute-start(f32[3,128,1]{2,1,0:T(8,128)S(1)} %get-tuple-element.44), channel_id=1, source_target_pairs={{1,0},{2,1},{3,2},{4,3},{5,4},{6,5},{7,6},{9,8},{10,9},{11,10},{12... | collective-permute-start | bytes 4616 | tf_op jit(solution)/shard_map/ppermute | solution.py:37
  188.0 2.7 %collective-permute-start.19 = (f32[3,128,1]{2,1,0:T(8,128)S(1)}, f32[3,128,1]{2,1,0:T(8,128)S(1)}, u32[]{:S(2)}, u32[]{:S(2)}) collective-permute-start(f32[3,128,1]{2,1,0:T(8,128)S(1)} %get-tuple-element.45), channel_id=1, source_target_pairs={{0,1},{1,2},{2,3},{3,4},{4,5},{5,6},{6,7},{8,9},{9,10},{10,11},{11... | collective-permute-start | bytes 4616 | tf_op jit(solution)/shard_map/ppermute | solution.py:36
  190.8 1.5 slice.214
  192.3 1.0 collective-permute-done.19
  (122 shorter events, 20.7 us)
Async XLA Ops:
  21.8 16.6 %copy-start.2 = (f32[2,3,2,32,128]{4,3,2,1,0:T(8,128)S(1)}, f32[2,3,2,32,128]{4,3,2,1,0:T(8,128)}, u32[]{:S(2)}) copy-start(f32[2,3,2,32,128]{4,3,2,1,0:T(8,128)} %param.12) | copy-start | bytes 589828
  21.8 16.6 %copy-start.3 = (f32[3,2,32,128]{3,2,1,0:T(8,128)S(1)}, f32[3,2,32,128]{3,2,1,0:T(8,128)}, u32[]{:S(2)}) copy-start(f32[3,2,32,128]{3,2,1,0:T(8,128)} %param.10) | copy-start | bytes 294916
  21.8 16.6 %copy-start.4 = (f32[2,2,32,128]{3,2,1,0:T(8,128)S(1)}, f32[2,2,32,128]{3,2,1,0:T(8,128)}, u32[]{:S(2)}) copy-start(f32[2,2,32,128]{3,2,1,0:T(8,128)} %param.11) | copy-start | bytes 196612
  25.0 43.8 %all-to-all-start.1 = ((f32[64,1,324]{2,1,0:T(1,128)}), f32[64,1,324]{2,1,0:T(1,128)S(1)}, u32[]{:S(2)}, u32[]{:S(2)}) async-start(f32[64,1,324]{2,1,0:T(1,128)} %reshape.115), calls=%async_computation.1 | async-start | bytes 196608 | tf_op jit(solution)/shard_map/all_to_all | solution.py:63
  38.5 9.3 %collective-permute-start = (f32[11,2,4,128]{3,2,1,0:T(4,128)S(1)}, f32[11,2,4,128]{3,2,1,0:T(4,128)S(1)}, u32[]{:S(2)}, u32[]{:S(2)}) collective-permute-start(f32[11,2,4,128]{3,2,1,0:T(4,128)S(1)} %get-tuple-element.52), channel_id=1, source_target_pairs={{8,0},{16,8},{24,16},{32,24},{40,32},{48,40},{56,48},{64,56},{72,6... | collective-permute-start | bytes 135176 | tf_op jit(solution)/shard_map/ppermute | solution.py:205
  39.8 10.4 %collective-permute-start.1 = (f32[11,2,4,128]{3,2,1,0:T(4,128)S(1)}, f32[11,2,4,128]{3,2,1,0:T(4,128)S(1)}, u32[]{:S(2)}, u32[]{:S(2)}) collective-permute-start(f32[11,2,4,128]{3,2,1,0:T(4,128)S(1)} %get-tuple-element.53), channel_id=1, source_target_pairs={{0,8},{8,16},{16,24},{24,32},{32,40},{40,48},{48,56},{56,64},{64,7... | collective-permute-start | bytes 135176 | tf_op jit(solution)/shard_map/ppermute | solution.py:205
  47.7 9.0 %copy-start.13 = (f32[3,3,3]{2,1,0:T(4,128)S(1)}, f32[3,3,3]{2,1,0:T(4,128)}, u32[]{:S(2)}) copy-start(f32[3,3,3]{2,1,0:T(4,128)} %param.13) | copy-start | bytes 328
  50.4 9.7 %collective-permute-start.2 = (f32[11,2,4,40]{2,3,1,0:T(8,128)S(1)}, f32[11,2,4,40]{2,3,1,0:T(8,128)S(1)}, u32[]{:S(2)}, u32[]{:S(2)}) collective-permute-start(f32[11,2,4,40]{2,3,1,0:T(8,128)S(1)} %get-tuple-element.42), channel_id=1, source_target_pairs={{1,0},{2,1},{3,2},{4,3},{5,4},{6,5},{7,6},{9,8},{10,9},{11,10},{12... | collective-permute-start | bytes 42248 | tf_op jit(solution)/shard_map/ppermute | solution.py:205
  53.1 8.3 %collective-permute-start.3 = (f32[11,2,4,40]{2,3,1,0:T(8,128)S(1)}, f32[11,2,4,40]{2,3,1,0:T(8,128)S(1)}, u32[]{:S(2)}, u32[]{:S(2)}) collective-permute-start(f32[11,2,4,40]{2,3,1,0:T(8,128)S(1)} %get-tuple-element.43), channel_id=1, source_target_pairs={{0,1},{1,2},{2,3},{3,4},{4,5},{5,6},{6,7},{8,9},{9,10},{10,11},{11... | collective-permute-start | bytes 42248 | tf_op jit(solution)/shard_map/ppermute | solution.py:205
  63.8 19.5 %collective-permute-start.4 = (f32[3,1,40,256]{3,2,1,0:T(8,128)S(1)}, f32[3,1,40,256]{3,2,1,0:T(8,128)S(1)}, u32[]{:S(2)}, u32[]{:S(2)}) collective-permute-start(f32[3,1,40,256]{3,2,1,0:T(8,128)S(1)} %get-tuple-element.39), channel_id=1, source_target_pairs={{0,128},{128,256},{256,384},{1,129},{129,257},{257,385},{2,130},{1... | collective-permute-start | bytes 368648 | tf_op jit(solution)/shard_map/ppermute | solution.py:205
  67.5 15.8 %collective-permute-start.5 = (f32[3,1,40,256]{3,2,1,0:T(8,128)S(1)}, f32[3,1,40,256]{3,2,1,0:T(8,128)S(1)}, u32[]{:S(2)}, u32[]{:S(2)}) collective-permute-start(f32[3,1,40,256]{3,2,1,0:T(8,128)S(1)} %get-tuple-element.38), channel_id=1, source_target_pairs={{128,0},{256,128},{384,256},{129,1},{257,129},{385,257},{130,2},{2... | collective-permute-start | bytes 368648 | tf_op jit(solution)/shard_map/ppermute | solution.py:205
  83.3 0.6 copy-start.5
  83.3 0.7 copy-start.6
  86.8 5.3 %collective-permute-start.6 = (f32[3,1,40,256]{3,2,1,0:T(8,128)}, f32[3,1,40,256]{3,2,1,0:T(8,128)S(1)}, u32[]{:S(2)}, u32[]{:S(2)}) collective-permute-start(f32[3,1,40,256]{3,2,1,0:T(8,128)} %get-tuple-element.13), channel_id=1, source_target_pairs={{0,128},{128,256},{256,384},{1,129},{129,257},{257,385},{2,130},{1... | collective-permute-start | bytes 368648 | tf_op jit(solution)/shard_map/ppermute | solution.py:205
  89.2 6.8 %collective-permute-start.7 = (f32[3,1,40,256]{3,2,1,0:T(8,128)}, f32[3,1,40,256]{3,2,1,0:T(8,128)S(1)}, u32[]{:S(2)}, u32[]{:S(2)}) collective-permute-start(f32[3,1,40,256]{3,2,1,0:T(8,128)} %get-tuple-element.14), channel_id=1, source_target_pairs={{128,0},{256,128},{384,256},{129,1},{257,129},{385,257},{130,2},{2... | collective-permute-start | bytes 368648 | tf_op jit(solution)/shard_map/ppermute | solution.py:205
  92.1 4.5 %copy-start.9 = (f32[3,1,40,256]{3,2,1,0:T(8,128)}, f32[3,1,40,256]{3,2,1,0:T(8,128)S(1)}, u32[]{:S(2)}) copy-start(f32[3,1,40,256]{3,2,1,0:T(8,128)S(1)} %collective-permute-done.6.lo_ref) | copy-start | bytes 368644
  96.0 0.7 copy-start.11
  96.7 19.9 %copy-start = (f32[3,128,256]{2,1,0:T(8,128)S(1)}, f32[3,128,256]{2,1,0:T(8,128)}, u32[]{:S(2)}) copy-start(f32[3,128,256]{2,1,0:T(8,128)} %param.14) | copy-start | bytes 1179652
  99.5 5.5 %collective-permute-start.8 = (f32[3,1,40,256]{3,2,1,0:T(8,128)}, f32[3,1,40,256]{3,2,1,0:T(8,128)S(1)}, u32[]{:S(2)}, u32[]{:S(2)}) collective-permute-start(f32[3,1,40,256]{3,2,1,0:T(8,128)} %get-tuple-element.16), channel_id=1, source_target_pairs={{0,128},{128,256},{256,384},{1,129},{129,257},{257,385},{2,130},{1... | collective-permute-start | bytes 368648 | tf_op jit(solution)/shard_map/ppermute | solution.py:205
  102.0 6.9 %collective-permute-start.9 = (f32[3,1,40,256]{3,2,1,0:T(8,128)}, f32[3,1,40,256]{3,2,1,0:T(8,128)S(1)}, u32[]{:S(2)}, u32[]{:S(2)}) collective-permute-start(f32[3,1,40,256]{3,2,1,0:T(8,128)} %get-tuple-element.17), channel_id=1, source_target_pairs={{128,0},{256,128},{384,256},{129,1},{257,129},{385,257},{130,2},{2... | collective-permute-start | bytes 368648 | tf_op jit(solution)/shard_map/ppermute | solution.py:205
  104.9 4.0 %copy-start.10 = (f32[3,1,40,256]{3,2,1,0:T(8,128)}, f32[3,1,40,256]{3,2,1,0:T(8,128)S(1)}, u32[]{:S(2)}) copy-start(f32[3,1,40,256]{3,2,1,0:T(8,128)S(1)} %collective-permute-done.8.lo_ref) | copy-start | bytes 368644
  108.9 0.6 copy-start.12
  112.3 15.9 %collective-permute-start.10 = (f32[3,1,40,256]{3,2,1,0:T(8,128)}, f32[3,1,40,256]{3,2,1,0:T(8,128)S(1)}, u32[]{:S(2)}, u32[]{:S(2)}) collective-permute-start(f32[3,1,40,256]{3,2,1,0:T(8,128)} %get-tuple-element.19), channel_id=1, source_target_pairs={{0,128},{128,256},{256,384},{1,129},{129,257},{257,385},{2,130},{1... | collective-permute-start | bytes 368648 | tf_op jit(solution)/shard_map/ppermute | solution.py:205
  115.4 12.9 %collective-permute-start.11 = (f32[3,1,40,256]{3,2,1,0:T(8,128)}, f32[3,1,40,256]{3,2,1,0:T(8,128)S(1)}, u32[]{:S(2)}, u32[]{:S(2)}) collective-permute-start(f32[3,1,40,256]{3,2,1,0:T(8,128)} %get-tuple-element.20), channel_id=1, source_target_pairs={{128,0},{256,128},{384,256},{129,1},{257,129},{385,257},{130,2},{2... | collective-permute-start | bytes 368648 | tf_op jit(solution)/shard_map/ppermute | solution.py:205
  116.8 57.9 %collective-permute-start.14 = (f32[3,128,1]{2,1,0:T(8,128)S(1)}, f32[3,128,1]{2,1,0:T(8,128)S(1)}, u32[]{:S(2)}, u32[]{:S(2)}) collective-permute-start(f32[3,128,1]{2,1,0:T(8,128)S(1)} %get-tuple-element.48), channel_id=1, source_target_pairs={{1,0},{2,1},{3,2},{4,3},{5,4},{6,5},{7,6},{9,8},{10,9},{11,10},{12... | collective-permute-start | bytes 4616 | tf_op jit(solution)/shard_map/ppermute | solution.py:37
  120.5 54.2 %collective-permute-start.15 = (f32[3,128,1]{2,1,0:T(8,128)S(1)}, f32[3,128,1]{2,1,0:T(8,128)S(1)}, u32[]{:S(2)}, u32[]{:S(2)}) collective-permute-start(f32[3,128,1]{2,1,0:T(8,128)S(1)} %get-tuple-element.49), channel_id=1, source_target_pairs={{0,1},{1,2},{2,3},{3,4},{4,5},{5,6},{6,7},{8,9},{9,10},{10,11},{11... | collective-permute-start | bytes 4616 | tf_op jit(solution)/shard_map/ppermute | solution.py:36
  128.2 0.6 copy-start.7
  128.2 0.7 copy-start.8
  134.0 31.9 %all-to-all-start.2 = ((f32[64,1,192]{2,1,0:T(1,128)}), f32[64,1,192]{2,1,0:T(1,128)S(1)}, u32[]{:S(2)}, u32[]{:S(2)}) async-start(f32[64,1,192]{2,1,0:T(1,128)} %reshape.117), calls=%async_computation.2 | async-start | bytes 131072 | tf_op jit(solution)/shard_map/all_to_all | solution.py:72
  152.6 22.1 %collective-permute-start.12 = (f32[3,1,256]{2,1,0:T(1,128)S(1)}, f32[3,1,256]{2,1,0:T(1,128)S(1)}, u32[]{:S(2)}, u32[]{:S(2)}) collective-permute-start(f32[3,1,256]{2,1,0:T(1,128)S(1)} %get-tuple-element.51), channel_id=1, source_target_pairs={{8,0},{16,8},{24,16},{32,24},{40,32},{48,40},{56,48},{64,56},{72,6... | collective-permute-start | bytes 9224 | tf_op jit(solution)/shard_map/ppermute | solution.py:37
  153.9 20.8 %collective-permute-start.13 = (f32[3,1,256]{2,1,0:T(1,128)S(1)}, f32[3,1,256]{2,1,0:T(1,128)S(1)}, u32[]{:S(2)}, u32[]{:S(2)}) collective-permute-start(f32[3,1,256]{2,1,0:T(1,128)S(1)} %get-tuple-element.50), channel_id=1, source_target_pairs={{0,8},{8,16},{16,24},{24,32},{32,40},{40,48},{48,56},{56,64},{64,7... | collective-permute-start | bytes 9224 | tf_op jit(solution)/shard_map/ppermute | solution.py:36
  174.7 0.9 copy-start.1
  175.9 17.5 %collective-permute-start.16 = (f32[3,1,256]{2,1,0:T(1,128)S(1)}, f32[3,1,256]{2,1,0:T(1,128)S(1)}, u32[]{:S(2)}, u32[]{:S(2)}) collective-permute-start(f32[3,1,256]{2,1,0:T(1,128)S(1)} %get-tuple-element.47), channel_id=1, source_target_pairs={{8,0},{16,8},{24,16},{32,24},{40,32},{48,40},{56,48},{64,56},{72,6... | collective-permute-start | bytes 9224 | tf_op jit(solution)/shard_map/ppermute | solution.py:37
  177.2 16.2 %collective-permute-start.17 = (f32[3,1,256]{2,1,0:T(1,128)S(1)}, f32[3,1,256]{2,1,0:T(1,128)S(1)}, u32[]{:S(2)}, u32[]{:S(2)}) collective-permute-start(f32[3,1,256]{2,1,0:T(1,128)S(1)} %get-tuple-element.46), channel_id=1, source_target_pairs={{0,8},{8,16},{16,24},{24,32},{32,40},{40,48},{48,56},{56,64},{64,7... | collective-permute-start | bytes 9224 | tf_op jit(solution)/shard_map/ppermute | solution.py:36
  185.2 7.1 %collective-permute-start.18 = (f32[3,128,1]{2,1,0:T(8,128)S(1)}, f32[3,128,1]{2,1,0:T(8,128)S(1)}, u32[]{:S(2)}, u32[]{:S(2)}) collective-permute-start(f32[3,128,1]{2,1,0:T(8,128)S(1)} %get-tuple-element.44), channel_id=1, source_target_pairs={{1,0},{2,1},{3,2},{4,3},{5,4},{6,5},{7,6},{9,8},{10,9},{11,10},{12... | collective-permute-start | bytes 4616 | tf_op jit(solution)/shard_map/ppermute | solution.py:37
  188.0 5.3 %collective-permute-start.19 = (f32[3,128,1]{2,1,0:T(8,128)S(1)}, f32[3,128,1]{2,1,0:T(8,128)S(1)}, u32[]{:S(2)}, u32[]{:S(2)}) collective-permute-start(f32[3,128,1]{2,1,0:T(8,128)S(1)} %get-tuple-element.45), channel_id=1, source_target_pairs={{0,1},{1,2},{2,3},{3,4},{4,5},{5,6},{6,7},{8,9},{9,10},{10,11},{11... | collective-permute-start | bytes 4616 | tf_op jit(solution)/shard_map/ppermute | solution.py:36

commit v4 on v3

--- a/solution.py
+++ b/solution.py
@@ -205,17 +205,44 @@
     return lax.ppermute(array, axis, up if from_lower else [(b, a) for a, b in up])
 
 
-def extended(array, width, wide):
+def packed(*arrays):
+    return jnp.concatenate([array.reshape(-1) for array in arrays])
+
+
+def unpacked(flat, *likes):
+    out, at = [], 0
+    for like in likes:
+        out.append(flat[at : at + like.size].reshape(like.shape))
+        at += like.size
+    return out
+
+
+def extended(array, film, width, film_width, wide):
     rows, cols = array.shape[-2:]
-    below = shift_in(array[..., rows - width :, :], GX, True)
-    above = shift_in(array[..., :width, :], GX, False)
-    array = jnp.concatenate([array, above, below], axis=-2)
-    left = shift_in(jnp.swapaxes(array[..., cols - width :], -1, -2), GY, True)
-    right = shift_in(jnp.swapaxes(array[..., :width], -1, -2), GY, False)
+    gx_pos = lax.axis_index(GX)
+    last = lax.axis_size(GX) - 1
+    s_low, f_low = array[..., rows - width :, :], film[:, -film_width:, :]
+    s_high, f_high = array[..., :width, :], film[:, :film_width, :]
+    below = unpacked(shift_in(packed(s_low, f_low), REGION_GX, True), s_low, f_low)
+    above = unpacked(shift_in(packed(s_high, f_high), REGION_GX, False), s_high, f_high)
+    array = jnp.concatenate(
+        [array, jnp.where(gx_pos == last, 0.0, above[0]), jnp.where(gx_pos == 0, 0.0, below[0])], axis=-2
+    )
+    film = jnp.concatenate([below[1], film, above[1]], axis=1)
+    s_low = jnp.swapaxes(array[..., cols - width :], -1, -2)
+    f_low = jnp.swapaxes(film[:, :, -film_width:], -1, -2)
+    s_high = jnp.swapaxes(array[..., :width], -1, -2)
+    f_high = jnp.swapaxes(film[:, :, :film_width], -1, -2)
+    left = unpacked(shift_in(packed(s_low, f_low), GY, True), s_low, f_low)
+    right = unpacked(shift_in(packed(s_high, f_high), GY, False), s_high, f_high)
     gap = jnp.zeros(array.shape[:-1] + (wide - cols - 2 * width,), array.dtype)
-    return jnp.concatenate(
-        [array, jnp.swapaxes(right, -1, -2), gap, jnp.swapaxes(left, -1, -2)], axis=-1
-    )
+    array = jnp.concatenate(
+        [array, jnp.swapaxes(right[0], -1, -2), gap, jnp.swapaxes(left[0], -1, -2)], axis=-1
+    )
+    film = jnp.concatenate(
+        [jnp.swapaxes(left[1], -1, -2), film, jnp.swapaxes(right[1], -1, -2)], axis=-1
+    )
+    return array, film
 
 
 def cells_for_sites(patch, rows_x, rows_y, width, wide):
@@ -308,7 +335,9 @@
     channels = jnp.concatenate(
         [stack_spins, trial_all.reshape(-1, layers_dev, rows_x, rows_y), unif_all], axis=0
     )
-    channels = extended(channels, width, wide)
+    film_width = 2
+    film_all = jnp.concatenate([film_m, film_anis[None]], axis=0)
+    channels, film_e4 = extended(channels, film_all, width, film_width, wide)
     spins_e = channels[:3]
     trials_e = channels[3 : 3 + 3 * SWEEPS].reshape(SWEEPS, 3, layers_dev, ext_x, wide)
     unif_e = channels[3 + 3 * SWEEPS :]
@@ -348,9 +377,14 @@
         ),
     )
     interface = jnp.where(first_tile, padded_block, 0.0)
-    rate_start = film_rate(film_m, film_halo(film_m), film_anis, interface)
-    predicted = film_m + time_step * rate_start
-    rate_trial = film_rate(predicted, film_halo(predicted), film_anis, interface)
+    magnet_e = film_e4[:3]
+    anis_e = film_e4[3]
+    interface_e = jnp.pad(interface, ((0, 0), (film_width, film_width), (film_width, film_width)))
+    inner = (slice(None), slice(1, -1), slice(1, -1))
+    rate_ring = film_rate(magnet_e[inner], magnet_e, anis_e[1:-1, 1:-1], interface_e[inner])
+    predicted = magnet_e[inner] + time_step * rate_ring
+    rate_start = rate_ring[inner]
+    rate_trial = film_rate(predicted[inner], predicted, film_anis, interface)
     corrected = film_m + 0.5 * time_step * (rate_start + rate_trial)
     return (stack_spins, normalized(corrected))
 

time: 196 us -> 178 us (0.908)
  starting transfers between devices: 99.1 us -> 57.2 us
  waiting for transfers between devices: 22.6 us -> 31.4 us
  blocking collectives: 26.8 us -> 35.2 us
  local copies, waits for them, and re-layouts: 19.8 us -> 23.3 us
  other arithmetic: 14.2 us -> 17.6 us
    ppermute x8 -> x0, starting transfers between devices: 35.3 us -> none  [the longest x4 26.2 us: with_halo(): lax.ppermute(last, axis, up)]
    all_to_all x1, blocking collectives: 5.47 us -> 12.9 us  [copy_for_each(): lax.all_to_all(jnp.broadcast_to(array[None], (count, *array.shape)), axis...]
    all_to_all x1, starting transfers between devices: 18.6 us -> 11.2 us  [copy_for_each(): lax.all_to_all(jnp.broadcast_to(array[None], (count, *array.shape)), axis...]
    all_to_all x1, waiting for transfers between devices: 4.11 us -> 11.1 us  [copy_for_each(): lax.all_to_all(jnp.broadcast_to(array[None], (count, *array.shape)), axis...]
    ppermute x12, waiting for transfers between devices: 17.5 us -> 20.3 us  [shift_in(): lax.ppermute(array, axis, up if from_lower else [(b, a) for a, b in up])]
    unnamed x40 -> x44, local copies, waits for them, and re-layouts: 6.26 us -> 6.56 us
  transfers between devices with their start and end apart: 22 -> 14, of which waited for: 10 -> 8; matrix products, arithmetic and copies ran while one was open for 8% -> 7% of each run, Pallas kernels for 1% -> 0%
where the time goes in v4:
time: 178 us; the launch traced here: 177 us
  starting transfers between devices  57.2 us (32%)
  blocking collectives  35.2 us (20%)
  waiting for transfers between devices  31.4 us (18%)
  local copies, waits for them, and re-layouts  23.3 us (13%)
  other arithmetic  17.6 us (10%)
  Pallas kernels  10.9 us (6%)
    ppermute x12, starting transfers between devices, shift_in(): lax.ppermute(array, axis, up if from_lower else [(b, a) for a, b in up])  32.6 us
    ppermute x12, waiting for transfers between devices, shift_in(): lax.ppermute(array, axis, up if from_lower else [(b, a) for a, b in up])  20.3 us
    all_to_all x1, starting transfers between devices, summed_rows(): return jnp.sum(lax.all_to_all(own, far, 0, 0, tiled=True), axis=0)  13.4 us
    all_to_all x1, blocking collectives, copy_for_each(): lax.all_to_all(jnp.broadcast_to(array[None], (count, *array.shape)), axis...  12.9 us
    all_gather x1, blocking collectives, picked(): lax.all_gather(array, axis)  12 us
    all_to_all x1, starting transfers between devices, copy_for_each(): lax.all_to_all(jnp.broadcast_to(array[None], (count, *array.shape)), axis...  11.2 us
    all_to_all x1, waiting for transfers between devices, copy_for_each(): lax.all_to_all(jnp.broadcast_to(array[None], (count, *array.shape)), axis...  11.1 us
    pallas_call x4, Pallas kernels, half_sweep(): pl.pallas_call(sweep_kernel, out_shape=out_shape, in_specs=[smem, smem] +...  10.9 us
  transfers between devices with their start and end apart: 14, of which 8 were waited for; matrix products, arithmetic and copies ran while one was open for 7% of the time, Pallas kernels for 0%

profile of v4, /device:TPU:1, one launch (start us, length us, event | category | flops | bytes accessed | tf_op | source)
XLA Modules:
  0.0 177.1 jit_solution(1300007904442385592)
XLA Ops:
  0.6 0.9 slice.282
  2.1 1.5 fusion.44
  3.5 1.9 %fusion = f32[16,8,3,6,18]{4,1,0,3,2:T(8,128)S(1)} fusion(f32[16,7,3,6,1]{4,1,0,3,2:T(8,128)} %get-tuple-element.39, f32[16,7,3,6,1]{4,1,0,3,2:T(8,128)S(1)} %get-tuple-element.38, f32[16,8,3,1,16]{4,1,0,3,2:T(8,128)S(1)} %concatenate.70, f32[16,8,3,4,16]{4,1,0,3,2:T(8,128)S(1)} %bitcast.236, f32[16,8,3,1,16]{4,1,0,3,2:T(8,128)S(1)} %concatenate.69, pred[]{:T(512)S(6)} %and.46), kind=kLoop, calls=%fused_computation.1 | loop fusion | flops 373248 | bytes 329473 | tf_op jit(solution)/shard_map/jit(_where)/select_n | solution.py:330
  6.8 1.5 reduce.6
  8.5 10.3 %all_to_all.20 = f32[2,1,20736]{2,1,0:T(1,128)S(1)} all-to-all(f32[2,1,20736]{2,1,0:T(1,128)S(1)} %reshape.203), channel_id=1, replica_groups=mesh['region'=4,'gx_0'=8,'gx_1'=2,'gy_0'=4,'gy_1'=2] {'gy_1'}, dimensions={0} | all-to-all | bytes 331776 | tf_op jit(solution)/shard_map/all_to_all | solution.py:56
  18.8 1.2 reduce.7
  22.0 2.2 %reduce.8 = f32[64,3,6,18]{3,2,1,0:T(8,128)S(1)} reduce(f32[64,3,6,1,18]{4,3,2,1,0:T(1,128)S(1)} %bitcast.243, f32[]{:T(128)} %broadcast.131), dimensions={3}, to_apply=%bitcast.229.reduce_sub_computation | reduce | bytes 165892
  24.3 1.1 reshape.205
  25.3 13.4 %all-to-all-start.1 = ((f32[64,1,324]{2,1,0:T(1,128)}), f32[64,1,324]{2,1,0:T(1,128)S(1)}, u32[]{:S(2)}, u32[]{:S(2)}) async-start(f32[64,1,324]{2,1,0:T(1,128)} %reshape.205), calls=%async_computation.1 | async-start | bytes 196608 | tf_op jit(solution)/shard_map/all_to_all | solution.py:63
  38.9 6.8 %collective-permute-start.1 = (f32[13312]{0:T(1024)S(1)}, f32[13312]{0:T(1024)S(1)}, u32[]{:S(2)}, u32[]{:S(2)}) collective-permute-start(f32[13312]{0:T(1024)S(1)} %pad_maximum_fusion.16), channel_id=1, source_target_pairs={{0,8},{8,16},{16,24},{24,32},{32,40},{40,48},{48,56},{56,64},{64,7... | collective-permute-start | bytes 159752 | tf_op jit(solution)/shard_map/ppermute | solution.py:205
  45.7 1.3 collective-permute-start
  47.1 7.8 %collective-permute-done = f32[13312]{0:T(1024)S(1)} collective-permute-done((f32[13312]{0:T(1024)S(1)}, f32[13312]{0:T(1024)S(1)}, u32[]{:S(2)}, u32[]{:S(2)}) %collective-permute-start) | collective-permute-done | bytes 53280 | tf_op jit(solution)/shard_map/ppermute | solution.py:205
  56.1 4.3 %collective-permute-start.2 = (f32[4576]{0:T(1024)S(1)}, f32[4576]{0:T(1024)S(1)}, u32[]{:S(2)}, u32[]{:S(2)}) collective-permute-start(f32[4576]{0:T(1024)S(1)} %pad_maximum_fusion.20), channel_id=1, source_target_pairs={{1,0},{2,1},{3,2},{4,3},{5,4},{6,5},{7,6},{9,8},{10,9},{11,10},{12... | collective-permute-start | bytes 54920 | tf_op jit(solution)/shard_map/ppermute | solution.py:205
  61.1 3.0 %collective-permute-start.3 = (f32[4576]{0:T(1024)S(1)}, f32[4576]{0:T(1024)S(1)}, u32[]{:S(2)}, u32[]{:S(2)}) collective-permute-start(f32[4576]{0:T(1024)S(1)} %pad_maximum_fusion.21), channel_id=1, source_target_pairs={{0,1},{1,2},{2,3},{3,4},{4,5},{5,6},{6,7},{8,9},{9,10},{10,11},{11... | collective-permute-start | bytes 54920 | tf_op jit(solution)/shard_map/ppermute | solution.py:205
  66.4 0.8 slice.356
  67.9 0.7 slice.343.s_ref
  68.7 3.0 %collective-permute-start.4 = (f32[3,1,40,256]{3,2,1,0:T(8,128)S(1)}, f32[3,1,40,256]{3,2,1,0:T(8,128)S(1)}, u32[]{:S(2)}, u32[]{:S(2)}) collective-permute-start(f32[3,1,40,256]{3,2,1,0:T(8,128)S(1)} %get-tuple-element.41), channel_id=1, source_target_pairs={{0,128},{128,256},{256,384},{1,129},{129,257},{257,385},{2,130},{1... | collective-permute-start | bytes 368648 | tf_op jit(solution)/shard_map/ppermute | solution.py:205
  71.6 1.3 collective-permute-start.5
  72.9 0.9 reduce.9
  73.9 0.7 reshape.206
  75.0 12.0 %all-gather = f32[12,6,18]{2,1,0:T(8,128)S(1)} all-gather(f32[3,6,18]{2,1,0:T(8,128)S(1)} %bitcast_reduce_fusion), channel_id=2, replica_groups=mesh['region'=4,'gx_0'=8,'gx_1'=2,'gy_0'=4,'gy_1'=2] {'region'}, dimensions={0}, use_global_device_ids=true | all-gather | bytes 6480 | tf_op jit(solution)/shard_map/all_gather | solution.py:67
  87.6 0.8 pad_maximum_fusion.13.film_ref
  89.1 2.7 %shard_map.113 = (f32[3,2,40,256]{3,2,1,0:T(8,128)}, f32[3,1,40,256]{3,2,1,0:T(8,128)}, f32[3,1,40,256]{3,2,1,0:T(8,128)}) custom-call(s32[2]{0:T(128)} %call_exported.0.step_ref, f32[27]{0:T(128)} %reshape.175.k_ref, f32[3,2,40,256]{3,2,1,0:T(8,128)} %slice.343.s_ref, f32[3,1,40,256]{3,2,1,0:T(8,128)} %copy-done.6, f32[3,1,40,256]{3,2,1,0:T(8,128)} %copy-done.7, ...), custom_call_target="tpu_custom_call" | custom-call | flops 4096000 | bytes 1146880 | tf_op jit(solution)/shard_map/pallas_call | solution.py:193
  91.8 2.7 %collective-permute-start.6 = (f32[3,1,40,256]{3,2,1,0:T(8,128)}, f32[3,1,40,256]{3,2,1,0:T(8,128)S(1)}, u32[]{:S(2)}, u32[]{:S(2)}) collective-permute-start(f32[3,1,40,256]{3,2,1,0:T(8,128)} %get-tuple-element.13), channel_id=1, source_target_pairs={{0,128},{128,256},{256,384},{1,129},{129,257},{257,385},{2,130},{1... | collective-permute-start | bytes 368648 | tf_op jit(solution)/shard_map/ppermute | solution.py:205
  94.5 1.3 collective-permute-start.7
  95.8 0.9 collective-permute-done.6.lo_ref
  96.7 3.7 %collective-permute-done.7.hi_ref = f32[3,1,40,256]{3,2,1,0:T(8,128)S(1)} collective-permute-done((f32[3,1,40,256]{3,2,1,0:T(8,128)}, f32[3,1,40,256]{3,2,1,0:T(8,128)S(1)}, u32[]{:S(2)}, u32[]{:S(2)}) %collective-permute-start.7) | collective-permute-done | bytes 122912 | tf_op jit(solution)/shard_map/ppermute | solution.py:205
  101.0 2.7 %shard_map.114 = (f32[3,2,40,256]{3,2,1,0:T(8,128)}, f32[3,1,40,256]{3,2,1,0:T(8,128)}, f32[3,1,40,256]{3,2,1,0:T(8,128)}) custom-call(s32[2]{0:T(128)} %call_exported.1.step_ref, f32[27]{0:T(128)} %reshape.175.k_ref, f32[3,2,40,256]{3,2,1,0:T(8,128)} %get-tuple-element.12.s_ref, f32[3,1,40,256]{3,2,1,0:T(8,128)} %copy-done.12, ...), custom_call_target="tpu_custom_call" | custom-call | flops 4096000 | bytes 1146880 | tf_op jit(solution)/shard_map/pallas_call | solution.py:193
  103.7 3.1 %collective-permute-start.8 = (f32[3,1,40,256]{3,2,1,0:T(8,128)}, f32[3,1,40,256]{3,2,1,0:T(8,128)S(1)}, u32[]{:S(2)}, u32[]{:S(2)}) collective-permute-start(f32[3,1,40,256]{3,2,1,0:T(8,128)} %get-tuple-element.16), channel_id=1, source_target_pairs={{0,128},{128,256},{256,384},{1,129},{129,257},{257,385},{2,130},{1... | collective-permute-start | bytes 368648 | tf_op jit(solution)/shard_map/ppermute | solution.py:205
  106.8 1.3 collective-permute-start.9
  109.0 3.7 %collective-permute-done.9.hi_ref = f32[3,1,40,256]{3,2,1,0:T(8,128)S(1)} collective-permute-done((f32[3,1,40,256]{3,2,1,0:T(8,128)}, f32[3,1,40,256]{3,2,1,0:T(8,128)S(1)}, u32[]{:S(2)}, u32[]{:S(2)}) %collective-permute-start.9) | collective-permute-done | bytes 122912 | tf_op jit(solution)/shard_map/ppermute | solution.py:205
  113.3 2.7 %shard_map.115 = (f32[3,2,40,256]{3,2,1,0:T(8,128)}, f32[3,1,40,256]{3,2,1,0:T(8,128)}, f32[3,1,40,256]{3,2,1,0:T(8,128)}) custom-call(s32[2]{0:T(128)} %constant.90.clone.step_ref, f32[27]{0:T(128)} %reshape.175.k_ref, f32[3,2,40,256]{3,2,1,0:T(8,128)} %get-tuple-element.15.s_ref, f32[3,1,40,256]{3,2,1,0:T(8,128)} %copy-done.8, ...), custom_call_target="tpu_custom_call" | custom-call | flops 4096000 | bytes 1146880 | tf_op jit(solution)/shard_map/pallas_call | solution.py:193
  116.0 3.3 %collective-permute-start.10 = (f32[3,1,40,256]{3,2,1,0:T(8,128)}, f32[3,1,40,256]{3,2,1,0:T(8,128)S(1)}, u32[]{:S(2)}, u32[]{:S(2)}) collective-permute-start(f32[3,1,40,256]{3,2,1,0:T(8,128)} %get-tuple-element.19), channel_id=1, source_target_pairs={{0,128},{128,256},{256,384},{1,129},{129,257},{257,385},{2,130},{1... | collective-permute-start | bytes 368648 | tf_op jit(solution)/shard_map/ppermute | solution.py:205
  119.4 1.3 collective-permute-start.11
  121.6 3.7 %collective-permute-done.11.hi_ref = f32[3,1,40,256]{3,2,1,0:T(8,128)S(1)} collective-permute-done((f32[3,1,40,256]{3,2,1,0:T(8,128)}, f32[3,1,40,256]{3,2,1,0:T(8,128)S(1)}, u32[]{:S(2)}, u32[]{:S(2)}) %collective-permute-start.11) | collective-permute-done | bytes 122912 | tf_op jit(solution)/shard_map/ppermute | solution.py:205
  125.9 2.7 %shard_map.116 = (f32[3,2,40,256]{3,2,1,0:T(8,128)}, f32[3,1,40,256]{3,2,1,0:T(8,128)}, f32[3,1,40,256]{3,2,1,0:T(8,128)}) custom-call(s32[2]{0:T(128)} %call_exported.2.step_ref, f32[27]{0:T(128)} %reshape.175.k_ref, f32[3,2,40,256]{3,2,1,0:T(8,128)} %get-tuple-element.18.s_ref, f32[3,1,40,256]{3,2,1,0:T(8,128)} %copy-done.10, ...), custom_call_target="tpu_custom_call" | custom-call | flops 4096000 | bytes 1146880 | tf_op jit(solution)/shard_map/pallas_call | solution.py:193
  128.6 0.8 slice.308
  130.1 1.0 reshape.207
  131.0 11.2 %all-to-all-start.2 = ((f32[64,1,192]{2,1,0:T(1,128)}), f32[64,1,192]{2,1,0:T(1,128)S(1)}, u32[]{:S(2)}, u32[]{:S(2)}) async-start(f32[64,1,192]{2,1,0:T(1,128)} %reshape.207), calls=%async_computation.2 | async-start | bytes 131072 | tf_op jit(solution)/shard_map/all_to_all | solution.py:72
  142.2 0.7 slice_bitcast_fusion.5
  142.9 1.5 slice.299
  144.4 11.1 %all-to-all-done.2 = f32[64,1,192]{2,1,0:T(1,128)S(1)} async-done(((f32[64,1,192]{2,1,0:T(1,128)}), f32[64,1,192]{2,1,0:T(1,128)S(1)}, u32[]{:S(2)}, u32[]{:S(2)}) %all-to-all-start.2) | async-done | bytes 49184 | tf_op jit(solution)/shard_map/all_to_all | solution.py:72
  155.5 0.8 reduce.10
  156.9 12.9 %all_to_all.21 = f32[2,1,12288]{2,1,0:T(1,128)S(1)} all-to-all(f32[2,1,12288]{2,1,0:T(1,128)S(1)} %reshape.209), channel_id=1, replica_groups=mesh['region'=4,'gx_0'=8,'gx_1'=2,'gy_0'=4,'gy_1'=2] {'gy_1'}, dimensions={0} | all-to-all | bytes 196608 | tf_op jit(solution)/shard_map/all_to_all | solution.py:72
  169.9 1.0 reduce.11
  171.9 1.0 fusion.3
  173.1 0.7 copy-done.2
  176.3 0.8 broadcast_divide_fusion
  (142 shorter events, 19.0 us)
Async XLA Ops:
  22.0 16.8 %copy-start = (f32[3,128,256]{2,1,0:T(8,128)S(1)}, f32[3,128,256]{2,1,0:T(8,128)}, u32[]{:S(2)}) copy-start(f32[3,128,256]{2,1,0:T(8,128)} %param.14) | copy-start | bytes 1179652
  22.0 16.8 %copy-start.1 = (f32[128,256]{1,0:T(8,128)S(1)}, f32[128,256]{1,0:T(8,128)}, u32[]{:S(2)}) copy-start(f32[128,256]{1,0:T(8,128)} %param.15) | copy-start | bytes 393220
  22.0 16.8 %copy-start.3 = (f32[2,3,2,32,128]{4,3,2,1,0:T(8,128)S(1)}, f32[2,3,2,32,128]{4,3,2,1,0:T(8,128)}, u32[]{:S(2)}) copy-start(f32[2,3,2,32,128]{4,3,2,1,0:T(8,128)} %param.12) | copy-start | bytes 589828
  22.0 16.8 %copy-start.4 = (f32[3,2,32,128]{3,2,1,0:T(8,128)S(1)}, f32[3,2,32,128]{3,2,1,0:T(8,128)}, u32[]{:S(2)}) copy-start(f32[3,2,32,128]{3,2,1,0:T(8,128)} %param.10) | copy-start | bytes 294916
  22.0 16.8 %copy-start.5 = (f32[2,2,32,128]{3,2,1,0:T(8,128)S(1)}, f32[2,2,32,128]{3,2,1,0:T(8,128)}, u32[]{:S(2)}) copy-start(f32[2,2,32,128]{3,2,1,0:T(8,128)} %param.11) | copy-start | bytes 196612
  25.3 47.6 %all-to-all-start.1 = ((f32[64,1,324]{2,1,0:T(1,128)}), f32[64,1,324]{2,1,0:T(1,128)S(1)}, u32[]{:S(2)}, u32[]{:S(2)}) async-start(f32[64,1,324]{2,1,0:T(1,128)} %reshape.205), calls=%async_computation.1 | async-start | bytes 196608 | tf_op jit(solution)/shard_map/all_to_all | solution.py:63
  38.9 8.2 %collective-permute-start.1 = (f32[13312]{0:T(1024)S(1)}, f32[13312]{0:T(1024)S(1)}, u32[]{:S(2)}, u32[]{:S(2)}) collective-permute-start(f32[13312]{0:T(1024)S(1)} %pad_maximum_fusion.16), channel_id=1, source_target_pairs={{0,8},{8,16},{16,24},{24,32},{32,40},{40,48},{48,56},{56,64},{64,7... | collective-permute-start | bytes 159752 | tf_op jit(solution)/shard_map/ppermute | solution.py:205
  45.7 9.2 %collective-permute-start = (f32[13312]{0:T(1024)S(1)}, f32[13312]{0:T(1024)S(1)}, u32[]{:S(2)}, u32[]{:S(2)}) collective-permute-start(f32[13312]{0:T(1024)S(1)} %pad_maximum_fusion.15), channel_id=1, source_target_pairs={{8,0},{16,8},{24,16},{32,24},{40,32},{48,40},{56,48},{64,56},{72,6... | collective-permute-start | bytes 159752 | tf_op jit(solution)/shard_map/ppermute | solution.py:205
  55.6 9.2 %copy-start.14 = (f32[3,3,3]{2,1,0:T(4,128)S(1)}, f32[3,3,3]{2,1,0:T(4,128)}, u32[]{:S(2)}) copy-start(f32[3,3,3]{2,1,0:T(4,128)} %param.13) | copy-start | bytes 328
  56.1 9.4 %collective-permute-start.2 = (f32[4576]{0:T(1024)S(1)}, f32[4576]{0:T(1024)S(1)}, u32[]{:S(2)}, u32[]{:S(2)}) collective-permute-start(f32[4576]{0:T(1024)S(1)} %pad_maximum_fusion.20), channel_id=1, source_target_pairs={{1,0},{2,1},{3,2},{4,3},{5,4},{6,5},{7,6},{9,8},{10,9},{11,10},{12... | collective-permute-start | bytes 54920 | tf_op jit(solution)/shard_map/ppermute | solution.py:205
  61.1 4.8 %collective-permute-start.3 = (f32[4576]{0:T(1024)S(1)}, f32[4576]{0:T(1024)S(1)}, u32[]{:S(2)}, u32[]{:S(2)}) collective-permute-start(f32[4576]{0:T(1024)S(1)} %pad_maximum_fusion.21), channel_id=1, source_target_pairs={{0,1},{1,2},{2,3},{3,4},{4,5},{5,6},{6,7},{8,9},{9,10},{10,11},{11... | collective-permute-start | bytes 54920 | tf_op jit(solution)/shard_map/ppermute | solution.py:205
  68.7 19.7 %collective-permute-start.4 = (f32[3,1,40,256]{3,2,1,0:T(8,128)S(1)}, f32[3,1,40,256]{3,2,1,0:T(8,128)S(1)}, u32[]{:S(2)}, u32[]{:S(2)}) collective-permute-start(f32[3,1,40,256]{3,2,1,0:T(8,128)S(1)} %get-tuple-element.41), channel_id=1, source_target_pairs={{0,128},{128,256},{256,384},{1,129},{129,257},{257,385},{2,130},{1... | collective-permute-start | bytes 368648 | tf_op jit(solution)/shard_map/ppermute | solution.py:205
  71.6 16.8 %collective-permute-start.5 = (f32[3,1,40,256]{3,2,1,0:T(8,128)S(1)}, f32[3,1,40,256]{3,2,1,0:T(8,128)S(1)}, u32[]{:S(2)}, u32[]{:S(2)}) collective-permute-start(f32[3,1,40,256]{3,2,1,0:T(8,128)S(1)} %get-tuple-element.40), channel_id=1, source_target_pairs={{128,0},{256,128},{384,256},{129,1},{257,129},{385,257},{130,2},{2... | collective-permute-start | bytes 368648 | tf_op jit(solution)/shard_map/ppermute | solution.py:205
  88.4 0.6 copy-start.6
  88.4 0.7 copy-start.7
  91.8 4.8 %collective-permute-start.6 = (f32[3,1,40,256]{3,2,1,0:T(8,128)}, f32[3,1,40,256]{3,2,1,0:T(8,128)S(1)}, u32[]{:S(2)}, u32[]{:S(2)}) collective-permute-start(f32[3,1,40,256]{3,2,1,0:T(8,128)} %get-tuple-element.13), channel_id=1, source_target_pairs={{0,128},{128,256},{256,384},{1,129},{129,257},{257,385},{2,130},{1... | collective-permute-start | bytes 368648 | tf_op jit(solution)/shard_map/ppermute | solution.py:205
  94.5 5.8 %collective-permute-start.7 = (f32[3,1,40,256]{3,2,1,0:T(8,128)}, f32[3,1,40,256]{3,2,1,0:T(8,128)S(1)}, u32[]{:S(2)}, u32[]{:S(2)}) collective-permute-start(f32[3,1,40,256]{3,2,1,0:T(8,128)} %get-tuple-element.14), channel_id=1, source_target_pairs={{128,0},{256,128},{384,256},{129,1},{257,129},{385,257},{130,2},{2... | collective-permute-start | bytes 368648 | tf_op jit(solution)/shard_map/ppermute | solution.py:205
  96.7 4.2 %copy-start.12 = (f32[3,1,40,256]{3,2,1,0:T(8,128)}, f32[3,1,40,256]{3,2,1,0:T(8,128)S(1)}, u32[]{:S(2)}) copy-start(f32[3,1,40,256]{3,2,1,0:T(8,128)S(1)} %collective-permute-done.6.lo_ref) | copy-start | bytes 368644
  100.3 0.6 copy-start.13
  103.7 5.3 %collective-permute-start.8 = (f32[3,1,40,256]{3,2,1,0:T(8,128)}, f32[3,1,40,256]{3,2,1,0:T(8,128)S(1)}, u32[]{:S(2)}, u32[]{:S(2)}) collective-permute-start(f32[3,1,40,256]{3,2,1,0:T(8,128)} %get-tuple-element.16), channel_id=1, source_target_pairs={{0,128},{128,256},{256,384},{1,129},{129,257},{257,385},{2,130},{1... | collective-permute-start | bytes 368648 | tf_op jit(solution)/shard_map/ppermute | solution.py:205
  106.8 5.8 %collective-permute-start.9 = (f32[3,1,40,256]{3,2,1,0:T(8,128)}, f32[3,1,40,256]{3,2,1,0:T(8,128)S(1)}, u32[]{:S(2)}, u32[]{:S(2)}) collective-permute-start(f32[3,1,40,256]{3,2,1,0:T(8,128)} %get-tuple-element.17), channel_id=1, source_target_pairs={{128,0},{256,128},{384,256},{129,1},{257,129},{385,257},{130,2},{2... | collective-permute-start | bytes 368648 | tf_op jit(solution)/shard_map/ppermute | solution.py:205
  109.0 3.7 %copy-start.8 = (f32[3,1,40,256]{3,2,1,0:T(8,128)}, f32[3,1,40,256]{3,2,1,0:T(8,128)S(1)}, u32[]{:S(2)}) copy-start(f32[3,1,40,256]{3,2,1,0:T(8,128)S(1)} %collective-permute-done.8.lo_ref) | copy-start | bytes 368644
  112.7 0.7 copy-start.9
  116.0 5.5 %collective-permute-start.10 = (f32[3,1,40,256]{3,2,1,0:T(8,128)}, f32[3,1,40,256]{3,2,1,0:T(8,128)S(1)}, u32[]{:S(2)}, u32[]{:S(2)}) collective-permute-start(f32[3,1,40,256]{3,2,1,0:T(8,128)} %get-tuple-element.19), channel_id=1, source_target_pairs={{0,128},{128,256},{256,384},{1,129},{129,257},{257,385},{2,130},{1... | collective-permute-start | bytes 368648 | tf_op jit(solution)/shard_map/ppermute | solution.py:205
  119.4 5.8 %collective-permute-start.11 = (f32[3,1,40,256]{3,2,1,0:T(8,128)}, f32[3,1,40,256]{3,2,1,0:T(8,128)S(1)}, u32[]{:S(2)}, u32[]{:S(2)}) collective-permute-start(f32[3,1,40,256]{3,2,1,0:T(8,128)} %get-tuple-element.20), channel_id=1, source_target_pairs={{128,0},{256,128},{384,256},{129,1},{257,129},{385,257},{130,2},{2... | collective-permute-start | bytes 368648 | tf_op jit(solution)/shard_map/ppermute | solution.py:205
  121.6 4.2 %copy-start.10 = (f32[3,1,40,256]{3,2,1,0:T(8,128)}, f32[3,1,40,256]{3,2,1,0:T(8,128)S(1)}, u32[]{:S(2)}) copy-start(f32[3,1,40,256]{3,2,1,0:T(8,128)S(1)} %collective-permute-done.10.lo_ref) | copy-start | bytes 368644
  125.2 0.7 copy-start.11
  131.0 24.5 %all-to-all-start.2 = ((f32[64,1,192]{2,1,0:T(1,128)}), f32[64,1,192]{2,1,0:T(1,128)S(1)}, u32[]{:S(2)}, u32[]{:S(2)}) async-start(f32[64,1,192]{2,1,0:T(1,128)} %reshape.207), calls=%async_computation.2 | async-start | bytes 131072 | tf_op jit(solution)/shard_map/all_to_all | solution.py:72
  172.9 0.9 copy-start.2

commit v5 on v4

--- a/solution.py
+++ b/solution.py
@@ -13,6 +13,7 @@
 REGION_GX = ("region", "gx_0", "gx_1")
 GY = ("gy_0", "gy_1")
 GX = ("gx_0", "gx_1")
+ALL_AXES = ("region", "gx_0", "gx_1", "gy_0", "gy_1")
 
 
 coupling_down = 1.0
@@ -61,6 +62,26 @@
     far, near = axes
     own = summed_on_arrival(split_up(array, dim, lax.axis_size(far)), near, dim + 1)
     return jnp.sum(lax.all_to_all(own, far, 0, 0, tiled=True), axis=0)
+
+
+def picked_on_arrival(array, axis, dim):
+    parts = split_up(array, dim, lax.axis_size(axis))
+    return lax.all_to_all(parts, axis, split_axis=0, concat_axis=0, tiled=True)[0]
+
+
+def picked_rows(array, axes, dim):
+    far, near = axes
+    own = picked_on_arrival(split_up(array, dim, lax.axis_size(far)), near, dim + 1)
+    return lax.all_to_all(own, far, 0, 0, tiled=True)[0]
+
+
+def from_first_region(array):
+    count = lax.axis_size("region")
+    tile = lax.axis_size(GX) * lax.axis_size(GY)
+    total = array
+    for region in range(1, count):
+        total = total + lax.ppermute(array, ALL_AXES, [(0, region * tile)])
+    return total
 
 
 def picked(array, axis, root):
@@ -327,9 +348,8 @@
         axis=4,
     )
     pieces = tiles.reshape(tile_count, 3, piece_x + 2, piece_y + 2)
-    pieces = jnp.where(first_tile, pieces, 0.0)
-    placed = summed_rows(pieces, (("gx_0", "gx_1", "gy_0"), "gy_1"), 0)[0]
-    own_patch = picked(placed, "region", 0)
+    pieces = from_first_region(jnp.where(first_tile, pieces, 0.0))
+    own_patch = picked_rows(pieces, (("gx_0", "gx_1", "gy_0"), "gy_1"), 0)[0]
     film_e = cells_for_sites(own_patch, rows_x, rows_y, width, wide)
     exch_flat = exch_kernel.reshape(-1)
     channels = jnp.concatenate(

time: 178 us -> 167 us (0.938)
  blocking collectives: 35.2 us -> 14.3 us
  waiting for transfers between devices: 31.4 us -> 38.2 us
  starting transfers between devices: 57.2 us -> 59.4 us
    all_gather x1 -> x0, blocking collectives: 12 us -> none  [picked(): lax.all_gather(array, axis)]
    all_to_all x1, waiting for transfers between devices: 0.01 us -> 9.47 us  [picked_rows(): return lax.all_to_all(own, far, 0, 0, tiled=True)[0]]
    all_to_all x1, blocking collectives: 10.3 us -> 3.5 us  [picked_on_arrival(): lax.all_to_all(parts, axis, split_axis=0, concat_axis=0, tiled=True)[0]]
    ppermute x12, starting transfers between devices: 32.6 us -> 39.4 us  [shift_in(): lax.ppermute(array, axis, up if from_lower else [(b, a) for a, b in up])]
    all_to_all x1, starting transfers between devices: 11.2 us -> 7.04 us  [copy_for_each(): lax.all_to_all(jnp.broadcast_to(array[None], (count, *array.shape)), axis...]
    ppermute x12, waiting for transfers between devices: 20.3 us -> 17.6 us  [shift_in(): lax.ppermute(array, axis, up if from_lower else [(b, a) for a, b in up])]
    all_to_all x1, starting transfers between devices: 13.4 us -> 11 us  [picked_rows(): return lax.all_to_all(own, far, 0, 0, tiled=True)[0]]
    all_to_all x1, blocking collectives: 12.9 us -> 10.8 us  [copy_for_each(): lax.all_to_all(jnp.broadcast_to(array[None], (count, *array.shape)), axis...]
  transfers between devices with their start and end apart: 14 -> 17, of which waited for: 8 -> 10; matrix products, arithmetic and copies ran while one was open for 7% -> 8% of each run, Pallas kernels for 0% -> 0%
where the time goes in v5:
time: 167 us; the launch traced here: 166 us
  starting transfers between devices  59.4 us (36%)
  waiting for transfers between devices  38.2 us (23%)
  local copies, waits for them, and re-layouts  24.8 us (15%)
  other arithmetic  17.1 us (10%)
  blocking collectives  14.3 us (9%)
  Pallas kernels  10.9 us (7%)
    ppermute x12, starting transfers between devices, shift_in(): lax.ppermute(array, axis, up if from_lower else [(b, a) for a, b in up])  39.4 us
    ppermute x12, waiting for transfers between devices, shift_in(): lax.ppermute(array, axis, up if from_lower else [(b, a) for a, b in up])  17.6 us
    all_to_all x1, waiting for transfers between devices, copy_for_each(): lax.all_to_all(jnp.broadcast_to(array[None], (count, *array.shape)), axis...  11.1 us
    all_to_all x1, starting transfers between devices, picked_rows(): return lax.all_to_all(own, far, 0, 0, tiled=True)[0]  11 us
    pallas_call x4, Pallas kernels, half_sweep(): pl.pallas_call(sweep_kernel, out_shape=out_shape, in_specs=[smem, smem] +...  10.9 us
    all_to_all x1, blocking collectives, copy_for_each(): lax.all_to_all(jnp.broadcast_to(array[None], (count, *array.shape)), axis...  10.8 us
    all_to_all x1, waiting for transfers between devices, picked_rows(): return lax.all_to_all(own, far, 0, 0, tiled=True)[0]  9.47 us
    all_to_all x1, starting transfers between devices, copy_for_each(): lax.all_to_all(jnp.broadcast_to(array[None], (count, *array.shape)), axis...  7.04 us
  transfers between devices with their start and end apart: 17, of which 10 were waited for; matrix products, arithmetic and copies ran while one was open for 8% of the time, Pallas kernels for 0%

profile of v5, /device:TPU:1, one launch (start us, length us, event | category | flops | bytes accessed | tf_op | source)
XLA Modules:
  0.0 166.3 jit_solution(17470016098675380257)
XLA Ops:
  0.6 0.9 slice.287
  2.1 1.4 fusion.45
  3.5 1.9 %fusion.1 = f32[128,3,6,18]{3,0,2,1:T(8,128)S(1)} fusion(f32[16,7,3,6,1]{4,1,0,3,2:T(8,128)} %get-tuple-element.39, f32[16,7,3,6,1]{4,1,0,3,2:T(8,128)S(1)} %get-tuple-element.38, f32[16,8,3,1,16]{4,1,0,3,2:T(8,128)S(1)} %concatenate.70, f32[16,8,3,4,16]{4,1,0,3,2:T(8,128)S(1)} %bitcast.238, f32[16,8,3,1,16]{4,1,0,3,2:T(8,128)S(1)} %concatenate.69, pred[]{:T(512)S(6)} %and.46), kind=kLoop, calls=%fused_computation.2 | loop fusion | flops 373248 | bytes 329473 | tf_op jit(solution)/shard_map/jit(_where)/select_n | solution.py:351
  5.5 1.1 copy.99
  8.7 11.5 %collective-permute-start.1 = (f32[13312]{0:T(1024)S(1)}, f32[13312]{0:T(1024)S(1)}, u32[]{:S(2)}, u32[]{:S(2)}) collective-permute-start(f32[13312]{0:T(1024)S(1)} %pad_maximum_fusion.16), channel_id=1, source_target_pairs={{0,8},{8,16},{16,24},{24,32},{32,40},{40,48},{48,56},{56,64},{64,7... | collective-permute-start | bytes 159752 | tf_op jit(solution)/shard_map/ppermute | solution.py:226
  20.2 1.3 collective-permute-start
  21.8 7.2 %collective-permute-done = f32[13312]{0:T(1024)S(1)} collective-permute-done((f32[13312]{0:T(1024)S(1)}, f32[13312]{0:T(1024)S(1)}, u32[]{:S(2)}, u32[]{:S(2)}) %collective-permute-start) | collective-permute-done | bytes 53280 | tf_op jit(solution)/shard_map/ppermute | solution.py:226
  30.5 4.4 %collective-permute-start.2 = (f32[4576]{0:T(1024)S(1)}, f32[4576]{0:T(1024)S(1)}, u32[]{:S(2)}, u32[]{:S(2)}) collective-permute-start(f32[4576]{0:T(1024)S(1)} %pad_maximum_fusion.20), channel_id=1, source_target_pairs={{1,0},{2,1},{3,2},{4,3},{5,4},{6,5},{7,6},{9,8},{10,9},{11,10},{12... | collective-permute-start | bytes 54920 | tf_op jit(solution)/shard_map/ppermute | solution.py:226
  35.5 3.2 %collective-permute-start.3 = (f32[4576]{0:T(1024)S(1)}, f32[4576]{0:T(1024)S(1)}, u32[]{:S(2)}, u32[]{:S(2)}) collective-permute-start(f32[4576]{0:T(1024)S(1)} %pad_maximum_fusion.21), channel_id=1, source_target_pairs={{0,1},{1,2},{2,3},{3,4},{4,5},{5,6},{6,7},{8,9},{9,10},{10,11},{11... | collective-permute-start | bytes 54920 | tf_op jit(solution)/shard_map/ppermute | solution.py:226
  41.0 0.8 slice.361
  42.5 0.7 slice.346.s_ref
  43.3 1.0 add_add_fusion
  45.9 1.4 reduce.4
  47.6 3.5 %all_to_all.20 = f32[2,1,20736]{2,1,0:T(1,128)S(1)} all-to-all(f32[2,1,20736]{2,1,0:T(1,128)S(1)} %reshape.188), channel_id=1, replica_groups=mesh['region'=4,'gx_0'=8,'gx_1'=2,'gy_0'=4,'gy_1'=2] {'gy_1'}, dimensions={0} | all-to-all | bytes 331776 | tf_op jit(solution)/shard_map/all_to_all | solution.py:69
  51.1 1.1 reduce.5
  53.2 2.1 %reduce.6 = f32[64,3,6,18]{3,2,1,0:T(8,128)S(1)} reduce(f32[64,3,6,1,18]{4,3,2,1,0:T(1,128)S(1)} %bitcast.245, f32[]{:T(128)} %broadcast.117), dimensions={3}, to_apply=%bitcast.199.reduce_sub_computation | reduce | bytes 165892
  55.3 1.1 reshape.190
  56.3 11.0 %all-to-all-start.1 = ((f32[64,1,324]{2,1,0:T(1,128)}), f32[64,1,324]{2,1,0:T(1,128)S(1)}, u32[]{:S(2)}, u32[]{:S(2)}) async-start(f32[64,1,324]{2,1,0:T(1,128)} %reshape.190), calls=%async_computation.1 | async-start | bytes 196608 | tf_op jit(solution)/shard_map/all_to_all | solution.py:75
  67.3 2.6 %collective-permute-start.4 = (f32[3,1,40,256]{3,2,1,0:T(8,128)S(1)}, f32[3,1,40,256]{3,2,1,0:T(8,128)S(1)}, u32[]{:S(2)}, u32[]{:S(2)}) collective-permute-start(f32[3,1,40,256]{3,2,1,0:T(8,128)S(1)} %get-tuple-element.41), channel_id=1, source_target_pairs={{0,128},{128,256},{256,384},{1,129},{129,257},{257,385},{2,130},{1... | collective-permute-start | bytes 368648 | tf_op jit(solution)/shard_map/ppermute | solution.py:226
  69.9 1.5 collective-permute-start.5
  71.4 9.5 %all-to-all-done.1 = f32[64,1,324]{2,1,0:T(1,128)S(1)} async-done(((f32[64,1,324]{2,1,0:T(1,128)}), f32[64,1,324]{2,1,0:T(1,128)S(1)}, u32[]{:S(2)}, u32[]{:S(2)}) %all-to-all-start.1) | async-done | bytes 82976 | tf_op jit(solution)/shard_map/all_to_all | solution.py:75
  80.9 0.8 reduce.7
  83.2 0.8 pad_maximum_fusion.13.film_ref
  84.6 2.7 %shard_map.113 = (f32[3,2,40,256]{3,2,1,0:T(8,128)}, f32[3,1,40,256]{3,2,1,0:T(8,128)}, f32[3,1,40,256]{3,2,1,0:T(8,128)}) custom-call(s32[2]{0:T(128)} %call_exported.0.step_ref, f32[27]{0:T(128)} %reshape.163.k_ref, f32[3,2,40,256]{3,2,1,0:T(8,128)} %slice.346.s_ref, f32[3,1,40,256]{3,2,1,0:T(8,128)} %copy-done.13, f32[3,1,40,256]{3,2,1,0:T(8,128)} %copy-done.14, ...), custom_call_target="tpu_custom_call" | custom-call | flops 4096000 | bytes 1146880 | tf_op jit(solution)/shard_map/pallas_call | solution.py:214
  87.4 1.3 collective-permute-start.10
  88.7 4.0 %collective-permute-start.9 = (f32[3,1,40,256]{3,2,1,0:T(8,128)}, f32[3,1,40,256]{3,2,1,0:T(8,128)S(1)}, u32[]{:S(2)}, u32[]{:S(2)}) collective-permute-start(f32[3,1,40,256]{3,2,1,0:T(8,128)} %get-tuple-element.13), channel_id=1, source_target_pairs={{0,128},{128,256},{256,384},{1,129},{129,257},{257,385},{2,130},{1... | collective-permute-start | bytes 368648 | tf_op jit(solution)/shard_map/ppermute | solution.py:226
  93.2 1.6 collective-permute-done.9.lo_ref
  95.5 2.7 %shard_map.114 = (f32[3,2,40,256]{3,2,1,0:T(8,128)}, f32[3,1,40,256]{3,2,1,0:T(8,128)}, f32[3,1,40,256]{3,2,1,0:T(8,128)}) custom-call(s32[2]{0:T(128)} %call_exported.1.step_ref, f32[27]{0:T(128)} %reshape.163.k_ref, f32[3,2,40,256]{3,2,1,0:T(8,128)} %get-tuple-element.12.s_ref, f32[3,1,40,256]{3,2,1,0:T(8,128)} %copy-done.20, ...), custom_call_target="tpu_custom_call" | custom-call | flops 4096000 | bytes 1146880 | tf_op jit(solution)/shard_map/pallas_call | solution.py:214
  98.2 3.8 %collective-permute-start.11 = (f32[3,1,40,256]{3,2,1,0:T(8,128)}, f32[3,1,40,256]{3,2,1,0:T(8,128)S(1)}, u32[]{:S(2)}, u32[]{:S(2)}) collective-permute-start(f32[3,1,40,256]{3,2,1,0:T(8,128)} %get-tuple-element.16), channel_id=1, source_target_pairs={{0,128},{128,256},{256,384},{1,129},{129,257},{257,385},{2,130},{1... | collective-permute-start | bytes 368648 | tf_op jit(solution)/shard_map/ppermute | solution.py:226
  102.0 1.3 collective-permute-start.12
  104.2 3.7 %collective-permute-done.12.hi_ref = f32[3,1,40,256]{3,2,1,0:T(8,128)S(1)} collective-permute-done((f32[3,1,40,256]{3,2,1,0:T(8,128)}, f32[3,1,40,256]{3,2,1,0:T(8,128)S(1)}, u32[]{:S(2)}, u32[]{:S(2)}) %collective-permute-start.12) | collective-permute-done | bytes 122912 | tf_op jit(solution)/shard_map/ppermute | solution.py:226
  108.5 2.7 %shard_map.115 = (f32[3,2,40,256]{3,2,1,0:T(8,128)}, f32[3,1,40,256]{3,2,1,0:T(8,128)}, f32[3,1,40,256]{3,2,1,0:T(8,128)}) custom-call(s32[2]{0:T(128)} %constant.85.clone.step_ref, f32[27]{0:T(128)} %reshape.163.k_ref, f32[3,2,40,256]{3,2,1,0:T(8,128)} %get-tuple-element.15.s_ref, f32[3,1,40,256]{3,2,1,0:T(8,128)} %copy-done.15, ...), custom_call_target="tpu_custom_call" | custom-call | flops 4096000 | bytes 1146880 | tf_op jit(solution)/shard_map/pallas_call | solution.py:214
  111.2 3.4 %collective-permute-start.13 = (f32[3,1,40,256]{3,2,1,0:T(8,128)}, f32[3,1,40,256]{3,2,1,0:T(8,128)S(1)}, u32[]{:S(2)}, u32[]{:S(2)}) collective-permute-start(f32[3,1,40,256]{3,2,1,0:T(8,128)} %get-tuple-element.19), channel_id=1, source_target_pairs={{0,128},{128,256},{256,384},{1,129},{129,257},{257,385},{2,130},{1... | collective-permute-start | bytes 368648 | tf_op jit(solution)/shard_map/ppermute | solution.py:226
  114.6 1.3 collective-permute-start.14
  116.8 3.7 %collective-permute-done.14.hi_ref = f32[3,1,40,256]{3,2,1,0:T(8,128)S(1)} collective-permute-done((f32[3,1,40,256]{3,2,1,0:T(8,128)}, f32[3,1,40,256]{3,2,1,0:T(8,128)S(1)}, u32[]{:S(2)}, u32[]{:S(2)}) %collective-permute-start.14) | collective-permute-done | bytes 122912 | tf_op jit(solution)/shard_map/ppermute | solution.py:226
  121.1 2.7 %shard_map.116 = (f32[3,2,40,256]{3,2,1,0:T(8,128)}, f32[3,1,40,256]{3,2,1,0:T(8,128)}, f32[3,1,40,256]{3,2,1,0:T(8,128)}) custom-call(s32[2]{0:T(128)} %call_exported.2.step_ref, f32[27]{0:T(128)} %reshape.163.k_ref, f32[3,2,40,256]{3,2,1,0:T(8,128)} %get-tuple-element.18.s_ref, f32[3,1,40,256]{3,2,1,0:T(8,128)} %copy-done.17, ...), custom_call_target="tpu_custom_call" | custom-call | flops 4096000 | bytes 1146880 | tf_op jit(solution)/shard_map/pallas_call | solution.py:214
  123.9 0.8 slice.315
  125.3 1.0 reshape.192
  126.3 7.0 %all-to-all-start.2 = ((f32[64,1,192]{2,1,0:T(1,128)}), f32[64,1,192]{2,1,0:T(1,128)S(1)}, u32[]{:S(2)}, u32[]{:S(2)}) async-start(f32[64,1,192]{2,1,0:T(1,128)} %reshape.192), calls=%async_computation.2 | async-start | bytes 131072 | tf_op jit(solution)/shard_map/all_to_all | solution.py:93
  133.3 0.7 slice_bitcast_fusion.5
  134.0 1.5 slice.306
  135.6 11.1 %all-to-all-done.2 = f32[64,1,192]{2,1,0:T(1,128)S(1)} async-done(((f32[64,1,192]{2,1,0:T(1,128)}), f32[64,1,192]{2,1,0:T(1,128)S(1)}, u32[]{:S(2)}, u32[]{:S(2)}) %all-to-all-start.2) | async-done | bytes 49184 | tf_op jit(solution)/shard_map/all_to_all | solution.py:93
  146.6 0.8 reduce.8
  148.0 10.8 %all_to_all.21 = f32[2,1,12288]{2,1,0:T(1,128)S(1)} all-to-all(f32[2,1,12288]{2,1,0:T(1,128)S(1)} %reshape.194), channel_id=1, replica_groups=mesh['region'=4,'gx_0'=8,'gx_1'=2,'gy_0'=4,'gy_1'=2] {'gy_1'}, dimensions={0} | all-to-all | bytes 196608 | tf_op jit(solution)/shard_map/all_to_all | solution.py:93
  158.8 0.9 reduce.9
  161.1 1.0 fusion.4
  162.3 0.7 copy-done.2
  165.5 0.8 broadcast_divide_fusion
  (164 shorter events, 21.9 us)
Async XLA Ops:
  5.5 3.2 %copy-start = (f32[3,128,256]{2,1,0:T(8,128)S(1)}, f32[3,128,256]{2,1,0:T(8,128)}, u32[]{:S(2)}) copy-start(f32[3,128,256]{2,1,0:T(8,128)} %param.14) | copy-start | bytes 1179652
  5.5 3.2 %copy-start.1 = (f32[128,256]{1,0:T(8,128)S(1)}, f32[128,256]{1,0:T(8,128)}, u32[]{:S(2)}) copy-start(f32[128,256]{1,0:T(8,128)} %param.15) | copy-start | bytes 393220
  5.5 3.2 %copy-start.3 = (f32[2,3,2,32,128]{4,3,2,1,0:T(8,128)S(1)}, f32[2,3,2,32,128]{4,3,2,1,0:T(8,128)}, u32[]{:S(2)}) copy-start(f32[2,3,2,32,128]{4,3,2,1,0:T(8,128)} %param.12) | copy-start | bytes 589828
  5.5 3.2 %copy-start.4 = (f32[3,2,32,128]{3,2,1,0:T(8,128)S(1)}, f32[3,2,32,128]{3,2,1,0:T(8,128)}, u32[]{:S(2)}) copy-start(f32[3,2,32,128]{3,2,1,0:T(8,128)} %param.10) | copy-start | bytes 294916
  5.5 3.2 %copy-start.6 = (f32[2,2,32,128]{3,2,1,0:T(8,128)S(1)}, f32[2,2,32,128]{3,2,1,0:T(8,128)}, u32[]{:S(2)}) copy-start(f32[2,2,32,128]{3,2,1,0:T(8,128)} %param.11) | copy-start | bytes 196612
  6.6 36.7 %collective-permute-start.6 = (f32[128,3,6,18]{0,3,2,1:T(8,128)}, f32[128,3,6,18]{0,3,2,1:T(8,128)S(1)}, u32[]{:S(2)}, u32[]{:S(2)}) collective-permute-start(f32[128,3,6,18]{0,3,2,1:T(8,128)} %copy.99), channel_id=1, source_target_pairs={{0,128}} | collective-permute-start | bytes 497672 | tf_op jit(solution)/shard_map/ppermute | solution.py:83
  7.3 36.0 %collective-permute-start.7 = (f32[128,3,6,18]{0,3,2,1:T(8,128)}, f32[128,3,6,18]{0,3,2,1:T(8,128)S(1)}, u32[]{:S(2)}, u32[]{:S(2)}) collective-permute-start(f32[128,3,6,18]{0,3,2,1:T(8,128)} %copy.99), channel_id=1, source_target_pairs={{0,256}} | collective-permute-start | bytes 497672 | tf_op jit(solution)/shard_map/ppermute | solution.py:83
  7.9 35.3 %collective-permute-start.8 = (f32[128,3,6,18]{0,3,2,1:T(8,128)}, f32[128,3,6,18]{0,3,2,1:T(8,128)S(1)}, u32[]{:S(2)}, u32[]{:S(2)}) collective-permute-start(f32[128,3,6,18]{0,3,2,1:T(8,128)} %copy.99), channel_id=1, source_target_pairs={{0,384}} | collective-permute-start | bytes 497672 | tf_op jit(solution)/shard_map/ppermute | solution.py:83
  8.7 13.1 %collective-permute-start.1 = (f32[13312]{0:T(1024)S(1)}, f32[13312]{0:T(1024)S(1)}, u32[]{:S(2)}, u32[]{:S(2)}) collective-permute-start(f32[13312]{0:T(1024)S(1)} %pad_maximum_fusion.16), channel_id=1, source_target_pairs={{0,8},{8,16},{16,24},{24,32},{32,40},{40,48},{48,56},{56,64},{64,7... | collective-permute-start | bytes 159752 | tf_op jit(solution)/shard_map/ppermute | solution.py:226
  20.2 8.8 %collective-permute-start = (f32[13312]{0:T(1024)S(1)}, f32[13312]{0:T(1024)S(1)}, u32[]{:S(2)}, u32[]{:S(2)}) collective-permute-start(f32[13312]{0:T(1024)S(1)} %pad_maximum_fusion.15), channel_id=1, source_target_pairs={{8,0},{16,8},{24,16},{32,24},{40,32},{48,40},{56,48},{64,56},{72,6... | collective-permute-start | bytes 159752 | tf_op jit(solution)/shard_map/ppermute | solution.py:226
  29.7 0.6 copy-start.7
  29.7 0.6 copy-start.10
  29.8 9.6 %copy-start.21 = (f32[3,3,3]{2,1,0:T(4,128)S(1)}, f32[3,3,3]{2,1,0:T(4,128)}, u32[]{:S(2)}) copy-start(f32[3,3,3]{2,1,0:T(4,128)} %param.13) | copy-start | bytes 328
  29.9 10.9 %copy-start.5 = (f32[3,2,32,128]{3,2,1,0:T(8,128)S(1)}, f32[3,2,32,128]{3,2,1,0:T(8,128)}, u32[]{:S(2)}) copy-start(f32[3,2,32,128]{3,2,1,0:T(8,128)} %param.10) | copy-start | bytes 294916
  30.5 9.6 %collective-permute-start.2 = (f32[4576]{0:T(1024)S(1)}, f32[4576]{0:T(1024)S(1)}, u32[]{:S(2)}, u32[]{:S(2)}) collective-permute-start(f32[4576]{0:T(1024)S(1)} %pad_maximum_fusion.20), channel_id=1, source_target_pairs={{1,0},{2,1},{3,2},{4,3},{5,4},{6,5},{7,6},{9,8},{10,9},{11,10},{12... | collective-permute-start | bytes 54920 | tf_op jit(solution)/shard_map/ppermute | solution.py:226
  35.5 4.9 %collective-permute-start.3 = (f32[4576]{0:T(1024)S(1)}, f32[4576]{0:T(1024)S(1)}, u32[]{:S(2)}, u32[]{:S(2)}) collective-permute-start(f32[4576]{0:T(1024)S(1)} %pad_maximum_fusion.21), channel_id=1, source_target_pairs={{0,1},{1,2},{2,3},{3,4},{4,5},{5,6},{6,7},{8,9},{9,10},{10,11},{11... | collective-permute-start | bytes 54920 | tf_op jit(solution)/shard_map/ppermute | solution.py:226
  56.3 24.6 %all-to-all-start.1 = ((f32[64,1,324]{2,1,0:T(1,128)}), f32[64,1,324]{2,1,0:T(1,128)S(1)}, u32[]{:S(2)}, u32[]{:S(2)}) async-start(f32[64,1,324]{2,1,0:T(1,128)} %reshape.190), calls=%async_computation.1 | async-start | bytes 196608 | tf_op jit(solution)/shard_map/all_to_all | solution.py:75
  67.3 16.6 %collective-permute-start.4 = (f32[3,1,40,256]{3,2,1,0:T(8,128)S(1)}, f32[3,1,40,256]{3,2,1,0:T(8,128)S(1)}, u32[]{:S(2)}, u32[]{:S(2)}) collective-permute-start(f32[3,1,40,256]{3,2,1,0:T(8,128)S(1)} %get-tuple-element.41), channel_id=1, source_target_pairs={{0,128},{128,256},{256,384},{1,129},{129,257},{257,385},{2,130},{1... | collective-permute-start | bytes 368648 | tf_op jit(solution)/shard_map/ppermute | solution.py:226
  69.9 14.0 %collective-permute-start.5 = (f32[3,1,40,256]{3,2,1,0:T(8,128)S(1)}, f32[3,1,40,256]{3,2,1,0:T(8,128)S(1)}, u32[]{:S(2)}, u32[]{:S(2)}) collective-permute-start(f32[3,1,40,256]{3,2,1,0:T(8,128)S(1)} %get-tuple-element.40), channel_id=1, source_target_pairs={{128,0},{256,128},{384,256},{129,1},{257,129},{385,257},{130,2},{2... | collective-permute-start | bytes 368648 | tf_op jit(solution)/shard_map/ppermute | solution.py:226
  84.0 0.7 copy-start.13
  84.0 0.7 copy-start.14
  87.4 5.8 %collective-permute-start.10 = (f32[3,1,40,256]{3,2,1,0:T(8,128)}, f32[3,1,40,256]{3,2,1,0:T(8,128)S(1)}, u32[]{:S(2)}, u32[]{:S(2)}) collective-permute-start(f32[3,1,40,256]{3,2,1,0:T(8,128)} %get-tuple-element.14), channel_id=1, source_target_pairs={{128,0},{256,128},{384,256},{129,1},{257,129},{385,257},{130,2},{2... | collective-permute-start | bytes 368648 | tf_op jit(solution)/shard_map/ppermute | solution.py:226
  88.7 6.2 %collective-permute-start.9 = (f32[3,1,40,256]{3,2,1,0:T(8,128)}, f32[3,1,40,256]{3,2,1,0:T(8,128)S(1)}, u32[]{:S(2)}, u32[]{:S(2)}) collective-permute-start(f32[3,1,40,256]{3,2,1,0:T(8,128)} %get-tuple-element.13), channel_id=1, source_target_pairs={{0,128},{128,256},{256,384},{1,129},{129,257},{257,385},{2,130},{1... | collective-permute-start | bytes 368648 | tf_op jit(solution)/shard_map/ppermute | solution.py:226
  93.2 2.2 %copy-start.19 = (f32[3,1,40,256]{3,2,1,0:T(8,128)}, f32[3,1,40,256]{3,2,1,0:T(8,128)S(1)}, u32[]{:S(2)}) copy-start(f32[3,1,40,256]{3,2,1,0:T(8,128)S(1)} %collective-permute-done.10.hi_ref) | copy-start | bytes 368644
  94.8 0.6 copy-start.20
  98.2 17.7 %copy-start.8 = (f32[4,2,256]{2,1,0:T(2,128)S(1)}, f32[4,2,256]{2,1,0:T(2,128)}, u32[]{:S(2)}) copy-start(f32[4,2,256]{2,1,0:T(2,128)} %copy-done.7) | copy-start | bytes 24580
  98.2 17.7 %copy-start.11 = (f32[4,2,256]{2,1,0:T(2,128)S(1)}, f32[4,2,256]{2,1,0:T(2,128)}, u32[]{:S(2)}) copy-start(f32[4,2,256]{2,1,0:T(2,128)} %copy-done.10) | copy-start | bytes 24580
  98.2 6.0 %collective-permute-start.11 = (f32[3,1,40,256]{3,2,1,0:T(8,128)}, f32[3,1,40,256]{3,2,1,0:T(8,128)S(1)}, u32[]{:S(2)}, u32[]{:S(2)}) collective-permute-start(f32[3,1,40,256]{3,2,1,0:T(8,128)} %get-tuple-element.16), channel_id=1, source_target_pairs={{0,128},{128,256},{256,384},{1,129},{129,257},{257,385},{2,130},{1... | collective-permute-start | bytes 368648 | tf_op jit(solution)/shard_map/ppermute | solution.py:226
  102.0 5.8 %collective-permute-start.12 = (f32[3,1,40,256]{3,2,1,0:T(8,128)}, f32[3,1,40,256]{3,2,1,0:T(8,128)S(1)}, u32[]{:S(2)}, u32[]{:S(2)}) collective-permute-start(f32[3,1,40,256]{3,2,1,0:T(8,128)} %get-tuple-element.17), channel_id=1, source_target_pairs={{128,0},{256,128},{384,256},{129,1},{257,129},{385,257},{130,2},{2... | collective-permute-start | bytes 368648 | tf_op jit(solution)/shard_map/ppermute | solution.py:226
  104.2 3.7 %copy-start.15 = (f32[3,1,40,256]{3,2,1,0:T(8,128)}, f32[3,1,40,256]{3,2,1,0:T(8,128)S(1)}, u32[]{:S(2)}) copy-start(f32[3,1,40,256]{3,2,1,0:T(8,128)S(1)} %collective-permute-done.11.lo_ref) | copy-start | bytes 368644
  107.8 0.6 copy-start.16
  111.2 5.6 %collective-permute-start.13 = (f32[3,1,40,256]{3,2,1,0:T(8,128)}, f32[3,1,40,256]{3,2,1,0:T(8,128)S(1)}, u32[]{:S(2)}, u32[]{:S(2)}) collective-permute-start(f32[3,1,40,256]{3,2,1,0:T(8,128)} %get-tuple-element.19), channel_id=1, source_target_pairs={{0,128},{128,256},{256,384},{1,129},{129,257},{257,385},{2,130},{1... | collective-permute-start | bytes 368648 | tf_op jit(solution)/shard_map/ppermute | solution.py:226
  114.6 5.8 %collective-permute-start.14 = (f32[3,1,40,256]{3,2,1,0:T(8,128)}, f32[3,1,40,256]{3,2,1,0:T(8,128)S(1)}, u32[]{:S(2)}, u32[]{:S(2)}) collective-permute-start(f32[3,1,40,256]{3,2,1,0:T(8,128)} %get-tuple-element.20), channel_id=1, source_target_pairs={{128,0},{256,128},{384,256},{129,1},{257,129},{385,257},{130,2},{2... | collective-permute-start | bytes 368648 | tf_op jit(solution)/shard_map/ppermute | solution.py:226
  116.8 4.2 %copy-start.17 = (f32[3,1,40,256]{3,2,1,0:T(8,128)}, f32[3,1,40,256]{3,2,1,0:T(8,128)S(1)}, u32[]{:S(2)}) copy-start(f32[3,1,40,256]{3,2,1,0:T(8,128)S(1)} %collective-permute-done.13.lo_ref) | copy-start | bytes 368644
  120.5 0.7 copy-start.18
  126.3 20.4 %all-to-all-start.2 = ((f32[64,1,192]{2,1,0:T(1,128)}), f32[64,1,192]{2,1,0:T(1,128)S(1)}, u32[]{:S(2)}, u32[]{:S(2)}) async-start(f32[64,1,192]{2,1,0:T(1,128)} %reshape.192), calls=%async_computation.2 | async-start | bytes 131072 | tf_op jit(solution)/shard_map/all_to_all | solution.py:93
  160.4 0.7 copy-start.9
  160.4 0.7 copy-start.12
  162.1 0.9 copy-start.2

commit v6 on v5

--- a/solution.py
+++ b/solution.py
@@ -349,7 +349,7 @@
     )
     pieces = tiles.reshape(tile_count, 3, piece_x + 2, piece_y + 2)
     pieces = from_first_region(jnp.where(first_tile, pieces, 0.0))
-    own_patch = picked_rows(pieces, (("gx_0", "gx_1", "gy_0"), "gy_1"), 0)[0]
+    own_patch = lax.all_to_all(pieces, GX + GY, 0, 0, tiled=True)[0]
     film_e = cells_for_sites(own_patch, rows_x, rows_y, width, wide)
     exch_flat = exch_kernel.reshape(-1)
     channels = jnp.concatenate(
@@ -382,7 +382,7 @@
             )
     stack_spins = spins_e[:, :, :rows_x, :rows_y]
     averages = stack_spins[:, 0].reshape(3, piece_x, K, piece_y, K).mean(axis=(2, 4))
-    gathered = whole_of(averages[None], (("gx_0", "gx_1", "gy_0"), "gy_1"), 0)
+    gathered = copy_for_each(averages, GX + GY)
     assembled = (
         gathered.reshape(gx_count, gy_count, 3, piece_x, piece_y)
         .transpose(2, 0, 3, 1, 4)

time: 167 us -> 155 us (0.928)
  blocking collectives: 14.3 us -> 0 us
  starting transfers between devices: 59.4 us -> 65.4 us
  waiting for transfers between devices: 38.2 us -> 43.9 us
  other arithmetic: 17.1 us -> 11.9 us
  local copies, waits for them, and re-layouts: 24.8 us -> 20.4 us
    all_to_all x2 -> x0, blocking collectives: 14.3 us -> none  [the longest x1 10.8 us: copy_for_each(): lax.all_to_all(jnp.broadcast_to(array[None], (count, *array.shape)), axis...]
    all_to_all x1, starting transfers between devices: 7.04 us -> 12.4 us  [copy_for_each(): lax.all_to_all(jnp.broadcast_to(array[None], (count, *array.shape)), axis...]
    unnamed x3 -> x1, other arithmetic: 3.55 us -> 0.01 us
    all_to_all x1, waiting for transfers between devices: 11.1 us -> 14.4 us  [copy_for_each(): lax.all_to_all(jnp.broadcast_to(array[None], (count, *array.shape)), axis...]
    unnamed x58 -> x41, local copies, waits for them, and re-layouts: 6.81 us -> 4.47 us
where the time goes in v6:
time: 155 us; the launch traced here: 154 us
  starting transfers between devices  65.4 us (42%)
  waiting for transfers between devices  43.9 us (28%)
  local copies, waits for them, and re-layouts  20.4 us (13%)
  other arithmetic  11.9 us (8%)
  Pallas kernels  10.8 us (7%)
    ppermute x12, starting transfers between devices, shift_in(): lax.ppermute(array, axis, up if from_lower else [(b, a) for a, b in up])  38.2 us
    ppermute x12, waiting for transfers between devices, shift_in(): lax.ppermute(array, axis, up if from_lower else [(b, a) for a, b in up])  18.7 us
    all_to_all x1, waiting for transfers between devices, copy_for_each(): lax.all_to_all(jnp.broadcast_to(array[None], (count, *array.shape)), axis...  14.4 us
    all_to_all x1, starting transfers between devices, copy_for_each(): lax.all_to_all(jnp.broadcast_to(array[None], (count, *array.shape)), axis...  12.4 us
    all_to_all x1, starting transfers between devices, body(): own_patch = lax.all_to_all(pieces, GX + GY, 0, 0, tiled=True)[0]  11.5 us
    pallas_call x4, Pallas kernels, half_sweep(): pl.pallas_call(sweep_kernel, out_shape=out_shape, in_specs=[smem, smem] +...  10.8 us
    all_to_all x1, waiting for transfers between devices, body(): own_patch = lax.all_to_all(pieces, GX + GY, 0, 0, tiled=True)[0]  10.8 us
    unnamed x41, local copies, waits for them, and re-layouts  4.47 us
  transfers between devices with their start and end apart: 17, of which 10 were waited for; matrix products, arithmetic and copies ran while one was open for 8% of the time, Pallas kernels for 0%

profile of v6, /device:TPU:1, one launch (start us, length us, event | category | flops | bytes accessed | tf_op | source)
XLA Modules:
  0.0 153.8 jit_solution(7371745050543769395)
XLA Ops:
  0.6 0.9 slice.284
  2.1 1.5 fusion.45
  3.5 1.9 %fusion.1 = f32[128,3,6,18]{3,0,2,1:T(8,128)S(1)} fusion(f32[16,7,3,6,1]{4,1,0,3,2:T(8,128)} %get-tuple-element.39, f32[16,7,3,6,1]{4,1,0,3,2:T(8,128)S(1)} %get-tuple-element.38, f32[16,8,3,1,16]{4,1,0,3,2:T(8,128)S(1)} %concatenate.70, f32[16,8,3,4,16]{4,1,0,3,2:T(8,128)S(1)} %bitcast.223, f32[16,8,3,1,16]{4,1,0,3,2:T(8,128)S(1)} %concatenate.69, pred[]{:T(512)S(6)} %and.46), kind=kLoop, calls=%fused_computation.2 | loop fusion | flops 373248 | bytes 329473 | tf_op jit(solution)/shard_map/jit(_where)/select_n | solution.py:351
  5.9 0.7 collective-permute-start.6
  6.6 1.3 collective-permute-start.7
  8.0 1.3 collective-permute-start.8
  9.4 11.5 %collective-permute-start.1 = (f32[13312]{0:T(1024)S(1)}, f32[13312]{0:T(1024)S(1)}, u32[]{:S(2)}, u32[]{:S(2)}) collective-permute-start(f32[13312]{0:T(1024)S(1)} %pad_maximum_fusion.16), channel_id=1, source_target_pairs={{0,8},{8,16},{16,24},{24,32},{32,40},{40,48},{48,56},{56,64},{64,7... | collective-permute-start | bytes 159752 | tf_op jit(solution)/shard_map/ppermute | solution.py:226
  20.9 1.3 collective-permute-start
  22.5 8.4 %collective-permute-done = f32[13312]{0:T(1024)S(1)} collective-permute-done((f32[13312]{0:T(1024)S(1)}, f32[13312]{0:T(1024)S(1)}, u32[]{:S(2)}, u32[]{:S(2)}) %collective-permute-start) | collective-permute-done | bytes 53280 | tf_op jit(solution)/shard_map/ppermute | solution.py:226
  32.1 3.4 %collective-permute-start.2 = (f32[4576]{0:T(1024)S(1)}, f32[4576]{0:T(1024)S(1)}, u32[]{:S(2)}, u32[]{:S(2)}) collective-permute-start(f32[4576]{0:T(1024)S(1)} %pad_maximum_fusion.20), channel_id=1, source_target_pairs={{1,0},{2,1},{3,2},{4,3},{5,4},{6,5},{7,6},{9,8},{10,9},{11,10},{12... | collective-permute-start | bytes 54920 | tf_op jit(solution)/shard_map/ppermute | solution.py:226
  36.2 2.9 %collective-permute-start.3 = (f32[4576]{0:T(1024)S(1)}, f32[4576]{0:T(1024)S(1)}, u32[]{:S(2)}, u32[]{:S(2)}) collective-permute-start(f32[4576]{0:T(1024)S(1)} %pad_maximum_fusion.21), channel_id=1, source_target_pairs={{0,1},{1,2},{2,3},{3,4},{4,5},{5,6},{6,7},{8,9},{9,10},{10,11},{11... | collective-permute-start | bytes 54920 | tf_op jit(solution)/shard_map/ppermute | solution.py:226
  39.2 0.7 and_convert_fusion.valid_ref
  39.9 0.7 reshape.161.k_ref
  41.4 1.1 add_add_fusion
  43.1 1.5 reshape.187
  44.6 11.5 %all-to-all-start = ((f32[128,1,324]{2,1,0:T(1,128)}), f32[128,1,324]{2,1,0:T(1,128)S(1)}, u32[]{:S(2)}, u32[]{:S(2)}) async-start(f32[128,1,324]{2,1,0:T(1,128)} %reshape.187), calls=%async_computation | async-start | bytes 393216 | tf_op jit(solution)/shard_map/all_to_all | solution.py:352
  56.4 0.8 slice.356
  57.2 0.7 slice.357.unif_ref
  57.9 0.7 slice.342.s_ref
  58.6 2.6 %collective-permute-start.4 = (f32[3,1,40,256]{3,2,1,0:T(8,128)S(1)}, f32[3,1,40,256]{3,2,1,0:T(8,128)S(1)}, u32[]{:S(2)}, u32[]{:S(2)}) collective-permute-start(f32[3,1,40,256]{3,2,1,0:T(8,128)S(1)} %get-tuple-element.41), channel_id=1, source_target_pairs={{0,128},{128,256},{256,384},{1,129},{129,257},{257,385},{2,130},{1... | collective-permute-start | bytes 368648 | tf_op jit(solution)/shard_map/ppermute | solution.py:226
  61.2 1.3 collective-permute-start.5
  62.5 10.8 %all-to-all-done = f32[128,1,324]{2,1,0:T(1,128)S(1)} async-done(((f32[128,1,324]{2,1,0:T(1,128)}), f32[128,1,324]{2,1,0:T(1,128)S(1)}, u32[]{:S(2)}, u32[]{:S(2)}) %all-to-all-start) | async-done | bytes 165920 | tf_op jit(solution)/shard_map/all_to_all | solution.py:352
  73.8 1.0 reduce.4
  76.0 0.7 pad_maximum_fusion.13.film_ref
  76.7 0.6 call_exported.0.step_ref
  77.4 2.7 %shard_map.113 = (f32[3,2,40,256]{3,2,1,0:T(8,128)}, f32[3,1,40,256]{3,2,1,0:T(8,128)}, f32[3,1,40,256]{3,2,1,0:T(8,128)}) custom-call(s32[2]{0:T(128)} %call_exported.0.step_ref, f32[27]{0:T(128)} %reshape.161.k_ref, f32[3,2,40,256]{3,2,1,0:T(8,128)} %slice.342.s_ref, f32[3,1,40,256]{3,2,1,0:T(8,128)} %copy-done.8, f32[3,1,40,256]{3,2,1,0:T(8,128)} %copy-done.9, ...), custom_call_target="tpu_custom_call" | custom-call | flops 4096000 | bytes 1146880 | tf_op jit(solution)/shard_map/pallas_call | solution.py:214
  80.1 1.3 collective-permute-start.10
  81.4 4.0 %collective-permute-start.9 = (f32[3,1,40,256]{3,2,1,0:T(8,128)}, f32[3,1,40,256]{3,2,1,0:T(8,128)S(1)}, u32[]{:S(2)}, u32[]{:S(2)}) collective-permute-start(f32[3,1,40,256]{3,2,1,0:T(8,128)} %get-tuple-element.13), channel_id=1, source_target_pairs={{0,128},{128,256},{256,384},{1,129},{129,257},{257,385},{2,130},{1... | collective-permute-start | bytes 368648 | tf_op jit(solution)/shard_map/ppermute | solution.py:226
  85.4 1.2 collective-permute-done.10.hi_ref
  86.6 1.0 collective-permute-done.9.lo_ref
  88.2 2.7 %shard_map.114 = (f32[3,2,40,256]{3,2,1,0:T(8,128)}, f32[3,1,40,256]{3,2,1,0:T(8,128)}, f32[3,1,40,256]{3,2,1,0:T(8,128)}) custom-call(s32[2]{0:T(128)} %call_exported.1.step_ref, f32[27]{0:T(128)} %reshape.161.k_ref, f32[3,2,40,256]{3,2,1,0:T(8,128)} %get-tuple-element.12.s_ref, f32[3,1,40,256]{3,2,1,0:T(8,128)} %copy-done.15, ...), custom_call_target="tpu_custom_call" | custom-call | flops 4096000 | bytes 1146880 | tf_op jit(solution)/shard_map/pallas_call | solution.py:214
  90.9 4.0 %collective-permute-start.11 = (f32[3,1,40,256]{3,2,1,0:T(8,128)}, f32[3,1,40,256]{3,2,1,0:T(8,128)S(1)}, u32[]{:S(2)}, u32[]{:S(2)}) collective-permute-start(f32[3,1,40,256]{3,2,1,0:T(8,128)} %get-tuple-element.16), channel_id=1, source_target_pairs={{0,128},{128,256},{256,384},{1,129},{129,257},{257,385},{2,130},{1... | collective-permute-start | bytes 368648 | tf_op jit(solution)/shard_map/ppermute | solution.py:226
  95.0 1.3 collective-permute-start.12
  97.1 3.7 %collective-permute-done.12.hi_ref = f32[3,1,40,256]{3,2,1,0:T(8,128)S(1)} collective-permute-done((f32[3,1,40,256]{3,2,1,0:T(8,128)}, f32[3,1,40,256]{3,2,1,0:T(8,128)S(1)}, u32[]{:S(2)}, u32[]{:S(2)}) %collective-permute-start.12) | collective-permute-done | bytes 122912 | tf_op jit(solution)/shard_map/ppermute | solution.py:226
  100.8 0.6 copy-done.11
  101.5 2.7 %shard_map.115 = (f32[3,2,40,256]{3,2,1,0:T(8,128)}, f32[3,1,40,256]{3,2,1,0:T(8,128)}, f32[3,1,40,256]{3,2,1,0:T(8,128)}) custom-call(s32[2]{0:T(128)} %constant.85.clone.step_ref, f32[27]{0:T(128)} %reshape.161.k_ref, f32[3,2,40,256]{3,2,1,0:T(8,128)} %get-tuple-element.15.s_ref, f32[3,1,40,256]{3,2,1,0:T(8,128)} %copy-done.10, ...), custom_call_target="tpu_custom_call" | custom-call | flops 4096000 | bytes 1146880 | tf_op jit(solution)/shard_map/pallas_call | solution.py:214
  104.2 3.1 %collective-permute-start.13 = (f32[3,1,40,256]{3,2,1,0:T(8,128)}, f32[3,1,40,256]{3,2,1,0:T(8,128)S(1)}, u32[]{:S(2)}, u32[]{:S(2)}) collective-permute-start(f32[3,1,40,256]{3,2,1,0:T(8,128)} %get-tuple-element.19), channel_id=1, source_target_pairs={{0,128},{128,256},{256,384},{1,129},{129,257},{257,385},{2,130},{1... | collective-permute-start | bytes 368648 | tf_op jit(solution)/shard_map/ppermute | solution.py:226
  107.3 1.5 collective-permute-start.14
  109.5 3.7 %collective-permute-done.14.hi_ref = f32[3,1,40,256]{3,2,1,0:T(8,128)S(1)} collective-permute-done((f32[3,1,40,256]{3,2,1,0:T(8,128)}, f32[3,1,40,256]{3,2,1,0:T(8,128)S(1)}, u32[]{:S(2)}, u32[]{:S(2)}) %collective-permute-start.14) | collective-permute-done | bytes 122912 | tf_op jit(solution)/shard_map/ppermute | solution.py:226
  113.8 2.7 %shard_map.116 = (f32[3,2,40,256]{3,2,1,0:T(8,128)}, f32[3,1,40,256]{3,2,1,0:T(8,128)}, f32[3,1,40,256]{3,2,1,0:T(8,128)}) custom-call(s32[2]{0:T(128)} %call_exported.2.step_ref, f32[27]{0:T(128)} %reshape.161.k_ref, f32[3,2,40,256]{3,2,1,0:T(8,128)} %get-tuple-element.18.s_ref, f32[3,1,40,256]{3,2,1,0:T(8,128)} %copy-done.12, ...), custom_call_target="tpu_custom_call" | custom-call | flops 4096000 | bytes 1146880 | tf_op jit(solution)/shard_map/pallas_call | solution.py:214
  116.5 0.8 slice.311
  118.0 1.3 reshape.189
  119.3 12.4 %all-to-all-start.1 = ((f32[128,1,192]{2,1,0:T(1,128)}), f32[128,1,192]{2,1,0:T(1,128)S(1)}, u32[]{:S(2)}, u32[]{:S(2)}) async-start(f32[128,1,192]{2,1,0:T(1,128)} %reshape.189), calls=%async_computation.1 | async-start | bytes 262144 | tf_op jit(solution)/shard_map/all_to_all | solution.py:93
  131.7 1.5 %slice.302 = f32[3,2,32,128]{3,2,1,0:T(8,128)} slice(f32[3,2,40,256]{3,2,1,0:T(8,128)} %get-tuple-element.21), slice={[0:3], [0:2], [0:32], [0:128]} | slice | bytes 196608 | tf_op jit(solution)/shard_map/slice | solution.py:383
  133.2 14.4 %all-to-all-done.1 = f32[128,1,192]{2,1,0:T(1,128)S(1)} async-done(((f32[128,1,192]{2,1,0:T(1,128)}), f32[128,1,192]{2,1,0:T(1,128)S(1)}, u32[]{:S(2)}, u32[]{:S(2)}) %all-to-all-start.1) | async-done | bytes 98336 | tf_op jit(solution)/shard_map/all_to_all | solution.py:93
  147.6 0.9 reduce.5
  149.4 1.0 fusion.4
  153.0 0.8 broadcast_divide_fusion
  (137 shorter events, 13.2 us)
Async XLA Ops:
  5.5 3.8 %copy-start = (f32[3,128,256]{2,1,0:T(8,128)S(1)}, f32[3,128,256]{2,1,0:T(8,128)}, u32[]{:S(2)}) copy-start(f32[3,128,256]{2,1,0:T(8,128)} %param.14) | copy-start | bytes 1179652
  5.5 3.8 %copy-start.1 = (f32[128,256]{1,0:T(8,128)S(1)}, f32[128,256]{1,0:T(8,128)}, u32[]{:S(2)}) copy-start(f32[128,256]{1,0:T(8,128)} %param.15) | copy-start | bytes 393220
  5.5 3.8 %copy-start.2 = (f32[2,3,2,32,128]{4,3,2,1,0:T(8,128)S(1)}, f32[2,3,2,32,128]{4,3,2,1,0:T(8,128)}, u32[]{:S(2)}) copy-start(f32[2,3,2,32,128]{4,3,2,1,0:T(8,128)} %param.12) | copy-start | bytes 589828
  5.5 3.8 %copy-start.4 = (f32[3,2,32,128]{3,2,1,0:T(8,128)S(1)}, f32[3,2,32,128]{3,2,1,0:T(8,128)}, u32[]{:S(2)}) copy-start(f32[3,2,32,128]{3,2,1,0:T(8,128)} %param.10) | copy-start | bytes 294916
  5.5 3.8 %copy-start.6 = (f32[2,2,32,128]{3,2,1,0:T(8,128)S(1)}, f32[2,2,32,128]{3,2,1,0:T(8,128)}, u32[]{:S(2)}) copy-start(f32[2,2,32,128]{3,2,1,0:T(8,128)} %param.11) | copy-start | bytes 196612
  5.9 35.4 %collective-permute-start.6 = (f32[128,3,6,18]{0,3,2,1:T(8,128)S(1)}, f32[128,3,6,18]{0,3,2,1:T(8,128)S(1)}, u32[]{:S(2)}, u32[]{:S(2)}) collective-permute-start(f32[128,3,6,18]{0,3,2,1:T(8,128)S(1)} %copy.112), channel_id=1, source_target_pairs={{0,128}} | collective-permute-start | bytes 497672 | tf_op jit(solution)/shard_map/ppermute | solution.py:83
  6.6 34.7 %collective-permute-start.7 = (f32[128,3,6,18]{0,3,2,1:T(8,128)S(1)}, f32[128,3,6,18]{0,3,2,1:T(8,128)}, u32[]{:S(2)}, u32[]{:S(2)}) collective-permute-start(f32[128,3,6,18]{0,3,2,1:T(8,128)S(1)} %copy.112), channel_id=1, source_target_pairs={{0,256}} | collective-permute-start | bytes 497672 | tf_op jit(solution)/shard_map/ppermute | solution.py:83
  8.0 33.4 %collective-permute-start.8 = (f32[128,3,6,18]{0,3,2,1:T(8,128)S(1)}, f32[128,3,6,18]{0,3,2,1:T(8,128)}, u32[]{:S(2)}, u32[]{:S(2)}) collective-permute-start(f32[128,3,6,18]{0,3,2,1:T(8,128)S(1)} %copy.112), channel_id=1, source_target_pairs={{0,384}} | collective-permute-start | bytes 497672 | tf_op jit(solution)/shard_map/ppermute | solution.py:83
  9.4 13.1 %collective-permute-start.1 = (f32[13312]{0:T(1024)S(1)}, f32[13312]{0:T(1024)S(1)}, u32[]{:S(2)}, u32[]{:S(2)}) collective-permute-start(f32[13312]{0:T(1024)S(1)} %pad_maximum_fusion.16), channel_id=1, source_target_pairs={{0,8},{8,16},{16,24},{24,32},{32,40},{40,48},{48,56},{56,64},{64,7... | collective-permute-start | bytes 159752 | tf_op jit(solution)/shard_map/ppermute | solution.py:226
  20.9 10.1 %collective-permute-start = (f32[13312]{0:T(1024)S(1)}, f32[13312]{0:T(1024)S(1)}, u32[]{:S(2)}, u32[]{:S(2)}) collective-permute-start(f32[13312]{0:T(1024)S(1)} %pad_maximum_fusion.15), channel_id=1, source_target_pairs={{8,0},{16,8},{24,16},{32,24},{40,32},{48,40},{56,48},{64,56},{72,6... | collective-permute-start | bytes 159752 | tf_op jit(solution)/shard_map/ppermute | solution.py:226
  31.6 8.2 %copy-start.16 = (f32[3,3,3]{2,1,0:T(4,128)S(1)}, f32[3,3,3]{2,1,0:T(4,128)}, u32[]{:S(2)}) copy-start(f32[3,3,3]{2,1,0:T(4,128)} %param.13) | copy-start | bytes 328
  32.1 8.5 %collective-permute-start.2 = (f32[4576]{0:T(1024)S(1)}, f32[4576]{0:T(1024)S(1)}, u32[]{:S(2)}, u32[]{:S(2)}) collective-permute-start(f32[4576]{0:T(1024)S(1)} %pad_maximum_fusion.20), channel_id=1, source_target_pairs={{1,0},{2,1},{3,2},{4,3},{5,4},{6,5},{7,6},{9,8},{10,9},{11,10},{12... | collective-permute-start | bytes 54920 | tf_op jit(solution)/shard_map/ppermute | solution.py:226
  36.2 4.8 %collective-permute-start.3 = (f32[4576]{0:T(1024)S(1)}, f32[4576]{0:T(1024)S(1)}, u32[]{:S(2)}, u32[]{:S(2)}) collective-permute-start(f32[4576]{0:T(1024)S(1)} %pad_maximum_fusion.21), channel_id=1, source_target_pairs={{0,1},{1,2},{2,3},{3,4},{4,5},{5,6},{6,7},{8,9},{9,10},{10,11},{11... | collective-permute-start | bytes 54920 | tf_op jit(solution)/shard_map/ppermute | solution.py:226
  43.0 13.1 %copy-start.3 = (f32[2,3,2,32,128]{4,3,2,1,0:T(8,128)S(1)}, f32[2,3,2,32,128]{4,3,2,1,0:T(8,128)}, u32[]{:S(2)}) copy-start(f32[2,3,2,32,128]{4,3,2,1,0:T(8,128)} %param.12) | copy-start | bytes 589828
  43.0 13.1 %copy-start.5 = (f32[3,2,32,128]{3,2,1,0:T(8,128)S(1)}, f32[3,2,32,128]{3,2,1,0:T(8,128)}, u32[]{:S(2)}) copy-start(f32[3,2,32,128]{3,2,1,0:T(8,128)} %param.10) | copy-start | bytes 294916
  43.1 13.1 %copy-start.7 = (f32[2,2,32,128]{3,2,1,0:T(8,128)S(1)}, f32[2,2,32,128]{3,2,1,0:T(8,128)}, u32[]{:S(2)}) copy-start(f32[2,2,32,128]{3,2,1,0:T(8,128)} %param.11) | copy-start | bytes 196612
  44.6 28.7 %all-to-all-start = ((f32[128,1,324]{2,1,0:T(1,128)}), f32[128,1,324]{2,1,0:T(1,128)S(1)}, u32[]{:S(2)}, u32[]{:S(2)}) async-start(f32[128,1,324]{2,1,0:T(1,128)} %reshape.187), calls=%async_computation | async-start | bytes 393216 | tf_op jit(solution)/shard_map/all_to_all | solution.py:352
  58.6 18.1 %collective-permute-start.4 = (f32[3,1,40,256]{3,2,1,0:T(8,128)S(1)}, f32[3,1,40,256]{3,2,1,0:T(8,128)S(1)}, u32[]{:S(2)}, u32[]{:S(2)}) collective-permute-start(f32[3,1,40,256]{3,2,1,0:T(8,128)S(1)} %get-tuple-element.41), channel_id=1, source_target_pairs={{0,128},{128,256},{256,384},{1,129},{129,257},{257,385},{2,130},{1... | collective-permute-start | bytes 368648 | tf_op jit(solution)/shard_map/ppermute | solution.py:226
  61.2 15.5 %collective-permute-start.5 = (f32[3,1,40,256]{3,2,1,0:T(8,128)S(1)}, f32[3,1,40,256]{3,2,1,0:T(8,128)S(1)}, u32[]{:S(2)}, u32[]{:S(2)}) collective-permute-start(f32[3,1,40,256]{3,2,1,0:T(8,128)S(1)} %get-tuple-element.40), channel_id=1, source_target_pairs={{128,0},{256,128},{384,256},{129,1},{257,129},{385,257},{130,2},{2... | collective-permute-start | bytes 368648 | tf_op jit(solution)/shard_map/ppermute | solution.py:226
  76.7 0.6 copy-start.8
  76.7 0.7 copy-start.9
  80.1 6.5 %collective-permute-start.10 = (f32[3,1,40,256]{3,2,1,0:T(8,128)}, f32[3,1,40,256]{3,2,1,0:T(8,128)S(1)}, u32[]{:S(2)}, u32[]{:S(2)}) collective-permute-start(f32[3,1,40,256]{3,2,1,0:T(8,128)} %get-tuple-element.14), channel_id=1, source_target_pairs={{128,0},{256,128},{384,256},{129,1},{257,129},{385,257},{130,2},{2... | collective-permute-start | bytes 368648 | tf_op jit(solution)/shard_map/ppermute | solution.py:226
  81.4 6.2 %collective-permute-start.9 = (f32[3,1,40,256]{3,2,1,0:T(8,128)}, f32[3,1,40,256]{3,2,1,0:T(8,128)S(1)}, u32[]{:S(2)}, u32[]{:S(2)}) collective-permute-start(f32[3,1,40,256]{3,2,1,0:T(8,128)} %get-tuple-element.13), channel_id=1, source_target_pairs={{0,128},{128,256},{256,384},{1,129},{129,257},{257,385},{2,130},{1... | collective-permute-start | bytes 368648 | tf_op jit(solution)/shard_map/ppermute | solution.py:226
  86.6 1.6 %copy-start.14 = (f32[3,1,40,256]{3,2,1,0:T(8,128)}, f32[3,1,40,256]{3,2,1,0:T(8,128)S(1)}, u32[]{:S(2)}) copy-start(f32[3,1,40,256]{3,2,1,0:T(8,128)S(1)} %collective-permute-done.10.hi_ref) | copy-start | bytes 368644
  87.6 0.6 copy-start.15
  90.9 6.2 %collective-permute-start.11 = (f32[3,1,40,256]{3,2,1,0:T(8,128)}, f32[3,1,40,256]{3,2,1,0:T(8,128)S(1)}, u32[]{:S(2)}, u32[]{:S(2)}) collective-permute-start(f32[3,1,40,256]{3,2,1,0:T(8,128)} %get-tuple-element.16), channel_id=1, source_target_pairs={{0,128},{128,256},{256,384},{1,129},{129,257},{257,385},{2,130},{1... | collective-permute-start | bytes 368648 | tf_op jit(solution)/shard_map/ppermute | solution.py:226
  95.0 5.8 %collective-permute-start.12 = (f32[3,1,40,256]{3,2,1,0:T(8,128)}, f32[3,1,40,256]{3,2,1,0:T(8,128)S(1)}, u32[]{:S(2)}, u32[]{:S(2)}) collective-permute-start(f32[3,1,40,256]{3,2,1,0:T(8,128)} %get-tuple-element.17), channel_id=1, source_target_pairs={{128,0},{256,128},{384,256},{129,1},{257,129},{385,257},{130,2},{2... | collective-permute-start | bytes 368648 | tf_op jit(solution)/shard_map/ppermute | solution.py:226
  97.1 3.7 %copy-start.10 = (f32[3,1,40,256]{3,2,1,0:T(8,128)}, f32[3,1,40,256]{3,2,1,0:T(8,128)S(1)}, u32[]{:S(2)}) copy-start(f32[3,1,40,256]{3,2,1,0:T(8,128)S(1)} %collective-permute-done.11.lo_ref) | copy-start | bytes 368644
  100.8 0.6 copy-start.11
  104.2 5.3 %collective-permute-start.13 = (f32[3,1,40,256]{3,2,1,0:T(8,128)}, f32[3,1,40,256]{3,2,1,0:T(8,128)S(1)}, u32[]{:S(2)}, u32[]{:S(2)}) collective-permute-start(f32[3,1,40,256]{3,2,1,0:T(8,128)} %get-tuple-element.19), channel_id=1, source_target_pairs={{0,128},{128,256},{256,384},{1,129},{129,257},{257,385},{2,130},{1... | collective-permute-start | bytes 368648 | tf_op jit(solution)/shard_map/ppermute | solution.py:226
  107.3 5.8 %collective-permute-start.14 = (f32[3,1,40,256]{3,2,1,0:T(8,128)}, f32[3,1,40,256]{3,2,1,0:T(8,128)S(1)}, u32[]{:S(2)}, u32[]{:S(2)}) collective-permute-start(f32[3,1,40,256]{3,2,1,0:T(8,128)} %get-tuple-element.20), channel_id=1, source_target_pairs={{128,0},{256,128},{384,256},{129,1},{257,129},{385,257},{130,2},{2... | collective-permute-start | bytes 368648 | tf_op jit(solution)/shard_map/ppermute | solution.py:226
  109.5 4.3 %copy-start.12 = (f32[3,1,40,256]{3,2,1,0:T(8,128)}, f32[3,1,40,256]{3,2,1,0:T(8,128)S(1)}, u32[]{:S(2)}) copy-start(f32[3,1,40,256]{3,2,1,0:T(8,128)S(1)} %collective-permute-done.13.lo_ref) | copy-start | bytes 368644
  113.1 0.6 copy-start.13
  119.3 28.4 %all-to-all-start.1 = ((f32[128,1,192]{2,1,0:T(1,128)}), f32[128,1,192]{2,1,0:T(1,128)S(1)}, u32[]{:S(2)}, u32[]{:S(2)}) async-start(f32[128,1,192]{2,1,0:T(1,128)} %reshape.189), calls=%async_computation.1 | async-start | bytes 262144 | tf_op jit(solution)/shard_map/all_to_all | solution.py:93

commit v7 on v6

--- a/solution.py
+++ b/solution.py
@@ -26,55 +26,6 @@
 time_step = 0.05
 
 
-def with_halo(array, sides, width):
-    edges = {}
-    for axis, dim in sides:
-        count, length = (lax.axis_size(axis), array.shape[dim])
-        up = [(i, (i + 1) % count) for i in range(count - 1)]
-        last = lax.slice_in_dim(array, length - width, length, axis=dim)
-        leading = lax.slice_in_dim(array, 0, width, axis=dim)
-        edges[dim] = (
-            lax.ppermute(last, axis, up),
-            lax.ppermute(leading, axis, [(b, a) for a, b in up]),
-        )
-    done = []
-    for _, dim in sides:
-        low, high = edges[dim]
-        around = [(width, width) if d in done else (0, 0) for d in range(array.ndim)]
-        array = jnp.concatenate([jnp.pad(low, around), array, jnp.pad(high, around)], axis=dim)
-        done.append(dim)
-    return array
-
-
-def split_up(array, dim, count):
-    shape = array.shape
-    parts = array.reshape(*shape[:dim], count, shape[dim] // count, *shape[dim + 1 :])
-    return jnp.moveaxis(parts, dim, 0)
-
-
-def summed_on_arrival(array, axis, dim):
-    parts = split_up(array, dim, lax.axis_size(axis))
-    arrived = lax.all_to_all(parts, axis, split_axis=0, concat_axis=0, tiled=True)
-    return arrived.sum(axis=0)
-
-
-def summed_rows(array, axes, dim):
-    far, near = axes
-    own = summed_on_arrival(split_up(array, dim, lax.axis_size(far)), near, dim + 1)
-    return jnp.sum(lax.all_to_all(own, far, 0, 0, tiled=True), axis=0)
-
-
-def picked_on_arrival(array, axis, dim):
-    parts = split_up(array, dim, lax.axis_size(axis))
-    return lax.all_to_all(parts, axis, split_axis=0, concat_axis=0, tiled=True)[0]
-
-
-def picked_rows(array, axes, dim):
-    far, near = axes
-    own = picked_on_arrival(split_up(array, dim, lax.axis_size(far)), near, dim + 1)
-    return lax.all_to_all(own, far, 0, 0, tiled=True)[0]
-
-
 def from_first_region(array):
     count = lax.axis_size("region")
     tile = lax.axis_size(GX) * lax.axis_size(GY)
@@ -84,10 +35,6 @@
     return total
 
 
-def picked(array, axis, root):
-    return lax.dynamic_index_in_dim(lax.all_gather(array, axis), root, 0, keepdims=False)
-
-
 def copy_for_each(array, axis):
     count = lax.axis_size(axis)
     return lax.all_to_all(
@@ -95,76 +42,16 @@
     )
 
 
-def laid_out(parts, dim):
-    shape = list(parts.shape[1:])
-    shape[dim] *= parts.shape[0]
-    return jnp.moveaxis(parts, 0, dim).reshape(shape)
-
-
-def whole_of(array, axes, dim):
-    far, near = axes
-    parts = copy_for_each(copy_for_each(array, far), near)
-    return laid_out(parts.swapaxes(0, 1).reshape(-1, *array.shape), dim)
-
-
 def normalized(vector):
     return vector / jnp.sqrt(jnp.sum(vector * vector, axis=0, keepdims=True))
 
 
-def apply_kernel(matrix, vector):
-    return jnp.stack(
-        [
-            matrix[component, 0] * vector[0]
-            + matrix[component, 1] * vector[1]
-            + matrix[component, 2] * vector[2]
-            for component in range(3)
-        ]
-    )
-
-
-def apply_transposed(matrix, vector):
-    return jnp.stack(
-        [
-            matrix[0, component] * vector[0]
-            + matrix[1, component] * vector[1]
-            + matrix[2, component] * vector[2]
-            for component in range(3)
-        ]
-    )
-
-
-def local_field(padded, exch_kernel):
-    forward = (padded[:, 2:, 1:-1, 1:-1], padded[:, 1:-1, 2:, 1:-1], padded[:, 1:-1, 1:-1, 2:])
-    backward = (padded[:, :-2, 1:-1, 1:-1], padded[:, 1:-1, :-2, 1:-1], padded[:, 1:-1, 1:-1, :-2])
-    summed = apply_kernel(exch_kernel[0], forward[0]) + apply_transposed(
-        exch_kernel[0], backward[0]
-    )
-    for direction in (1, 2):
-        summed = summed + apply_kernel(exch_kernel[direction], forward[direction])
-        summed = summed + apply_transposed(exch_kernel[direction], backward[direction])
-    return summed
-
-
-def metropolis(spins, padded, exch_kernel, film_near, trial_move, uniform_draw, colour_mask):
-    field_sum = local_field(padded, exch_kernel) + coupling_down * film_near
-    proposal = normalized(spins + step_cone * trial_move)
-    change = -jnp.sum((proposal - spins) * field_sum, axis=0) - anisotropy * (
-        proposal[2] * proposal[2] - spins[2] * spins[2]
-    )
-    accept = jnp.exp(jnp.minimum(-inverse_temp * change, 0.0))
-    weight = jax.nn.sigmoid((accept - uniform_draw) / softness)
-    blended = normalized((1.0 - weight) * spins + weight * proposal)
-    return jnp.where(colour_mask[None], blended, spins)
-
-
-def sweep_kernel(step_ref, k_ref, s_ref, lo_ref, hi_ref, film_ref, valid_ref, trial_ref, unif_ref,
+def sweep_kernel(sweep, colour, k_ref, s_ref, lo_ref, hi_ref, film_ref, valid_ref, trial_ref, unif_ref,
                  out_ref, olo_ref, ohi_ref):
     layers, rows_x, rows_y = s_ref.shape[1:]
     row = lax.broadcasted_iota(jnp.int32, (rows_x, rows_y), 0)
     col = lax.broadcasted_iota(jnp.int32, (rows_x, rows_y), 1)
     live = valid_ref[...] > 0.5
-    sweep = step_ref[0]
-    colour = step_ref[1]
     kk = [[[k_ref[d * 9 + a * 3 + b] for b in range(3)] for a in range(3)] for d in range(3)]
     for l in range(layers):
         s = [s_ref[c, l] for c in range(3)]
@@ -212,12 +99,12 @@
     out_shape = (jax.ShapeDtypeStruct(spins.shape, dt), face, face)
     sites = layers * rows_x * rows_y
     return pl.pallas_call(
-        sweep_kernel,
+        functools.partial(sweep_kernel, sweep, colour),
         out_shape=out_shape,
-        in_specs=[smem, smem] + [vmem] * 7,
+        in_specs=[smem] + [vmem] * 7,
         out_specs=tuple([vmem] * 3),
         cost_estimate=pl.CostEstimate(flops=200 * sites, transcendentals=4 * sites, bytes_accessed=4 * 14 * sites),
-    )(jnp.array([sweep, colour], jnp.int32), exch_flat, spins, lo, hi, film_e, valid, trials, uniforms)
+    )(exch_flat, spins, lo, hi, film_e, valid, trials, uniforms)
 
 
 def shift_in(array, axis, from_lower):
@@ -266,7 +153,7 @@
     return array, film
 
 
-def cells_for_sites(patch, rows_x, rows_y, width, wide):
+def cells_for_sites(patch, rows_y, width, wide):
     inner = jnp.repeat(patch[:, 1:-1], K, axis=1)
     rows = jnp.concatenate(
         [inner, jnp.repeat(patch[:, -1:], width, axis=1), jnp.repeat(patch[:, :1], width, axis=1)], axis=1
@@ -304,11 +191,7 @@
     return -(precession + damping * relaxation) / (1.0 + damping * damping)
 
 
-def film_halo(magnet):
-    return with_halo(magnet, ((REGION_GX, 1), (GY, 2)), 1)
-
-
-def body(spins, uniforms, trials, exch_kernel, film_m, film_anis):
+def step_body(spins, uniforms, trials, exch_kernel, film_m, film_anis):
     layers_dev = spins.shape[1]
     rows_x = spins.shape[2]
     rows_y = spins.shape[3]
@@ -350,7 +233,7 @@
     pieces = tiles.reshape(tile_count, 3, piece_x + 2, piece_y + 2)
     pieces = from_first_region(jnp.where(first_tile, pieces, 0.0))
     own_patch = lax.all_to_all(pieces, GX + GY, 0, 0, tiled=True)[0]
-    film_e = cells_for_sites(own_patch, rows_x, rows_y, width, wide)
+    film_e = cells_for_sites(own_patch, rows_y, width, wide)
     exch_flat = exch_kernel.reshape(-1)
     channels = jnp.concatenate(
         [stack_spins, trial_all.reshape(-1, layers_dev, rows_x, rows_y), unif_all], axis=0
@@ -423,4 +306,4 @@
         P(REGION_GX, GY),
     )
     out_specs = (P(None, "region", GX, GY), P(None, REGION_GX, GY))
-    return jax.shard_map(body, mesh=finer, in_specs=in_specs, out_specs=out_specs, check_vma=False)
+    return jax.shard_map(step_body, mesh=finer, in_specs=in_specs, out_specs=out_specs, check_vma=False)

time: 155 us -> 155 us (level)
    unnamed x41, local copies, waits for them, and re-layouts: 4.47 us -> 6.3 us
    another operation x4 -> x1, local copies, waits for them, and re-layouts: 2.26 us -> 0.43 us  [step_body(): stack_spins[:, 0].reshape(3, piece_x, K, piece_y, K).mean(axis=(2, 4))]
where the time goes in v7:
time: 155 us; the launch traced here: 154 us
  starting transfers between devices  65.4 us (42%)
  waiting for transfers between devices  43.9 us (28%)
  local copies, waits for them, and re-layouts  20.4 us (13%)
  other arithmetic  11.9 us (8%)
  Pallas kernels  10.8 us (7%)
    ppermute x12, starting transfers between devices, shift_in(): lax.ppermute(array, axis, up if from_lower else [(b, a) for a, b in up])  38.2 us
    ppermute x12, waiting for transfers between devices, shift_in(): lax.ppermute(array, axis, up if from_lower else [(b, a) for a, b in up])  18.7 us
    all_to_all x1, waiting for transfers between devices, copy_for_each(): lax.all_to_all(jnp.broadcast_to(array[None], (count, *array.shape)), axis...  14.4 us
    all_to_all x1, starting transfers between devices, copy_for_each(): lax.all_to_all(jnp.broadcast_to(array[None], (count, *array.shape)), axis...  12.4 us
    all_to_all x1, starting transfers between devices, step_body(): own_patch = lax.all_to_all(pieces, GX + GY, 0, 0, tiled=True)[0]  11.5 us
    pallas_call x4, Pallas kernels, half_sweep(): pl.pallas_call(functools.partial(sweep_kernel, sweep, colour), out_shape=...  10.8 us
    all_to_all x1, waiting for transfers between devices, step_body(): own_patch = lax.all_to_all(pieces, GX + GY, 0, 0, tiled=True)[0]  10.8 us
    unnamed x41, local copies, waits for them, and re-layouts  6.3 us
  transfers between devices with their start and end apart: 17, of which 10 were waited for; matrix products, arithmetic and copies ran while one was open for 8% of the time, Pallas kernels for 0%

profile of v7, /device:TPU:1, one launch (start us, length us, event | category | flops | bytes accessed | tf_op | source)
XLA Modules:
  0.0 153.8 jit_solution(16065984527464010085)
XLA Ops:
  0.6 0.9 slice.284
  2.1 1.5 fusion.45
  3.5 1.9 %fusion.1 = f32[128,3,6,18]{3,0,2,1:T(8,128)S(1)} fusion(f32[16,7,3,6,1]{4,1,0,3,2:T(8,128)} %get-tuple-element.39, f32[16,7,3,6,1]{4,1,0,3,2:T(8,128)S(1)} %get-tuple-element.38, f32[16,8,3,1,16]{4,1,0,3,2:T(8,128)S(1)} %concatenate.70, f32[16,8,3,4,16]{4,1,0,3,2:T(8,128)S(1)} %bitcast.223, f32[16,8,3,1,16]{4,1,0,3,2:T(8,128)S(1)} %concatenate.69, pred[]{:T(512)S(6)} %and.46), kind=kLoop, calls=%fused_computation.2 | loop fusion | flops 373248 | bytes 329473 | tf_op jit(solution)/shard_map/jit(_where)/select_n | solution.py:234
  5.9 0.7 collective-permute-start.6
  6.6 1.3 collective-permute-start.7
  8.0 1.3 collective-permute-start.8
  9.4 11.5 %collective-permute-start.1 = (f32[13312]{0:T(1024)S(1)}, f32[13312]{0:T(1024)S(1)}, u32[]{:S(2)}, u32[]{:S(2)}) collective-permute-start(f32[13312]{0:T(1024)S(1)} %pad_maximum_fusion.16), channel_id=1, source_target_pairs={{0,8},{8,16},{16,24},{24,32},{32,40},{40,48},{48,56},{56,64},{64,7... | collective-permute-start | bytes 159752 | tf_op jit(solution)/shard_map/ppermute | solution.py:113
  20.9 1.3 collective-permute-start
  22.5 8.4 %collective-permute-done = f32[13312]{0:T(1024)S(1)} collective-permute-done((f32[13312]{0:T(1024)S(1)}, f32[13312]{0:T(1024)S(1)}, u32[]{:S(2)}, u32[]{:S(2)}) %collective-permute-start) | collective-permute-done | bytes 53280 | tf_op jit(solution)/shard_map/ppermute | solution.py:113
  32.1 3.4 %collective-permute-start.2 = (f32[4576]{0:T(1024)S(1)}, f32[4576]{0:T(1024)S(1)}, u32[]{:S(2)}, u32[]{:S(2)}) collective-permute-start(f32[4576]{0:T(1024)S(1)} %pad_maximum_fusion.20), channel_id=1, source_target_pairs={{1,0},{2,1},{3,2},{4,3},{5,4},{6,5},{7,6},{9,8},{10,9},{11,10},{12... | collective-permute-start | bytes 54920 | tf_op jit(solution)/shard_map/ppermute | solution.py:113
  36.2 2.9 %collective-permute-start.3 = (f32[4576]{0:T(1024)S(1)}, f32[4576]{0:T(1024)S(1)}, u32[]{:S(2)}, u32[]{:S(2)}) collective-permute-start(f32[4576]{0:T(1024)S(1)} %pad_maximum_fusion.21), channel_id=1, source_target_pairs={{0,1},{1,2},{2,3},{3,4},{4,5},{5,6},{6,7},{8,9},{9,10},{10,11},{11... | collective-permute-start | bytes 54920 | tf_op jit(solution)/shard_map/ppermute | solution.py:113
  39.2 0.7 and_convert_fusion.valid_ref
  39.9 0.7 reshape.161.k_ref
  41.4 1.1 add_add_fusion
  43.1 1.5 reshape.187
  44.6 11.5 %all-to-all-start = ((f32[128,1,324]{2,1,0:T(1,128)}), f32[128,1,324]{2,1,0:T(1,128)S(1)}, u32[]{:S(2)}, u32[]{:S(2)}) async-start(f32[128,1,324]{2,1,0:T(1,128)} %reshape.187), calls=%async_computation | async-start | bytes 393216 | tf_op jit(solution)/shard_map/all_to_all | solution.py:235
  56.4 0.8 slice.356
  57.2 0.7 slice.357.unif_ref
  57.9 0.7 slice.342.s_ref
  58.6 2.6 %collective-permute-start.4 = (f32[3,1,40,256]{3,2,1,0:T(8,128)S(1)}, f32[3,1,40,256]{3,2,1,0:T(8,128)S(1)}, u32[]{:S(2)}, u32[]{:S(2)}) collective-permute-start(f32[3,1,40,256]{3,2,1,0:T(8,128)S(1)} %get-tuple-element.41), channel_id=1, source_target_pairs={{0,128},{128,256},{256,384},{1,129},{129,257},{257,385},{2,130},{1... | collective-permute-start | bytes 368648 | tf_op jit(solution)/shard_map/ppermute | solution.py:113
  61.2 1.3 collective-permute-start.5
  62.5 10.8 %all-to-all-done = f32[128,1,324]{2,1,0:T(1,128)S(1)} async-done(((f32[128,1,324]{2,1,0:T(1,128)}), f32[128,1,324]{2,1,0:T(1,128)S(1)}, u32[]{:S(2)}, u32[]{:S(2)}) %all-to-all-start) | async-done | bytes 165920 | tf_op jit(solution)/shard_map/all_to_all | solution.py:235
  73.8 1.0 reduce.4
  76.0 0.7 pad_maximum_fusion.13.film_ref
  77.4 2.7 %shard_map.77 = (f32[3,2,40,256]{3,2,1,0:T(8,128)}, f32[3,1,40,256]{3,2,1,0:T(8,128)}, f32[3,1,40,256]{3,2,1,0:T(8,128)}) custom-call(f32[27]{0:T(128)} %reshape.161.k_ref, f32[3,2,40,256]{3,2,1,0:T(8,128)} %slice.342.s_ref, f32[3,1,40,256]{3,2,1,0:T(8,128)} %copy-done.8, f32[3,1,40,256]{3,2,1,0:T(8,128)} %copy-done.9, ...), custom_call_target="tpu_custom_call" | custom-call | flops 4096000 | bytes 1146880 | tf_op jit(solution)/shard_map/pallas_call | solution.py:101
  80.1 1.3 collective-permute-start.10
  81.4 4.0 %collective-permute-start.9 = (f32[3,1,40,256]{3,2,1,0:T(8,128)}, f32[3,1,40,256]{3,2,1,0:T(8,128)S(1)}, u32[]{:S(2)}, u32[]{:S(2)}) collective-permute-start(f32[3,1,40,256]{3,2,1,0:T(8,128)} %get-tuple-element.13), channel_id=1, source_target_pairs={{0,128},{128,256},{256,384},{1,129},{129,257},{257,385},{2,130},{1... | collective-permute-start | bytes 368648 | tf_op jit(solution)/shard_map/ppermute | solution.py:113
  85.4 1.2 collective-permute-done.10.hi_ref
  86.6 1.0 collective-permute-done.9.lo_ref
  87.6 0.6 copy-done.15
  88.2 2.7 %shard_map.78 = (f32[3,2,40,256]{3,2,1,0:T(8,128)}, f32[3,1,40,256]{3,2,1,0:T(8,128)}, f32[3,1,40,256]{3,2,1,0:T(8,128)}) custom-call(f32[27]{0:T(128)} %reshape.161.k_ref, f32[3,2,40,256]{3,2,1,0:T(8,128)} %get-tuple-element.12.s_ref, f32[3,1,40,256]{3,2,1,0:T(8,128)} %copy-done.15, f32[3,1,40,256]{3,2,1,0:T(8,128)} %copy-done.14, ...), custom_call_target="tpu_custom_call" | custom-call | flops 4096000 | bytes 1146880 | tf_op jit(solution)/shard_map/pallas_call | solution.py:101
  90.9 4.0 %collective-permute-start.11 = (f32[3,1,40,256]{3,2,1,0:T(8,128)}, f32[3,1,40,256]{3,2,1,0:T(8,128)S(1)}, u32[]{:S(2)}, u32[]{:S(2)}) collective-permute-start(f32[3,1,40,256]{3,2,1,0:T(8,128)} %get-tuple-element.16), channel_id=1, source_target_pairs={{0,128},{128,256},{256,384},{1,129},{129,257},{257,385},{2,130},{1... | collective-permute-start | bytes 368648 | tf_op jit(solution)/shard_map/ppermute | solution.py:113
  95.0 1.3 collective-permute-start.12
  97.1 3.7 %collective-permute-done.12.hi_ref = f32[3,1,40,256]{3,2,1,0:T(8,128)S(1)} collective-permute-done((f32[3,1,40,256]{3,2,1,0:T(8,128)}, f32[3,1,40,256]{3,2,1,0:T(8,128)S(1)}, u32[]{:S(2)}, u32[]{:S(2)}) %collective-permute-start.12) | collective-permute-done | bytes 122912 | tf_op jit(solution)/shard_map/ppermute | solution.py:113
  100.8 0.6 copy-done.11
  101.4 2.7 %shard_map.79 = (f32[3,2,40,256]{3,2,1,0:T(8,128)}, f32[3,1,40,256]{3,2,1,0:T(8,128)}, f32[3,1,40,256]{3,2,1,0:T(8,128)}) custom-call(f32[27]{0:T(128)} %reshape.161.k_ref, f32[3,2,40,256]{3,2,1,0:T(8,128)} %get-tuple-element.15.s_ref, f32[3,1,40,256]{3,2,1,0:T(8,128)} %copy-done.10, f32[3,1,40,256]{3,2,1,0:T(8,128)} %copy-done.11, ...), custom_call_target="tpu_custom_call" | custom-call | flops 4096000 | bytes 1146880 | tf_op jit(solution)/shard_map/pallas_call | solution.py:101
  104.1 3.1 %collective-permute-start.13 = (f32[3,1,40,256]{3,2,1,0:T(8,128)}, f32[3,1,40,256]{3,2,1,0:T(8,128)S(1)}, u32[]{:S(2)}, u32[]{:S(2)}) collective-permute-start(f32[3,1,40,256]{3,2,1,0:T(8,128)} %get-tuple-element.19), channel_id=1, source_target_pairs={{0,128},{128,256},{256,384},{1,129},{129,257},{257,385},{2,130},{1... | collective-permute-start | bytes 368648 | tf_op jit(solution)/shard_map/ppermute | solution.py:113
  107.3 1.5 collective-permute-start.14
  109.4 3.7 %collective-permute-done.14.hi_ref = f32[3,1,40,256]{3,2,1,0:T(8,128)S(1)} collective-permute-done((f32[3,1,40,256]{3,2,1,0:T(8,128)}, f32[3,1,40,256]{3,2,1,0:T(8,128)S(1)}, u32[]{:S(2)}, u32[]{:S(2)}) %collective-permute-start.14) | collective-permute-done | bytes 122912 | tf_op jit(solution)/shard_map/ppermute | solution.py:113
  113.8 2.7 %shard_map.80 = (f32[3,2,40,256]{3,2,1,0:T(8,128)}, f32[3,1,40,256]{3,2,1,0:T(8,128)}, f32[3,1,40,256]{3,2,1,0:T(8,128)}) custom-call(f32[27]{0:T(128)} %reshape.161.k_ref, f32[3,2,40,256]{3,2,1,0:T(8,128)} %get-tuple-element.18.s_ref, f32[3,1,40,256]{3,2,1,0:T(8,128)} %copy-done.12, f32[3,1,40,256]{3,2,1,0:T(8,128)} %copy-done.13, ...), custom_call_target="tpu_custom_call" | custom-call | flops 4096000 | bytes 1146880 | tf_op jit(solution)/shard_map/pallas_call | solution.py:101
  116.5 0.8 slice.311
  118.0 1.3 reshape.189
  119.2 12.4 %all-to-all-start.1 = ((f32[128,1,192]{2,1,0:T(1,128)}), f32[128,1,192]{2,1,0:T(1,128)S(1)}, u32[]{:S(2)}, u32[]{:S(2)}) async-start(f32[128,1,192]{2,1,0:T(1,128)} %reshape.189), calls=%async_computation.1 | async-start | bytes 262144 | tf_op jit(solution)/shard_map/all_to_all | solution.py:40
  131.6 1.5 %slice.302 = f32[3,2,32,128]{3,2,1,0:T(8,128)} slice(f32[3,2,40,256]{3,2,1,0:T(8,128)} %get-tuple-element.21), slice={[0:3], [0:2], [0:32], [0:128]} | slice | bytes 196608 | tf_op jit(solution)/shard_map/slice | solution.py:266
  133.2 14.4 %all-to-all-done.1 = f32[128,1,192]{2,1,0:T(1,128)S(1)} async-done(((f32[128,1,192]{2,1,0:T(1,128)}), f32[128,1,192]{2,1,0:T(1,128)S(1)}, u32[]{:S(2)}, u32[]{:S(2)}) %all-to-all-start.1) | async-done | bytes 98336 | tf_op jit(solution)/shard_map/all_to_all | solution.py:40
  147.6 0.9 reduce.5
  149.4 1.0 fusion.4
  153.0 0.8 broadcast_divide_fusion
  (134 shorter events, 13.1 us)
Async XLA Ops:
  5.5 3.8 %copy-start = (f32[3,128,256]{2,1,0:T(8,128)S(1)}, f32[3,128,256]{2,1,0:T(8,128)}, u32[]{:S(2)}) copy-start(f32[3,128,256]{2,1,0:T(8,128)} %param.10) | copy-start | bytes 1179652
  5.5 3.8 %copy-start.1 = (f32[128,256]{1,0:T(8,128)S(1)}, f32[128,256]{1,0:T(8,128)}, u32[]{:S(2)}) copy-start(f32[128,256]{1,0:T(8,128)} %param.11) | copy-start | bytes 393220
  5.5 3.8 %copy-start.2 = (f32[2,3,2,32,128]{4,3,2,1,0:T(8,128)S(1)}, f32[2,3,2,32,128]{4,3,2,1,0:T(8,128)}, u32[]{:S(2)}) copy-start(f32[2,3,2,32,128]{4,3,2,1,0:T(8,128)} %param.8) | copy-start | bytes 589828
  5.5 3.8 %copy-start.4 = (f32[3,2,32,128]{3,2,1,0:T(8,128)S(1)}, f32[3,2,32,128]{3,2,1,0:T(8,128)}, u32[]{:S(2)}) copy-start(f32[3,2,32,128]{3,2,1,0:T(8,128)} %param.6) | copy-start | bytes 294916
  5.5 3.8 %copy-start.6 = (f32[2,2,32,128]{3,2,1,0:T(8,128)S(1)}, f32[2,2,32,128]{3,2,1,0:T(8,128)}, u32[]{:S(2)}) copy-start(f32[2,2,32,128]{3,2,1,0:T(8,128)} %param.7) | copy-start | bytes 196612
  5.9 35.4 %collective-permute-start.6 = (f32[128,3,6,18]{0,3,2,1:T(8,128)S(1)}, f32[128,3,6,18]{0,3,2,1:T(8,128)S(1)}, u32[]{:S(2)}, u32[]{:S(2)}) collective-permute-start(f32[128,3,6,18]{0,3,2,1:T(8,128)S(1)} %copy.108), channel_id=1, source_target_pairs={{0,128}} | collective-permute-start | bytes 497672 | tf_op jit(solution)/shard_map/ppermute | solution.py:34
  6.6 34.7 %collective-permute-start.7 = (f32[128,3,6,18]{0,3,2,1:T(8,128)S(1)}, f32[128,3,6,18]{0,3,2,1:T(8,128)}, u32[]{:S(2)}, u32[]{:S(2)}) collective-permute-start(f32[128,3,6,18]{0,3,2,1:T(8,128)S(1)} %copy.108), channel_id=1, source_target_pairs={{0,256}} | collective-permute-start | bytes 497672 | tf_op jit(solution)/shard_map/ppermute | solution.py:34
  8.0 33.4 %collective-permute-start.8 = (f32[128,3,6,18]{0,3,2,1:T(8,128)S(1)}, f32[128,3,6,18]{0,3,2,1:T(8,128)}, u32[]{:S(2)}, u32[]{:S(2)}) collective-permute-start(f32[128,3,6,18]{0,3,2,1:T(8,128)S(1)} %copy.108), channel_id=1, source_target_pairs={{0,384}} | collective-permute-start | bytes 497672 | tf_op jit(solution)/shard_map/ppermute | solution.py:34
  9.4 13.1 %collective-permute-start.1 = (f32[13312]{0:T(1024)S(1)}, f32[13312]{0:T(1024)S(1)}, u32[]{:S(2)}, u32[]{:S(2)}) collective-permute-start(f32[13312]{0:T(1024)S(1)} %pad_maximum_fusion.16), channel_id=1, source_target_pairs={{0,8},{8,16},{16,24},{24,32},{32,40},{40,48},{48,56},{56,64},{64,7... | collective-permute-start | bytes 159752 | tf_op jit(solution)/shard_map/ppermute | solution.py:113
  20.9 10.1 %collective-permute-start = (f32[13312]{0:T(1024)S(1)}, f32[13312]{0:T(1024)S(1)}, u32[]{:S(2)}, u32[]{:S(2)}) collective-permute-start(f32[13312]{0:T(1024)S(1)} %pad_maximum_fusion.15), channel_id=1, source_target_pairs={{8,0},{16,8},{24,16},{32,24},{40,32},{48,40},{56,48},{64,56},{72,6... | collective-permute-start | bytes 159752 | tf_op jit(solution)/shard_map/ppermute | solution.py:113
  31.6 8.2 %copy-start.16 = (f32[3,3,3]{2,1,0:T(4,128)S(1)}, f32[3,3,3]{2,1,0:T(4,128)}, u32[]{:S(2)}) copy-start(f32[3,3,3]{2,1,0:T(4,128)} %param.9) | copy-start | bytes 328
  32.1 8.5 %collective-permute-start.2 = (f32[4576]{0:T(1024)S(1)}, f32[4576]{0:T(1024)S(1)}, u32[]{:S(2)}, u32[]{:S(2)}) collective-permute-start(f32[4576]{0:T(1024)S(1)} %pad_maximum_fusion.20), channel_id=1, source_target_pairs={{1,0},{2,1},{3,2},{4,3},{5,4},{6,5},{7,6},{9,8},{10,9},{11,10},{12... | collective-permute-start | bytes 54920 | tf_op jit(solution)/shard_map/ppermute | solution.py:113
  36.2 4.8 %collective-permute-start.3 = (f32[4576]{0:T(1024)S(1)}, f32[4576]{0:T(1024)S(1)}, u32[]{:S(2)}, u32[]{:S(2)}) collective-permute-start(f32[4576]{0:T(1024)S(1)} %pad_maximum_fusion.21), channel_id=1, source_target_pairs={{0,1},{1,2},{2,3},{3,4},{4,5},{5,6},{6,7},{8,9},{9,10},{10,11},{11... | collective-permute-start | bytes 54920 | tf_op jit(solution)/shard_map/ppermute | solution.py:113
  43.0 13.1 %copy-start.3 = (f32[2,3,2,32,128]{4,3,2,1,0:T(8,128)S(1)}, f32[2,3,2,32,128]{4,3,2,1,0:T(8,128)}, u32[]{:S(2)}) copy-start(f32[2,3,2,32,128]{4,3,2,1,0:T(8,128)} %param.8) | copy-start | bytes 589828
  43.0 13.1 %copy-start.5 = (f32[3,2,32,128]{3,2,1,0:T(8,128)S(1)}, f32[3,2,32,128]{3,2,1,0:T(8,128)}, u32[]{:S(2)}) copy-start(f32[3,2,32,128]{3,2,1,0:T(8,128)} %param.6) | copy-start | bytes 294916
  43.1 13.1 %copy-start.7 = (f32[2,2,32,128]{3,2,1,0:T(8,128)S(1)}, f32[2,2,32,128]{3,2,1,0:T(8,128)}, u32[]{:S(2)}) copy-start(f32[2,2,32,128]{3,2,1,0:T(8,128)} %param.7) | copy-start | bytes 196612
  44.6 28.7 %all-to-all-start = ((f32[128,1,324]{2,1,0:T(1,128)}), f32[128,1,324]{2,1,0:T(1,128)S(1)}, u32[]{:S(2)}, u32[]{:S(2)}) async-start(f32[128,1,324]{2,1,0:T(1,128)} %reshape.187), calls=%async_computation | async-start | bytes 393216 | tf_op jit(solution)/shard_map/all_to_all | solution.py:235
  58.6 18.1 %collective-permute-start.4 = (f32[3,1,40,256]{3,2,1,0:T(8,128)S(1)}, f32[3,1,40,256]{3,2,1,0:T(8,128)S(1)}, u32[]{:S(2)}, u32[]{:S(2)}) collective-permute-start(f32[3,1,40,256]{3,2,1,0:T(8,128)S(1)} %get-tuple-element.41), channel_id=1, source_target_pairs={{0,128},{128,256},{256,384},{1,129},{129,257},{257,385},{2,130},{1... | collective-permute-start | bytes 368648 | tf_op jit(solution)/shard_map/ppermute | solution.py:113
  61.2 15.5 %collective-permute-start.5 = (f32[3,1,40,256]{3,2,1,0:T(8,128)S(1)}, f32[3,1,40,256]{3,2,1,0:T(8,128)S(1)}, u32[]{:S(2)}, u32[]{:S(2)}) collective-permute-start(f32[3,1,40,256]{3,2,1,0:T(8,128)S(1)} %get-tuple-element.40), channel_id=1, source_target_pairs={{128,0},{256,128},{384,256},{129,1},{257,129},{385,257},{130,2},{2... | collective-permute-start | bytes 368648 | tf_op jit(solution)/shard_map/ppermute | solution.py:113
  76.7 0.6 copy-start.8
  76.7 0.7 copy-start.9
  80.1 6.5 %collective-permute-start.10 = (f32[3,1,40,256]{3,2,1,0:T(8,128)}, f32[3,1,40,256]{3,2,1,0:T(8,128)S(1)}, u32[]{:S(2)}, u32[]{:S(2)}) collective-permute-start(f32[3,1,40,256]{3,2,1,0:T(8,128)} %get-tuple-element.14), channel_id=1, source_target_pairs={{128,0},{256,128},{384,256},{129,1},{257,129},{385,257},{130,2},{2... | collective-permute-start | bytes 368648 | tf_op jit(solution)/shard_map/ppermute | solution.py:113
  81.4 6.2 %collective-permute-start.9 = (f32[3,1,40,256]{3,2,1,0:T(8,128)}, f32[3,1,40,256]{3,2,1,0:T(8,128)S(1)}, u32[]{:S(2)}, u32[]{:S(2)}) collective-permute-start(f32[3,1,40,256]{3,2,1,0:T(8,128)} %get-tuple-element.13), channel_id=1, source_target_pairs={{0,128},{128,256},{256,384},{1,129},{129,257},{257,385},{2,130},{1... | collective-permute-start | bytes 368648 | tf_op jit(solution)/shard_map/ppermute | solution.py:113
  86.6 1.0 copy-start.14
  87.6 0.6 copy-start.15
  90.9 6.2 %collective-permute-start.11 = (f32[3,1,40,256]{3,2,1,0:T(8,128)}, f32[3,1,40,256]{3,2,1,0:T(8,128)S(1)}, u32[]{:S(2)}, u32[]{:S(2)}) collective-permute-start(f32[3,1,40,256]{3,2,1,0:T(8,128)} %get-tuple-element.16), channel_id=1, source_target_pairs={{0,128},{128,256},{256,384},{1,129},{129,257},{257,385},{2,130},{1... | collective-permute-start | bytes 368648 | tf_op jit(solution)/shard_map/ppermute | solution.py:113
  95.0 5.8 %collective-permute-start.12 = (f32[3,1,40,256]{3,2,1,0:T(8,128)}, f32[3,1,40,256]{3,2,1,0:T(8,128)S(1)}, u32[]{:S(2)}, u32[]{:S(2)}) collective-permute-start(f32[3,1,40,256]{3,2,1,0:T(8,128)} %get-tuple-element.17), channel_id=1, source_target_pairs={{128,0},{256,128},{384,256},{129,1},{257,129},{385,257},{130,2},{2... | collective-permute-start | bytes 368648 | tf_op jit(solution)/shard_map/ppermute | solution.py:113
  97.1 3.7 %copy-start.10 = (f32[3,1,40,256]{3,2,1,0:T(8,128)}, f32[3,1,40,256]{3,2,1,0:T(8,128)S(1)}, u32[]{:S(2)}) copy-start(f32[3,1,40,256]{3,2,1,0:T(8,128)S(1)} %collective-permute-done.11.lo_ref) | copy-start | bytes 368644
  100.8 0.6 copy-start.11
  104.1 5.3 %collective-permute-start.13 = (f32[3,1,40,256]{3,2,1,0:T(8,128)}, f32[3,1,40,256]{3,2,1,0:T(8,128)S(1)}, u32[]{:S(2)}, u32[]{:S(2)}) collective-permute-start(f32[3,1,40,256]{3,2,1,0:T(8,128)} %get-tuple-element.19), channel_id=1, source_target_pairs={{0,128},{128,256},{256,384},{1,129},{129,257},{257,385},{2,130},{1... | collective-permute-start | bytes 368648 | tf_op jit(solution)/shard_map/ppermute | solution.py:113
  107.3 5.8 %collective-permute-start.14 = (f32[3,1,40,256]{3,2,1,0:T(8,128)}, f32[3,1,40,256]{3,2,1,0:T(8,128)S(1)}, u32[]{:S(2)}, u32[]{:S(2)}) collective-permute-start(f32[3,1,40,256]{3,2,1,0:T(8,128)} %get-tuple-element.20), channel_id=1, source_target_pairs={{128,0},{256,128},{384,256},{129,1},{257,129},{385,257},{130,2},{2... | collective-permute-start | bytes 368648 | tf_op jit(solution)/shard_map/ppermute | solution.py:113
  109.4 3.7 %copy-start.12 = (f32[3,1,40,256]{3,2,1,0:T(8,128)}, f32[3,1,40,256]{3,2,1,0:T(8,128)S(1)}, u32[]{:S(2)}) copy-start(f32[3,1,40,256]{3,2,1,0:T(8,128)S(1)} %collective-permute-done.13.lo_ref) | copy-start | bytes 368644
  113.1 0.6 copy-start.13
  119.2 28.4 %all-to-all-start.1 = ((f32[128,1,192]{2,1,0:T(1,128)}), f32[128,1,192]{2,1,0:T(1,128)S(1)}, u32[]{:S(2)}, u32[]{:S(2)}) async-start(f32[128,1,192]{2,1,0:T(1,128)} %reshape.189), calls=%async_computation.1 | async-start | bytes 262144 | tf_op jit(solution)/shard_map/all_to_all | solution.py:40

commit v8 on v7

--- a/solution.py
+++ b/solution.py
@@ -46,65 +46,76 @@
     return vector / jnp.sqrt(jnp.sum(vector * vector, axis=0, keepdims=True))
 
 
-def sweep_kernel(sweep, colour, k_ref, s_ref, lo_ref, hi_ref, film_ref, valid_ref, trial_ref, unif_ref,
-                 out_ref, olo_ref, ohi_ref):
+def updated(s, below, above, film, trial, unif, chosen, kk):
+    rows_x, rows_y = s[0].shape
+    xp = [pltpu.roll(s[c], rows_x - 1, 0) for c in range(3)]
+    xm = [pltpu.roll(s[c], 1, 0) for c in range(3)]
+    yp = [pltpu.roll(s[c], rows_y - 1, 1) for c in range(3)]
+    ym = [pltpu.roll(s[c], 1, 1) for c in range(3)]
+    fwd = (above, xp, yp)
+    bwd = (below, xm, ym)
+    field = []
+    for c in range(3):
+        total = film[c] * coupling_down
+        for d in range(3):
+            m = kk[d]
+            total = total + (m[c][0] * fwd[d][0] + m[c][1] * fwd[d][1] + m[c][2] * fwd[d][2])
+            total = total + (m[0][c] * bwd[d][0] + m[1][c] * bwd[d][1] + m[2][c] * bwd[d][2])
+        field.append(total)
+    raw = [s[c] + step_cone * trial[c] for c in range(3)]
+    norm = jnp.sqrt(raw[0] * raw[0] + raw[1] * raw[1] + raw[2] * raw[2])
+    prop = [raw[c] / norm for c in range(3)]
+    dot = (prop[0] - s[0]) * field[0] + (prop[1] - s[1]) * field[1] + (prop[2] - s[2]) * field[2]
+    change = -dot - anisotropy * (prop[2] * prop[2] - s[2] * s[2])
+    accept = jnp.exp(jnp.minimum(-inverse_temp * change, 0.0))
+    weight = 1.0 / (1.0 + jnp.exp(-((accept - unif) / softness)))
+    mix = [(1.0 - weight) * s[c] + weight * prop[c] for c in range(3)]
+    mnorm = jnp.sqrt(mix[0] * mix[0] + mix[1] * mix[1] + mix[2] * mix[2])
+    return [jnp.where(chosen, mix[c] / mnorm, s[c]) for c in range(3)]
+
+
+def sweep_kernel(sweep, k_ref, edge_ref, s_ref, b_ref, a_ref, film_ref, valid_ref, trial_ref, unif_ref,
+                 tb_ref, ta_ref, out_ref):
     layers, rows_x, rows_y = s_ref.shape[1:]
     row = lax.broadcasted_iota(jnp.int32, (rows_x, rows_y), 0)
     col = lax.broadcasted_iota(jnp.int32, (rows_x, rows_y), 1)
     live = valid_ref[...] > 0.5
     kk = [[[k_ref[d * 9 + a * 3 + b] for b in range(3)] for a in range(3)] for d in range(3)]
+    film = [film_ref[c] for c in range(3)]
+    halo = b_ref.shape[1]
+    stack = [[b_ref[c, l] for c in range(3)] for l in range(halo)]
+    stack += [[s_ref[c, l] for c in range(3)] for l in range(layers)]
+    stack += [[a_ref[c, l] for c in range(3)] for l in range(halo)]
+    trial = [[tb_ref[3 * sweep + c] for c in range(3)]]
+    trial += [[trial_ref[sweep, c, l] for c in range(3)] for l in range(layers)]
+    trial += [[ta_ref[3 * sweep + c] for c in range(3)]]
+    unif = [tb_ref[3 * SWEEPS + sweep]] + [unif_ref[sweep, l] for l in range(layers)] + [ta_ref[3 * SWEEPS + sweep]]
+    layer_live = [edge_ref[0] > 0.5] + [True] * layers + [edge_ref[1] > 0.5]
+    for colour, first, last in ((0, halo - 1, halo + layers + 1), (1, halo, halo + layers)):
+        new = list(stack)
+        for i in range(first, last):
+            parity = ((row + col + (i - halo) + 2) % 2) == colour
+            chosen = parity & live & layer_live[i - halo + 1]
+            j = i - (halo - 1)
+            new[i] = updated(stack[i], stack[i - 1], stack[i + 1], film, trial[j], unif[j], chosen, kk)
+        stack = new
     for l in range(layers):
-        s = [s_ref[c, l] for c in range(3)]
-        below = [lo_ref[c, 0] if l == 0 else s_ref[c, l - 1] for c in range(3)]
-        above = [hi_ref[c, 0] if l == layers - 1 else s_ref[c, l + 1] for c in range(3)]
-        xp = [pltpu.roll(s[c], rows_x - 1, 0) for c in range(3)]
-        xm = [pltpu.roll(s[c], 1, 0) for c in range(3)]
-        yp = [pltpu.roll(s[c], rows_y - 1, 1) for c in range(3)]
-        ym = [pltpu.roll(s[c], 1, 1) for c in range(3)]
-        fwd = (above, xp, yp)
-        bwd = (below, xm, ym)
-        field = []
         for c in range(3):
-            total = film_ref[c] * coupling_down
-            for d in range(3):
-                m = kk[d]
-                total = total + (m[c][0] * fwd[d][0] + m[c][1] * fwd[d][1] + m[c][2] * fwd[d][2])
-                total = total + (m[0][c] * bwd[d][0] + m[1][c] * bwd[d][1] + m[2][c] * bwd[d][2])
-            field.append(total)
-        raw = [s[c] + step_cone * trial_ref[sweep, c, l] for c in range(3)]
-        norm = jnp.sqrt(raw[0] * raw[0] + raw[1] * raw[1] + raw[2] * raw[2])
-        prop = [raw[c] / norm for c in range(3)]
-        dot = (prop[0] - s[0]) * field[0] + (prop[1] - s[1]) * field[1] + (prop[2] - s[2]) * field[2]
-        change = -dot - anisotropy * (prop[2] * prop[2] - s[2] * s[2])
-        accept = jnp.exp(jnp.minimum(-inverse_temp * change, 0.0))
-        weight = 1.0 / (1.0 + jnp.exp(-((accept - unif_ref[sweep, l]) / softness)))
-        mix = [(1.0 - weight) * s[c] + weight * prop[c] for c in range(3)]
-        mnorm = jnp.sqrt(mix[0] * mix[0] + mix[1] * mix[1] + mix[2] * mix[2])
-        chosen = (((row + col + l) % 2) == colour) & live
-        for c in range(3):
-            new = jnp.where(chosen, mix[c] / mnorm, s[c])
-            out_ref[c, l] = new
-            if l == 0:
-                olo_ref[c, 0] = new
-            if l == layers - 1:
-                ohi_ref[c, 0] = new
-
-
-def half_sweep(spins, lo, hi, exch_flat, film_e, valid, trials, uniforms, sweep, colour):
-    comps, layers, rows_x, rows_y = spins.shape
+            out_ref[c, l] = stack[halo + l][c]
+
+
+def sweep_pair(spins, below, above, exch_flat, edge, film_e, valid, trials, uniforms, tb, ta, sweep):
+    _, layers, rows_x, rows_y = spins.shape
     vmem = pl.BlockSpec(memory_space=pltpu.VMEM)
     smem = pl.BlockSpec(memory_space=pltpu.SMEM)
-    dt = spins.dtype
-    face = jax.ShapeDtypeStruct((comps, 1, rows_x, rows_y), dt)
-    out_shape = (jax.ShapeDtypeStruct(spins.shape, dt), face, face)
     sites = layers * rows_x * rows_y
     return pl.pallas_call(
-        functools.partial(sweep_kernel, sweep, colour),
-        out_shape=out_shape,
-        in_specs=[smem] + [vmem] * 7,
-        out_specs=tuple([vmem] * 3),
-        cost_estimate=pl.CostEstimate(flops=200 * sites, transcendentals=4 * sites, bytes_accessed=4 * 14 * sites),
-    )(exch_flat, spins, lo, hi, film_e, valid, trials, uniforms)
+        functools.partial(sweep_kernel, sweep),
+        out_shape=jax.ShapeDtypeStruct(spins.shape, spins.dtype),
+        in_specs=[smem, smem] + [vmem] * 9,
+        out_specs=vmem,
+        cost_estimate=pl.CostEstimate(flops=600 * sites, transcendentals=12 * sites, bytes_accessed=4 * 30 * sites),
+    )(exch_flat, edge, spins, below, above, film_e, valid, trials, uniforms, tb, ta)
 
 
 def shift_in(array, axis, from_lower):
@@ -254,15 +265,17 @@
     valid_x = (global_x >= 0) & (global_x < rows_x * gx_count)
     valid_y = real_y & (global_y >= 0) & (global_y < rows_y * gy_count)
     valid = (valid_x[:, None] & valid_y[None, :]).astype(jnp.float32)
-    lo = spins_e[:, :1]
-    hi = spins_e[:, -1:]
+    region_count = lax.axis_size("region")
+    edge = jnp.stack([region_pos > 0, region_pos < region_count - 1]).astype(jnp.float32)
+    draws = jnp.concatenate([trials_e.reshape(3 * SWEEPS, layers_dev, ext_x, wide), unif_e], axis=0)
+    tb = shift_in(draws[:, -1], "region", True)
+    ta = shift_in(draws[:, 0], "region", False)
     for sweep_index in range(SWEEPS):
-        for colour in (0, 1):
-            below = shift_in(hi, "region", True)
-            above = shift_in(lo, "region", False)
-            spins_e, lo, hi = half_sweep(
-                spins_e, below, above, exch_flat, film_e, valid, trials_e, unif_e, sweep_index, colour
-            )
+        below = shift_in(spins_e, "region", True)
+        above = shift_in(spins_e, "region", False)
+        spins_e = sweep_pair(
+            spins_e, below, above, exch_flat, edge, film_e, valid, trials_e, unif_e, tb, ta, sweep_index
+        )
     stack_spins = spins_e[:, :, :rows_x, :rows_y]
     averages = stack_spins[:, 0].reshape(3, piece_x, K, piece_y, K).mean(axis=(2, 4))
     gathered = copy_for_each(averages, GX + GY)

time: 155 us -> 141 us (0.910)
  waiting for transfers between devices: 43.9 us -> 30.5 us
  local copies, waits for them, and re-layouts: 20.4 us -> 23.6 us
  Pallas kernels: 10.8 us -> 8.37 us
    all_to_all x1, waiting for transfers between devices: 10.8 us -> 2.3 us  [step_body(): own_patch = lax.all_to_all(pieces, GX + GY, 0, 0, tiled=True)[0]]
    ppermute x12 -> x10, waiting for transfers between devices: 18.7 us -> 13.8 us  [shift_in(): lax.ppermute(array, axis, up if from_lower else [(b, a) for a, b in up])]
    ppermute x12 -> x10, starting transfers between devices: 38.2 us -> 34.2 us  [shift_in(): lax.ppermute(array, axis, up if from_lower else [(b, a) for a, b in up])]
    all_to_all x1, starting transfers between devices: 12.4 us -> 15.5 us  [copy_for_each(): lax.all_to_all(jnp.broadcast_to(array[None], (count, *array.shape)), axis...]
    pallas_call x4 -> x2, Pallas kernels: 10.8 us -> 8.37 us  [sweep_pair(): pl.pallas_call(functools.partial(sweep_kernel, sweep), out_shape=jax.Shap...]
    unnamed x41 -> x36, local copies, waits for them, and re-layouts: 6.3 us -> 6.55 us
  transfers between devices with their start and end apart: 17 -> 15, of which waited for: 10 -> 6; matrix products, arithmetic and copies ran while one was open for 8% -> 11% of each run, Pallas kernels for 0% -> 0%
where the time goes in v8:
time: 141 us; the launch traced here: 140 us
  starting transfers between devices  64 us (45%)
  waiting for transfers between devices  30.5 us (22%)
  local copies, waits for them, and re-layouts  23.6 us (17%)
  other arithmetic  12.5 us (9%)
  Pallas kernels  8.37 us (6%)
  between operations  1.47 us (1%)
    ppermute x10, starting transfers between devices, shift_in(): lax.ppermute(array, axis, up if from_lower else [(b, a) for a, b in up])  34.2 us
    all_to_all x1, starting transfers between devices, copy_for_each(): lax.all_to_all(jnp.broadcast_to(array[None], (count, *array.shape)), axis...  15.5 us
    all_to_all x1, waiting for transfers between devices, copy_for_each(): lax.all_to_all(jnp.broadcast_to(array[None], (count, *array.shape)), axis...  14.4 us
    ppermute x10, waiting for transfers between devices, shift_in(): lax.ppermute(array, axis, up if from_lower else [(b, a) for a, b in up])  13.8 us
    all_to_all x1, starting transfers between devices, step_body(): own_patch = lax.all_to_all(pieces, GX + GY, 0, 0, tiled=True)[0]  11.6 us
    pallas_call x2, Pallas kernels, sweep_pair(): pl.pallas_call(functools.partial(sweep_kernel, sweep), out_shape=jax.Shap...  8.37 us
    unnamed x36, local copies, waits for them, and re-layouts  6.55 us
  transfers between devices with their start and end apart: 15, of which 6 were waited for; matrix products, arithmetic and copies ran while one was open for 11% of the time, Pallas kernels for 0%

profile of v8, /device:TPU:1, one launch (start us, length us, event | category | flops | bytes accessed | tf_op | source)
XLA Modules:
  0.0 140.4 jit_solution(17579013804642577319)
XLA Ops:
  0.7 0.9 slice.283
  2.1 1.5 %fusion.45 = (f32[16,7,3,6,1]{4,1,0,3,2:T(8,128)S(1)}, f32[16,7,3,6,1]{4,1,0,3,2:T(8,128)}) fusion(f32[16,8,3,6,16]{4,1,0,3,2:T(8,128)S(1)} %pad_maximum_fusion), kind=kLoop, calls=%fused_computation.133 | loop fusion | bytes 32256 | tf_op jit(solution)/shard_map/slice | solution.py:238
  3.5 1.9 %fusion.1 = f32[128,3,6,18]{3,0,2,1:T(8,128)S(1)} fusion(f32[16,7,3,6,1]{4,1,0,3,2:T(8,128)} %get-tuple-element.19, f32[16,7,3,6,1]{4,1,0,3,2:T(8,128)S(1)} %get-tuple-element.18, f32[16,8,3,1,16]{4,1,0,3,2:T(8,128)S(1)} %concatenate.71, f32[16,8,3,4,16]{4,1,0,3,2:T(8,128)S(1)} %bitcast.225, f32[16,8,3,1,16]{4,1,0,3,2:T(8,128)S(1)} %concatenate.70, pred[]{:T(512)S(6)} %and.46), kind=kLoop, calls=%fused_computation.2 | loop fusion | flops 373248 | bytes 329473 | tf_op jit(solution)/shard_map/jit(_where)/select_n | solution.py:245
  5.9 0.7 collective-permute-start.6
  6.6 0.7 collective-permute-start.7
  7.3 1.4 collective-permute-start.8
  8.8 11.5 %collective-permute-start.1 = (f32[13312]{0:T(1024)S(1)}, f32[13312]{0:T(1024)S(1)}, u32[]{:S(2)}, u32[]{:S(2)}) collective-permute-start(f32[13312]{0:T(1024)S(1)} %pad_maximum_fusion.16), channel_id=1, source_target_pairs={{0,8},{8,16},{16,24},{24,32},{32,40},{40,48},{48,56},{56,64},{64,7... | collective-permute-start | bytes 159752 | tf_op jit(solution)/shard_map/ppermute | solution.py:124
  20.3 1.3 collective-permute-start
  21.6 0.7 and_convert_fusion.valid_ref
  22.3 8.6 %collective-permute-done = f32[13312]{0:T(1024)S(1)} collective-permute-done((f32[13312]{0:T(1024)S(1)}, f32[13312]{0:T(1024)S(1)}, u32[]{:S(2)}, u32[]{:S(2)}) %collective-permute-start) | collective-permute-done | bytes 53280 | tf_op jit(solution)/shard_map/ppermute | solution.py:124
  32.1 3.1 %collective-permute-start.2 = (f32[4576]{0:T(1024)S(1)}, f32[4576]{0:T(1024)S(1)}, u32[]{:S(2)}, u32[]{:S(2)}) collective-permute-start(f32[4576]{0:T(1024)S(1)} %pad_maximum_fusion.20), channel_id=1, source_target_pairs={{1,0},{2,1},{3,2},{4,3},{5,4},{6,5},{7,6},{9,8},{10,9},{11,10},{12... | collective-permute-start | bytes 54920 | tf_op jit(solution)/shard_map/ppermute | solution.py:124
  35.9 2.7 %collective-permute-start.3 = (f32[4576]{0:T(1024)S(1)}, f32[4576]{0:T(1024)S(1)}, u32[]{:S(2)}, u32[]{:S(2)}) collective-permute-start(f32[4576]{0:T(1024)S(1)} %pad_maximum_fusion.21), channel_id=1, source_target_pairs={{0,1},{1,2},{2,3},{3,4},{4,5},{5,6},{6,7},{8,9},{9,10},{10,11},{11... | collective-permute-start | bytes 54920 | tf_op jit(solution)/shard_map/ppermute | solution.py:124
  39.1 0.7 reshape.161.k_ref
  40.7 0.7 copy-done.10
  41.3 1.1 add_add_fusion
  43.0 1.5 %reshape.187 = f32[128,1,324]{2,1,0:T(1,128)} reshape(f32[128,3,6,18]{3,2,1,0:T(8,128)S(1)} %copy.198) | data formatting | bytes 331776
  44.6 11.6 %all-to-all-start = ((f32[128,1,324]{2,1,0:T(1,128)}), f32[128,1,324]{2,1,0:T(1,128)S(1)}, u32[]{:S(2)}, u32[]{:S(2)}) async-start(f32[128,1,324]{2,1,0:T(1,128)} %reshape.187), calls=%async_computation | async-start | bytes 393216 | tf_op jit(solution)/shard_map/all_to_all | solution.py:246
  56.4 2.6 %collective-permute-start.4 = (f32[3,2,40,256]{3,2,0,1:T(8,128)S(1)}, f32[3,2,40,256]{3,2,0,1:T(8,128)S(1)}, u32[]{:S(2)}, u32[]{:S(2)}) collective-permute-start(f32[3,2,40,256]{3,2,0,1:T(8,128)S(1)} %slice.343), channel_id=1, source_target_pairs={{0,128},{128,256},{256,384},{1,129},{129,257},{257,385},{2,130},{1... | collective-permute-start | bytes 737288 | tf_op jit(solution)/shard_map/ppermute | solution.py:124
  59.1 1.3 collective-permute-start.5
  60.4 0.7 copy.201.s_ref
  61.1 0.8 slice_bitcast_fusion.2
  61.9 1.3 collective-permute-start.10
  63.2 4.9 %collective-permute-start.9 = (f32[8,40,256]{2,1,0:T(8,128)S(1)}, f32[8,40,256]{2,1,0:T(8,128)S(1)}, u32[]{:S(2)}, u32[]{:S(2)}) collective-permute-start(f32[8,40,256]{2,1,0:T(8,128)S(1)} %get-tuple-element.21), channel_id=1, source_target_pairs={{0,128},{128,256},{256,384},{1,129},{129,257},{257,385},{2,130},{1... | collective-permute-start | bytes 983048 | tf_op jit(solution)/shard_map/ppermute | solution.py:124
  68.1 0.8 copy.204.trial_ref
  68.9 0.7 copy.205.unif_ref
  69.6 0.7 copy.202.b_ref
  70.3 0.7 copy.203.a_ref
  71.0 2.3 %all-to-all-done = f32[128,1,324]{2,1,0:T(1,128)S(1)} async-done(((f32[128,1,324]{2,1,0:T(1,128)}), f32[128,1,324]{2,1,0:T(1,128)S(1)}, u32[]{:S(2)}, u32[]{:S(2)}) %all-to-all-start) | async-done | bytes 165920 | tf_op jit(solution)/shard_map/all_to_all | solution.py:246
  73.8 1.0 reduce.4
  76.0 0.8 pad_maximum_fusion.13.film_ref
  77.1 0.7 copy-done.2
  77.8 0.7 copy-done.3
  78.5 4.2 %shard_map.77.s_ref = f32[3,2,40,256]{3,2,1,0:T(8,128)} custom-call(f32[27]{0:T(128)} %reshape.161.k_ref, f32[2]{0:T(128)} %add_convert_fusion.edge_ref, f32[3,2,40,256]{3,2,1,0:T(8,128)} %copy.201.s_ref, f32[3,2,40,256]{3,2,1,0:T(8,128)} %copy.202.b_ref, f32[3,2,40,256]{3,2,1,0:T(8,128)} %copy.203.a_ref, f32[3,40,256]{2,1,0:T(8,128)} %pad_maximum_fusion.13.film_ref, ...), custom_call_target="tpu_custom_call" | custom-call | flops 12288000 | bytes 2457600 | tf_op jit(solution)/shard_map/pallas_call | solution.py:112
  82.7 4.2 %collective-permute-start.11 = (f32[3,2,40,256]{3,2,1,0:T(8,128)}, f32[3,2,40,256]{3,2,1,0:T(8,128)S(1)}, u32[]{:S(2)}, u32[]{:S(2)}) collective-permute-start(f32[3,2,40,256]{3,2,1,0:T(8,128)} %shard_map.77.s_ref), channel_id=1, source_target_pairs={{0,128},{128,256},{256,384},{1,129},{129,257},{257,385},{2,130},{1... | collective-permute-start | bytes 737288 | tf_op jit(solution)/shard_map/ppermute | solution.py:124
  86.9 1.5 %collective-permute-start.12 = (f32[3,2,40,256]{3,2,1,0:T(8,128)}, f32[3,2,40,256]{3,2,1,0:T(8,128)S(1)}, u32[]{:S(2)}, u32[]{:S(2)}) collective-permute-start(f32[3,2,40,256]{3,2,1,0:T(8,128)} %shard_map.77.s_ref), channel_id=1, source_target_pairs={{128,0},{256,128},{384,256},{129,1},{257,129},{385,257},{130,2},{2... | collective-permute-start | bytes 737288 | tf_op jit(solution)/shard_map/ppermute | solution.py:124
  88.7 0.8 slice.360
  90.1 1.2 collective-permute-done.11.b_ref
  91.4 3.7 %collective-permute-done.12.a_ref = f32[3,2,40,256]{3,2,1,0:T(8,128)S(1)} collective-permute-done((f32[3,2,40,256]{3,2,1,0:T(8,128)}, f32[3,2,40,256]{3,2,1,0:T(8,128)S(1)}, u32[]{:S(2)}, u32[]{:S(2)}) %collective-permute-start.12) | collective-permute-done | bytes 245792 | tf_op jit(solution)/shard_map/ppermute | solution.py:124
  95.1 0.7 copy-done.9
  95.8 4.2 %shard_map.78 = f32[3,2,40,256]{3,2,1,0:T(8,128)} custom-call(f32[27]{0:T(128)} %reshape.161.k_ref, f32[2]{0:T(128)} %add_convert_fusion.edge_ref, f32[3,2,40,256]{3,2,1,0:T(8,128)} %shard_map.77.s_ref, f32[3,2,40,256]{3,2,1,0:T(8,128)} %copy-done.8, f32[3,2,40,256]{3,2,1,0:T(8,128)} %copy-done.9, f32[3,40,256]{2,1,0:T(8,128)} %pad_maximum_fusion.13.film_ref, ...), custom_call_target="tpu_custom_call" | custom-call | flops 12288000 | bytes 2457600 | tf_op jit(solution)/shard_map/pallas_call | solution.py:112
  100.0 0.8 slice.366
  101.5 1.3 reshape.189
  102.8 15.5 %all-to-all-start.1 = ((f32[128,1,192]{2,1,0:T(1,128)}), f32[128,1,192]{2,1,0:T(1,128)S(1)}, u32[]{:S(2)}, u32[]{:S(2)}) async-start(f32[128,1,192]{2,1,0:T(1,128)} %reshape.189), calls=%async_computation.1 | async-start | bytes 262144 | tf_op jit(solution)/shard_map/all_to_all | solution.py:40
  118.3 1.5 %slice.359 = f32[3,2,32,128]{3,2,1,0:T(8,128)} slice(f32[3,2,40,256]{3,2,1,0:T(8,128)} %shard_map.78), slice={[0:3], [0:2], [0:32], [0:128]} | slice | bytes 196608 | tf_op jit(solution)/shard_map/slice | solution.py:279
  119.9 14.4 %all-to-all-done.1 = f32[128,1,192]{2,1,0:T(1,128)S(1)} async-done(((f32[128,1,192]{2,1,0:T(1,128)}), f32[128,1,192]{2,1,0:T(1,128)S(1)}, u32[]{:S(2)}, u32[]{:S(2)}) %all-to-all-start.1) | async-done | bytes 98336 | tf_op jit(solution)/shard_map/all_to_all | solution.py:40
  134.3 0.9 reduce.5
  136.0 1.0 fusion.4
  139.6 0.8 broadcast_divide_fusion
  (131 shorter events, 12.0 us)
Async XLA Ops:
  5.5 3.2 %copy-start = (f32[3,128,256]{2,1,0:T(8,128)S(1)}, f32[3,128,256]{2,1,0:T(8,128)}, u32[]{:S(2)}) copy-start(f32[3,128,256]{2,1,0:T(8,128)} %param.10) | copy-start | bytes 1179652
  5.5 3.1 %copy-start.1 = (f32[128,256]{1,0:T(8,128)S(1)}, f32[128,256]{1,0:T(8,128)}, u32[]{:S(2)}) copy-start(f32[128,256]{1,0:T(8,128)} %param.11) | copy-start | bytes 393220
  5.5 3.2 %copy-start.11 = (f32[2,3,2,32,128]{4,3,2,1,0:T(8,128)S(1)}, f32[2,3,2,32,128]{4,3,2,1,0:T(8,128)}, u32[]{:S(2)}) copy-start(f32[2,3,2,32,128]{4,3,2,1,0:T(8,128)} %param.8) | copy-start | bytes 589828
  5.5 3.2 %copy-start.4 = (f32[3,2,32,128]{3,2,1,0:T(8,128)S(1)}, f32[3,2,32,128]{3,2,1,0:T(8,128)}, u32[]{:S(2)}) copy-start(f32[3,2,32,128]{3,2,1,0:T(8,128)} %param.6) | copy-start | bytes 294916
  5.5 3.2 %copy-start.6 = (f32[2,2,32,128]{3,2,1,0:T(8,128)S(1)}, f32[2,2,32,128]{3,2,1,0:T(8,128)}, u32[]{:S(2)}) copy-start(f32[2,2,32,128]{3,2,1,0:T(8,128)} %param.7) | copy-start | bytes 196612
  5.9 34.7 %collective-permute-start.6 = (f32[128,3,6,18]{0,3,2,1:T(8,128)S(1)}, f32[128,3,6,18]{0,3,2,1:T(8,128)S(1)}, u32[]{:S(2)}, u32[]{:S(2)}) collective-permute-start(f32[128,3,6,18]{0,3,2,1:T(8,128)S(1)} %copy.195), channel_id=1, source_target_pairs={{0,128}} | collective-permute-start | bytes 497672 | tf_op jit(solution)/shard_map/ppermute | solution.py:34
  6.6 34.1 %collective-permute-start.7 = (f32[128,3,6,18]{0,3,2,1:T(8,128)S(1)}, f32[128,3,6,18]{0,3,2,1:T(8,128)S(1)}, u32[]{:S(2)}, u32[]{:S(2)}) collective-permute-start(f32[128,3,6,18]{0,3,2,1:T(8,128)S(1)} %copy.195), channel_id=1, source_target_pairs={{0,256}} | collective-permute-start | bytes 497672 | tf_op jit(solution)/shard_map/ppermute | solution.py:34
  7.3 34.1 %collective-permute-start.8 = (f32[128,3,6,18]{0,3,2,1:T(8,128)S(1)}, f32[128,3,6,18]{0,3,2,1:T(8,128)}, u32[]{:S(2)}, u32[]{:S(2)}) collective-permute-start(f32[128,3,6,18]{0,3,2,1:T(8,128)S(1)} %copy.195), channel_id=1, source_target_pairs={{0,384}} | collective-permute-start | bytes 497672 | tf_op jit(solution)/shard_map/ppermute | solution.py:34
  8.8 13.5 %collective-permute-start.1 = (f32[13312]{0:T(1024)S(1)}, f32[13312]{0:T(1024)S(1)}, u32[]{:S(2)}, u32[]{:S(2)}) collective-permute-start(f32[13312]{0:T(1024)S(1)} %pad_maximum_fusion.16), channel_id=1, source_target_pairs={{0,8},{8,16},{16,24},{24,32},{32,40},{40,48},{48,56},{56,64},{64,7... | collective-permute-start | bytes 159752 | tf_op jit(solution)/shard_map/ppermute | solution.py:124
  20.3 10.6 %collective-permute-start = (f32[13312]{0:T(1024)S(1)}, f32[13312]{0:T(1024)S(1)}, u32[]{:S(2)}, u32[]{:S(2)}) collective-permute-start(f32[13312]{0:T(1024)S(1)} %pad_maximum_fusion.15), channel_id=1, source_target_pairs={{8,0},{16,8},{24,16},{32,24},{40,32},{48,40},{56,48},{64,56},{72,6... | collective-permute-start | bytes 159752 | tf_op jit(solution)/shard_map/ppermute | solution.py:124
  31.6 7.6 %copy-start.13 = (f32[3,3,3]{2,1,0:T(4,128)S(1)}, f32[3,3,3]{2,1,0:T(4,128)}, u32[]{:S(2)}) copy-start(f32[3,3,3]{2,1,0:T(4,128)} %param.9) | copy-start | bytes 328
  32.1 7.8 %collective-permute-start.2 = (f32[4576]{0:T(1024)S(1)}, f32[4576]{0:T(1024)S(1)}, u32[]{:S(2)}, u32[]{:S(2)}) collective-permute-start(f32[4576]{0:T(1024)S(1)} %pad_maximum_fusion.20), channel_id=1, source_target_pairs={{1,0},{2,1},{3,2},{4,3},{5,4},{6,5},{7,6},{9,8},{10,9},{11,10},{12... | collective-permute-start | bytes 54920 | tf_op jit(solution)/shard_map/ppermute | solution.py:124
  35.9 4.4 %collective-permute-start.3 = (f32[4576]{0:T(1024)S(1)}, f32[4576]{0:T(1024)S(1)}, u32[]{:S(2)}, u32[]{:S(2)}) collective-permute-start(f32[4576]{0:T(1024)S(1)} %pad_maximum_fusion.21), channel_id=1, source_target_pairs={{0,1},{1,2},{2,3},{3,4},{4,5},{5,6},{6,7},{8,9},{9,10},{10,11},{11... | collective-permute-start | bytes 54920 | tf_op jit(solution)/shard_map/ppermute | solution.py:124
  40.3 1.1 copy-start.12
  40.6 0.7 copy-start.10
  43.0 13.2 %copy-start.5 = (f32[3,2,32,128]{3,2,1,0:T(8,128)S(1)}, f32[3,2,32,128]{3,2,1,0:T(8,128)}, u32[]{:S(2)}) copy-start(f32[3,2,32,128]{3,2,1,0:T(8,128)} %param.6) | copy-start | bytes 294916
  43.0 13.1 %copy-start.7 = (f32[2,2,32,128]{3,2,1,0:T(8,128)S(1)}, f32[2,2,32,128]{3,2,1,0:T(8,128)}, u32[]{:S(2)}) copy-start(f32[2,2,32,128]{3,2,1,0:T(8,128)} %param.7) | copy-start | bytes 196612
  44.6 28.8 %all-to-all-start = ((f32[128,1,324]{2,1,0:T(1,128)}), f32[128,1,324]{2,1,0:T(1,128)S(1)}, u32[]{:S(2)}, u32[]{:S(2)}) async-start(f32[128,1,324]{2,1,0:T(1,128)} %reshape.187), calls=%async_computation | async-start | bytes 393216 | tf_op jit(solution)/shard_map/all_to_all | solution.py:246
  56.4 13.1 %collective-permute-start.4 = (f32[3,2,40,256]{3,2,0,1:T(8,128)S(1)}, f32[3,2,40,256]{3,2,0,1:T(8,128)S(1)}, u32[]{:S(2)}, u32[]{:S(2)}) collective-permute-start(f32[3,2,40,256]{3,2,0,1:T(8,128)S(1)} %slice.343), channel_id=1, source_target_pairs={{0,128},{128,256},{256,384},{1,129},{129,257},{257,385},{2,130},{1... | collective-permute-start | bytes 737288 | tf_op jit(solution)/shard_map/ppermute | solution.py:124
  59.1 11.2 %collective-permute-start.5 = (f32[3,2,40,256]{3,2,0,1:T(8,128)S(1)}, f32[3,2,40,256]{3,2,0,1:T(8,128)S(1)}, u32[]{:S(2)}, u32[]{:S(2)}) collective-permute-start(f32[3,2,40,256]{3,2,0,1:T(8,128)S(1)} %slice.343), channel_id=1, source_target_pairs={{128,0},{256,128},{384,256},{129,1},{257,129},{385,257},{130,2},{2... | collective-permute-start | bytes 737288 | tf_op jit(solution)/shard_map/ppermute | solution.py:124
  61.9 15.2 %collective-permute-start.10 = (f32[8,40,256]{2,1,0:T(8,128)}, f32[8,40,256]{2,1,0:T(8,128)S(1)}, u32[]{:S(2)}, u32[]{:S(2)}) collective-permute-start(f32[8,40,256]{2,1,0:T(8,128)} %get-tuple-element.20), channel_id=1, source_target_pairs={{128,0},{256,128},{384,256},{129,1},{257,129},{385,257},{130,2},{2... | collective-permute-start | bytes 983048 | tf_op jit(solution)/shard_map/ppermute | solution.py:124
  63.2 13.9 %collective-permute-start.9 = (f32[8,40,256]{2,1,0:T(8,128)S(1)}, f32[8,40,256]{2,1,0:T(8,128)S(1)}, u32[]{:S(2)}, u32[]{:S(2)}) collective-permute-start(f32[8,40,256]{2,1,0:T(8,128)S(1)} %get-tuple-element.21), channel_id=1, source_target_pairs={{0,128},{128,256},{256,384},{1,129},{129,257},{257,385},{2,130},{1... | collective-permute-start | bytes 983048 | tf_op jit(solution)/shard_map/ppermute | solution.py:124
  77.1 0.7 copy-start.2
  77.8 0.7 copy-start.3
  82.7 8.7 %collective-permute-start.11 = (f32[3,2,40,256]{3,2,1,0:T(8,128)}, f32[3,2,40,256]{3,2,1,0:T(8,128)S(1)}, u32[]{:S(2)}, u32[]{:S(2)}) collective-permute-start(f32[3,2,40,256]{3,2,1,0:T(8,128)} %shard_map.77.s_ref), channel_id=1, source_target_pairs={{0,128},{128,256},{256,384},{1,129},{129,257},{257,385},{2,130},{1... | collective-permute-start | bytes 737288 | tf_op jit(solution)/shard_map/ppermute | solution.py:124
  86.9 8.2 %collective-permute-start.12 = (f32[3,2,40,256]{3,2,1,0:T(8,128)}, f32[3,2,40,256]{3,2,1,0:T(8,128)S(1)}, u32[]{:S(2)}, u32[]{:S(2)}) collective-permute-start(f32[3,2,40,256]{3,2,1,0:T(8,128)} %shard_map.77.s_ref), channel_id=1, source_target_pairs={{128,0},{256,128},{384,256},{129,1},{257,129},{385,257},{130,2},{2... | collective-permute-start | bytes 737288 | tf_op jit(solution)/shard_map/ppermute | solution.py:124
  91.4 3.7 %copy-start.8 = (f32[3,2,40,256]{3,2,1,0:T(8,128)}, f32[3,2,40,256]{3,2,1,0:T(8,128)S(1)}, u32[]{:S(2)}) copy-start(f32[3,2,40,256]{3,2,1,0:T(8,128)S(1)} %collective-permute-done.11.b_ref) | copy-start | bytes 737284
  95.1 0.7 copy-start.9
  102.8 31.5 %all-to-all-start.1 = ((f32[128,1,192]{2,1,0:T(1,128)}), f32[128,1,192]{2,1,0:T(1,128)S(1)}, u32[]{:S(2)}, u32[]{:S(2)}) async-start(f32[128,1,192]{2,1,0:T(1,128)} %reshape.189), calls=%async_computation.1 | async-start | bytes 262144 | tf_op jit(solution)/shard_map/all_to_all | solution.py:40

commit v9 on v8

--- a/solution.py
+++ b/solution.py
@@ -268,11 +268,16 @@
     region_count = lax.axis_size("region")
     edge = jnp.stack([region_pos > 0, region_pos < region_count - 1]).astype(jnp.float32)
     draws = jnp.concatenate([trials_e.reshape(3 * SWEEPS, layers_dev, ext_x, wide), unif_e], axis=0)
-    tb = shift_in(draws[:, -1], "region", True)
-    ta = shift_in(draws[:, 0], "region", False)
+    block = spins_e.reshape(-1, ext_x, wide)
+    below = shift_in(jnp.concatenate([block, draws[:, -1]], axis=0), "region", True)
+    above = shift_in(jnp.concatenate([block, draws[:, 0]], axis=0), "region", False)
+    tb, ta = below[block.shape[0] :], above[block.shape[0] :]
+    below = below[: block.shape[0]].reshape(spins_e.shape)
+    above = above[: block.shape[0]].reshape(spins_e.shape)
     for sweep_index in range(SWEEPS):
-        below = shift_in(spins_e, "region", True)
-        above = shift_in(spins_e, "region", False)
+        if sweep_index > 0:
+            below = shift_in(spins_e, "region", True)
+            above = shift_in(spins_e, "region", False)
         spins_e = sweep_pair(
             spins_e, below, above, exch_flat, edge, film_e, valid, trials_e, unif_e, tb, ta, sweep_index
         )

time: 141 us -> 144 us (1.021)
  starting transfers between devices: 64 us -> 57.2 us
  waiting for transfers between devices: 30.5 us -> 36.1 us
  local copies, waits for them, and re-layouts: 23.6 us -> 25.7 us
  other arithmetic: 12.5 us -> 14.3 us
    all_to_all x1, waiting for transfers between devices: 2.3 us -> 10.7 us  [step_body(): own_patch = lax.all_to_all(pieces, GX + GY, 0, 0, tiled=True)[0]]
    ppermute x10 -> x8, starting transfers between devices: 34.2 us -> 29 us  [shift_in(): lax.ppermute(array, axis, up if from_lower else [(b, a) for a, b in up])]
    slice x0 -> x4, local copies, waits for them, and re-layouts: none -> 2.96 us  [the longest x2 1.5 us: step_body(): tb, ta = (below[block.shape[0]:], above[block.shape[0]:])]
    ppermute x10 -> x8, waiting for transfers between devices: 13.8 us -> 11 us  [shift_in(): lax.ppermute(array, axis, up if from_lower else [(b, a) for a, b in up])]
    all_to_all x1, starting transfers between devices: 15.5 us -> 13.2 us  [copy_for_each(): lax.all_to_all(jnp.broadcast_to(array[None], (count, *array.shape)), axis...]
    ppermute x2 -> x0, local copies, waits for them, and re-layouts: 1.46 us -> none  [shift_in(): lax.ppermute(array, axis, up if from_lower else [(b, a) for a, b in up])]
    unnamed x36 -> x28, local copies, waits for them, and re-layouts: 6.55 us -> 6.99 us
  transfers between devices with their start and end apart: 15 -> 13, of which waited for: 6 -> 5; matrix products, arithmetic and copies ran while one was open for 11% -> 12% of each run, Pallas kernels for 0% -> 0%
where the time goes in v9:
time: 144 us; the launch traced here: 143 us
  starting transfers between devices  57.2 us (40%)
  waiting for transfers between devices  36.1 us (25%)
  local copies, waits for them, and re-layouts  25.7 us (18%)
  other arithmetic  14.3 us (10%)
  Pallas kernels  8.35 us (6%)
    ppermute x8, starting transfers between devices, shift_in(): lax.ppermute(array, axis, up if from_lower else [(b, a) for a, b in up])  29 us
    all_to_all x1, waiting for transfers between devices, copy_for_each(): lax.all_to_all(jnp.broadcast_to(array[None], (count, *array.shape)), axis...  14.4 us
    all_to_all x1, starting transfers between devices, copy_for_each(): lax.all_to_all(jnp.broadcast_to(array[None], (count, *array.shape)), axis...  13.2 us
    all_to_all x1, starting transfers between devices, step_body(): own_patch = lax.all_to_all(pieces, GX + GY, 0, 0, tiled=True)[0]  11.6 us
    ppermute x8, waiting for transfers between devices, shift_in(): lax.ppermute(array, axis, up if from_lower else [(b, a) for a, b in up])  11 us
    all_to_all x1, waiting for transfers between devices, step_body(): own_patch = lax.all_to_all(pieces, GX + GY, 0, 0, tiled=True)[0]  10.7 us
    pallas_call x2, Pallas kernels, sweep_pair(): pl.pallas_call(functools.partial(sweep_kernel, sweep), out_shape=jax.Shap...  8.35 us
    unnamed x28, local copies, waits for them, and re-layouts  6.99 us
  transfers between devices with their start and end apart: 13, of which 5 were waited for; matrix products, arithmetic and copies ran while one was open for 12% of the time, Pallas kernels for 0%

profile of v9, /device:TPU:1, one launch (start us, length us, event | category | flops | bytes accessed | tf_op | source)
XLA Modules:
  0.0 143.1 jit_solution(10891393741938783422)
XLA Ops:
  0.7 0.9 slice.299
  2.1 1.9 %fusion.45 = (f32[16,7,3,6,1]{4,1,0,3,2:T(8,128)}, f32[16,7,3,6,1]{4,1,0,3,2:T(8,128)}) fusion(f32[16,8,3,6,16]{4,1,0,3,2:T(8,128)S(1)} %pad_maximum_fusion), kind=kLoop, calls=%fused_computation.135 | loop fusion | bytes 32256 | tf_op jit(solution)/shard_map/slice | solution.py:238
  3.9 2.3 %fusion.1 = f32[128,3,6,18]{3,0,2,1:T(8,128)S(1)} fusion(f32[16,7,3,6,1]{4,1,0,3,2:T(8,128)} %get-tuple-element.19, f32[16,7,3,6,1]{4,1,0,3,2:T(8,128)} %get-tuple-element.18, f32[16,8,3,1,16]{4,1,0,3,2:T(8,128)S(1)} %concatenate.79, f32[16,8,3,4,16]{4,1,0,3,2:T(8,128)S(1)} %bitcast.228, f32[16,8,3,1,16]{4,1,0,3,2:T(8,128)S(1)} %concatenate.78, pred[]{:T(512)S(6)} %and.46), kind=kLoop, calls=%fused_computation.2 | loop fusion | flops 373248 | bytes 329473 | tf_op jit(solution)/shard_map/jit(_where)/select_n | solution.py:245
  6.7 0.7 collective-permute-start.6
  7.4 1.4 collective-permute-start.7
  8.7 1.4 collective-permute-start.8
  10.2 11.5 %collective-permute-start.1 = (f32[13312]{0:T(1024)S(1)}, f32[13312]{0:T(1024)S(1)}, u32[]{:S(2)}, u32[]{:S(2)}) collective-permute-start(f32[13312]{0:T(1024)S(1)} %pad_maximum_fusion.18), channel_id=1, source_target_pairs={{0,8},{8,16},{16,24},{24,32},{32,40},{40,48},{48,56},{56,64},{64,7... | collective-permute-start | bytes 159752 | tf_op jit(solution)/shard_map/ppermute | solution.py:124
  21.7 1.3 collective-permute-start
  23.1 0.7 and_convert_fusion.valid_ref
  23.8 7.4 %collective-permute-done = f32[13312]{0:T(1024)S(1)} collective-permute-done((f32[13312]{0:T(1024)S(1)}, f32[13312]{0:T(1024)S(1)}, u32[]{:S(2)}, u32[]{:S(2)}) %collective-permute-start) | collective-permute-done | bytes 53280 | tf_op jit(solution)/shard_map/ppermute | solution.py:124
  32.4 3.9 %collective-permute-start.2 = (f32[4576]{0:T(1024)S(1)}, f32[4576]{0:T(1024)S(1)}, u32[]{:S(2)}, u32[]{:S(2)}) collective-permute-start(f32[4576]{0:T(1024)S(1)} %pad_maximum_fusion.22), channel_id=1, source_target_pairs={{1,0},{2,1},{3,2},{4,3},{5,4},{6,5},{7,6},{9,8},{10,9},{11,10},{12... | collective-permute-start | bytes 54920 | tf_op jit(solution)/shard_map/ppermute | solution.py:124
  37.0 3.0 %collective-permute-start.3 = (f32[4576]{0:T(1024)S(1)}, f32[4576]{0:T(1024)S(1)}, u32[]{:S(2)}, u32[]{:S(2)}) collective-permute-start(f32[4576]{0:T(1024)S(1)} %pad_maximum_fusion.23), channel_id=1, source_target_pairs={{0,1},{1,2},{2,3},{3,4},{4,5},{5,6},{6,7},{8,9},{9,10},{10,11},{11... | collective-permute-start | bytes 54920 | tf_op jit(solution)/shard_map/ppermute | solution.py:124
  40.0 0.6 add_convert_fusion.edge_ref
  40.6 0.7 reshape.170.k_ref
  42.4 1.4 %add_add_fusion = f32[128,3,6,18]{0,3,2,1:T(8,128)S(1)} fusion(f32[128,3,6,18]{0,3,2,1:T(8,128)} %collective-permute-done.8, f32[128,3,6,18]{0,3,2,1:T(8,128)} %collective-permute-done.7, f32[128,3,6,18]{0,3,2,1:T(8,128)S(1)} %copy.190, f32[128,3,6,18]{0,3,2,1:T(8,128)S(1)} %collective-permute-done.6), kind=kLoop, calls=%fused_computation.54 | loop fusion | flops 124416 | bytes 829440 | tf_op jit(solution)/shard_map/add | solution.py:34
  43.8 1.7 %copy.193 = f32[128,3,6,18]{3,2,1,0:T(8,128)} copy(f32[128,3,6,18]{0,3,2,1:T(8,128)S(1)} %add_add_fusion) | data formatting | bytes 331776 | tf_op jit(solution)/shard_map/add | solution.py:34
  45.5 2.9 %reshape.199 = f32[128,1,324]{2,1,0:T(1,128)} reshape(f32[128,3,6,18]{3,2,1,0:T(8,128)} %copy.193) | data formatting | bytes 331776
  48.4 11.6 %all-to-all-start = ((f32[128,1,324]{2,1,0:T(1,128)}), f32[128,1,324]{2,1,0:T(1,128)S(1)}, u32[]{:S(2)}, u32[]{:S(2)}) async-start(f32[128,1,324]{2,1,0:T(1,128)} %reshape.199), calls=%async_computation | async-start | bytes 393216 | tf_op jit(solution)/shard_map/all_to_all | solution.py:246
  60.1 0.9 pad_maximum_fusion.3
  61.0 2.6 %collective-permute-start.4 = (f32[14,40,256]{2,1,0:T(8,128)}, f32[14,40,256]{2,1,0:T(8,128)S(1)}, u32[]{:S(2)}, u32[]{:S(2)}) collective-permute-start(f32[14,40,256]{2,1,0:T(8,128)} %get-tuple-element.33), channel_id=1, source_target_pairs={{0,128},{128,256},{256,384},{1,129},{129,257},{257,385},{2,130},{1... | collective-permute-start | bytes 1720328 | tf_op jit(solution)/shard_map/ppermute | solution.py:124
  63.7 1.3 collective-permute-start.5
  65.0 0.8 copy.197.trial_ref
  65.8 0.7 copy.198.unif_ref
  66.5 10.7 %all-to-all-done = f32[128,1,324]{2,1,0:T(1,128)S(1)} async-done(((f32[128,1,324]{2,1,0:T(1,128)}), f32[128,1,324]{2,1,0:T(1,128)S(1)}, u32[]{:S(2)}, u32[]{:S(2)}) %all-to-all-start) | async-done | bytes 165920 | tf_op jit(solution)/shard_map/all_to_all | solution.py:246
  77.2 0.6 broadcast.111
  77.8 1.1 reduce.4
  78.9 1.6 %reshape.200 = f32[128,3,6,18]{3,2,1,0:T(8,128)} reshape(f32[128,324]{1,0:T(8,128)S(1)} %reduce.4) | data formatting | bytes 331776
  80.5 0.7 slice_bitcast_fusion.11
  81.9 0.8 pad_maximum_fusion.15.film_ref
  82.7 0.7 slice.377.tb_ref
  83.4 0.7 slice.361
  84.2 0.8 slice.378.ta_ref
  84.9 0.7 slice.363
  85.7 4.2 %shard_map.77.s_ref = f32[3,2,40,256]{3,2,1,0:T(8,128)} custom-call(f32[27]{0:T(128)} %reshape.170.k_ref, f32[2]{0:T(128)} %add_convert_fusion.edge_ref, f32[3,2,40,256]{3,2,1,0:T(8,128)} %copy-done.3, f32[3,2,40,256]{3,2,1,0:T(8,128)} %bitcast.245, f32[3,2,40,256]{3,2,1,0:T(8,128)} %bitcast.246, f32[3,40,256]{2,1,0:T(8,128)} %pad_maximum_fusion.15.film_ref, ...), custom_call_target="tpu_custom_call" | custom-call | flops 12288000 | bytes 2457600 | tf_op jit(solution)/shard_map/pallas_call | solution.py:112
  89.8 1.3 collective-permute-start.10
  91.1 4.2 %collective-permute-start.9 = (f32[3,2,40,256]{3,2,1,0:T(8,128)}, f32[3,2,40,256]{3,2,1,0:T(8,128)S(1)}, u32[]{:S(2)}, u32[]{:S(2)}) collective-permute-start(f32[3,2,40,256]{3,2,1,0:T(8,128)} %shard_map.77.s_ref), channel_id=1, source_target_pairs={{0,128},{128,256},{256,384},{1,129},{129,257},{257,385},{2,130},{1... | collective-permute-start | bytes 737288 | tf_op jit(solution)/shard_map/ppermute | solution.py:124
  96.4 2.6 %collective-permute-done.10.a_ref = f32[3,2,40,256]{3,2,1,0:T(8,128)S(1)} collective-permute-done((f32[3,2,40,256]{3,2,1,0:T(8,128)}, f32[3,2,40,256]{3,2,1,0:T(8,128)S(1)}, u32[]{:S(2)}, u32[]{:S(2)}) %collective-permute-start.10) | collective-permute-done | bytes 245792 | tf_op jit(solution)/shard_map/ppermute | solution.py:124
  99.0 1.0 collective-permute-done.9.b_ref
  100.0 0.7 copy-done.7
  100.7 4.2 %shard_map.78 = f32[3,2,40,256]{3,2,1,0:T(8,128)} custom-call(f32[27]{0:T(128)} %reshape.170.k_ref, f32[2]{0:T(128)} %add_convert_fusion.edge_ref, f32[3,2,40,256]{3,2,1,0:T(8,128)} %shard_map.77.s_ref, f32[3,2,40,256]{3,2,1,0:T(8,128)} %copy-done.7, f32[3,2,40,256]{3,2,1,0:T(8,128)} %copy-done.6, f32[3,40,256]{2,1,0:T(8,128)} %pad_maximum_fusion.15.film_ref, ...), custom_call_target="tpu_custom_call" | custom-call | flops 12288000 | bytes 2457600 | tf_op jit(solution)/shard_map/pallas_call | solution.py:112
  104.9 0.8 slice.386
  106.4 1.3 reshape.201
  107.6 13.2 %all-to-all-start.1 = ((f32[128,1,192]{2,1,0:T(1,128)}), f32[128,1,192]{2,1,0:T(1,128)S(1)}, u32[]{:S(2)}, u32[]{:S(2)}) async-start(f32[128,1,192]{2,1,0:T(1,128)} %reshape.201), calls=%async_computation.1 | async-start | bytes 262144 | tf_op jit(solution)/shard_map/all_to_all | solution.py:40
  120.9 1.5 %slice.379 = f32[3,2,32,128]{3,2,1,0:T(8,128)} slice(f32[3,2,40,256]{3,2,1,0:T(8,128)} %shard_map.78), slice={[0:3], [0:2], [0:32], [0:128]} | slice | bytes 196608 | tf_op jit(solution)/shard_map/slice | solution.py:284
  122.4 14.4 %all-to-all-done.1 = f32[128,1,192]{2,1,0:T(1,128)S(1)} async-done(((f32[128,1,192]{2,1,0:T(1,128)}), f32[128,1,192]{2,1,0:T(1,128)S(1)}, u32[]{:S(2)}, u32[]{:S(2)}) %all-to-all-start.1) | async-done | bytes 98336 | tf_op jit(solution)/shard_map/all_to_all | solution.py:40
  136.8 1.0 reduce.5
  138.7 1.0 fusion.4
  142.3 0.8 broadcast_divide_fusion
  (124 shorter events, 9.7 us)
Async XLA Ops:
  6.2 3.8 %copy-start = (f32[3,128,256]{2,1,0:T(8,128)S(1)}, f32[3,128,256]{2,1,0:T(8,128)}, u32[]{:S(2)}) copy-start(f32[3,128,256]{2,1,0:T(8,128)} %param.10) | copy-start | bytes 1179652
  6.3 3.8 %copy-start.2 = (f32[128,256]{1,0:T(8,128)S(1)}, f32[128,256]{1,0:T(8,128)}, u32[]{:S(2)}) copy-start(f32[128,256]{1,0:T(8,128)} %param.11) | copy-start | bytes 393220
  6.3 3.9 %copy-start.8 = (f32[2,3,2,32,128]{4,3,2,1,0:T(8,128)S(1)}, f32[2,3,2,32,128]{4,3,2,1,0:T(8,128)}, u32[]{:S(2)}) copy-start(f32[2,3,2,32,128]{4,3,2,1,0:T(8,128)} %param.8) | copy-start | bytes 589828
  6.3 3.9 %copy-start.4 = (f32[3,2,32,128]{3,2,1,0:T(8,128)S(1)}, f32[3,2,32,128]{3,2,1,0:T(8,128)}, u32[]{:S(2)}) copy-start(f32[3,2,32,128]{3,2,1,0:T(8,128)} %param.6) | copy-start | bytes 294916
  6.3 3.9 %copy-start.5 = (f32[2,2,32,128]{3,2,1,0:T(8,128)S(1)}, f32[2,2,32,128]{3,2,1,0:T(8,128)}, u32[]{:S(2)}) copy-start(f32[2,2,32,128]{3,2,1,0:T(8,128)} %param.7) | copy-start | bytes 196612
  6.7 35.7 %collective-permute-start.6 = (f32[128,3,6,18]{0,3,2,1:T(8,128)S(1)}, f32[128,3,6,18]{0,3,2,1:T(8,128)S(1)}, u32[]{:S(2)}, u32[]{:S(2)}) collective-permute-start(f32[128,3,6,18]{0,3,2,1:T(8,128)S(1)} %copy.190), channel_id=1, source_target_pairs={{0,128}} | collective-permute-start | bytes 497672 | tf_op jit(solution)/shard_map/ppermute | solution.py:34
  7.4 35.0 %collective-permute-start.7 = (f32[128,3,6,18]{0,3,2,1:T(8,128)S(1)}, f32[128,3,6,18]{0,3,2,1:T(8,128)}, u32[]{:S(2)}, u32[]{:S(2)}) collective-permute-start(f32[128,3,6,18]{0,3,2,1:T(8,128)S(1)} %copy.190), channel_id=1, source_target_pairs={{0,256}} | collective-permute-start | bytes 497672 | tf_op jit(solution)/shard_map/ppermute | solution.py:34
  8.7 33.6 %collective-permute-start.8 = (f32[128,3,6,18]{0,3,2,1:T(8,128)S(1)}, f32[128,3,6,18]{0,3,2,1:T(8,128)}, u32[]{:S(2)}, u32[]{:S(2)}) collective-permute-start(f32[128,3,6,18]{0,3,2,1:T(8,128)S(1)} %copy.190), channel_id=1, source_target_pairs={{0,384}} | collective-permute-start | bytes 497672 | tf_op jit(solution)/shard_map/ppermute | solution.py:34
  10.2 13.5 %collective-permute-start.1 = (f32[13312]{0:T(1024)S(1)}, f32[13312]{0:T(1024)S(1)}, u32[]{:S(2)}, u32[]{:S(2)}) collective-permute-start(f32[13312]{0:T(1024)S(1)} %pad_maximum_fusion.18), channel_id=1, source_target_pairs={{0,8},{8,16},{16,24},{24,32},{32,40},{40,48},{48,56},{56,64},{64,7... | collective-permute-start | bytes 159752 | tf_op jit(solution)/shard_map/ppermute | solution.py:124
  21.7 9.5 %collective-permute-start = (f32[13312]{0:T(1024)S(1)}, f32[13312]{0:T(1024)S(1)}, u32[]{:S(2)}, u32[]{:S(2)}) collective-permute-start(f32[13312]{0:T(1024)S(1)} %pad_maximum_fusion.17), channel_id=1, source_target_pairs={{8,0},{16,8},{24,16},{32,24},{40,32},{48,40},{56,48},{64,56},{72,6... | collective-permute-start | bytes 159752 | tf_op jit(solution)/shard_map/ppermute | solution.py:124
  31.9 8.7 %copy-start.9 = (f32[3,3,3]{2,1,0:T(4,128)S(1)}, f32[3,3,3]{2,1,0:T(4,128)}, u32[]{:S(2)}) copy-start(f32[3,3,3]{2,1,0:T(4,128)} %param.9) | copy-start | bytes 328
  32.4 8.9 %collective-permute-start.2 = (f32[4576]{0:T(1024)S(1)}, f32[4576]{0:T(1024)S(1)}, u32[]{:S(2)}, u32[]{:S(2)}) collective-permute-start(f32[4576]{0:T(1024)S(1)} %pad_maximum_fusion.22), channel_id=1, source_target_pairs={{1,0},{2,1},{3,2},{4,3},{5,4},{6,5},{7,6},{9,8},{10,9},{11,10},{12... | collective-permute-start | bytes 54920 | tf_op jit(solution)/shard_map/ppermute | solution.py:124
  37.0 4.7 %collective-permute-start.3 = (f32[4576]{0:T(1024)S(1)}, f32[4576]{0:T(1024)S(1)}, u32[]{:S(2)}, u32[]{:S(2)}) collective-permute-start(f32[4576]{0:T(1024)S(1)} %pad_maximum_fusion.23), channel_id=1, source_target_pairs={{0,1},{1,2},{2,3},{3,4},{4,5},{5,6},{6,7},{8,9},{9,10},{10,11},{11... | collective-permute-start | bytes 54920 | tf_op jit(solution)/shard_map/ppermute | solution.py:124
  42.3 17.8 %copy-start.1 = (f32[11,2,40,256]{3,2,0,1:T(8,128)}, f32[11,2,40,256]{3,2,0,1:T(8,128)S(1)}, u32[]{:S(2)}) copy-start(f32[11,2,40,256]{3,2,0,1:T(8,128)S(1)} %pad_maximum_fusion.1) | copy-start | bytes 2703364
  42.3 17.8 %copy-start.3 = (f32[3,2,40,256]{3,2,1,0:T(8,128)}, f32[3,2,40,256]{3,2,1,0:T(8,128)S(1)}, u32[]{:S(2)}) copy-start(f32[3,2,40,256]{3,2,1,0:T(8,128)S(1)} %copy.196.s_ref) | copy-start | bytes 737284
  48.4 28.8 %all-to-all-start = ((f32[128,1,324]{2,1,0:T(1,128)}), f32[128,1,324]{2,1,0:T(1,128)S(1)}, u32[]{:S(2)}, u32[]{:S(2)}) async-start(f32[128,1,324]{2,1,0:T(1,128)} %reshape.199), calls=%async_computation | async-start | bytes 393216 | tf_op jit(solution)/shard_map/all_to_all | solution.py:246
  60.1 4.9 %slice-start = ((f32[11,2,40,256]{3,2,0,1:T(8,128)}), f32[6,2,40,256]{3,2,0,1:T(8,128)S(1)}, s32[]{:S(2)}) async-start(f32[11,2,40,256]{3,2,0,1:T(8,128)} %copy-done.1), calls=%async_computation.2 | async-start | bytes 983040 | tf_op jit(solution)/shard_map/slice | solution.py:256
  60.1 5.7 %slice-start.1 = ((f32[11,2,40,256]{3,2,0,1:T(8,128)}), f32[2,2,40,256]{3,2,0,1:T(8,128)S(1)}, s32[]{:S(2)}) async-start(f32[11,2,40,256]{3,2,0,1:T(8,128)} %copy-done.1), calls=%async_computation.3 | async-start | bytes 327680 | tf_op jit(solution)/shard_map/slice | solution.py:257
  61.0 21.7 %collective-permute-start.4 = (f32[14,40,256]{2,1,0:T(8,128)}, f32[14,40,256]{2,1,0:T(8,128)S(1)}, u32[]{:S(2)}, u32[]{:S(2)}) collective-permute-start(f32[14,40,256]{2,1,0:T(8,128)} %get-tuple-element.33), channel_id=1, source_target_pairs={{0,128},{128,256},{256,384},{1,129},{129,257},{257,385},{2,130},{1... | collective-permute-start | bytes 1720328 | tf_op jit(solution)/shard_map/ppermute | solution.py:124
  63.7 20.5 %collective-permute-start.5 = (f32[14,40,256]{2,1,0:T(8,128)S(1)}, f32[14,40,256]{2,1,0:T(8,128)S(1)}, u32[]{:S(2)}, u32[]{:S(2)}) collective-permute-start(f32[14,40,256]{2,1,0:T(8,128)S(1)} %get-tuple-element.32), channel_id=1, source_target_pairs={{128,0},{256,128},{384,256},{129,1},{257,129},{385,257},{130,2},{2... | collective-permute-start | bytes 1720328 | tf_op jit(solution)/shard_map/ppermute | solution.py:124
  89.8 9.1 %collective-permute-start.10 = (f32[3,2,40,256]{3,2,1,0:T(8,128)}, f32[3,2,40,256]{3,2,1,0:T(8,128)S(1)}, u32[]{:S(2)}, u32[]{:S(2)}) collective-permute-start(f32[3,2,40,256]{3,2,1,0:T(8,128)} %shard_map.77.s_ref), channel_id=1, source_target_pairs={{128,0},{256,128},{384,256},{129,1},{257,129},{385,257},{130,2},{2... | collective-permute-start | bytes 737288 | tf_op jit(solution)/shard_map/ppermute | solution.py:124
  91.1 8.8 %collective-permute-start.9 = (f32[3,2,40,256]{3,2,1,0:T(8,128)}, f32[3,2,40,256]{3,2,1,0:T(8,128)S(1)}, u32[]{:S(2)}, u32[]{:S(2)}) collective-permute-start(f32[3,2,40,256]{3,2,1,0:T(8,128)} %shard_map.77.s_ref), channel_id=1, source_target_pairs={{0,128},{128,256},{256,384},{1,129},{129,257},{257,385},{2,130},{1... | collective-permute-start | bytes 737288 | tf_op jit(solution)/shard_map/ppermute | solution.py:124
  99.0 1.0 copy-start.6
  100.0 0.7 copy-start.7
  107.6 29.2 %all-to-all-start.1 = ((f32[128,1,192]{2,1,0:T(1,128)}), f32[128,1,192]{2,1,0:T(1,128)S(1)}, u32[]{:S(2)}, u32[]{:S(2)}) async-start(f32[128,1,192]{2,1,0:T(1,128)} %reshape.201), calls=%async_computation.1 | async-start | bytes 262144 | tf_op jit(solution)/shard_map/all_to_all | solution.py:40

commit v10 on v8

--- a/solution.py
+++ b/solution.py
@@ -74,7 +74,7 @@
     return [jnp.where(chosen, mix[c] / mnorm, s[c]) for c in range(3)]
 
 
-def sweep_kernel(sweep, k_ref, edge_ref, s_ref, b_ref, a_ref, film_ref, valid_ref, trial_ref, unif_ref,
+def sweep_kernel(sweep, k_ref, edge_ref, s_ref, b_ref, a_ref, film_ref, valid_ref, draw_ref,
                  tb_ref, ta_ref, out_ref):
     layers, rows_x, rows_y = s_ref.shape[1:]
     row = lax.broadcasted_iota(jnp.int32, (rows_x, rows_y), 0)
@@ -82,14 +82,16 @@
     live = valid_ref[...] > 0.5
     kk = [[[k_ref[d * 9 + a * 3 + b] for b in range(3)] for a in range(3)] for d in range(3)]
     film = [film_ref[c] for c in range(3)]
+    trial_at = 3 + 3 * sweep
+    unif_at = 3 + 3 * SWEEPS + sweep
     halo = b_ref.shape[1]
     stack = [[b_ref[c, l] for c in range(3)] for l in range(halo)]
     stack += [[s_ref[c, l] for c in range(3)] for l in range(layers)]
     stack += [[a_ref[c, l] for c in range(3)] for l in range(halo)]
     trial = [[tb_ref[3 * sweep + c] for c in range(3)]]
-    trial += [[trial_ref[sweep, c, l] for c in range(3)] for l in range(layers)]
+    trial += [[draw_ref[trial_at + c, l] for c in range(3)] for l in range(layers)]
     trial += [[ta_ref[3 * sweep + c] for c in range(3)]]
-    unif = [tb_ref[3 * SWEEPS + sweep]] + [unif_ref[sweep, l] for l in range(layers)] + [ta_ref[3 * SWEEPS + sweep]]
+    unif = [tb_ref[3 * SWEEPS + sweep]] + [draw_ref[unif_at, l] for l in range(layers)] + [ta_ref[3 * SWEEPS + sweep]]
     layer_live = [edge_ref[0] > 0.5] + [True] * layers + [edge_ref[1] > 0.5]
     for colour, first, last in ((0, halo - 1, halo + layers + 1), (1, halo, halo + layers)):
         new = list(stack)
@@ -104,18 +106,18 @@
             out_ref[c, l] = stack[halo + l][c]
 
 
-def sweep_pair(spins, below, above, exch_flat, edge, film_e, valid, trials, uniforms, tb, ta, sweep):
-    _, layers, rows_x, rows_y = spins.shape
+def sweep_pair(spins, below, above, exch_flat, edge, film_e, valid, draws, tb, ta, sweep):
+    layers, rows_x, rows_y = spins.shape[1:]
     vmem = pl.BlockSpec(memory_space=pltpu.VMEM)
     smem = pl.BlockSpec(memory_space=pltpu.SMEM)
     sites = layers * rows_x * rows_y
     return pl.pallas_call(
         functools.partial(sweep_kernel, sweep),
-        out_shape=jax.ShapeDtypeStruct(spins.shape, spins.dtype),
-        in_specs=[smem, smem] + [vmem] * 9,
+        out_shape=jax.ShapeDtypeStruct((3,) + spins.shape[1:], spins.dtype),
+        in_specs=[smem, smem] + [vmem] * 8,
         out_specs=vmem,
         cost_estimate=pl.CostEstimate(flops=600 * sites, transcendentals=12 * sites, bytes_accessed=4 * 30 * sites),
-    )(exch_flat, edge, spins, below, above, film_e, valid, trials, uniforms, tb, ta)
+    )(exch_flat, edge, spins, below, above, film_e, valid, draws, tb, ta)
 
 
 def shift_in(array, axis, from_lower):
@@ -270,12 +272,14 @@
     draws = jnp.concatenate([trials_e.reshape(3 * SWEEPS, layers_dev, ext_x, wide), unif_e], axis=0)
     tb = shift_in(draws[:, -1], "region", True)
     ta = shift_in(draws[:, 0], "region", False)
+    current = channels
     for sweep_index in range(SWEEPS):
         below = shift_in(spins_e, "region", True)
         above = shift_in(spins_e, "region", False)
         spins_e = sweep_pair(
-            spins_e, below, above, exch_flat, edge, film_e, valid, trials_e, unif_e, tb, ta, sweep_index
+            current, below, above, exch_flat, edge, film_e, valid, channels, tb, ta, sweep_index
         )
+        current = spins_e
     stack_spins = spins_e[:, :, :rows_x, :rows_y]
     averages = stack_spins[:, 0].reshape(3, piece_x, K, piece_y, K).mean(axis=(2, 4))
     gathered = copy_for_each(averages, GX + GY)

time: 141 us -> 143 us (1.014)
  waiting for transfers between devices: 30.5 us -> 32.1 us
    ppermute x10, waiting for transfers between devices: 13.8 us -> 15.5 us  [shift_in(): lax.ppermute(array, axis, up if from_lower else [(b, a) for a, b in up])]
  transfers between devices with their start and end apart: 15 -> 15, of which waited for: 6 -> 7; matrix products, arithmetic and copies ran while one was open for 11% -> 10% of each run, Pallas kernels for 0% -> 0%
where the time goes in v10:
time: 143 us; the launch traced here: 142 us
  starting transfers between devices  64.7 us (45%)
  waiting for transfers between devices  32.1 us (22%)
  local copies, waits for them, and re-layouts  22.3 us (16%)
  other arithmetic  12.6 us (9%)
  Pallas kernels  8.66 us (6%)
  between operations  1.46 us (1%)
    ppermute x10, starting transfers between devices, shift_in(): lax.ppermute(array, axis, up if from_lower else [(b, a) for a, b in up])  34.4 us
    all_to_all x1, starting transfers between devices, copy_for_each(): lax.all_to_all(jnp.broadcast_to(array[None], (count, *array.shape)), axis...  16 us
    ppermute x10, waiting for transfers between devices, shift_in(): lax.ppermute(array, axis, up if from_lower else [(b, a) for a, b in up])  15.5 us
    all_to_all x1, waiting for transfers between devices, copy_for_each(): lax.all_to_all(jnp.broadcast_to(array[None], (count, *array.shape)), axis...  14.4 us
    all_to_all x1, starting transfers between devices, step_body(): own_patch = lax.all_to_all(pieces, GX + GY, 0, 0, tiled=True)[0]  11.7 us
    pallas_call x2, Pallas kernels, sweep_pair(): pl.pallas_call(functools.partial(sweep_kernel, sweep), out_shape=jax.Shap...  8.66 us
    unnamed x36, local copies, waits for them, and re-layouts  6.56 us
  transfers between devices with their start and end apart: 15, of which 7 were waited for; matrix products, arithmetic and copies ran while one was open for 10% of the time, Pallas kernels for 0%

profile of v10, /device:TPU:1, one launch (start us, length us, event | category | flops | bytes accessed | tf_op | source)
XLA Modules:
  0.0 141.8 jit_solution(16626887711452668013)
XLA Ops:
  0.7 0.9 slice.279
  2.1 1.5 %fusion.45 = (f32[16,7,3,6,1]{4,1,0,3,2:T(8,128)S(1)}, f32[16,7,3,6,1]{4,1,0,3,2:T(8,128)}) fusion(f32[16,8,3,6,16]{4,1,0,3,2:T(8,128)S(1)} %pad_maximum_fusion), kind=kLoop, calls=%fused_computation.133 | loop fusion | bytes 32256 | tf_op jit(solution)/shard_map/slice | solution.py:240
  3.5 1.9 %fusion.1 = f32[128,3,6,18]{3,0,2,1:T(8,128)S(1)} fusion(f32[16,7,3,6,1]{4,1,0,3,2:T(8,128)} %get-tuple-element.19, f32[16,7,3,6,1]{4,1,0,3,2:T(8,128)S(1)} %get-tuple-element.18, f32[16,8,3,1,16]{4,1,0,3,2:T(8,128)S(1)} %concatenate.71, f32[16,8,3,4,16]{4,1,0,3,2:T(8,128)S(1)} %bitcast.224, f32[16,8,3,1,16]{4,1,0,3,2:T(8,128)S(1)} %concatenate.70, pred[]{:T(512)S(6)} %and.46), kind=kLoop, calls=%fused_computation.2 | loop fusion | flops 373248 | bytes 329473 | tf_op jit(solution)/shard_map/jit(_where)/select_n | solution.py:247
  5.9 0.7 collective-permute-start.6
  6.6 0.7 collective-permute-start.7
  7.3 1.4 collective-permute-start.8
  8.8 11.5 %collective-permute-start.1 = (f32[13312]{0:T(1024)S(1)}, f32[13312]{0:T(1024)S(1)}, u32[]{:S(2)}, u32[]{:S(2)}) collective-permute-start(f32[13312]{0:T(1024)S(1)} %pad_maximum_fusion.16), channel_id=1, source_target_pairs={{0,8},{8,16},{16,24},{24,32},{32,40},{40,48},{48,56},{56,64},{64,7... | collective-permute-start | bytes 159752 | tf_op jit(solution)/shard_map/ppermute | solution.py:126
  20.3 1.3 collective-permute-start
  21.6 0.7 and_convert_fusion.valid_ref
  22.3 8.6 %collective-permute-done = f32[13312]{0:T(1024)S(1)} collective-permute-done((f32[13312]{0:T(1024)S(1)}, f32[13312]{0:T(1024)S(1)}, u32[]{:S(2)}, u32[]{:S(2)}) %collective-permute-start) | collective-permute-done | bytes 53280 | tf_op jit(solution)/shard_map/ppermute | solution.py:126
  32.1 3.1 %collective-permute-start.2 = (f32[4576]{0:T(1024)S(1)}, f32[4576]{0:T(1024)S(1)}, u32[]{:S(2)}, u32[]{:S(2)}) collective-permute-start(f32[4576]{0:T(1024)S(1)} %pad_maximum_fusion.20), channel_id=1, source_target_pairs={{1,0},{2,1},{3,2},{4,3},{5,4},{6,5},{7,6},{9,8},{10,9},{11,10},{12... | collective-permute-start | bytes 54920 | tf_op jit(solution)/shard_map/ppermute | solution.py:126
  35.9 2.7 %collective-permute-start.3 = (f32[4576]{0:T(1024)S(1)}, f32[4576]{0:T(1024)S(1)}, u32[]{:S(2)}, u32[]{:S(2)}) collective-permute-start(f32[4576]{0:T(1024)S(1)} %pad_maximum_fusion.21), channel_id=1, source_target_pairs={{0,1},{1,2},{2,3},{3,4},{4,5},{5,6},{6,7},{8,9},{9,10},{10,11},{11... | collective-permute-start | bytes 54920 | tf_op jit(solution)/shard_map/ppermute | solution.py:126
  38.6 0.6 add_convert_fusion.edge_ref
  40.5 0.7 copy-done.10
  41.2 1.1 add_add_fusion
  42.3 0.6 copy.186
  42.9 1.5 %reshape.183 = f32[128,1,324]{2,1,0:T(1,128)} reshape(f32[128,3,6,18]{3,2,1,0:T(8,128)S(1)} %copy.186) | data formatting | bytes 331776
  44.5 11.7 %all-to-all-start = ((f32[128,1,324]{2,1,0:T(1,128)}), f32[128,1,324]{2,1,0:T(1,128)S(1)}, u32[]{:S(2)}, u32[]{:S(2)}) async-start(f32[128,1,324]{2,1,0:T(1,128)} %reshape.183), calls=%async_computation | async-start | bytes 393216 | tf_op jit(solution)/shard_map/all_to_all | solution.py:248
  56.4 1.0 copy.189.s_ref.draw_ref
  57.5 2.6 %collective-permute-start.4 = (f32[3,2,40,256]{3,2,0,1:T(8,128)S(1)}, f32[3,2,40,256]{3,2,0,1:T(8,128)S(1)}, u32[]{:S(2)}, u32[]{:S(2)}) collective-permute-start(f32[3,2,40,256]{3,2,0,1:T(8,128)S(1)} %slice.337), channel_id=1, source_target_pairs={{0,128},{128,256},{256,384},{1,129},{129,257},{257,385},{2,130},{1... | collective-permute-start | bytes 737288 | tf_op jit(solution)/shard_map/ppermute | solution.py:126
  60.1 1.3 collective-permute-start.5
  61.4 0.8 slice_bitcast_fusion.2
  62.2 1.3 collective-permute-start.10
  63.5 4.9 %collective-permute-start.9 = (f32[8,40,256]{2,1,0:T(8,128)S(1)}, f32[8,40,256]{2,1,0:T(8,128)S(1)}, u32[]{:S(2)}, u32[]{:S(2)}) collective-permute-start(f32[8,40,256]{2,1,0:T(8,128)S(1)} %get-tuple-element.21), channel_id=1, source_target_pairs={{0,128},{128,256},{256,384},{1,129},{129,257},{257,385},{2,130},{1... | collective-permute-start | bytes 983048 | tf_op jit(solution)/shard_map/ppermute | solution.py:126
  68.4 0.7 copy.190.b_ref
  69.1 1.3 collective-permute-done.5
  70.4 0.7 copy.191.a_ref
  71.1 2.3 %all-to-all-done = f32[128,1,324]{2,1,0:T(1,128)S(1)} async-done(((f32[128,1,324]{2,1,0:T(1,128)}), f32[128,1,324]{2,1,0:T(1,128)S(1)}, u32[]{:S(2)}, u32[]{:S(2)}) %all-to-all-start) | async-done | bytes 165920 | tf_op jit(solution)/shard_map/all_to_all | solution.py:248
  73.9 1.1 reduce.4
  76.1 0.8 pad_maximum_fusion.13.film_ref
  77.4 0.7 copy-done.2
  78.1 0.7 copy-done.3
  78.9 4.4 %shard_map.77.s_ref = f32[3,2,40,256]{3,2,1,0:T(8,128)} custom-call(f32[27]{0:T(128)} %reshape.158.k_ref, f32[2]{0:T(128)} %add_convert_fusion.edge_ref, f32[11,2,40,256]{3,2,1,0:T(8,128)} %copy.189.s_ref.draw_ref, f32[3,2,40,256]{3,2,1,0:T(8,128)} %copy.190.b_ref, f32[3,2,40,256]{3,2,1,0:T(8,128)} %copy.191.a_ref, ...), custom_call_target="tpu_custom_call" | custom-call | flops 12288000 | bytes 2457600 | tf_op jit(solution)/shard_map/pallas_call | solution.py:114
  83.3 4.3 %collective-permute-start.11 = (f32[3,2,40,256]{3,2,1,0:T(8,128)}, f32[3,2,40,256]{3,2,1,0:T(8,128)S(1)}, u32[]{:S(2)}, u32[]{:S(2)}) collective-permute-start(f32[3,2,40,256]{3,2,1,0:T(8,128)} %shard_map.77.s_ref), channel_id=1, source_target_pairs={{0,128},{128,256},{256,384},{1,129},{129,257},{257,385},{2,130},{1... | collective-permute-start | bytes 737288 | tf_op jit(solution)/shard_map/ppermute | solution.py:126
  87.6 1.5 %collective-permute-start.12 = (f32[3,2,40,256]{3,2,1,0:T(8,128)}, f32[3,2,40,256]{3,2,1,0:T(8,128)S(1)}, u32[]{:S(2)}, u32[]{:S(2)}) collective-permute-start(f32[3,2,40,256]{3,2,1,0:T(8,128)} %shard_map.77.s_ref), channel_id=1, source_target_pairs={{128,0},{256,128},{384,256},{129,1},{257,129},{385,257},{130,2},{2... | collective-permute-start | bytes 737288 | tf_op jit(solution)/shard_map/ppermute | solution.py:126
  89.4 0.8 slice.352
  90.9 1.3 collective-permute-done.11.b_ref
  92.2 3.7 %collective-permute-done.12.a_ref = f32[3,2,40,256]{3,2,1,0:T(8,128)S(1)} collective-permute-done((f32[3,2,40,256]{3,2,1,0:T(8,128)}, f32[3,2,40,256]{3,2,1,0:T(8,128)S(1)}, u32[]{:S(2)}, u32[]{:S(2)}) %collective-permute-start.12) | collective-permute-done | bytes 245792 | tf_op jit(solution)/shard_map/ppermute | solution.py:126
  96.0 0.7 copy-done.9
  96.7 4.2 %shard_map.78 = f32[3,2,40,256]{3,2,1,0:T(8,128)} custom-call(f32[27]{0:T(128)} %reshape.158.k_ref, f32[2]{0:T(128)} %add_convert_fusion.edge_ref, f32[3,2,40,256]{3,2,1,0:T(8,128)} %shard_map.77.s_ref, f32[3,2,40,256]{3,2,1,0:T(8,128)} %copy-done.8, f32[3,2,40,256]{3,2,1,0:T(8,128)} %copy-done.9, f32[3,40,256]{2,1,0:T(8,128)} %pad_maximum_fusion.13.film_ref, ...), custom_call_target="tpu_custom_call" | custom-call | flops 12288000 | bytes 2457600 | tf_op jit(solution)/shard_map/pallas_call | solution.py:114
  100.9 0.8 slice.358
  102.4 1.3 reshape.185
  103.7 16.0 %all-to-all-start.1 = ((f32[128,1,192]{2,1,0:T(1,128)}), f32[128,1,192]{2,1,0:T(1,128)S(1)}, u32[]{:S(2)}, u32[]{:S(2)}) async-start(f32[128,1,192]{2,1,0:T(1,128)} %reshape.185), calls=%async_computation.1 | async-start | bytes 262144 | tf_op jit(solution)/shard_map/all_to_all | solution.py:40
  119.7 1.5 %slice.351 = f32[3,2,32,128]{3,2,1,0:T(8,128)} slice(f32[3,2,40,256]{3,2,1,0:T(8,128)} %shard_map.78), slice={[0:3], [0:2], [0:32], [0:128]} | slice | bytes 196608 | tf_op jit(solution)/shard_map/slice | solution.py:283
  121.2 14.4 %all-to-all-done.1 = f32[128,1,192]{2,1,0:T(1,128)S(1)} async-done(((f32[128,1,192]{2,1,0:T(1,128)}), f32[128,1,192]{2,1,0:T(1,128)S(1)}, u32[]{:S(2)}, u32[]{:S(2)}) %all-to-all-start.1) | async-done | bytes 98336 | tf_op jit(solution)/shard_map/all_to_all | solution.py:40
  135.6 0.9 reduce.5
  137.4 1.0 fusion.4
  141.0 0.8 broadcast_divide_fusion
  (127 shorter events, 11.6 us)
Async XLA Ops:
  5.5 3.2 %copy-start = (f32[3,128,256]{2,1,0:T(8,128)S(1)}, f32[3,128,256]{2,1,0:T(8,128)}, u32[]{:S(2)}) copy-start(f32[3,128,256]{2,1,0:T(8,128)} %param.10) | copy-start | bytes 1179652
  5.5 3.1 %copy-start.1 = (f32[128,256]{1,0:T(8,128)S(1)}, f32[128,256]{1,0:T(8,128)}, u32[]{:S(2)}) copy-start(f32[128,256]{1,0:T(8,128)} %param.11) | copy-start | bytes 393220
  5.5 3.2 %copy-start.11 = (f32[2,3,2,32,128]{4,3,2,1,0:T(8,128)S(1)}, f32[2,3,2,32,128]{4,3,2,1,0:T(8,128)}, u32[]{:S(2)}) copy-start(f32[2,3,2,32,128]{4,3,2,1,0:T(8,128)} %param.8) | copy-start | bytes 589828
  5.5 3.2 %copy-start.4 = (f32[3,2,32,128]{3,2,1,0:T(8,128)S(1)}, f32[3,2,32,128]{3,2,1,0:T(8,128)}, u32[]{:S(2)}) copy-start(f32[3,2,32,128]{3,2,1,0:T(8,128)} %param.6) | copy-start | bytes 294916
  5.5 3.2 %copy-start.6 = (f32[2,2,32,128]{3,2,1,0:T(8,128)S(1)}, f32[2,2,32,128]{3,2,1,0:T(8,128)}, u32[]{:S(2)}) copy-start(f32[2,2,32,128]{3,2,1,0:T(8,128)} %param.7) | copy-start | bytes 196612
  5.9 34.6 %collective-permute-start.6 = (f32[128,3,6,18]{0,3,2,1:T(8,128)S(1)}, f32[128,3,6,18]{0,3,2,1:T(8,128)S(1)}, u32[]{:S(2)}, u32[]{:S(2)}) collective-permute-start(f32[128,3,6,18]{0,3,2,1:T(8,128)S(1)} %copy.183), channel_id=1, source_target_pairs={{0,128}} | collective-permute-start | bytes 497672 | tf_op jit(solution)/shard_map/ppermute | solution.py:34
  6.6 33.9 %collective-permute-start.7 = (f32[128,3,6,18]{0,3,2,1:T(8,128)S(1)}, f32[128,3,6,18]{0,3,2,1:T(8,128)S(1)}, u32[]{:S(2)}, u32[]{:S(2)}) collective-permute-start(f32[128,3,6,18]{0,3,2,1:T(8,128)S(1)} %copy.183), channel_id=1, source_target_pairs={{0,256}} | collective-permute-start | bytes 497672 | tf_op jit(solution)/shard_map/ppermute | solution.py:34
  7.3 34.0 %collective-permute-start.8 = (f32[128,3,6,18]{0,3,2,1:T(8,128)S(1)}, f32[128,3,6,18]{0,3,2,1:T(8,128)}, u32[]{:S(2)}, u32[]{:S(2)}) collective-permute-start(f32[128,3,6,18]{0,3,2,1:T(8,128)S(1)} %copy.183), channel_id=1, source_target_pairs={{0,384}} | collective-permute-start | bytes 497672 | tf_op jit(solution)/shard_map/ppermute | solution.py:34
  8.8 13.5 %collective-permute-start.1 = (f32[13312]{0:T(1024)S(1)}, f32[13312]{0:T(1024)S(1)}, u32[]{:S(2)}, u32[]{:S(2)}) collective-permute-start(f32[13312]{0:T(1024)S(1)} %pad_maximum_fusion.16), channel_id=1, source_target_pairs={{0,8},{8,16},{16,24},{24,32},{32,40},{40,48},{48,56},{56,64},{64,7... | collective-permute-start | bytes 159752 | tf_op jit(solution)/shard_map/ppermute | solution.py:126
  20.3 10.6 %collective-permute-start = (f32[13312]{0:T(1024)S(1)}, f32[13312]{0:T(1024)S(1)}, u32[]{:S(2)}, u32[]{:S(2)}) collective-permute-start(f32[13312]{0:T(1024)S(1)} %pad_maximum_fusion.15), channel_id=1, source_target_pairs={{8,0},{16,8},{24,16},{32,24},{40,32},{48,40},{56,48},{64,56},{72,6... | collective-permute-start | bytes 159752 | tf_op jit(solution)/shard_map/ppermute | solution.py:126
  31.6 7.6 %copy-start.13 = (f32[3,3,3]{2,1,0:T(4,128)S(1)}, f32[3,3,3]{2,1,0:T(4,128)}, u32[]{:S(2)}) copy-start(f32[3,3,3]{2,1,0:T(4,128)} %param.9) | copy-start | bytes 328
  32.1 7.7 %collective-permute-start.2 = (f32[4576]{0:T(1024)S(1)}, f32[4576]{0:T(1024)S(1)}, u32[]{:S(2)}, u32[]{:S(2)}) collective-permute-start(f32[4576]{0:T(1024)S(1)} %pad_maximum_fusion.20), channel_id=1, source_target_pairs={{1,0},{2,1},{3,2},{4,3},{5,4},{6,5},{7,6},{9,8},{10,9},{11,10},{12... | collective-permute-start | bytes 54920 | tf_op jit(solution)/shard_map/ppermute | solution.py:126
  35.9 4.3 %collective-permute-start.3 = (f32[4576]{0:T(1024)S(1)}, f32[4576]{0:T(1024)S(1)}, u32[]{:S(2)}, u32[]{:S(2)}) collective-permute-start(f32[4576]{0:T(1024)S(1)} %pad_maximum_fusion.21), channel_id=1, source_target_pairs={{0,1},{1,2},{2,3},{3,4},{4,5},{5,6},{6,7},{8,9},{9,10},{10,11},{11... | collective-permute-start | bytes 54920 | tf_op jit(solution)/shard_map/ppermute | solution.py:126
  40.1 1.1 copy-start.12
  40.5 0.7 copy-start.10
  42.9 13.3 %copy-start.5 = (f32[3,2,32,128]{3,2,1,0:T(8,128)S(1)}, f32[3,2,32,128]{3,2,1,0:T(8,128)}, u32[]{:S(2)}) copy-start(f32[3,2,32,128]{3,2,1,0:T(8,128)} %param.6) | copy-start | bytes 294916
  42.9 13.3 %copy-start.7 = (f32[2,2,32,128]{3,2,1,0:T(8,128)S(1)}, f32[2,2,32,128]{3,2,1,0:T(8,128)}, u32[]{:S(2)}) copy-start(f32[2,2,32,128]{3,2,1,0:T(8,128)} %param.7) | copy-start | bytes 196612
  44.5 28.9 %all-to-all-start = ((f32[128,1,324]{2,1,0:T(1,128)}), f32[128,1,324]{2,1,0:T(1,128)S(1)}, u32[]{:S(2)}, u32[]{:S(2)}) async-start(f32[128,1,324]{2,1,0:T(1,128)} %reshape.183), calls=%async_computation | async-start | bytes 393216 | tf_op jit(solution)/shard_map/all_to_all | solution.py:248
  57.5 10.9 %collective-permute-start.4 = (f32[3,2,40,256]{3,2,0,1:T(8,128)S(1)}, f32[3,2,40,256]{3,2,0,1:T(8,128)S(1)}, u32[]{:S(2)}, u32[]{:S(2)}) collective-permute-start(f32[3,2,40,256]{3,2,0,1:T(8,128)S(1)} %slice.337), channel_id=1, source_target_pairs={{0,128},{128,256},{256,384},{1,129},{129,257},{257,385},{2,130},{1... | collective-permute-start | bytes 737288 | tf_op jit(solution)/shard_map/ppermute | solution.py:126
  60.1 10.3 %collective-permute-start.5 = (f32[3,2,40,256]{3,2,0,1:T(8,128)S(1)}, f32[3,2,40,256]{3,2,0,1:T(8,128)S(1)}, u32[]{:S(2)}, u32[]{:S(2)}) collective-permute-start(f32[3,2,40,256]{3,2,0,1:T(8,128)S(1)} %slice.337), channel_id=1, source_target_pairs={{128,0},{256,128},{384,256},{129,1},{257,129},{385,257},{130,2},{2... | collective-permute-start | bytes 737288 | tf_op jit(solution)/shard_map/ppermute | solution.py:126
  62.2 15.2 %collective-permute-start.10 = (f32[8,40,256]{2,1,0:T(8,128)}, f32[8,40,256]{2,1,0:T(8,128)S(1)}, u32[]{:S(2)}, u32[]{:S(2)}) collective-permute-start(f32[8,40,256]{2,1,0:T(8,128)} %get-tuple-element.20), channel_id=1, source_target_pairs={{128,0},{256,128},{384,256},{129,1},{257,129},{385,257},{130,2},{2... | collective-permute-start | bytes 983048 | tf_op jit(solution)/shard_map/ppermute | solution.py:126
  63.5 13.9 %collective-permute-start.9 = (f32[8,40,256]{2,1,0:T(8,128)S(1)}, f32[8,40,256]{2,1,0:T(8,128)S(1)}, u32[]{:S(2)}, u32[]{:S(2)}) collective-permute-start(f32[8,40,256]{2,1,0:T(8,128)S(1)} %get-tuple-element.21), channel_id=1, source_target_pairs={{0,128},{128,256},{256,384},{1,129},{129,257},{257,385},{2,130},{1... | collective-permute-start | bytes 983048 | tf_op jit(solution)/shard_map/ppermute | solution.py:126
  77.4 0.7 copy-start.2
  78.1 0.7 copy-start.3
  83.3 8.9 %collective-permute-start.11 = (f32[3,2,40,256]{3,2,1,0:T(8,128)}, f32[3,2,40,256]{3,2,1,0:T(8,128)S(1)}, u32[]{:S(2)}, u32[]{:S(2)}) collective-permute-start(f32[3,2,40,256]{3,2,1,0:T(8,128)} %shard_map.77.s_ref), channel_id=1, source_target_pairs={{0,128},{128,256},{256,384},{1,129},{129,257},{257,385},{2,130},{1... | collective-permute-start | bytes 737288 | tf_op jit(solution)/shard_map/ppermute | solution.py:126
  87.6 8.3 %collective-permute-start.12 = (f32[3,2,40,256]{3,2,1,0:T(8,128)}, f32[3,2,40,256]{3,2,1,0:T(8,128)S(1)}, u32[]{:S(2)}, u32[]{:S(2)}) collective-permute-start(f32[3,2,40,256]{3,2,1,0:T(8,128)} %shard_map.77.s_ref), channel_id=1, source_target_pairs={{128,0},{256,128},{384,256},{129,1},{257,129},{385,257},{130,2},{2... | collective-permute-start | bytes 737288 | tf_op jit(solution)/shard_map/ppermute | solution.py:126
  92.2 3.7 %copy-start.8 = (f32[3,2,40,256]{3,2,1,0:T(8,128)}, f32[3,2,40,256]{3,2,1,0:T(8,128)S(1)}, u32[]{:S(2)}) copy-start(f32[3,2,40,256]{3,2,1,0:T(8,128)S(1)} %collective-permute-done.11.b_ref) | copy-start | bytes 737284
  96.0 0.7 copy-start.9
  103.7 31.9 %all-to-all-start.1 = ((f32[128,1,192]{2,1,0:T(1,128)}), f32[128,1,192]{2,1,0:T(1,128)S(1)}, u32[]{:S(2)}, u32[]{:S(2)}) async-start(f32[128,1,192]{2,1,0:T(1,128)} %reshape.185), calls=%async_computation.1 | async-start | bytes 262144 | tf_op jit(solution)/shard_map/all_to_all | solution.py:40
